TPU v7x, 32 devices: a whole 2x2x4 slice. The times are simulated.
32 devices in a mesh: tm: 8 (over y, x, core), night: 4 (over z).
Axes of the slice: x: 2, y: 2, z: 4, core: 2. Of those that a mesh axis runs over, the one named last changes fastest.
Arguments:
- patches: bfloat16 [4, 2048, 1024], P('night', 'tm'), may hold values from -6 to 6
- weights: bfloat16 [1024, 4, 512], replicated, may hold values from -0.1875 to 0.1875
- cotangent: bfloat16 [4, 2048, 1024], P('night', 'tm'), may hold values from -6 to 6
- loss_mask: int32 [4, 2048], P('night', 'tm'), may hold values from 0 to 1, as said below
Outputs:
- grad_input: bfloat16 [4, 2048, 1024], P('night', 'tm')
- grad_weights: float32 [1024, 4, 512], P(('tm', 'night'))
Inputs may be any that keep to these rules, and one draw needn't show every extreme that they name: `loss_mask`: 1 marks a masked patch; the last patch of every night is always 1.
All inputs are finite; a program needn't handle non-finite values.
Results may differ from a plain program's by a relative error of at most 0.0094.
Values may be sent and summed in bfloat16 or wider, within the bound.
No kernel may reach another device: no remote copies, remote signals or barrier semaphores. Data moves between devices by JAX's collectives and lax.ppermute only.
A program may use at most 128 MiB of HBM per device.

v0:
```python
import math

import jax
import jax.numpy as jnp
from jax import lax
from jax.sharding import PartitionSpec as P

HEADS = 8
HSIZE = 64
WIN = 1024


def shifted(value, axis, by):
    peers = lax.axis_size(axis)
    pairs = [(i, i + by) for i in range(peers) if 0 <= i + by < peers]
    return lax.ppermute(value, axis, pairs)


def band_block(queries, keys_blk, values_blk, grad_attn, valid, inv_scale):
    scores = (
        jnp.einsum("qgc,kgc->gqk", queries, keys_blk, preferred_element_type=jnp.float32)
        * inv_scale
    )
    exp_terms = jnp.exp(scores) * valid[None]
    probs = exp_terms / jnp.sum(exp_terms, axis=-1, keepdims=True)
    probs_low = probs.astype(jnp.bfloat16)
    attended = jnp.einsum(
        "gqk,kgc->qgc", probs_low, values_blk, preferred_element_type=jnp.float32
    ).astype(jnp.bfloat16)
    delta = jnp.sum(grad_attn.astype(jnp.float32) * attended.astype(jnp.float32), axis=-1)
    grad_probs = jnp.einsum(
        "qgc,kgc->gqk", grad_attn, values_blk, preferred_element_type=jnp.float32
    )
    grad_scores = (probs * (grad_probs - jnp.transpose(delta)[:, :, None]) * inv_scale).astype(
        jnp.bfloat16
    )
    grad_query = jnp.einsum(
        "gqk,kgc->qgc", grad_scores, keys_blk, preferred_element_type=jnp.float32
    )
    grad_key = jnp.einsum("gqk,qgc->kgc", grad_scores, queries, preferred_element_type=jnp.float32)
    grad_value = jnp.einsum(
        "gqk,qgc->kgc", probs_low, grad_attn, preferred_element_type=jnp.float32
    )
    return (attended, grad_query, grad_key, grad_value)


def shards(patches, weights, cotangent, loss_mask):
    rows = patches.shape[1]
    width = patches.shape[2]
    inner = weights.shape[2]
    span = (WIN + rows - 2) // rows
    block_rows = min(512, rows)
    key_len = block_rows + span * rows
    group = max(1, min(HEADS, 128 // HSIZE))
    group_cols = group * HSIZE
    inv_scale = 1.0 / math.sqrt(HSIZE)
    local_in = patches[0].astype(jnp.float32)
    inv_rms = lax.rsqrt(jnp.mean(local_in * local_in, axis=-1) + 1e-06)
    normed_full = local_in * inv_rms[:, None]
    normed = normed_full.astype(jnp.bfloat16)
    proj_weights = weights[:, :3, :]
    projected = jnp.einsum(
        "rd,dwh->wrh", normed, proj_weights, preferred_element_type=jnp.float32
    ).astype(jnp.bfloat16)
    queries = projected[0]
    key_vals = projected[1:]
    earlier = [shifted(key_vals, "tm", offset) for offset in range(span, 0, -1)]
    extended = jnp.concatenate(earlier + [key_vals], axis=1)
    local_count = jnp.sum(loss_mask.astype(jnp.float32))
    total_count = lax.psum(local_count, ("tm", "night"))
    tokens_all = rows * lax.axis_size("tm") * lax.axis_size("night")
    loss_scale = jnp.float32(tokens_all) / total_count
    local_cot = cotangent[0]
    grad_out = jnp.where(loss_mask[0][:, None] > 0, local_cot, jnp.zeros_like(local_cot))
    grad_attn = jnp.dot(grad_out, weights[:, 3, :], preferred_element_type=jnp.float32).astype(
        jnp.bfloat16
    )
    base = lax.axis_index("tm") * rows
    query_idx = jnp.arange(block_rows, dtype=jnp.int32)[:, None]
    key_idx = jnp.arange(key_len, dtype=jnp.int32)[None, :]
    offsets = query_idx - key_idx + span * rows
    band = (offsets >= 0) & (offsets < WIN)
    attended_cols = []
    grad_q_cols = []
    grad_kv_cols = []
    for first in range(0, inner, group_cols):
        accum = jnp.zeros((2, (span + 1) * rows, group_cols), jnp.float32)
        valid = (band & (key_idx >= span * rows - base - 0)).astype(jnp.float32)
        query_blk = queries[0:block_rows, first : first + group_cols].reshape(
            block_rows, group, HSIZE
        )
        kv_blk = extended[:, 0:key_len, first : first + group_cols].reshape(
            2, key_len, group, HSIZE
        )
        grad_blk = grad_attn[0:block_rows, first : first + group_cols].reshape(
            block_rows, group, HSIZE
        )
        attended, grad_query, grad_key, grad_value = band_block(
            query_blk, kv_blk[0], kv_blk[1], grad_blk, valid, inv_scale
        )
        attended_rows = attended.reshape(block_rows, group_cols)
        grad_q_rows = grad_query.reshape(block_rows, group_cols).astype(jnp.bfloat16)
        update = jnp.stack([grad_key, grad_value]).reshape(2, key_len, group_cols)
        accum = accum.at[:, 0:key_len].add(update)
        attended_cols.append(attended_rows)
        grad_q_cols.append(grad_q_rows)
        grad_kv_cols.append(accum)
    attended_all = jnp.concatenate(attended_cols, axis=1)
    grad_q = jnp.concatenate(grad_q_cols, axis=1)
    grad_kv_ext = jnp.concatenate(grad_kv_cols, axis=2)
    owned = grad_kv_ext[:, span * rows :]
    for offset in range(1, span + 1):
        lower = (span - offset) * rows
        owned = owned + shifted(
            grad_kv_ext[:, lower : lower + rows].astype(jnp.bfloat16), "tm", -offset
        ).astype(jnp.float32)
    grad_kv = owned.astype(jnp.bfloat16)
    grad_proj = jnp.concatenate([grad_q[None], grad_kv], axis=0)
    grad_normed = jnp.einsum(
        "wrh,dwh->rd", grad_proj, proj_weights, preferred_element_type=jnp.float32
    )
    along = jnp.sum(grad_normed * normed_full, axis=-1) / width
    grad_input = (
        loss_scale * inv_rms[:, None] * (grad_normed - normed_full * along[:, None])
    ).astype(jnp.bfloat16)
    proj_part = jnp.einsum("rd,wrh->dwh", normed, grad_proj, preferred_element_type=jnp.float32)
    out_part = jnp.einsum("rd,rh->dh", grad_out, attended_all, preferred_element_type=jnp.float32)
    summed = lax.psum_scatter(
        jnp.concatenate([proj_part, out_part[:, None]], axis=1),
        ("tm", "night"),
        scatter_dimension=0,
        tiled=True,
    )
    grad_weights = summed * (jnp.sqrt(jnp.float32(tokens_all)) / total_count)
    return (grad_input[None], grad_weights)


def solution(mesh):
    return jax.shard_map(
        shards,
        mesh=mesh,
        in_specs=(P("night", "tm", None), P(), P("night", "tm", None), P("night", "tm")),
        out_specs=(P("night", "tm", None), P(("tm", "night"), None, None)),
        check_vma=False,
    )
```

profile of v0, /device:TPU:0, one launch (start us, length us, event | category | flops | bytes accessed | tf_op | source)
XLA Modules:
  0.0 393.2 jit_solution(9651668186456590301)
XLA Ops:
  8.5 42.2 %psum.7 = f32[]{:T(128)} all-reduce(f32[]{:T(128)} %convert_reduce_fusion), channel_id=1, replica_groups=mesh['tm'=8,'night'=4] {'tm','night'}, use_global_device_ids=true, to_apply=%region_1.0 | all-reduce | flops 1 | bytes 8 | tf_op jit(solution)/shard_map/psum | solution.py:70
  52.6 3.7 fusion.46
  57.2 2.1 collective-permute-start.3
  59.3 4.8 %collective-permute-start.2 = (bf16[2,256,512]{2,1,0:T(8,128)(2,1)}, bf16[2,256,512]{2,1,0:T(8,128)(2,1)}, u32[]{:S(2)}, u32[]{:S(2)}) collective-permute-start(bf16[2,256,512]{2,1,0:T(8,128)(2,1)} %slice.200), channel_id=1, source_target_pairs={{0,8},{4,12},{8,16},{12,20},{16,24},{20,28},{1,9},{5,13},{9,17},{1... | collective-permute-start | bytes 1572872 | tf_op jit(solution)/shard_map/ppermute | solution.py:16
  64.1 3.6 collective-permute-start.1
  67.7 2.1 collective-permute-start
  69.8 2.2 slice.180
  78.9 18.2 %collective-permute-done = bf16[2,256,512]{2,1,0:T(8,128)(2,1)} collective-permute-done((bf16[2,256,512]{2,1,0:T(8,128)(2,1)}, bf16[2,256,512]{2,1,0:T(8,128)(2,1)}, u32[]{:S(2)}, u32[]{:S(2)}) %collective-permute-start) | collective-permute-done | bytes 524320 | tf_op jit(solution)/shard_map/ppermute | solution.py:16
  101.5 1.4 fusion.95
  104.0 2.3 fusion.40
  113.1 2.3 fusion.38
  122.2 2.3 fusion.36
  130.8 2.3 fusion.34
  139.4 2.2 copy.81
  142.8 2.2 copy.83
  146.3 2.2 copy.85
  152.9 1.4 collective-permute-start.4
  159.3 2.7 collective-permute-done.4
  162.0 4.6 %collective-permute-done.7 = bf16[2,256,512]{2,1,0:T(8,128)(2,1)S(1)} collective-permute-done((bf16[2,256,512]{2,1,0:T(8,128)(2,1)S(1)}, bf16[2,256,512]{2,1,0:T(8,128)(2,1)S(1)}, u32[]{:S(2)}, u32[]{:S(2)}) %collective-permute-start.7) | collective-permute-done | bytes 524320 | tf_op jit(solution)/shard_map/ppermute | solution.py:16
  166.6 1.9 collective-permute-done.6
  168.5 14.5 %collective-permute-done.5 = bf16[2,256,512]{2,1,0:T(8,128)(2,1)S(1)} collective-permute-done((bf16[2,256,512]{2,1,0:T(8,128)(2,1)S(1)}, bf16[2,256,512]{2,1,0:T(8,128)(2,1)S(1)}, u32[]{:S(2)}, u32[]{:S(2)}) %collective-permute-start.5) | collective-permute-done | bytes 524320 | tf_op jit(solution)/shard_map/ppermute | solution.py:16
  184.5 4.2 %pad_maximum_fusion = f32[1024,4,512]{2,0,1:T(8,128)} fusion(f32[1024,1,512]{2,0,1:T(8,128)S(1)} %convolution_bitcast_fusion, f32[1024,3,512]{2,0,1:T(8,128)S(1)} %fusion.76), kind=kLoop, calls=%fused_computation | loop fusion | flops 2097152 | bytes 16777216 | tf_op jit(solution)/shard_map/concatenate | solution.py:129
  189.4 3.5 fusion.49
  194.0 190.5 %reduce-scatter.2.cloned.1.call-done = f32[32,4,512]{2,0,1:T(8,128)} async-done(((f32[1024,4,512]{2,0,1:T(8,128)}), f32[32,4,512]{2,0,1:T(8,128)}) %reduce-scatter.2.cloned.1.call-update) | async-done | bytes 262160 | tf_op jit(solution)/shard_map/reduce_scatter | solution.py:128
  (152 shorter events, 57.8 us)
Async XLA Ops:
  7.2 377.3 %reduce-scatter.2.cloned.1.call-start = ((), (), s32[]{:S(2)}) async-start(), calls=%async_computation.1 | async-start | bytes 8650752 | tf_op jit(solution)/shard_map/reduce_scatter | solution.py:128
  52.6 17.2 %copy-start.34 = (s32[1,256]{1,0:T(1,128)S(1)}, s32[1,256]{1,0:T(1,128)}, u32[]{:S(2)}) copy-start(s32[1,256]{1,0:T(1,128)} %param.23) | copy-start | bytes 3076
  52.6 17.2 %copy-start.21 = (bf16[1024,4,512]{2,1,0:T(4,128)(2,1)S(1)}, bf16[1024,4,512]{2,1,0:T(4,128)(2,1)}, u32[]{:S(2)}) copy-start(bf16[1024,4,512]{2,1,0:T(4,128)(2,1)} %param.21) | copy-start | bytes 12582916
  57.2 43.2 %collective-permute-start.3 = (bf16[2,256,512]{2,1,0:T(8,128)(2,1)}, bf16[2,256,512]{2,1,0:T(8,128)(2,1)}, u32[]{:S(2)}, u32[]{:S(2)}) collective-permute-start(bf16[2,256,512]{2,1,0:T(8,128)(2,1)} %slice.200), channel_id=1, source_target_pairs={{0,4},{4,8},{8,12},{12,16},{16,20},{20,24},{24,28},{1,5},{5,9},{9,... | collective-permute-start | bytes 1572872 | tf_op jit(solution)/shard_map/ppermute | solution.py:16
  59.3 40.0 %collective-permute-start.2 = (bf16[2,256,512]{2,1,0:T(8,128)(2,1)}, bf16[2,256,512]{2,1,0:T(8,128)(2,1)}, u32[]{:S(2)}, u32[]{:S(2)}) collective-permute-start(bf16[2,256,512]{2,1,0:T(8,128)(2,1)} %slice.200), channel_id=1, source_target_pairs={{0,8},{4,12},{8,16},{12,20},{16,24},{20,28},{1,9},{5,13},{9,17},{1... | collective-permute-start | bytes 1572872 | tf_op jit(solution)/shard_map/ppermute | solution.py:16
  64.1 34.1 %collective-permute-start.1 = (bf16[2,256,512]{2,1,0:T(8,128)(2,1)}, bf16[2,256,512]{2,1,0:T(8,128)(2,1)}, u32[]{:S(2)}, u32[]{:S(2)}) collective-permute-start(bf16[2,256,512]{2,1,0:T(8,128)(2,1)} %slice.200), channel_id=1, source_target_pairs={{0,12},{4,16},{8,20},{12,24},{16,28},{1,13},{5,17},{9,21},{13,25},... | collective-permute-start | bytes 1572872 | tf_op jit(solution)/shard_map/ppermute | solution.py:16
  67.7 29.4 %collective-permute-start = (bf16[2,256,512]{2,1,0:T(8,128)(2,1)}, bf16[2,256,512]{2,1,0:T(8,128)(2,1)}, u32[]{:S(2)}, u32[]{:S(2)}) collective-permute-start(bf16[2,256,512]{2,1,0:T(8,128)(2,1)} %slice.200), channel_id=1, source_target_pairs={{0,16},{4,20},{8,24},{12,28},{1,17},{5,21},{9,25},{13,29},{2,18},{... | collective-permute-start | bytes 1572872 | tf_op jit(solution)/shard_map/ppermute | solution.py:16
  118.7 3.5 copy-start.25
  137.6 4.0 %copy-start.29 = (bf16[2,64,256]{2,1,0:T(8,128)(2,1)S(1)}, bf16[2,64,256]{2,1,0:T(8,128)(2,1)}, u32[]{:S(2)}) copy-start(bf16[2,64,256]{2,1,0:T(8,128)(2,1)} %convolution_convert_fusion.5) | copy-start | bytes 196612
  137.6 4.1 %copy-start.2 = (f32[2,64,1280]{2,1,0:T(8,128)S(1)}, f32[2,64,1280]{2,1,0:T(8,128)}, u32[]{:S(2)}) copy-start(f32[2,64,1280]{2,1,0:T(8,128)} %fusion.64) | copy-start | bytes 1966084
  139.2 6.0 %copy-start.3 = (f32[2,64,1280]{2,1,0:T(8,128)S(1)}, f32[2,64,1280]{2,1,0:T(8,128)}, u32[]{:S(2)}) copy-start(f32[2,64,1280]{2,1,0:T(8,128)} %fusion.61) | copy-start | bytes 1966084
  141.7 7.7 %copy-start.4 = (f32[2,64,1280]{2,1,0:T(8,128)S(1)}, f32[2,64,1280]{2,1,0:T(8,128)}, u32[]{:S(2)}) copy-start(f32[2,64,1280]{2,1,0:T(8,128)} %fusion.58) | copy-start | bytes 1966084
  142.8 7.7 %copy-start.5 = (f32[1,1,1280,128]{3,2,1,0:T(8,128)S(1)}, f32[1,1,1280,128]{3,2,1,0:T(8,128)}, u32[]{:S(2)}) copy-start(f32[1,1,1280,128]{3,2,1,0:T(8,128)} %copy.81) | copy-start | bytes 1966084
  146.3 4.3 %copy-start.7 = (f32[1,1,1280,128]{3,2,1,0:T(8,128)S(1)}, f32[1,1,1280,128]{3,2,1,0:T(8,128)}, u32[]{:S(2)}) copy-start(f32[1,1,1280,128]{3,2,1,0:T(8,128)} %copy.82) | copy-start | bytes 1966084
  152.7 5.5 %copy-start.23 = (bf16[1,256,1024]{2,1,0:T(8,128)(2,1)S(1)}, bf16[1,256,1024]{2,1,0:T(8,128)(2,1)}, u32[]{:S(2)}) copy-start(bf16[1,256,1024]{2,1,0:T(8,128)(2,1)} %param.22) | copy-start | bytes 1572868
  152.7 5.5 %copy-start.30 = (bf16[2,64,256]{2,1,0:T(8,128)(2,1)S(1)}, bf16[2,64,256]{2,1,0:T(8,128)(2,1)}, u32[]{:S(2)}) copy-start(bf16[2,64,256]{2,1,0:T(8,128)(2,1)} %get-tuple-element.115) | copy-start | bytes 196612
  152.7 5.5 %copy-start.31 = (bf16[2,64,256]{2,1,0:T(8,128)(2,1)S(1)}, bf16[2,64,256]{2,1,0:T(8,128)(2,1)}, u32[]{:S(2)}) copy-start(bf16[2,64,256]{2,1,0:T(8,128)(2,1)} %get-tuple-element.113) | copy-start | bytes 196612
  152.7 5.5 %copy-start.32 = (bf16[2,64,256]{2,1,0:T(8,128)(2,1)S(1)}, bf16[2,64,256]{2,1,0:T(8,128)(2,1)}, u32[]{:S(2)}) copy-start(bf16[2,64,256]{2,1,0:T(8,128)(2,1)} %get-tuple-element.111) | copy-start | bytes 196612
  152.8 5.5 %copy-start.33 = (bf16[2,64,256]{2,1,0:T(8,128)(2,1)S(1)}, bf16[2,64,256]{2,1,0:T(8,128)(2,1)}, u32[]{:S(2)}) copy-start(bf16[2,64,256]{2,1,0:T(8,128)(2,1)} %get-tuple-element.109) | copy-start | bytes 196612
  152.9 9.1 %collective-permute-start.4 = (bf16[2,256,512]{2,1,0:T(8,128)(2,1)S(1)}, bf16[2,256,512]{2,1,0:T(8,128)(2,1)S(1)}, u32[]{:S(2)}, u32[]{:S(2)}) collective-permute-start(bf16[2,256,512]{2,1,0:T(8,128)(2,1)S(1)} %get-tuple-element.86), channel_id=1, source_target_pairs={{4,0},{8,4},{12,8},{16,12},{20,16},{24,20},{28,24},{5,1},{9,5},{13... | collective-permute-start | bytes 1572872 | tf_op jit(solution)/shard_map/ppermute | solution.py:16
  154.3 12.3 %collective-permute-start.7 = (bf16[2,256,512]{2,1,0:T(8,128)(2,1)S(1)}, bf16[2,256,512]{2,1,0:T(8,128)(2,1)S(1)}, u32[]{:S(2)}, u32[]{:S(2)}) collective-permute-start(bf16[2,256,512]{2,1,0:T(8,128)(2,1)S(1)} %get-tuple-element.87), channel_id=1, source_target_pairs={{16,0},{20,4},{24,8},{28,12},{17,1},{21,5},{25,9},{29,13},{18,2},{... | collective-permute-start | bytes 1572872 | tf_op jit(solution)/shard_map/ppermute | solution.py:16
  155.6 12.8 %collective-permute-start.6 = (bf16[2,256,512]{2,1,0:T(8,128)(2,1)S(1)}, bf16[2,256,512]{2,1,0:T(8,128)(2,1)S(1)}, u32[]{:S(2)}, u32[]{:S(2)}) collective-permute-start(bf16[2,256,512]{2,1,0:T(8,128)(2,1)S(1)} %get-tuple-element.88), channel_id=1, source_target_pairs={{12,0},{16,4},{20,8},{24,12},{28,16},{13,1},{17,5},{21,9},{25,13},... | collective-permute-start | bytes 1572872 | tf_op jit(solution)/shard_map/ppermute | solution.py:16
  156.9 26.1 %collective-permute-start.5 = (bf16[2,256,512]{2,1,0:T(8,128)(2,1)S(1)}, bf16[2,256,512]{2,1,0:T(8,128)(2,1)S(1)}, u32[]{:S(2)}, u32[]{:S(2)}) collective-permute-start(bf16[2,256,512]{2,1,0:T(8,128)(2,1)S(1)} %get-tuple-element.89), channel_id=1, source_target_pairs={{8,0},{12,4},{16,8},{20,12},{24,16},{28,20},{9,1},{13,5},{17,9},{2... | collective-permute-start | bytes 1572872 | tf_op jit(solution)/shard_map/ppermute | solution.py:16
  159.3 24.1 %copy-start = (bf16[1,256,1024]{2,1,0:T(8,128)(2,1)S(1)}, bf16[1,256,1024]{2,1,0:T(8,128)(2,1)}, u32[]{:S(2)}) copy-start(bf16[1,256,1024]{2,1,0:T(8,128)(2,1)} %param.20) | copy-start | bytes 1572868
  (20 other events, 40.8 us)
Sparse Core Ops, SparseCore 0:
  188.8 195.5 reduce-scatter.1
where the time goes:
time: 394 us; the launch traced here: 393 us
  waiting for transfers between devices  232 us (59%)
  blocking collectives  42.2 us (11%)
  matrix products  39.7 us (10%)
  local copies, waits for them, and re-layouts  33.7 us (9%)
  starting transfers between devices  17.9 us (5%)
  between operations  16 us (4%)
  other arithmetic  11.4 us (3%)
    reduce_scatter x1, waiting for transfers between devices, shards(): lax.psum_scatter(jnp.concatenate([proj_part, out_part[:, None]], axis=1),...  190 us
    psum x1, blocking collectives, shards(): total_count = lax.psum(local_count, ('tm', 'night'))  42.2 us
    ppermute x8, waiting for transfers between devices, shifted(): return lax.ppermute(value, axis, pairs)  41.9 us
    ppermute x8, starting transfers between devices, shifted(): return lax.ppermute(value, axis, pairs)  17.9 us
    another operation x8, local copies, waits for them, and re-layouts, shards(): update = jnp.stack([grad_key, grad_value]).reshape(2, key_len, group_cols)  10.3 us
    div x4, matrix products, band_block(): probs = exp_terms / jnp.sum(exp_terms, axis=-1, keepdims=True)  9.05 us
    unnamed x75, local copies, waits for them, and re-layouts  8.43 us
  transfers between devices with their start and end apart: 9, of which 6 were waited for; matrix products, arithmetic and copies ran while one was open for 5% of the time, Pallas kernels for 0%

commit v1 on v0

--- a/solution.py
+++ b/solution.py
@@ -14,6 +14,70 @@
     peers = lax.axis_size(axis)
     pairs = [(i, i + by) for i in range(peers) if 0 <= i + by < peers]
     return lax.ppermute(value, axis, pairs)
+
+
+def is_power_of_two(n):
+    return n > 0 and n & (n - 1) == 0
+
+
+def butterfly_sum(value, axes):
+    for axis in axes:
+        peers = lax.axis_size(axis)
+        flip = 1
+        while flip < peers:
+            pairs = [(i, i ^ flip) for i in range(peers)]
+            value = value + lax.ppermute(value, axis, pairs)
+            flip *= 2
+    return value
+
+
+def halve(value, dim, axis, flip):
+    peers = lax.axis_size(axis)
+    bit = (lax.axis_index(axis) // flip) % 2
+    keep = lax.dynamic_index_in_dim(value, bit, dim, keepdims=False)
+    send = lax.dynamic_index_in_dim(value, 1 - bit, dim, keepdims=False)
+    pairs = [(i, i ^ flip) for i in range(peers)]
+    return keep + lax.ppermute(send, axis, pairs)
+
+
+def scatter_rows(value, axes):
+    sizes = [lax.axis_size(axis) for axis in axes]
+    rows = value.shape[0]
+    groups = math.prod(sizes)
+    if not all(is_power_of_two(n) for n in sizes) or rows % groups:
+        return lax.psum_scatter(value, axes, scatter_dimension=0, tiled=True)
+    stages = [
+        (axis, 1 << (n.bit_length() - 2 - i))
+        for axis, n in zip(axes, sizes)
+        for i in range(n.bit_length() - 1)
+    ]
+    rest = value.shape[1:]
+    value = value.reshape((2,) * len(stages) + (rows // groups,) + rest)
+    names = list(stages)
+
+    def step(part, part_names, stage):
+        dim = part_names.index(stage)
+        return halve(part, dim, *stage), part_names[:dim] + part_names[dim + 1 :]
+
+    first = ("tm", 1) if ("tm", 1) in stages else stages[-1]
+    value, names = step(value, names, first)
+    middle = [s for s in stages if s[0] == axes[0] and s != first]
+    tail = [s for s in stages if s[0] != axes[0] and s != first]
+    if len(middle) > 1 and rest[-1] % 2 == 0:
+        cut = rest[-1] // 2
+        left, right = value[..., :cut], value[..., cut:]
+        left_names, right_names = list(names), list(names)
+        for a, b in zip(middle, middle[::-1]):
+            left, left_names = step(left, left_names, a)
+            right, right_names = step(right, right_names, b)
+        value = jnp.concatenate([left, right], axis=-1)
+        names = left_names
+    else:
+        for stage in middle:
+            value, names = step(value, names, stage)
+    for stage in tail[::-1]:
+        value, names = step(value, names, stage)
+    return value
 
 
 def band_block(queries, keys_blk, values_blk, grad_attn, valid, inv_scale):
@@ -66,8 +130,11 @@
     key_vals = projected[1:]
     earlier = [shifted(key_vals, "tm", offset) for offset in range(span, 0, -1)]
     extended = jnp.concatenate(earlier + [key_vals], axis=1)
-    local_count = jnp.sum(loss_mask.astype(jnp.float32))
-    total_count = lax.psum(local_count, ("tm", "night"))
+    local_count = jnp.sum(loss_mask.astype(jnp.int32))
+    if all(is_power_of_two(lax.axis_size(axis)) for axis in ("tm", "night")):
+        total_count = butterfly_sum(local_count, ("tm", "night")).astype(jnp.float32)
+    else:
+        total_count = lax.psum(local_count, ("tm", "night")).astype(jnp.float32)
     tokens_all = rows * lax.axis_size("tm") * lax.axis_size("night")
     loss_scale = jnp.float32(tokens_all) / total_count
     local_cot = cotangent[0]
@@ -125,11 +192,8 @@
     ).astype(jnp.bfloat16)
     proj_part = jnp.einsum("rd,wrh->dwh", normed, grad_proj, preferred_element_type=jnp.float32)
     out_part = jnp.einsum("rd,rh->dh", grad_out, attended_all, preferred_element_type=jnp.float32)
-    summed = lax.psum_scatter(
-        jnp.concatenate([proj_part, out_part[:, None]], axis=1),
-        ("tm", "night"),
-        scatter_dimension=0,
-        tiled=True,
+    summed = scatter_rows(
+        jnp.concatenate([proj_part, out_part[:, None]], axis=1), ("tm", "night")
     )
     grad_weights = summed * (jnp.sqrt(jnp.float32(tokens_all)) / total_count)
     return (grad_input[None], grad_weights)

time: 394 us -> 270 us (0.69)
  waiting for transfers between devices: 232 us -> 94.3 us
  starting transfers between devices: 17.9 us -> 64.1 us
  blocking collectives: 42.2 us -> 0 us
  local copies, waits for them, and re-layouts: 33.7 us -> 46.4 us
  between operations: 16 us -> 5.32 us
  other arithmetic: 11.4 us -> 21.2 us
    reduce_scatter x1 -> x0, waiting for transfers between devices: 190 us -> none  [shards(): lax.psum_scatter(jnp.concatenate([proj_part, out_part[:, None]], axis=1),...]
    ppermute x0 -> x12, waiting for transfers between devices: none -> 50.8 us  [the longest x7 50.1 us: halve(): return keep + lax.ppermute(send, axis, pairs)]
    ppermute x0 -> x12, starting transfers between devices: none -> 47.3 us  [the longest x7 31.8 us: halve(): return keep + lax.ppermute(send, axis, pairs)]
    psum x1 -> x0, blocking collectives: 42.2 us -> none  [shards(): total_count = lax.psum(local_count, ('tm', 'night'))]
    add x0 -> x6, other arithmetic: none -> 9.55 us  [halve(): return keep + lax.ppermute(send, axis, pairs)]
    concatenate x1 -> x0, other arithmetic: 4.21 us -> none  [shards(): jnp.concatenate([proj_part, out_part[:, None]], axis=1)]
    unnamed x75 -> x83, local copies, waits for them, and re-layouts: 8.43 us -> 9.01 us
  transfers between devices with their start and end apart: 9 -> 20, of which waited for: 6 -> 13; matrix products, arithmetic and copies ran while one was open for 5% -> 9% of each run, Pallas kernels for 0% -> 0%
where the time goes in v1:
time: 270 us; the launch traced here: 269 us
  waiting for transfers between devices  94.3 us (35%)
  starting transfers between devices  64.1 us (24%)
  local copies, waits for them, and re-layouts  46.4 us (17%)
  matrix products  37.2 us (14%)
  other arithmetic  21.2 us (8%)
  between operations  5.32 us (2%)
    ppermute x7, waiting for transfers between devices, halve(): return keep + lax.ppermute(send, axis, pairs)  50.1 us
    ppermute x8, waiting for transfers between devices, shifted(): return lax.ppermute(value, axis, pairs)  43.5 us
    ppermute x7, starting transfers between devices, halve(): return keep + lax.ppermute(send, axis, pairs)  31.8 us
    ppermute x8, starting transfers between devices, shifted(): return lax.ppermute(value, axis, pairs)  16.8 us
    ppermute x5, starting transfers between devices, butterfly_sum(): value = value + lax.ppermute(value, axis, pairs)  15.5 us
    another operation x8, local copies, waits for them, and re-layouts, shards(): update = jnp.stack([grad_key, grad_value]).reshape(2, key_len, group_cols)  10.3 us
    add x6, other arithmetic, halve(): return keep + lax.ppermute(send, axis, pairs)  9.55 us
    div x4, matrix products, band_block(): probs = exp_terms / jnp.sum(exp_terms, axis=-1, keepdims=True)  9.06 us
  transfers between devices with their start and end apart: 20, of which 13 were waited for; matrix products, arithmetic and copies ran while one was open for 9% of the time, Pallas kernels for 0%

profile of v1, /device:TPU:0, one launch (start us, length us, event | category | flops | bytes accessed | tf_op | source)
XLA Modules:
  0.0 268.6 jit_solution(13961448865254618079)
XLA Ops:
  6.8 4.6 %slice.186 = bf16[1024,1,512]{2,1,0:T(2,128)(2,1)S(1)} slice(bf16[1024,4,512]{2,1,0:T(4,128)(2,1)} %param.21), slice={[0:1024], [3:4], [0:512]} | slice | bytes 2097152 | tf_op jit(solution)/shard_map/slice | solution.py:142
  14.0 3.9 %collective-permute-start.1 = (s32[]{:T(128)}, s32[]{:T(128)}, u32[]{:S(2)}, u32[]{:S(2)}) collective-permute-start(s32[]{:T(128)} %add.172), channel_id=1, source_target_pairs={{0,8},{4,12},{8,0},{12,4},{16,24},{20,28},{24,16},{28,20},{1,9},{5... | collective-permute-start | bytes 20 | tf_op jit(solution)/shard_map/ppermute | solution.py:29
  18.6 3.4 %collective-permute-start.2 = (s32[]{:T(128)}, s32[]{:T(128)}, u32[]{:S(2)}, u32[]{:S(2)}) collective-permute-start(s32[]{:T(128)} %add.173), channel_id=1, source_target_pairs={{0,16},{4,20},{8,24},{12,28},{16,0},{20,4},{24,8},{28,12},{1,17},{... | collective-permute-start | bytes 20 | tf_op jit(solution)/shard_map/ppermute | solution.py:29
  22.9 3.4 %collective-permute-start.3 = (s32[]{:T(128)}, s32[]{:T(128)}, u32[]{:S(2)}, u32[]{:S(2)}) collective-permute-start(s32[]{:T(128)} %add.174), channel_id=1, source_target_pairs={{0,1},{1,0},{2,3},{3,2},{4,5},{5,4},{6,7},{7,6},{8,9},{9,8},{10,11... | collective-permute-start | bytes 20 | tf_op jit(solution)/shard_map/ppermute | solution.py:29
  27.1 4.4 %collective-permute-start.4 = (s32[]{:T(128)}, s32[]{:T(128)}, u32[]{:S(2)}, u32[]{:S(2)}) collective-permute-start(s32[]{:T(128)} %add.175), channel_id=1, source_target_pairs={{0,2},{1,3},{2,0},{3,1},{4,6},{5,7},{6,4},{7,5},{8,10},{9,11},{10,... | collective-permute-start | bytes 20 | tf_op jit(solution)/shard_map/ppermute | solution.py:29
  32.4 3.4 %fusion.51 = bf16[3,256,512]{2,1,0:T(8,128)(2,1)S(1)} fusion(bf16[1024,3,512]{2,1,0:T(4,128)(2,1)} %bitcast.250, bf16[1,256,1024]{2,1,0:T(8,128)(2,1)S(1)} %copy-done.14, f32[256]{0:T(256)S(1)} %get-tuple-element.109), kind=kOutput, calls=%fused_computation.68 | convolution fusion | flops 806486016 | bytes 4457472 | tf_op jit(solution)/shard_map/rd,dwh->wrh/dot_general | solution.py:126
  35.9 3.8 %collective-permute-start.5 = (bf16[2,256,512]{2,1,0:T(8,128)(2,1)S(1)}, bf16[2,256,512]{2,1,0:T(8,128)(2,1)S(1)}, u32[]{:S(2)}, u32[]{:S(2)}) collective-permute-start(bf16[2,256,512]{2,1,0:T(8,128)(2,1)S(1)} %slice.208), channel_id=1, source_target_pairs={{0,16},{4,20},{8,24},{12,28},{1,17},{5,21},{9,25},{13,29},{2,18},{... | collective-permute-start | bytes 1572872 | tf_op jit(solution)/shard_map/ppermute | solution.py:16
  40.2 3.4 %collective-permute-start.7 = (bf16[2,256,512]{2,1,0:T(8,128)(2,1)S(1)}, bf16[2,256,512]{2,1,0:T(8,128)(2,1)S(1)}, u32[]{:S(2)}, u32[]{:S(2)}) collective-permute-start(bf16[2,256,512]{2,1,0:T(8,128)(2,1)S(1)} %slice.208), channel_id=1, source_target_pairs={{0,8},{4,12},{8,16},{12,20},{16,24},{20,28},{1,9},{5,13},{9,17},{1... | collective-permute-start | bytes 1572872 | tf_op jit(solution)/shard_map/ppermute | solution.py:16
  53.3 20.3 %collective-permute-done.5 = bf16[2,256,512]{2,1,0:T(8,128)(2,1)S(1)} collective-permute-done((bf16[2,256,512]{2,1,0:T(8,128)(2,1)S(1)}, bf16[2,256,512]{2,1,0:T(8,128)(2,1)S(1)}, u32[]{:S(2)}, u32[]{:S(2)}) %collective-permute-start.5) | collective-permute-done | bytes 524320 | tf_op jit(solution)/shard_map/ppermute | solution.py:16
  77.4 2.3 fusion.45
  86.4 2.3 fusion.43
  137.7 14.3 %collective-permute-done.12 = bf16[2,256,512]{2,1,0:T(8,128)(2,1)S(1)} collective-permute-done((bf16[2,256,512]{2,1,0:T(8,128)(2,1)S(1)}, bf16[2,256,512]{2,1,0:T(8,128)(2,1)S(1)}, u32[]{:S(2)}, u32[]{:S(2)}) %collective-permute-start.12) | collective-permute-done | bytes 524320 | tf_op jit(solution)/shard_map/ppermute | solution.py:16
  152.0 9.0 %collective-permute-done.10 = bf16[2,256,512]{2,1,0:T(8,128)(2,1)S(1)} collective-permute-done((bf16[2,256,512]{2,1,0:T(8,128)(2,1)S(1)}, bf16[2,256,512]{2,1,0:T(8,128)(2,1)S(1)}, u32[]{:S(2)}, u32[]{:S(2)}) %collective-permute-start.10) | collective-permute-done | bytes 524320 | tf_op jit(solution)/shard_map/ppermute | solution.py:16
  166.9 2.9 %fusion.1 = f32[2,2,2,2,32,4,512]{6,4,5,3,2,1,0:T(8,128)} fusion(s32[]{:T(128)S(6)} %select_n.95, f32[2,2,2,2,2,32,3,512]{7,5,6,4,3,2,1,0:T(8,128)S(1)} %fusion.63, f32[2,2,2,2,2,32,1,512]{7,5,6,4,3,2,1,0:T(8,128)S(1)} %convolution_bitcast_fusion), kind=kLoop, calls=%fused_computation.6 | loop fusion | flops 1048576 | bytes 12582916 | tf_op jit(solution)/shard_map/jit(dynamic_index_in_dim)/squeeze | solution.py:38
  171.0 7.4 %collective-permute-done.13 = f32[2,2,2,2,32,4,512]{6,4,5,3,2,1,0:T(8,128)} collective-permute-done((f32[2,2,2,2,32,4,512]{6,4,5,3,2,1,0:T(8,128)}, f32[2,2,2,2,32,4,512]{6,4,5,3,2,1,0:T(8,128)}, u32[]{:S(2)}, u32[]{:S(2)}) %collective-permute-start.13) | collective-permute-done | bytes 4194336 | tf_op jit(solution)/shard_map/ppermute | solution.py:40
  178.3 4.2 %fusion.4 = f32[2,2,2,2,32,4,512]{6,4,5,3,2,1,0:T(8,128)S(1)} fusion(f32[2,2,2,2,32,4,512]{6,4,5,3,2,1,0:T(8,128)} %collective-permute-done.13, s32[]{:T(128)S(6)} %select_n.94, f32[2,2,2,2,2,32,3,512]{7,5,6,4,3,2,1,0:T(8,128)} %copy-done, f32[2,2,2,2,2,32,1,512]{7,5,6,4,3,2,1,0:T(8,128)S(1)} %convolution_bitcast_fusion), kind=kLoop, calls=%fused_computation.9 | loop fusion | flops 2097152 | bytes 16777220 | tf_op jit(solution)/shard_map/add | solution.py:40
  186.3 12.9 %collective-permute-start.16 = (f32[2,2,2,32,4,256]{5,3,4,2,1,0:T(8,128)}, f32[2,2,2,32,4,256]{5,3,4,2,1,0:T(8,128)}, u32[]{:S(2)}, u32[]{:S(2)}) collective-permute-start(f32[2,2,2,32,4,256]{5,3,4,2,1,0:T(8,128)} %dynamic-slice_bitcast_fusion), channel_id=1, source_target_pairs={{0,8},{4,12},{8,0},{12,4},{16,24},{20,28},{24,16},{28,20},{1,9},{5... | collective-permute-start | bytes 3145736 | tf_op jit(solution)/shard_map/ppermute | solution.py:40
  199.2 10.8 %collective-permute-done.14 = f32[2,2,2,32,4,256]{5,3,4,2,1,0:T(8,128)} collective-permute-done((f32[2,2,2,32,4,256]{5,3,4,2,1,0:T(8,128)S(1)}, f32[2,2,2,32,4,256]{5,3,4,2,1,0:T(8,128)}, u32[]{:S(2)}, u32[]{:S(2)}) %collective-permute-start.14) | collective-permute-done | bytes 1048608 | tf_op jit(solution)/shard_map/ppermute | solution.py:40
  212.6 13.5 %collective-permute-start.15 = (f32[2,2,32,4,256]{4,2,3,1,0:T(8,128)}, f32[2,2,32,4,256]{4,2,3,1,0:T(8,128)}, u32[]{:S(2)}, u32[]{:S(2)}) collective-permute-start(f32[2,2,32,4,256]{4,2,3,1,0:T(8,128)} %dynamic-slice_bitcast_fusion.3), channel_id=1, source_target_pairs={{0,8},{4,12},{8,0},{12,4},{16,24},{20,28},{24,16},{28,20},{1,9},{5... | collective-permute-start | bytes 1572872 | tf_op jit(solution)/shard_map/ppermute | solution.py:40
  228.9 9.2 %collective-permute-done.15 = f32[2,2,32,4,256]{4,2,3,1,0:T(8,128)} collective-permute-done((f32[2,2,32,4,256]{4,2,3,1,0:T(8,128)}, f32[2,2,32,4,256]{4,2,3,1,0:T(8,128)}, u32[]{:S(2)}, u32[]{:S(2)}) %collective-permute-start.15) | collective-permute-done | bytes 524320 | tf_op jit(solution)/shard_map/ppermute | solution.py:40
  239.2 2.5 collective-permute-done.17
  244.5 10.6 %collective-permute-done.18 = f32[2,32,4,512]{3,1,2,0:T(8,128)S(1)} collective-permute-done((f32[2,32,4,512]{3,1,2,0:T(8,128)S(1)}, f32[2,32,4,512]{3,1,2,0:T(8,128)S(1)}, u32[]{:S(2)}, u32[]{:S(2)}) %collective-permute-start.18) | collective-permute-done | bytes 524320 | tf_op jit(solution)/shard_map/ppermute | solution.py:40
  255.4 2.7 collective-permute-start.19
  258.1 9.5 %collective-permute-done.19 = f32[32,4,512]{2,1,0:T(4,128)S(1)} collective-permute-done((f32[32,4,512]{2,1,0:T(4,128)S(1)}, f32[32,4,512]{2,1,0:T(4,128)S(1)}, u32[]{:S(2)}, u32[]{:S(2)}) %collective-permute-start.19) | collective-permute-done | bytes 262176 | tf_op jit(solution)/shard_map/ppermute | solution.py:40
  (200 shorter events, 98.6 us)
Async XLA Ops:
  1.9 10.7 %collective-permute-start = (s32[]{:T(128)}, s32[]{:T(128)}, u32[]{:S(2)}, u32[]{:S(2)}) collective-permute-start(s32[]{:T(128)} %reduce_sum.99), channel_id=1, source_target_pairs={{0,4},{4,0},{8,12},{12,8},{16,20},{20,16},{24,28},{28,24},{1,5},{5... | collective-permute-start | bytes 20 | tf_op jit(solution)/shard_map/ppermute | solution.py:29
  11.4 21.0 %copy-start.14 = (bf16[1,256,1024]{2,1,0:T(8,128)(2,1)S(1)}, bf16[1,256,1024]{2,1,0:T(8,128)(2,1)}, u32[]{:S(2)}) copy-start(bf16[1,256,1024]{2,1,0:T(8,128)(2,1)} %param.20) | copy-start | bytes 1572868
  14.0 4.0 %collective-permute-start.1 = (s32[]{:T(128)}, s32[]{:T(128)}, u32[]{:S(2)}, u32[]{:S(2)}) collective-permute-start(s32[]{:T(128)} %add.172), channel_id=1, source_target_pairs={{0,8},{4,12},{8,0},{12,4},{16,24},{20,28},{24,16},{28,20},{1,9},{5... | collective-permute-start | bytes 20 | tf_op jit(solution)/shard_map/ppermute | solution.py:29
  18.6 3.6 %collective-permute-start.2 = (s32[]{:T(128)}, s32[]{:T(128)}, u32[]{:S(2)}, u32[]{:S(2)}) collective-permute-start(s32[]{:T(128)} %add.173), channel_id=1, source_target_pairs={{0,16},{4,20},{8,24},{12,28},{16,0},{20,4},{24,8},{28,12},{1,17},{... | collective-permute-start | bytes 20 | tf_op jit(solution)/shard_map/ppermute | solution.py:29
  22.9 3.6 %collective-permute-start.3 = (s32[]{:T(128)}, s32[]{:T(128)}, u32[]{:S(2)}, u32[]{:S(2)}) collective-permute-start(s32[]{:T(128)} %add.174), channel_id=1, source_target_pairs={{0,1},{1,0},{2,3},{3,2},{4,5},{5,4},{6,7},{7,6},{8,9},{9,8},{10,11... | collective-permute-start | bytes 20 | tf_op jit(solution)/shard_map/ppermute | solution.py:29
  27.1 4.6 %collective-permute-start.4 = (s32[]{:T(128)}, s32[]{:T(128)}, u32[]{:S(2)}, u32[]{:S(2)}) collective-permute-start(s32[]{:T(128)} %add.175), channel_id=1, source_target_pairs={{0,2},{1,3},{2,0},{3,1},{4,6},{5,7},{6,4},{7,5},{8,10},{9,11},{10,... | collective-permute-start | bytes 20 | tf_op jit(solution)/shard_map/ppermute | solution.py:29
  35.9 37.6 %collective-permute-start.5 = (bf16[2,256,512]{2,1,0:T(8,128)(2,1)S(1)}, bf16[2,256,512]{2,1,0:T(8,128)(2,1)S(1)}, u32[]{:S(2)}, u32[]{:S(2)}) collective-permute-start(bf16[2,256,512]{2,1,0:T(8,128)(2,1)S(1)} %slice.208), channel_id=1, source_target_pairs={{0,16},{4,20},{8,24},{12,28},{1,17},{5,21},{9,25},{13,29},{2,18},{... | collective-permute-start | bytes 1572872 | tf_op jit(solution)/shard_map/ppermute | solution.py:16
  40.2 34.5 %collective-permute-start.7 = (bf16[2,256,512]{2,1,0:T(8,128)(2,1)S(1)}, bf16[2,256,512]{2,1,0:T(8,128)(2,1)S(1)}, u32[]{:S(2)}, u32[]{:S(2)}) collective-permute-start(bf16[2,256,512]{2,1,0:T(8,128)(2,1)S(1)} %slice.208), channel_id=1, source_target_pairs={{0,8},{4,12},{8,16},{12,20},{16,24},{20,28},{1,9},{5,13},{9,17},{1... | collective-permute-start | bytes 1572872 | tf_op jit(solution)/shard_map/ppermute | solution.py:16
  43.7 29.9 %collective-permute-start.6 = (bf16[2,256,512]{2,1,0:T(8,128)(2,1)S(1)}, bf16[2,256,512]{2,1,0:T(8,128)(2,1)}, u32[]{:S(2)}, u32[]{:S(2)}) collective-permute-start(bf16[2,256,512]{2,1,0:T(8,128)(2,1)S(1)} %slice.208), channel_id=1, source_target_pairs={{0,12},{4,16},{8,20},{12,24},{16,28},{1,13},{5,17},{9,21},{13,25},... | collective-permute-start | bytes 1572872 | tf_op jit(solution)/shard_map/ppermute | solution.py:16
  45.8 28.9 %collective-permute-start.8 = (bf16[2,256,512]{2,1,0:T(8,128)(2,1)S(1)}, bf16[2,256,512]{2,1,0:T(8,128)(2,1)S(1)}, u32[]{:S(2)}, u32[]{:S(2)}) collective-permute-start(bf16[2,256,512]{2,1,0:T(8,128)(2,1)S(1)} %slice.208), channel_id=1, source_target_pairs={{0,4},{4,8},{8,12},{12,16},{16,20},{20,24},{24,28},{1,5},{5,9},{9,... | collective-permute-start | bytes 1572872 | tf_op jit(solution)/shard_map/ppermute | solution.py:16
  117.2 10.9 %copy-start.6 = (f32[2,64,1280]{2,1,0:T(8,128)S(1)}, f32[2,64,1280]{2,1,0:T(8,128)}, u32[]{:S(2)}) copy-start(f32[2,64,1280]{2,1,0:T(8,128)} %fusion.65) | copy-start | bytes 1966084
  131.5 6.2 %collective-permute-start.9 = (bf16[2,256,512]{2,1,0:T(8,128)(2,1)S(1)}, bf16[2,256,512]{2,1,0:T(8,128)(2,1)S(1)}, u32[]{:S(2)}, u32[]{:S(2)}) collective-permute-start(bf16[2,256,512]{2,1,0:T(8,128)(2,1)S(1)} %get-tuple-element.84), channel_id=1, source_target_pairs={{4,0},{8,4},{12,8},{16,12},{20,16},{24,20},{28,24},{5,1},{9,5},{13... | collective-permute-start | bytes 1572872 | tf_op jit(solution)/shard_map/ppermute | solution.py:16
  132.9 19.1 %collective-permute-start.12 = (bf16[2,256,512]{2,1,0:T(8,128)(2,1)S(1)}, bf16[2,256,512]{2,1,0:T(8,128)(2,1)S(1)}, u32[]{:S(2)}, u32[]{:S(2)}) collective-permute-start(bf16[2,256,512]{2,1,0:T(8,128)(2,1)S(1)} %get-tuple-element.85), channel_id=1, source_target_pairs={{16,0},{20,4},{24,8},{28,12},{17,1},{21,5},{25,9},{29,13},{18,2},{... | collective-permute-start | bytes 1572872 | tf_op jit(solution)/shard_map/ppermute | solution.py:16
  134.2 17.8 %collective-permute-start.11 = (bf16[2,256,512]{2,1,0:T(8,128)(2,1)S(1)}, bf16[2,256,512]{2,1,0:T(8,128)(2,1)S(1)}, u32[]{:S(2)}, u32[]{:S(2)}) collective-permute-start(bf16[2,256,512]{2,1,0:T(8,128)(2,1)S(1)} %get-tuple-element.86), channel_id=1, source_target_pairs={{12,0},{16,4},{20,8},{24,12},{28,16},{13,1},{17,5},{21,9},{25,13},... | collective-permute-start | bytes 1572872 | tf_op jit(solution)/shard_map/ppermute | solution.py:16
  135.5 25.4 %collective-permute-start.10 = (bf16[2,256,512]{2,1,0:T(8,128)(2,1)S(1)}, bf16[2,256,512]{2,1,0:T(8,128)(2,1)S(1)}, u32[]{:S(2)}, u32[]{:S(2)}) collective-permute-start(bf16[2,256,512]{2,1,0:T(8,128)(2,1)S(1)} %get-tuple-element.87), channel_id=1, source_target_pairs={{8,0},{12,4},{16,8},{20,12},{24,16},{28,20},{9,1},{13,5},{17,9},{2... | collective-permute-start | bytes 1572872 | tf_op jit(solution)/shard_map/ppermute | solution.py:16
  137.4 24.0 %copy-start.26 = (bf16[1024,4,512]{2,1,0:T(4,128)(2,1)S(1)}, bf16[1024,4,512]{2,1,0:T(4,128)(2,1)}, u32[]{:S(2)}) copy-start(bf16[1024,4,512]{2,1,0:T(4,128)(2,1)} %param.21) | copy-start | bytes 12582916
  137.7 23.6 %copy-start.15 = (bf16[1,256,1024]{2,1,0:T(8,128)(2,1)S(1)}, bf16[1,256,1024]{2,1,0:T(8,128)(2,1)}, u32[]{:S(2)}) copy-start(bf16[1,256,1024]{2,1,0:T(8,128)(2,1)} %param.20) | copy-start | bytes 1572868
  170.8 7.5 %collective-permute-start.13 = (f32[2,2,2,2,32,4,512]{6,4,5,3,2,1,0:T(8,128)}, f32[2,2,2,2,32,4,512]{6,4,5,3,2,1,0:T(8,128)}, u32[]{:S(2)}, u32[]{:S(2)}) collective-permute-start(f32[2,2,2,2,32,4,512]{6,4,5,3,2,1,0:T(8,128)} %fusion.1), channel_id=1, source_target_pairs={{0,4},{4,0},{8,12},{12,8},{16,20},{20,16},{24,28},{28,24},{1,5},{5... | collective-permute-start | bytes 12582920 | tf_op jit(solution)/shard_map/ppermute | solution.py:40
  184.7 25.4 %collective-permute-start.14 = (f32[2,2,2,32,4,256]{5,3,4,2,1,0:T(8,128)S(1)}, f32[2,2,2,32,4,256]{5,3,4,2,1,0:T(8,128)}, u32[]{:S(2)}, u32[]{:S(2)}) collective-permute-start(f32[2,2,2,32,4,256]{5,3,4,2,1,0:T(8,128)S(1)} %dynamic-slice_bitcast_fusion.1), channel_id=1, source_target_pairs={{0,16},{4,20},{8,24},{12,28},{16,0},{20,4},{24,8},{28,12},{1,17},{... | collective-permute-start | bytes 3145736 | tf_op jit(solution)/shard_map/ppermute | solution.py:40
  186.3 39.8 %collective-permute-start.16 = (f32[2,2,2,32,4,256]{5,3,4,2,1,0:T(8,128)}, f32[2,2,2,32,4,256]{5,3,4,2,1,0:T(8,128)}, u32[]{:S(2)}, u32[]{:S(2)}) collective-permute-start(f32[2,2,2,32,4,256]{5,3,4,2,1,0:T(8,128)} %dynamic-slice_bitcast_fusion), channel_id=1, source_target_pairs={{0,8},{4,12},{8,0},{12,4},{16,24},{20,28},{24,16},{28,20},{1,9},{5... | collective-permute-start | bytes 3145736 | tf_op jit(solution)/shard_map/ppermute | solution.py:40
  212.6 25.5 %collective-permute-start.15 = (f32[2,2,32,4,256]{4,2,3,1,0:T(8,128)}, f32[2,2,32,4,256]{4,2,3,1,0:T(8,128)}, u32[]{:S(2)}, u32[]{:S(2)}) collective-permute-start(f32[2,2,32,4,256]{4,2,3,1,0:T(8,128)} %dynamic-slice_bitcast_fusion.3), channel_id=1, source_target_pairs={{0,8},{4,12},{8,0},{12,4},{16,24},{20,28},{24,16},{28,20},{1,9},{5... | collective-permute-start | bytes 1572872 | tf_op jit(solution)/shard_map/ppermute | solution.py:40
  228.5 13.2 %collective-permute-start.17 = (f32[2,2,32,4,256]{4,2,3,1,0:T(8,128)S(1)}, f32[2,2,32,4,256]{4,2,3,1,0:T(8,128)S(1)}, u32[]{:S(2)}, u32[]{:S(2)}) collective-permute-start(f32[2,2,32,4,256]{4,2,3,1,0:T(8,128)S(1)} %dynamic-slice_bitcast_fusion.2), channel_id=1, source_target_pairs={{0,16},{4,20},{8,24},{12,28},{16,0},{20,4},{24,8},{28,12},{1,17},{... | collective-permute-start | bytes 1572872 | tf_op jit(solution)/shard_map/ppermute | solution.py:40
  242.9 12.2 %collective-permute-start.18 = (f32[2,32,4,512]{3,1,2,0:T(8,128)S(1)}, f32[2,32,4,512]{3,1,2,0:T(8,128)S(1)}, u32[]{:S(2)}, u32[]{:S(2)}) collective-permute-start(f32[2,32,4,512]{3,1,2,0:T(8,128)S(1)} %fusion.79), channel_id=1, source_target_pairs={{0,1},{1,0},{2,3},{3,2},{4,5},{5,4},{6,7},{7,6},{8,9},{9,8},{10,11... | collective-permute-start | bytes 1572872 | tf_op jit(solution)/shard_map/ppermute | solution.py:40
  255.4 12.2 %collective-permute-start.19 = (f32[32,4,512]{2,1,0:T(4,128)S(1)}, f32[32,4,512]{2,1,0:T(4,128)S(1)}, u32[]{:S(2)}, u32[]{:S(2)}) collective-permute-start(f32[32,4,512]{2,1,0:T(4,128)S(1)} %bitcast.260), channel_id=1, source_target_pairs={{0,2},{1,3},{2,0},{3,1},{4,6},{5,7},{6,4},{7,5},{8,10},{9,11},{10,... | collective-permute-start | bytes 786440 | tf_op jit(solution)/shard_map/ppermute | solution.py:40
  (35 other events, 119.6 us)

commit v2 on v1

--- a/solution.py
+++ b/solution.py
@@ -130,13 +130,8 @@
     key_vals = projected[1:]
     earlier = [shifted(key_vals, "tm", offset) for offset in range(span, 0, -1)]
     extended = jnp.concatenate(earlier + [key_vals], axis=1)
-    local_count = jnp.sum(loss_mask.astype(jnp.int32))
-    if all(is_power_of_two(lax.axis_size(axis)) for axis in ("tm", "night")):
-        total_count = butterfly_sum(local_count, ("tm", "night")).astype(jnp.float32)
-    else:
-        total_count = lax.psum(local_count, ("tm", "night")).astype(jnp.float32)
+    local_count = jnp.sum(loss_mask.astype(jnp.float32))
     tokens_all = rows * lax.axis_size("tm") * lax.axis_size("night")
-    loss_scale = jnp.float32(tokens_all) / total_count
     local_cot = cotangent[0]
     grad_out = jnp.where(loss_mask[0][:, None] > 0, local_cot, jnp.zeros_like(local_cot))
     grad_attn = jnp.dot(grad_out, weights[:, 3, :], preferred_element_type=jnp.float32).astype(
@@ -187,15 +182,21 @@
         "wrh,dwh->rd", grad_proj, proj_weights, preferred_element_type=jnp.float32
     )
     along = jnp.sum(grad_normed * normed_full, axis=-1) / width
-    grad_input = (
-        loss_scale * inv_rms[:, None] * (grad_normed - normed_full * along[:, None])
-    ).astype(jnp.bfloat16)
+    unscaled_input = inv_rms[:, None] * (grad_normed - normed_full * along[:, None])
     proj_part = jnp.einsum("rd,wrh->dwh", normed, grad_proj, preferred_element_type=jnp.float32)
     out_part = jnp.einsum("rd,rh->dh", grad_out, attended_all, preferred_element_type=jnp.float32)
-    summed = scatter_rows(
-        jnp.concatenate([proj_part, out_part[:, None]], axis=1), ("tm", "night")
-    )
-    grad_weights = summed * (jnp.sqrt(jnp.float32(tokens_all)) / total_count)
+    blocks = lax.axis_size("tm") * lax.axis_size("night")
+    payload = jnp.concatenate([proj_part, out_part[:, None]], axis=1)
+    payload = payload.reshape((blocks, width // blocks) + payload.shape[1:])
+    count_row = jnp.zeros((blocks, 1) + payload.shape[2:], jnp.float32)
+    count_row = count_row.at[:, 0, 0, 0].set(local_count)
+    payload = jnp.concatenate([payload, count_row], axis=1)
+    payload = payload.reshape((-1,) + payload.shape[2:])
+    summed = scatter_rows(payload, ("tm", "night"))
+    total_count = summed[-1, 0, 0]
+    loss_scale = jnp.float32(tokens_all) / total_count
+    grad_input = (loss_scale * unscaled_input).astype(jnp.bfloat16)
+    grad_weights = summed[:-1] * (jnp.sqrt(jnp.float32(tokens_all)) / total_count)
     return (grad_input[None], grad_weights)
 
 

time: 270 us -> 286 us (1.059)
  starting transfers between devices: 64.1 us -> 44.4 us
  local copies, waits for them, and re-layouts: 46.4 us -> 62.2 us
  matrix products: 37.2 us -> 46.1 us
  other arithmetic: 21.2 us -> 30 us
  waiting for transfers between devices: 94.3 us -> 99.2 us
    ppermute x5 -> x0, starting transfers between devices: 15.5 us -> none  [butterfly_sum(): value = value + lax.ppermute(value, axis, pairs)]
    ppermute x7, waiting for transfers between devices: 50.1 us -> 63.6 us  [halve(): return keep + lax.ppermute(send, axis, pairs)]
    ppermute x8, waiting for transfers between devices: 43.5 us -> 35.7 us  [shifted(): return lax.ppermute(value, axis, pairs)]
    dynamic_slice x1, local copies, waits for them, and re-layouts: 0.17 us -> 7.44 us  [halve(): send = lax.dynamic_index_in_dim(value, 1 - bit, dim, keepdims=False)]
    ppermute x7, starting transfers between devices: 31.8 us -> 25.2 us  [halve(): return keep + lax.ppermute(send, axis, pairs)]
    dynamic_slice x1, local copies, waits for them, and re-layouts: 0.05 us -> 5.58 us  [halve(): keep = lax.dynamic_index_in_dim(value, bit, dim, keepdims=False)]
    add x6 -> x7, other arithmetic: 9.55 us -> 14.6 us  [halve(): return keep + lax.ppermute(send, axis, pairs)]
    concatenate x0 -> x1, other arithmetic: none -> 4.38 us  [shards(): payload = jnp.concatenate([payload, count_row], axis=1)]
  transfers between devices with their start and end apart: 20 -> 15, of which waited for: 13 -> 9; matrix products, arithmetic and copies ran while one was open for 9% -> 9% of each run, Pallas kernels for 0% -> 0%
where the time goes in v2:
time: 286 us; the launch traced here: 285 us
  waiting for transfers between devices  99.2 us (35%)
  local copies, waits for them, and re-layouts  62.2 us (22%)
  matrix products  46.1 us (16%)
  starting transfers between devices  44.4 us (16%)
  other arithmetic  30 us (10%)
    ppermute x7, waiting for transfers between devices, halve(): return keep + lax.ppermute(send, axis, pairs)  63.6 us
    ppermute x8, waiting for transfers between devices, shifted(): return lax.ppermute(value, axis, pairs)  35.7 us
    ppermute x7, starting transfers between devices, halve(): return keep + lax.ppermute(send, axis, pairs)  25.2 us
    ppermute x8, starting transfers between devices, shifted(): return lax.ppermute(value, axis, pairs)  19.2 us
    add x7, other arithmetic, halve(): return keep + lax.ppermute(send, axis, pairs)  14.6 us
    div x4, matrix products, band_block(): probs = exp_terms / jnp.sum(exp_terms, axis=-1, keepdims=True)  12.1 us
    unnamed x93, local copies, waits for them, and re-layouts  12 us
    another operation x8, local copies, waits for them, and re-layouts, shards(): update = jnp.stack([grad_key, grad_value]).reshape(2, key_len, group_cols)  8.93 us
  transfers between devices with their start and end apart: 15, of which 9 were waited for; matrix products, arithmetic and copies ran while one was open for 9% of the time, Pallas kernels for 0%

profile of v2, /device:TPU:0, one launch (start us, length us, event | category | flops | bytes accessed | tf_op | source)
XLA Modules:
  0.0 284.7 jit_solution(5807157865571245727)
XLA Ops:
  1.9 3.7 %fusion.46 = bf16[3,256,512]{2,1,0:T(8,128)(2,1)S(1)} fusion(bf16[1024,3,512]{2,1,0:T(4,128)(2,1)} %bitcast.247, bf16[1,256,1024]{2,1,0:T(8,128)(2,1)} %param.22, f32[256]{0:T(256)S(1)} %add_rsqrt_fusion), kind=kOutput, calls=%fused_computation.62 | convolution fusion | flops 806486016 | bytes 4457472 | tf_op jit(solution)/shard_map/rd,dwh->wrh/dot_general | solution.py:126
  6.4 5.7 %collective-permute-start = (bf16[2,256,512]{2,1,0:T(8,128)(2,1)}, bf16[2,256,512]{2,1,0:T(8,128)(2,1)}, u32[]{:S(2)}, u32[]{:S(2)}) collective-permute-start(bf16[2,256,512]{2,1,0:T(8,128)(2,1)} %slice.240), channel_id=1, source_target_pairs={{0,16},{4,20},{8,24},{12,28},{1,17},{5,21},{9,25},{13,29},{2,18},{... | collective-permute-start | bytes 1572872 | tf_op jit(solution)/shard_map/ppermute | solution.py:16
  12.1 3.4 %collective-permute-start.1 = (bf16[2,256,512]{2,1,0:T(8,128)(2,1)}, bf16[2,256,512]{2,1,0:T(8,128)(2,1)}, u32[]{:S(2)}, u32[]{:S(2)}) collective-permute-start(bf16[2,256,512]{2,1,0:T(8,128)(2,1)} %slice.240), channel_id=1, source_target_pairs={{0,12},{4,16},{8,20},{12,24},{16,28},{1,13},{5,17},{9,21},{13,25},... | collective-permute-start | bytes 1572872 | tf_op jit(solution)/shard_map/ppermute | solution.py:16
  15.5 2.9 %collective-permute-start.2 = (bf16[2,256,512]{2,1,0:T(8,128)(2,1)}, bf16[2,256,512]{2,1,0:T(8,128)(2,1)}, u32[]{:S(2)}, u32[]{:S(2)}) collective-permute-start(bf16[2,256,512]{2,1,0:T(8,128)(2,1)} %slice.240), channel_id=1, source_target_pairs={{0,8},{4,12},{8,16},{12,20},{16,24},{20,28},{1,9},{5,13},{9,17},{1... | collective-permute-start | bytes 1572872 | tf_op jit(solution)/shard_map/ppermute | solution.py:16
  32.6 13.8 %collective-permute-done = bf16[2,256,512]{2,1,0:T(8,128)(2,1)} collective-permute-done((bf16[2,256,512]{2,1,0:T(8,128)(2,1)}, bf16[2,256,512]{2,1,0:T(8,128)(2,1)}, u32[]{:S(2)}, u32[]{:S(2)}) %collective-permute-start) | collective-permute-done | bytes 524320 | tf_op jit(solution)/shard_map/ppermute | solution.py:16
  53.3 2.3 fusion.38
  62.2 3.8 %fusion.40 = f32[2,256,1280]{2,1,0:T(8,128)} fusion(bf16[256,2,64]{0,2,1:T(8,128)(2,1)} %bitcast.253, bf16[1280,2,64]{0,2,1:T(8,128)(2,1)} %bitcast.235, f32[256,1280]{1,0:T(8,128)} %fusion.45), kind=kOutput, calls=%fused_computation.55 | convolution fusion | flops 85853952 | bytes 4325376 | tf_op jit(solution)/shard_map/div | solution.py:89
  66.0 3.0 %multiply_reduce_fusion.3 = (f32[256,2]{0,1:T(2,128)S(1)}, bf16[2,64,256]{2,1,0:T(8,128)(2,1)}) fusion(bf16[256,128]{0,1:T(8,128)(2,1)S(1)} %copy.66, bf16[1280,2,64]{0,2,1:T(8,128)(2,1)S(1)} %bitcast.217, f32[2,256,1280]{2,1,0:T(8,128)} %fusion.40), kind=kOutput, calls=%fused_computation.139 | convolution fusion | flops 84704768 | bytes 3082240 | tf_op jit(solution)/shard_map/gqk,kgc->qgc/dot_general | solution.py:91
  76.8 2.3 fusion.34
  84.8 3.8 %fusion.36 = f32[2,256,1280]{2,1,0:T(8,128)} fusion(bf16[256,2,64]{0,2,1:T(8,128)(2,1)S(1)} %bitcast.249, bf16[1280,2,64]{0,2,1:T(8,128)(2,1)} %bitcast.231, f32[256,1280]{1,0:T(8,128)} %fusion.45), kind=kOutput, calls=%fused_computation.51 | convolution fusion | flops 85853952 | bytes 4325376 | tf_op jit(solution)/shard_map/div | solution.py:89
  88.6 3.0 %multiply_reduce_fusion.1 = (f32[256,2]{0,1:T(2,128)S(1)}, bf16[2,64,256]{2,1,0:T(8,128)(2,1)}) fusion(bf16[256,128]{0,1:T(8,128)(2,1)S(1)} %copy.74, bf16[1280,2,64]{0,2,1:T(8,128)(2,1)S(1)} %bitcast.213, f32[2,256,1280]{2,1,0:T(8,128)} %fusion.36), kind=kOutput, calls=%fused_computation.137 | convolution fusion | flops 84704768 | bytes 3082240 | tf_op jit(solution)/shard_map/gqk,kgc->qgc/dot_general | solution.py:91
  123.2 20.4 %collective-permute-done.5 = bf16[2,256,512]{2,1,0:T(8,128)(2,1)} collective-permute-done((bf16[2,256,512]{2,1,0:T(8,128)(2,1)}, bf16[2,256,512]{2,1,0:T(8,128)(2,1)}, u32[]{:S(2)}, u32[]{:S(2)}) %collective-permute-start.5) | collective-permute-done | bytes 524320 | tf_op jit(solution)/shard_map/ppermute | solution.py:16
  149.8 3.6 %fusion.59 = f32[32,32,3,512]{3,1,2,0:T(8,128)} fusion(bf16[32,32,256,1]{2,1,3,0:T(8,128)(2,1)S(1)} %bitcast.230, bf16[2,256,512]{2,1,0:T(8,128)(2,1)S(1)} %fusion.58, bf16[1,256,512]{2,1,0:T(8,128)(2,1)S(1)} %maximum_bitcast_fusion.4), kind=kOutput, calls=%fused_computation.93 | convolution fusion | flops 806879232 | bytes 7602176 | tf_op jit(solution)/shard_map/rd,wrh->dwh/dot_general | solution.py:186
  153.6 4.4 %pad_maximum_fusion = f32[32,33,4,512]{3,1,2,0:T(8,128)S(1)} fusion(f32[32,1,4,512]{3,1,2,0:T(1,128)S(1)} %scatter.8, f32[32,32,1,512]{3,1,2,0:T(8,128)S(1)} %copy-done.7, f32[32,32,3,512]{3,1,2,0:T(8,128)} %fusion.59), kind=kLoop, calls=%fused_computation | loop fusion | flops 4325376 | bytes 17301504 | tf_op jit(solution)/shard_map/concatenate | solution.py:193
  158.0 5.6 %constant_dynamic-slice_fusion.1 = (f32[2,2,1,2,2,33,4,512]{7,5,6,4,3,2,1,0:T(8,128)}, f32[2,2,1,2,2,33,4,512]{7,5,6,4,3,2,1,0:T(8,128)}) fusion(f32[2,2,2,2,2,33,4,512]{7,5,6,4,3,2,1,0:T(8,128)S(1)} %bitcast.212, s32[]{:T(128)S(6)} %select_n.94, s32[]{:T(128)S(6)} %select_n.95), kind=kLoop, calls=%fused_computation.147 | loop fusion | bytes 17301512 | tf_op jit(solution)/shard_map/jit(dynamic_index_in_dim)/dynamic_slice | solution.py:37
  163.5 7.4 %copy.116 = f32[2,2,1,2,2,33,4,512]{7,6,5,4,3,0,1,2:T(4,128)} copy(f32[2,2,1,2,2,33,4,512]{7,5,6,4,3,2,1,0:T(8,128)} %get-tuple-element.95) | data formatting | bytes 8650752 | tf_op jit(solution)/shard_map/jit(dynamic_index_in_dim)/dynamic_slice | solution.py:38
  171.0 7.7 %collective-permute-done.8 = f32[2,2,2,2,33,4,512]{6,5,4,3,2,0,1:T(4,128)} collective-permute-done((f32[2,2,2,2,33,4,512]{6,5,4,3,2,0,1:T(4,128)}, f32[2,2,2,2,33,4,512]{6,5,4,3,2,0,1:T(4,128)}, u32[]{:S(2)}, u32[]{:S(2)}) %collective-permute-start.8) | collective-permute-done | bytes 4325408 | tf_op jit(solution)/shard_map/ppermute | solution.py:40
  178.7 7.5 %bitcast_add_fusion = f32[2,2,2,2,33,4,512]{6,5,4,3,2,0,1:T(4,128)S(1)} fusion(f32[2,2,2,2,33,4,512]{6,5,4,3,2,0,1:T(4,128)} %collective-permute-done.8, f32[2,2,1,2,2,33,4,512]{7,5,6,4,3,2,1,0:T(8,128)} %get-tuple-element.94), kind=kLoop, calls=%fused_computation.2 | loop fusion | flops 1081344 | bytes 12976128 | tf_op jit(solution)/shard_map/add | solution.py:40
  189.5 19.1 %collective-permute-start.11 = (f32[2,2,2,33,4,256]{5,4,3,2,1,0:T(4,128)}, f32[2,2,2,33,4,256]{5,4,3,2,1,0:T(4,128)}, u32[]{:S(2)}, u32[]{:S(2)}) collective-permute-start(f32[2,2,2,33,4,256]{5,4,3,2,1,0:T(4,128)} %dynamic-slice_bitcast_fusion), channel_id=1, source_target_pairs={{0,8},{4,12},{8,0},{12,4},{16,24},{20,28},{24,16},{28,20},{1,9},{5... | collective-permute-start | bytes 3244040 | tf_op jit(solution)/shard_map/ppermute | solution.py:40
  209.7 23.3 %collective-permute-done.11 = f32[2,2,2,33,4,256]{5,4,3,2,1,0:T(4,128)} collective-permute-done((f32[2,2,2,33,4,256]{5,4,3,2,1,0:T(4,128)}, f32[2,2,2,33,4,256]{5,4,3,2,1,0:T(4,128)}, u32[]{:S(2)}, u32[]{:S(2)}) %collective-permute-start.11) | collective-permute-done | bytes 1081376 | tf_op jit(solution)/shard_map/ppermute | solution.py:40
  240.1 9.6 %collective-permute-done.12 = f32[2,2,33,4,256]{4,3,2,1,0:T(4,128)S(1)} collective-permute-done((f32[2,2,33,4,256]{4,3,2,1,0:T(4,128)}, f32[2,2,33,4,256]{4,3,2,1,0:T(4,128)S(1)}, u32[]{:S(2)}, u32[]{:S(2)}) %collective-permute-start.12) | collective-permute-done | bytes 540704 | tf_op jit(solution)/shard_map/ppermute | solution.py:40
  255.2 11.4 %collective-permute-done.13 = f32[2,33,4,512]{3,2,1,0:T(4,128)} collective-permute-done((f32[2,33,4,512]{3,2,1,0:T(4,128)S(1)}, f32[2,33,4,512]{3,2,1,0:T(4,128)}, u32[]{:S(2)}, u32[]{:S(2)}) %collective-permute-start.13) | collective-permute-done | bytes 540704 | tf_op jit(solution)/shard_map/ppermute | solution.py:40
  267.9 2.7 collective-permute-start.14
  270.5 10.3 %collective-permute-done.14 = f32[33,4,512]{2,1,0:T(4,128)S(1)} collective-permute-done((f32[33,4,512]{2,1,0:T(4,128)S(1)}, f32[33,4,512]{2,1,0:T(4,128)S(1)}, u32[]{:S(2)}, u32[]{:S(2)}) %collective-permute-start.14) | collective-permute-done | bytes 270368 | tf_op jit(solution)/shard_map/ppermute | solution.py:40
  (206 shorter events, 101.3 us)
Async XLA Ops:
  1.9 18.6 %copy-start.29 = (bf16[1024,4,512]{2,1,0:T(4,128)(2,1)S(1)}, bf16[1024,4,512]{2,1,0:T(4,128)(2,1)}, u32[]{:S(2)}) copy-start(bf16[1024,4,512]{2,1,0:T(4,128)(2,1)} %param.23) | copy-start | bytes 12582916
  6.4 40.0 %collective-permute-start = (bf16[2,256,512]{2,1,0:T(8,128)(2,1)}, bf16[2,256,512]{2,1,0:T(8,128)(2,1)}, u32[]{:S(2)}, u32[]{:S(2)}) collective-permute-start(bf16[2,256,512]{2,1,0:T(8,128)(2,1)} %slice.240), channel_id=1, source_target_pairs={{0,16},{4,20},{8,24},{12,28},{1,17},{5,21},{9,25},{13,29},{2,18},{... | collective-permute-start | bytes 1572872 | tf_op jit(solution)/shard_map/ppermute | solution.py:16
  12.1 35.4 %collective-permute-start.1 = (bf16[2,256,512]{2,1,0:T(8,128)(2,1)}, bf16[2,256,512]{2,1,0:T(8,128)(2,1)}, u32[]{:S(2)}, u32[]{:S(2)}) collective-permute-start(bf16[2,256,512]{2,1,0:T(8,128)(2,1)} %slice.240), channel_id=1, source_target_pairs={{0,12},{4,16},{8,20},{12,24},{16,28},{1,13},{5,17},{9,21},{13,25},... | collective-permute-start | bytes 1572872 | tf_op jit(solution)/shard_map/ppermute | solution.py:16
  15.5 33.1 %collective-permute-start.2 = (bf16[2,256,512]{2,1,0:T(8,128)(2,1)}, bf16[2,256,512]{2,1,0:T(8,128)(2,1)}, u32[]{:S(2)}, u32[]{:S(2)}) collective-permute-start(bf16[2,256,512]{2,1,0:T(8,128)(2,1)} %slice.240), channel_id=1, source_target_pairs={{0,8},{4,12},{8,16},{12,20},{16,24},{20,28},{1,9},{5,13},{9,17},{1... | collective-permute-start | bytes 1572872 | tf_op jit(solution)/shard_map/ppermute | solution.py:16
  18.4 31.3 %collective-permute-start.3 = (bf16[2,256,512]{2,1,0:T(8,128)(2,1)}, bf16[2,256,512]{2,1,0:T(8,128)(2,1)}, u32[]{:S(2)}, u32[]{:S(2)}) collective-permute-start(bf16[2,256,512]{2,1,0:T(8,128)(2,1)} %slice.240), channel_id=1, source_target_pairs={{0,4},{4,8},{8,12},{12,16},{16,20},{20,24},{24,28},{1,5},{5,9},{9,... | collective-permute-start | bytes 1572872 | tf_op jit(solution)/shard_map/ppermute | solution.py:16
  95.3 7.4 %copy-start.13 = (f32[2,64,1280]{2,1,0:T(8,128)S(1)}, f32[2,64,1280]{2,1,0:T(8,128)}, u32[]{:S(2)}) copy-start(f32[2,64,1280]{2,1,0:T(8,128)} %fusion.70) | copy-start | bytes 1966084
  95.7 8.1 %copy-start.14 = (f32[2,64,1280]{2,1,0:T(8,128)S(1)}, f32[2,64,1280]{2,1,0:T(8,128)}, u32[]{:S(2)}) copy-start(f32[2,64,1280]{2,1,0:T(8,128)} %fusion.67) | copy-start | bytes 1966084
  112.3 6.6 %copy-start.40 = (bf16[2,64,256]{2,1,0:T(8,128)(2,1)S(1)}, bf16[2,64,256]{2,1,0:T(8,128)(2,1)}, u32[]{:S(2)}) copy-start(bf16[2,64,256]{2,1,0:T(8,128)(2,1)} %get-tuple-element.125) | copy-start | bytes 196612
  112.3 6.7 %copy-start.41 = (bf16[2,64,256]{2,1,0:T(8,128)(2,1)S(1)}, bf16[2,64,256]{2,1,0:T(8,128)(2,1)}, u32[]{:S(2)}) copy-start(bf16[2,64,256]{2,1,0:T(8,128)(2,1)} %get-tuple-element.127) | copy-start | bytes 196612
  112.3 6.8 %copy-start.42 = (bf16[2,64,256]{2,1,0:T(8,128)(2,1)S(1)}, bf16[2,64,256]{2,1,0:T(8,128)(2,1)}, u32[]{:S(2)}) copy-start(bf16[2,64,256]{2,1,0:T(8,128)(2,1)} %get-tuple-element.121) | copy-start | bytes 196612
  112.3 8.0 %copy-start.21 = (bf16[256,1024]{0,1:T(8,128)(2,1)S(1)}, bf16[256,1024]{0,1:T(8,128)(2,1)}, u32[]{:S(2)}) copy-start(bf16[256,1024]{0,1:T(8,128)(2,1)} %bitcast_select_fusion) | copy-start | bytes 1572868
  113.7 9.5 %collective-permute-start.4 = (bf16[2,256,512]{2,1,0:T(8,128)(2,1)}, bf16[2,256,512]{2,1,0:T(8,128)(2,1)}, u32[]{:S(2)}, u32[]{:S(2)}) collective-permute-start(bf16[2,256,512]{2,1,0:T(8,128)(2,1)} %get-tuple-element.98), channel_id=1, source_target_pairs={{4,0},{8,4},{12,8},{16,12},{20,16},{24,20},{28,24},{5,1},{9,5},{13... | collective-permute-start | bytes 1572872 | tf_op jit(solution)/shard_map/ppermute | solution.py:16
  115.0 28.7 %collective-permute-start.5 = (bf16[2,256,512]{2,1,0:T(8,128)(2,1)}, bf16[2,256,512]{2,1,0:T(8,128)(2,1)}, u32[]{:S(2)}, u32[]{:S(2)}) collective-permute-start(bf16[2,256,512]{2,1,0:T(8,128)(2,1)} %get-tuple-element.101), channel_id=1, source_target_pairs={{8,0},{12,4},{16,8},{20,12},{24,16},{28,20},{9,1},{13,5},{17,9},{2... | collective-permute-start | bytes 1572872 | tf_op jit(solution)/shard_map/ppermute | solution.py:16
  116.3 28.8 %collective-permute-start.6 = (bf16[2,256,512]{2,1,0:T(8,128)(2,1)}, bf16[2,256,512]{2,1,0:T(8,128)(2,1)}, u32[]{:S(2)}, u32[]{:S(2)}) collective-permute-start(bf16[2,256,512]{2,1,0:T(8,128)(2,1)} %get-tuple-element.100), channel_id=1, source_target_pairs={{12,0},{16,4},{20,8},{24,12},{28,16},{13,1},{17,5},{21,9},{25,13},... | collective-permute-start | bytes 1572872 | tf_op jit(solution)/shard_map/ppermute | solution.py:16
  117.6 27.5 %collective-permute-start.7 = (bf16[2,256,512]{2,1,0:T(8,128)(2,1)}, bf16[2,256,512]{2,1,0:T(8,128)(2,1)}, u32[]{:S(2)}, u32[]{:S(2)}) collective-permute-start(bf16[2,256,512]{2,1,0:T(8,128)(2,1)} %get-tuple-element.99), channel_id=1, source_target_pairs={{16,0},{20,4},{24,8},{28,12},{17,1},{21,5},{25,9},{29,13},{18,2},{... | collective-permute-start | bytes 1572872 | tf_op jit(solution)/shard_map/ppermute | solution.py:16
  122.8 24.2 %copy-start.30 = (bf16[1024,4,512]{2,1,0:T(4,128)(2,1)S(1)}, bf16[1024,4,512]{2,1,0:T(4,128)(2,1)}, u32[]{:S(2)}) copy-start(bf16[1024,4,512]{2,1,0:T(4,128)(2,1)} %param.23) | copy-start | bytes 12582916
  171.0 7.7 %collective-permute-start.8 = (f32[2,2,2,2,33,4,512]{6,5,4,3,2,0,1:T(4,128)}, f32[2,2,2,2,33,4,512]{6,5,4,3,2,0,1:T(4,128)}, u32[]{:S(2)}, u32[]{:S(2)}) collective-permute-start(f32[2,2,2,2,33,4,512]{6,5,4,3,2,0,1:T(4,128)} %bitcast.210), channel_id=1, source_target_pairs={{0,4},{4,0},{8,12},{12,8},{16,20},{20,16},{24,28},{28,24},{1,5},{5... | collective-permute-start | bytes 12976136 | tf_op jit(solution)/shard_map/ppermute | solution.py:40
  189.5 43.5 %collective-permute-start.11 = (f32[2,2,2,33,4,256]{5,4,3,2,1,0:T(4,128)}, f32[2,2,2,33,4,256]{5,4,3,2,1,0:T(4,128)}, u32[]{:S(2)}, u32[]{:S(2)}) collective-permute-start(f32[2,2,2,33,4,256]{5,4,3,2,1,0:T(4,128)} %dynamic-slice_bitcast_fusion), channel_id=1, source_target_pairs={{0,8},{4,12},{8,0},{12,4},{16,24},{20,28},{24,16},{28,20},{1,9},{5... | collective-permute-start | bytes 3244040 | tf_op jit(solution)/shard_map/ppermute | solution.py:40
  209.7 26.0 %collective-permute-start.9 = (f32[2,2,2,33,4,256]{5,4,3,2,1,0:T(4,128)}, f32[2,2,2,33,4,256]{5,4,3,2,1,0:T(4,128)}, u32[]{:S(2)}, u32[]{:S(2)}) collective-permute-start(f32[2,2,2,33,4,256]{5,4,3,2,1,0:T(4,128)} %dynamic-slice_bitcast_fusion.1), channel_id=1, source_target_pairs={{0,16},{4,20},{8,24},{12,28},{16,0},{20,4},{24,8},{28,12},{1,17},{... | collective-permute-start | bytes 3244040 | tf_op jit(solution)/shard_map/ppermute | solution.py:40
  235.8 14.0 %collective-permute-start.12 = (f32[2,2,33,4,256]{4,3,2,1,0:T(4,128)}, f32[2,2,33,4,256]{4,3,2,1,0:T(4,128)S(1)}, u32[]{:S(2)}, u32[]{:S(2)}) collective-permute-start(f32[2,2,33,4,256]{4,3,2,1,0:T(4,128)} %dynamic-slice_bitcast_fusion.2), channel_id=1, source_target_pairs={{0,16},{4,20},{8,24},{12,28},{16,0},{20,4},{24,8},{28,12},{1,17},{... | collective-permute-start | bytes 1622024 | tf_op jit(solution)/shard_map/ppermute | solution.py:40
  238.3 13.9 %collective-permute-start.10 = (f32[2,2,33,4,256]{4,3,2,1,0:T(4,128)S(1)}, f32[2,2,33,4,256]{4,3,2,1,0:T(4,128)S(1)}, u32[]{:S(2)}, u32[]{:S(2)}) collective-permute-start(f32[2,2,33,4,256]{4,3,2,1,0:T(4,128)S(1)} %dynamic-slice_bitcast_fusion.3), channel_id=1, source_target_pairs={{0,8},{4,12},{8,0},{12,4},{16,24},{20,28},{24,16},{28,20},{1,9},{5... | collective-permute-start | bytes 1622024 | tf_op jit(solution)/shard_map/ppermute | solution.py:40
  253.4 30.2 %copy-start.12 = (f32[256,1024]{1,0:T(8,128)S(1)}, f32[256,1024]{1,0:T(8,128)}, u32[]{:S(2)}) copy-start(f32[256,1024]{1,0:T(8,128)} %copy-done.11) | copy-start | bytes 3145732
  253.5 13.1 %collective-permute-start.13 = (f32[2,33,4,512]{3,2,1,0:T(4,128)S(1)}, f32[2,33,4,512]{3,2,1,0:T(4,128)}, u32[]{:S(2)}, u32[]{:S(2)}) collective-permute-start(f32[2,33,4,512]{3,2,1,0:T(4,128)S(1)} %fusion.74), channel_id=1, source_target_pairs={{0,1},{1,0},{2,3},{3,2},{4,5},{5,4},{6,7},{7,6},{8,9},{9,8},{10,11... | collective-permute-start | bytes 1622024 | tf_op jit(solution)/shard_map/ppermute | solution.py:40
  267.9 12.9 %collective-permute-start.14 = (f32[33,4,512]{2,1,0:T(4,128)S(1)}, f32[33,4,512]{2,1,0:T(4,128)S(1)}, u32[]{:S(2)}, u32[]{:S(2)}) collective-permute-start(f32[33,4,512]{2,1,0:T(4,128)S(1)} %dynamic-slice_bitcast_fusion.4), channel_id=1, source_target_pairs={{0,2},{1,3},{2,0},{3,1},{4,6},{5,7},{6,4},{7,5},{8,10},{9,11},{10,... | collective-permute-start | bytes 811016 | tf_op jit(solution)/shard_map/ppermute | solution.py:40
  (35 other events, 78.9 us)

commit v3 on v1

--- a/solution.py
+++ b/solution.py
@@ -20,64 +20,68 @@
     return n > 0 and n & (n - 1) == 0
 
 
-def butterfly_sum(value, axes):
-    for axis in axes:
-        peers = lax.axis_size(axis)
-        flip = 1
-        while flip < peers:
-            pairs = [(i, i ^ flip) for i in range(peers)]
-            value = value + lax.ppermute(value, axis, pairs)
-            flip *= 2
-    return value
-
-
-def halve(value, dim, axis, flip):
+def halve(value, dim, axis, flip, send_type):
     peers = lax.axis_size(axis)
     bit = (lax.axis_index(axis) // flip) % 2
     keep = lax.dynamic_index_in_dim(value, bit, dim, keepdims=False)
     send = lax.dynamic_index_in_dim(value, 1 - bit, dim, keepdims=False)
     pairs = [(i, i ^ flip) for i in range(peers)]
-    return keep + lax.ppermute(send, axis, pairs)
-
-
-def scatter_rows(value, axes):
+    return keep + lax.ppermute(send.astype(send_type), axis, pairs).astype(keep.dtype)
+
+
+def swap_add(value, axis, flip):
+    peers = lax.axis_size(axis)
+    pairs = [(i, i ^ flip) for i in range(peers)]
+    return value + lax.ppermute(value, axis, pairs)
+
+
+def scatter_rows(value, tally, axes, first_axis, wire_type):
     sizes = [lax.axis_size(axis) for axis in axes]
     rows = value.shape[0]
     groups = math.prod(sizes)
     if not all(is_power_of_two(n) for n in sizes) or rows % groups:
-        return lax.psum_scatter(value, axes, scatter_dimension=0, tiled=True)
+        return (
+            lax.psum_scatter(value, axes, scatter_dimension=0, tiled=True),
+            lax.psum(tally, axes),
+        )
     stages = [
         (axis, 1 << (n.bit_length() - 2 - i))
         for axis, n in zip(axes, sizes)
         for i in range(n.bit_length() - 1)
     ]
+    if not stages:
+        return value, tally
     rest = value.shape[1:]
     value = value.reshape((2,) * len(stages) + (rows // groups,) + rest)
     names = list(stages)
 
-    def step(part, part_names, stage):
+    def step(part, part_names, stage, send_type):
         dim = part_names.index(stage)
-        return halve(part, dim, *stage), part_names[:dim] + part_names[dim + 1 :]
-
-    first = ("tm", 1) if ("tm", 1) in stages else stages[-1]
-    value, names = step(value, names, first)
-    middle = [s for s in stages if s[0] == axes[0] and s != first]
-    tail = [s for s in stages if s[0] != axes[0] and s != first]
+        return halve(part, dim, *stage, send_type), part_names[:dim] + part_names[dim + 1 :]
+
+    first = (first_axis, 1) if (first_axis, 1) in stages else stages[-1]
+    value, names = step(value, names, first, value.dtype)
+    tally = swap_add(tally, *first)
+    middle = [s for s in stages if s[0] == first[0] and s != first]
+    tail = [s for s in stages if s[0] != first[0]][::-1]
     if len(middle) > 1 and rest[-1] % 2 == 0:
         cut = rest[-1] // 2
         left, right = value[..., :cut], value[..., cut:]
         left_names, right_names = list(names), list(names)
         for a, b in zip(middle, middle[::-1]):
-            left, left_names = step(left, left_names, a)
-            right, right_names = step(right, right_names, b)
+            left, left_names = step(left, left_names, a, wire_type)
+            tally = swap_add(tally, *a)
+            right, right_names = step(right, right_names, b, wire_type)
         value = jnp.concatenate([left, right], axis=-1)
         names = left_names
     else:
         for stage in middle:
-            value, names = step(value, names, stage)
-    for stage in tail[::-1]:
-        value, names = step(value, names, stage)
-    return value
+            value, names = step(value, names, stage, wire_type)
+            tally = swap_add(tally, *stage)
+    for stage in tail:
+        value, names = step(value, names, stage, wire_type)
+        tally = swap_add(tally, *stage)
+    return value, tally
 
 
 def band_block(queries, keys_blk, values_blk, grad_attn, valid, inv_scale):
@@ -131,12 +135,7 @@
     earlier = [shifted(key_vals, "tm", offset) for offset in range(span, 0, -1)]
     extended = jnp.concatenate(earlier + [key_vals], axis=1)
     local_count = jnp.sum(loss_mask.astype(jnp.int32))
-    if all(is_power_of_two(lax.axis_size(axis)) for axis in ("tm", "night")):
-        total_count = butterfly_sum(local_count, ("tm", "night")).astype(jnp.float32)
-    else:
-        total_count = lax.psum(local_count, ("tm", "night")).astype(jnp.float32)
     tokens_all = rows * lax.axis_size("tm") * lax.axis_size("night")
-    loss_scale = jnp.float32(tokens_all) / total_count
     local_cot = cotangent[0]
     grad_out = jnp.where(loss_mask[0][:, None] > 0, local_cot, jnp.zeros_like(local_cot))
     grad_attn = jnp.dot(grad_out, weights[:, 3, :], preferred_element_type=jnp.float32).astype(
@@ -187,14 +186,19 @@
         "wrh,dwh->rd", grad_proj, proj_weights, preferred_element_type=jnp.float32
     )
     along = jnp.sum(grad_normed * normed_full, axis=-1) / width
-    grad_input = (
-        loss_scale * inv_rms[:, None] * (grad_normed - normed_full * along[:, None])
-    ).astype(jnp.bfloat16)
+    unscaled_input = inv_rms[:, None] * (grad_normed - normed_full * along[:, None])
     proj_part = jnp.einsum("rd,wrh->dwh", normed, grad_proj, preferred_element_type=jnp.float32)
     out_part = jnp.einsum("rd,rh->dh", grad_out, attended_all, preferred_element_type=jnp.float32)
-    summed = scatter_rows(
-        jnp.concatenate([proj_part, out_part[:, None]], axis=1), ("tm", "night")
-    )
+    summed, count = scatter_rows(
+        jnp.concatenate([proj_part, out_part[:, None]], axis=1),
+        local_count,
+        ("tm", "night"),
+        "tm",
+        jnp.float32,
+    )
+    total_count = count.astype(jnp.float32)
+    loss_scale = jnp.float32(tokens_all) / total_count
+    grad_input = (loss_scale * unscaled_input).astype(jnp.bfloat16)
     grad_weights = summed * (jnp.sqrt(jnp.float32(tokens_all)) / total_count)
     return (grad_input[None], grad_weights)
 

time: 270 us -> 265 us (0.981)
  waiting for transfers between devices: 94.3 us -> 72 us
  starting transfers between devices: 64.1 us -> 80.4 us
    ppermute x8, waiting for transfers between devices: 43.5 us -> 22.8 us  [shifted(): return lax.ppermute(value, axis, pairs)]
    ppermute x12, starting transfers between devices: 47.3 us -> 61.1 us  [the longest x7 41.5 us: halve(): lax.ppermute(send.astype(send_type), axis, pairs).astype(keep.dtype)]
    unnamed x83 -> x81, local copies, waits for them, and re-layouts: 9.01 us -> 12 us
  transfers between devices with their start and end apart: 20 -> 20, of which waited for: 13 -> 12; matrix products, arithmetic and copies ran while one was open for 9% -> 9% of each run, Pallas kernels for 0% -> 0%
where the time goes in v3:
time: 265 us; the launch traced here: 264 us
  starting transfers between devices  80.4 us (30%)
  waiting for transfers between devices  72 us (27%)
  local copies, waits for them, and re-layouts  47.8 us (18%)
  matrix products  38.6 us (15%)
  other arithmetic  19.9 us (8%)
  between operations  5.24 us (2%)
    ppermute x7, waiting for transfers between devices, halve(): lax.ppermute(send.astype(send_type), axis, pairs).astype(keep.dtype)  45.8 us
    ppermute x7, starting transfers between devices, halve(): lax.ppermute(send.astype(send_type), axis, pairs).astype(keep.dtype)  41.5 us
    ppermute x8, waiting for transfers between devices, shifted(): return lax.ppermute(value, axis, pairs)  22.8 us
    ppermute x5, starting transfers between devices, swap_add(): return value + lax.ppermute(value, axis, pairs)  19.7 us
    ppermute x8, starting transfers between devices, shifted(): return lax.ppermute(value, axis, pairs)  19.3 us
    unnamed x81, local copies, waits for them, and re-layouts  12 us
    another operation x8, local copies, waits for them, and re-layouts, shards(): update = jnp.stack([grad_key, grad_value]).reshape(2, key_len, group_cols)  10.3 us
    add x6, other arithmetic, halve(): keep + lax.ppermute(send.astype(send_type), axis, pairs).astype(keep.dtype)  9.55 us
  transfers between devices with their start and end apart: 20, of which 12 were waited for; matrix products, arithmetic and copies ran while one was open for 9% of the time, Pallas kernels for 0%

profile of v3, /device:TPU:0, one launch (start us, length us, event | category | flops | bytes accessed | tf_op | source)
XLA Modules:
  0.0 263.9 jit_solution(10410113645345326544)
XLA Ops:
  1.9 3.6 %fusion.51 = bf16[3,256,512]{2,1,0:T(8,128)(2,1)S(1)} fusion(bf16[1024,3,512]{2,1,0:T(4,128)(2,1)} %bitcast.250, bf16[1,256,1024]{2,1,0:T(8,128)(2,1)} %param.20, f32[256]{0:T(256)S(1)} %add_rsqrt_fusion), kind=kOutput, calls=%fused_computation.68 | convolution fusion | flops 806486016 | bytes 4457472 | tf_op jit(solution)/shard_map/rd,dwh->wrh/dot_general | solution.py:130
  6.3 3.2 %collective-permute-start.8 = (bf16[2,256,512]{2,1,0:T(8,128)(2,1)}, bf16[2,256,512]{2,1,0:T(8,128)(2,1)}, u32[]{:S(2)}, u32[]{:S(2)}) collective-permute-start(bf16[2,256,512]{2,1,0:T(8,128)(2,1)} %slice.208), channel_id=1, source_target_pairs={{0,4},{4,8},{8,12},{12,16},{16,20},{20,24},{24,28},{1,5},{5,9},{9,... | collective-permute-start | bytes 1572872 | tf_op jit(solution)/shard_map/ppermute | solution.py:16
  9.5 4.4 %collective-permute-start.7 = (bf16[2,256,512]{2,1,0:T(8,128)(2,1)}, bf16[2,256,512]{2,1,0:T(8,128)(2,1)}, u32[]{:S(2)}, u32[]{:S(2)}) collective-permute-start(bf16[2,256,512]{2,1,0:T(8,128)(2,1)} %slice.208), channel_id=1, source_target_pairs={{0,8},{4,12},{8,16},{12,20},{16,24},{20,28},{1,9},{5,13},{9,17},{1... | collective-permute-start | bytes 1572872 | tf_op jit(solution)/shard_map/ppermute | solution.py:16
  13.9 4.3 %collective-permute-start.6 = (bf16[2,256,512]{2,1,0:T(8,128)(2,1)}, bf16[2,256,512]{2,1,0:T(8,128)(2,1)}, u32[]{:S(2)}, u32[]{:S(2)}) collective-permute-start(bf16[2,256,512]{2,1,0:T(8,128)(2,1)} %slice.208), channel_id=1, source_target_pairs={{0,12},{4,16},{8,20},{12,24},{16,28},{1,13},{5,17},{9,21},{13,25},... | collective-permute-start | bytes 1572872 | tf_op jit(solution)/shard_map/ppermute | solution.py:16
  21.0 4.5 %slice.186 = bf16[1024,1,512]{2,1,0:T(2,128)(2,1)S(1)} slice(bf16[1024,4,512]{2,1,0:T(4,128)(2,1)} %param.21), slice={[0:1024], [3:4], [0:512]} | slice | bytes 2097152 | tf_op jit(solution)/shard_map/slice | solution.py:141
  35.3 11.4 %collective-permute-start.1 = (s32[]{:T(128)}, s32[]{:T(128)}, u32[]{:S(2)}, u32[]{:S(2)}) collective-permute-start(s32[]{:T(128)} %add.169), channel_id=1, source_target_pairs={{0,16},{4,20},{8,24},{12,28},{16,0},{20,4},{24,8},{28,12},{1,17},{... | collective-permute-start | bytes 20 | tf_op jit(solution)/shard_map/ppermute | solution.py:35
  51.5 2.9 %collective-permute-start.3 = (s32[]{:T(128)}, s32[]{:T(128)}, u32[]{:S(2)}, u32[]{:S(2)}) collective-permute-start(s32[]{:T(128)} %add.171), channel_id=1, source_target_pairs={{0,1},{1,0},{2,3},{3,2},{4,5},{5,4},{6,7},{7,6},{8,9},{9,8},{10,11... | collective-permute-start | bytes 20 | tf_op jit(solution)/shard_map/ppermute | solution.py:35
  55.7 4.0 %collective-permute-start.4 = (s32[]{:T(128)}, s32[]{:T(128)}, u32[]{:S(2)}, u32[]{:S(2)}) collective-permute-start(s32[]{:T(128)} %add.172), channel_id=1, source_target_pairs={{0,2},{1,3},{2,0},{3,1},{4,6},{5,7},{6,4},{7,5},{8,10},{9,11},{10,... | collective-permute-start | bytes 20 | tf_op jit(solution)/shard_map/ppermute | solution.py:35
  67.7 2.3 fusion.45
  76.8 2.3 fusion.43
  128.1 13.5 %collective-permute-done.12 = bf16[2,256,512]{2,1,0:T(8,128)(2,1)S(1)} collective-permute-done((bf16[2,256,512]{2,1,0:T(8,128)(2,1)S(1)}, bf16[2,256,512]{2,1,0:T(8,128)(2,1)S(1)}, u32[]{:S(2)}, u32[]{:S(2)}) %collective-permute-start.12) | collective-permute-done | bytes 524320 | tf_op jit(solution)/shard_map/ppermute | solution.py:16
  142.1 8.8 %collective-permute-done.10 = bf16[2,256,512]{2,1,0:T(8,128)(2,1)S(1)} collective-permute-done((bf16[2,256,512]{2,1,0:T(8,128)(2,1)S(1)}, bf16[2,256,512]{2,1,0:T(8,128)(2,1)S(1)}, u32[]{:S(2)}, u32[]{:S(2)}) %collective-permute-start.10) | collective-permute-done | bytes 524320 | tf_op jit(solution)/shard_map/ppermute | solution.py:16
  156.8 2.9 %fusion.1 = f32[2,2,2,2,32,4,512]{6,4,5,3,2,1,0:T(8,128)} fusion(s32[]{:T(128)S(6)} %select_n.95, f32[2,2,2,2,2,32,3,512]{7,5,6,4,3,2,1,0:T(8,128)S(1)} %fusion.64, f32[2,2,2,2,2,32,1,512]{7,5,6,4,3,2,1,0:T(8,128)S(1)} %convolution_bitcast_fusion), kind=kLoop, calls=%fused_computation.6 | loop fusion | flops 1048576 | bytes 12582916 | tf_op jit(solution)/shard_map/jit(dynamic_index_in_dim)/squeeze | solution.py:27
  161.8 7.1 %collective-permute-done.13 = f32[2,2,2,2,32,4,512]{6,4,5,3,2,1,0:T(8,128)} collective-permute-done((f32[2,2,2,2,32,4,512]{6,4,5,3,2,1,0:T(8,128)}, f32[2,2,2,2,32,4,512]{6,4,5,3,2,1,0:T(8,128)}, u32[]{:S(2)}, u32[]{:S(2)}) %collective-permute-start.13) | collective-permute-done | bytes 4194336 | tf_op jit(solution)/shard_map/ppermute | solution.py:29
  168.9 4.2 %fusion.4 = f32[2,2,2,2,32,4,512]{6,4,5,3,2,1,0:T(8,128)S(1)} fusion(f32[2,2,2,2,32,4,512]{6,4,5,3,2,1,0:T(8,128)} %collective-permute-done.13, s32[]{:T(128)S(6)} %select_n.94, f32[2,2,2,2,2,32,3,512]{7,5,6,4,3,2,1,0:T(8,128)} %copy-done, f32[2,2,2,2,2,32,1,512]{7,5,6,4,3,2,1,0:T(8,128)S(1)} %convolution_bitcast_fusion), kind=kLoop, calls=%fused_computation.9 | loop fusion | flops 2097152 | bytes 16777220 | tf_op jit(solution)/shard_map/add | solution.py:29
  175.2 2.3 collective-permute-start.14
  178.6 15.9 %collective-permute-start.16 = (f32[2,2,2,32,4,256]{5,3,4,2,1,0:T(8,128)}, f32[2,2,2,32,4,256]{5,3,4,2,1,0:T(8,128)}, u32[]{:S(2)}, u32[]{:S(2)}) collective-permute-start(f32[2,2,2,32,4,256]{5,3,4,2,1,0:T(8,128)} %dynamic-slice_bitcast_fusion), channel_id=1, source_target_pairs={{0,8},{4,12},{8,0},{12,4},{16,24},{20,28},{24,16},{28,20},{1,9},{5... | collective-permute-start | bytes 3145736 | tf_op jit(solution)/shard_map/ppermute | solution.py:29
  194.5 6.8 %collective-permute-done.14 = f32[2,2,2,32,4,256]{5,3,4,2,1,0:T(8,128)} collective-permute-done((f32[2,2,2,32,4,256]{5,3,4,2,1,0:T(8,128)S(1)}, f32[2,2,2,32,4,256]{5,3,4,2,1,0:T(8,128)}, u32[]{:S(2)}, u32[]{:S(2)}) %collective-permute-start.14) | collective-permute-done | bytes 1048608 | tf_op jit(solution)/shard_map/ppermute | solution.py:29
  203.9 17.5 %collective-permute-start.15 = (f32[2,2,32,4,256]{4,2,3,1,0:T(8,128)}, f32[2,2,32,4,256]{4,2,3,1,0:T(8,128)}, u32[]{:S(2)}, u32[]{:S(2)}) collective-permute-start(f32[2,2,32,4,256]{4,2,3,1,0:T(8,128)} %dynamic-slice_bitcast_fusion.3), channel_id=1, source_target_pairs={{0,8},{4,12},{8,0},{12,4},{16,24},{20,28},{24,16},{28,20},{1,9},{5... | collective-permute-start | bytes 1572872 | tf_op jit(solution)/shard_map/ppermute | solution.py:29
  224.2 9.2 %collective-permute-done.15 = f32[2,2,32,4,256]{4,2,3,1,0:T(8,128)} collective-permute-done((f32[2,2,32,4,256]{4,2,3,1,0:T(8,128)}, f32[2,2,32,4,256]{4,2,3,1,0:T(8,128)}, u32[]{:S(2)}, u32[]{:S(2)}) %collective-permute-start.15) | collective-permute-done | bytes 524320 | tf_op jit(solution)/shard_map/ppermute | solution.py:29
  234.5 2.5 collective-permute-done.17
  239.8 10.6 %collective-permute-done.18 = f32[2,32,4,512]{3,1,2,0:T(8,128)S(1)} collective-permute-done((f32[2,32,4,512]{3,1,2,0:T(8,128)S(1)}, f32[2,32,4,512]{3,1,2,0:T(8,128)S(1)}, u32[]{:S(2)}, u32[]{:S(2)}) %collective-permute-start.18) | collective-permute-done | bytes 524320 | tf_op jit(solution)/shard_map/ppermute | solution.py:29
  250.7 2.7 %collective-permute-start.19 = (f32[32,4,512]{2,1,0:T(4,128)S(1)}, f32[32,4,512]{2,1,0:T(4,128)S(1)}, u32[]{:S(2)}, u32[]{:S(2)}) collective-permute-start(f32[32,4,512]{2,1,0:T(4,128)S(1)} %bitcast.260), channel_id=1, source_target_pairs={{0,2},{1,3},{2,0},{3,1},{4,6},{5,7},{6,4},{7,5},{8,10},{9,11},{10,... | collective-permute-start | bytes 786440 | tf_op jit(solution)/shard_map/ppermute | solution.py:29
  253.4 9.5 %collective-permute-done.19 = f32[32,4,512]{2,1,0:T(4,128)S(1)} collective-permute-done((f32[32,4,512]{2,1,0:T(4,128)S(1)}, f32[32,4,512]{2,1,0:T(4,128)S(1)}, u32[]{:S(2)}, u32[]{:S(2)}) %collective-permute-start.19) | collective-permute-done | bytes 262176 | tf_op jit(solution)/shard_map/ppermute | solution.py:29
  (198 shorter events, 102.2 us)
Async XLA Ops:
  1.9 18.4 %copy-start.37 = (s32[1,256]{1,0:T(1,128)S(1)}, s32[1,256]{1,0:T(1,128)}, u32[]{:S(2)}) copy-start(s32[1,256]{1,0:T(1,128)} %param.23) | copy-start | bytes 3076
  6.3 57.8 %collective-permute-start.8 = (bf16[2,256,512]{2,1,0:T(8,128)(2,1)}, bf16[2,256,512]{2,1,0:T(8,128)(2,1)}, u32[]{:S(2)}, u32[]{:S(2)}) collective-permute-start(bf16[2,256,512]{2,1,0:T(8,128)(2,1)} %slice.208), channel_id=1, source_target_pairs={{0,4},{4,8},{8,12},{12,16},{16,20},{20,24},{24,28},{1,5},{5,9},{9,... | collective-permute-start | bytes 1572872 | tf_op jit(solution)/shard_map/ppermute | solution.py:16
  9.5 53.5 %collective-permute-start.7 = (bf16[2,256,512]{2,1,0:T(8,128)(2,1)}, bf16[2,256,512]{2,1,0:T(8,128)(2,1)}, u32[]{:S(2)}, u32[]{:S(2)}) collective-permute-start(bf16[2,256,512]{2,1,0:T(8,128)(2,1)} %slice.208), channel_id=1, source_target_pairs={{0,8},{4,12},{8,16},{12,20},{16,24},{20,28},{1,9},{5,13},{9,17},{1... | collective-permute-start | bytes 1572872 | tf_op jit(solution)/shard_map/ppermute | solution.py:16
  13.9 48.0 %collective-permute-start.6 = (bf16[2,256,512]{2,1,0:T(8,128)(2,1)}, bf16[2,256,512]{2,1,0:T(8,128)(2,1)}, u32[]{:S(2)}, u32[]{:S(2)}) collective-permute-start(bf16[2,256,512]{2,1,0:T(8,128)(2,1)} %slice.208), channel_id=1, source_target_pairs={{0,12},{4,16},{8,20},{12,24},{16,28},{1,13},{5,17},{9,21},{13,25},... | collective-permute-start | bytes 1572872 | tf_op jit(solution)/shard_map/ppermute | solution.py:16
  18.2 42.6 %collective-permute-start.5 = (bf16[2,256,512]{2,1,0:T(8,128)(2,1)}, bf16[2,256,512]{2,1,0:T(8,128)(2,1)}, u32[]{:S(2)}, u32[]{:S(2)}) collective-permute-start(bf16[2,256,512]{2,1,0:T(8,128)(2,1)} %slice.208), channel_id=1, source_target_pairs={{0,16},{4,20},{8,24},{12,28},{1,17},{5,21},{9,25},{13,29},{2,18},{... | collective-permute-start | bytes 1572872 | tf_op jit(solution)/shard_map/ppermute | solution.py:16
  21.0 13.0 %collective-permute-start = (s32[]{:T(128)}, s32[]{:T(128)}, u32[]{:S(2)}, u32[]{:S(2)}) collective-permute-start(s32[]{:T(128)} %reduce_sum.99), channel_id=1, source_target_pairs={{0,4},{4,0},{8,12},{12,8},{16,20},{20,16},{24,28},{28,24},{1,5},{5... | collective-permute-start | bytes 20 | tf_op jit(solution)/shard_map/ppermute | solution.py:35
  35.3 11.4 %collective-permute-start.1 = (s32[]{:T(128)}, s32[]{:T(128)}, u32[]{:S(2)}, u32[]{:S(2)}) collective-permute-start(s32[]{:T(128)} %add.169), channel_id=1, source_target_pairs={{0,16},{4,20},{8,24},{12,28},{16,0},{20,4},{24,8},{28,12},{1,17},{... | collective-permute-start | bytes 20 | tf_op jit(solution)/shard_map/ppermute | solution.py:35
  47.3 3.6 %collective-permute-start.2 = (s32[]{:T(128)}, s32[]{:T(128)}, u32[]{:S(2)}, u32[]{:S(2)}) collective-permute-start(s32[]{:T(128)} %add.170), channel_id=1, source_target_pairs={{0,8},{4,12},{8,0},{12,4},{16,24},{20,28},{24,16},{28,20},{1,9},{5... | collective-permute-start | bytes 20 | tf_op jit(solution)/shard_map/ppermute | solution.py:35
  51.5 3.6 %collective-permute-start.3 = (s32[]{:T(128)}, s32[]{:T(128)}, u32[]{:S(2)}, u32[]{:S(2)}) collective-permute-start(s32[]{:T(128)} %add.171), channel_id=1, source_target_pairs={{0,1},{1,0},{2,3},{3,2},{4,5},{5,4},{6,7},{7,6},{8,9},{9,8},{10,11... | collective-permute-start | bytes 20 | tf_op jit(solution)/shard_map/ppermute | solution.py:35
  55.7 4.5 %collective-permute-start.4 = (s32[]{:T(128)}, s32[]{:T(128)}, u32[]{:S(2)}, u32[]{:S(2)}) collective-permute-start(s32[]{:T(128)} %add.172), channel_id=1, source_target_pairs={{0,2},{1,3},{2,0},{3,1},{4,6},{5,7},{6,4},{7,5},{8,10},{9,11},{10,... | collective-permute-start | bytes 20 | tf_op jit(solution)/shard_map/ppermute | solution.py:35
  107.5 10.9 %copy-start.6 = (f32[2,64,1280]{2,1,0:T(8,128)S(1)}, f32[2,64,1280]{2,1,0:T(8,128)}, u32[]{:S(2)}) copy-start(f32[2,64,1280]{2,1,0:T(8,128)} %fusion.66) | copy-start | bytes 1966084
  121.8 6.2 %collective-permute-start.9 = (bf16[2,256,512]{2,1,0:T(8,128)(2,1)S(1)}, bf16[2,256,512]{2,1,0:T(8,128)(2,1)S(1)}, u32[]{:S(2)}, u32[]{:S(2)}) collective-permute-start(bf16[2,256,512]{2,1,0:T(8,128)(2,1)S(1)} %get-tuple-element.84), channel_id=1, source_target_pairs={{4,0},{8,4},{12,8},{16,12},{20,16},{24,20},{28,24},{5,1},{9,5},{13... | collective-permute-start | bytes 1572872 | tf_op jit(solution)/shard_map/ppermute | solution.py:16
  123.2 18.4 %collective-permute-start.12 = (bf16[2,256,512]{2,1,0:T(8,128)(2,1)S(1)}, bf16[2,256,512]{2,1,0:T(8,128)(2,1)S(1)}, u32[]{:S(2)}, u32[]{:S(2)}) collective-permute-start(bf16[2,256,512]{2,1,0:T(8,128)(2,1)S(1)} %get-tuple-element.85), channel_id=1, source_target_pairs={{16,0},{20,4},{24,8},{28,12},{17,1},{21,5},{25,9},{29,13},{18,2},{... | collective-permute-start | bytes 1572872 | tf_op jit(solution)/shard_map/ppermute | solution.py:16
  124.5 17.6 %collective-permute-start.11 = (bf16[2,256,512]{2,1,0:T(8,128)(2,1)S(1)}, bf16[2,256,512]{2,1,0:T(8,128)(2,1)S(1)}, u32[]{:S(2)}, u32[]{:S(2)}) collective-permute-start(bf16[2,256,512]{2,1,0:T(8,128)(2,1)S(1)} %get-tuple-element.86), channel_id=1, source_target_pairs={{12,0},{16,4},{20,8},{24,12},{28,16},{13,1},{17,5},{21,9},{25,13},... | collective-permute-start | bytes 1572872 | tf_op jit(solution)/shard_map/ppermute | solution.py:16
  125.8 25.0 %collective-permute-start.10 = (bf16[2,256,512]{2,1,0:T(8,128)(2,1)S(1)}, bf16[2,256,512]{2,1,0:T(8,128)(2,1)S(1)}, u32[]{:S(2)}, u32[]{:S(2)}) collective-permute-start(bf16[2,256,512]{2,1,0:T(8,128)(2,1)S(1)} %get-tuple-element.87), channel_id=1, source_target_pairs={{8,0},{12,4},{16,8},{20,12},{24,16},{28,20},{9,1},{13,5},{17,9},{2... | collective-permute-start | bytes 1572872 | tf_op jit(solution)/shard_map/ppermute | solution.py:16
  127.7 23.6 %copy-start.25 = (bf16[1024,4,512]{2,1,0:T(4,128)(2,1)S(1)}, bf16[1024,4,512]{2,1,0:T(4,128)(2,1)}, u32[]{:S(2)}) copy-start(bf16[1024,4,512]{2,1,0:T(4,128)(2,1)} %param.21) | copy-start | bytes 12582916
  128.0 23.2 %copy-start.14 = (bf16[1,256,1024]{2,1,0:T(8,128)(2,1)S(1)}, bf16[1,256,1024]{2,1,0:T(8,128)(2,1)}, u32[]{:S(2)}) copy-start(bf16[1,256,1024]{2,1,0:T(8,128)(2,1)} %param.20) | copy-start | bytes 1572868
  160.7 8.2 %collective-permute-start.13 = (f32[2,2,2,2,32,4,512]{6,4,5,3,2,1,0:T(8,128)}, f32[2,2,2,2,32,4,512]{6,4,5,3,2,1,0:T(8,128)}, u32[]{:S(2)}, u32[]{:S(2)}) collective-permute-start(f32[2,2,2,2,32,4,512]{6,4,5,3,2,1,0:T(8,128)} %fusion.1), channel_id=1, source_target_pairs={{0,4},{4,0},{8,12},{12,8},{16,20},{20,16},{24,28},{28,24},{1,5},{5... | collective-permute-start | bytes 12582920 | tf_op jit(solution)/shard_map/ppermute | solution.py:29
  175.2 26.1 %collective-permute-start.14 = (f32[2,2,2,32,4,256]{5,3,4,2,1,0:T(8,128)S(1)}, f32[2,2,2,32,4,256]{5,3,4,2,1,0:T(8,128)}, u32[]{:S(2)}, u32[]{:S(2)}) collective-permute-start(f32[2,2,2,32,4,256]{5,3,4,2,1,0:T(8,128)S(1)} %dynamic-slice_bitcast_fusion.1), channel_id=1, source_target_pairs={{0,16},{4,20},{8,24},{12,28},{16,0},{20,4},{24,8},{28,12},{1,17},{... | collective-permute-start | bytes 3145736 | tf_op jit(solution)/shard_map/ppermute | solution.py:29
  178.6 42.8 %collective-permute-start.16 = (f32[2,2,2,32,4,256]{5,3,4,2,1,0:T(8,128)}, f32[2,2,2,32,4,256]{5,3,4,2,1,0:T(8,128)}, u32[]{:S(2)}, u32[]{:S(2)}) collective-permute-start(f32[2,2,2,32,4,256]{5,3,4,2,1,0:T(8,128)} %dynamic-slice_bitcast_fusion), channel_id=1, source_target_pairs={{0,8},{4,12},{8,0},{12,4},{16,24},{20,28},{24,16},{28,20},{1,9},{5... | collective-permute-start | bytes 3145736 | tf_op jit(solution)/shard_map/ppermute | solution.py:29
  203.9 29.5 %collective-permute-start.15 = (f32[2,2,32,4,256]{4,2,3,1,0:T(8,128)}, f32[2,2,32,4,256]{4,2,3,1,0:T(8,128)}, u32[]{:S(2)}, u32[]{:S(2)}) collective-permute-start(f32[2,2,32,4,256]{4,2,3,1,0:T(8,128)} %dynamic-slice_bitcast_fusion.3), channel_id=1, source_target_pairs={{0,8},{4,12},{8,0},{12,4},{16,24},{20,28},{24,16},{28,20},{1,9},{5... | collective-permute-start | bytes 1572872 | tf_op jit(solution)/shard_map/ppermute | solution.py:29
  223.8 13.2 %collective-permute-start.17 = (f32[2,2,32,4,256]{4,2,3,1,0:T(8,128)S(1)}, f32[2,2,32,4,256]{4,2,3,1,0:T(8,128)S(1)}, u32[]{:S(2)}, u32[]{:S(2)}) collective-permute-start(f32[2,2,32,4,256]{4,2,3,1,0:T(8,128)S(1)} %dynamic-slice_bitcast_fusion.2), channel_id=1, source_target_pairs={{0,16},{4,20},{8,24},{12,28},{16,0},{20,4},{24,8},{28,12},{1,17},{... | collective-permute-start | bytes 1572872 | tf_op jit(solution)/shard_map/ppermute | solution.py:29
  238.2 12.2 %collective-permute-start.18 = (f32[2,32,4,512]{3,1,2,0:T(8,128)S(1)}, f32[2,32,4,512]{3,1,2,0:T(8,128)S(1)}, u32[]{:S(2)}, u32[]{:S(2)}) collective-permute-start(f32[2,32,4,512]{3,1,2,0:T(8,128)S(1)} %fusion.80), channel_id=1, source_target_pairs={{0,1},{1,0},{2,3},{3,2},{4,5},{5,4},{6,7},{7,6},{8,9},{9,8},{10,11... | collective-permute-start | bytes 1572872 | tf_op jit(solution)/shard_map/ppermute | solution.py:29
  250.7 12.2 %collective-permute-start.19 = (f32[32,4,512]{2,1,0:T(4,128)S(1)}, f32[32,4,512]{2,1,0:T(4,128)S(1)}, u32[]{:S(2)}, u32[]{:S(2)}) collective-permute-start(f32[32,4,512]{2,1,0:T(4,128)S(1)} %bitcast.260), channel_id=1, source_target_pairs={{0,2},{1,3},{2,0},{3,1},{4,6},{5,7},{6,4},{7,5},{8,10},{9,11},{10,... | collective-permute-start | bytes 786440 | tf_op jit(solution)/shard_map/ppermute | solution.py:29
  (34 other events, 114.2 us)

commit v4 on v3

--- a/solution.py
+++ b/solution.py
@@ -29,10 +29,11 @@
     return keep + lax.ppermute(send.astype(send_type), axis, pairs).astype(keep.dtype)
 
 
-def swap_add(value, axis, flip):
+def swap_add(value, anchor, axis, flip):
+    value, anchor = lax.optimization_barrier((value, anchor))
     peers = lax.axis_size(axis)
     pairs = [(i, i ^ flip) for i in range(peers)]
-    return value + lax.ppermute(value, axis, pairs)
+    return value + lax.ppermute(value, axis, pairs), anchor
 
 
 def scatter_rows(value, tally, axes, first_axis, wire_type):
@@ -61,7 +62,7 @@
 
     first = (first_axis, 1) if (first_axis, 1) in stages else stages[-1]
     value, names = step(value, names, first, value.dtype)
-    tally = swap_add(tally, *first)
+    tally, value = swap_add(tally, value, *first)
     middle = [s for s in stages if s[0] == first[0] and s != first]
     tail = [s for s in stages if s[0] != first[0]][::-1]
     if len(middle) > 1 and rest[-1] % 2 == 0:
@@ -70,17 +71,17 @@
         left_names, right_names = list(names), list(names)
         for a, b in zip(middle, middle[::-1]):
             left, left_names = step(left, left_names, a, wire_type)
-            tally = swap_add(tally, *a)
+            tally, left = swap_add(tally, left, *a)
             right, right_names = step(right, right_names, b, wire_type)
         value = jnp.concatenate([left, right], axis=-1)
         names = left_names
     else:
         for stage in middle:
             value, names = step(value, names, stage, wire_type)
-            tally = swap_add(tally, *stage)
+            tally, value = swap_add(tally, value, *stage)
     for stage in tail:
         value, names = step(value, names, stage, wire_type)
-        tally = swap_add(tally, *stage)
+        tally, value = swap_add(tally, value, *stage)
     return value, tally
 
 

time: 265 us -> 256 us (0.966)
  starting transfers between devices: 80.4 us -> 65.5 us
  waiting for transfers between devices: 72 us -> 76.9 us
    ppermute x8, waiting for transfers between devices: 22.8 us -> 39.6 us  [shifted(): return lax.ppermute(value, axis, pairs)]
    ppermute x7, waiting for transfers between devices: 45.8 us -> 29.2 us  [halve(): lax.ppermute(send.astype(send_type), axis, pairs).astype(keep.dtype)]
    ppermute x7, starting transfers between devices: 41.5 us -> 28 us  [halve(): lax.ppermute(send.astype(send_type), axis, pairs).astype(keep.dtype)]
    ppermute x5, waiting for transfers between devices: 3.32 us -> 8.07 us  [swap_add(): return (value + lax.ppermute(value, axis, pairs), anchor)]
    unnamed x81 -> x91, local copies, waits for them, and re-layouts: 12 us -> 13.1 us
    add x6 -> x7, other arithmetic: 9.55 us -> 9.77 us  [halve(): keep + lax.ppermute(send.astype(send_type), axis, pairs).astype(keep.dtype)]
  transfers between devices with their start and end apart: 20 -> 20, of which waited for: 12 -> 13; matrix products, arithmetic and copies ran while one was open for 9% -> 8% of each run, Pallas kernels for 0% -> 0%
where the time goes in v4:
time: 256 us; the launch traced here: 255 us
  waiting for transfers between devices  76.9 us (30%)
  starting transfers between devices  65.5 us (26%)
  local copies, waits for them, and re-layouts  47.7 us (19%)
  matrix products  38.6 us (15%)
  other arithmetic  21 us (8%)
  between operations  5.2 us (2%)
    ppermute x8, waiting for transfers between devices, shifted(): return lax.ppermute(value, axis, pairs)  39.6 us
    ppermute x7, waiting for transfers between devices, halve(): lax.ppermute(send.astype(send_type), axis, pairs).astype(keep.dtype)  29.2 us
    ppermute x7, starting transfers between devices, halve(): lax.ppermute(send.astype(send_type), axis, pairs).astype(keep.dtype)  28 us
    ppermute x8, starting transfers between devices, shifted(): return lax.ppermute(value, axis, pairs)  19.4 us
    ppermute x5, starting transfers between devices, swap_add(): return (value + lax.ppermute(value, axis, pairs), anchor)  18.1 us
    unnamed x91, local copies, waits for them, and re-layouts  13.1 us
    another operation x8, local copies, waits for them, and re-layouts, shards(): update = jnp.stack([grad_key, grad_value]).reshape(2, key_len, group_cols)  10.2 us
    add x7, other arithmetic, halve(): keep + lax.ppermute(send.astype(send_type), axis, pairs).astype(keep.dtype)  9.77 us
  transfers between devices with their start and end apart: 20, of which 13 were waited for; matrix products, arithmetic and copies ran while one was open for 8% of the time, Pallas kernels for 0%

profile of v4, /device:TPU:0, one launch (start us, length us, event | category | flops | bytes accessed | tf_op | source)
XLA Modules:
  0.0 254.8 jit_solution(1523510721579095480)
XLA Ops:
  1.9 3.7 %fusion.51 = bf16[3,256,512]{2,1,0:T(8,128)(2,1)S(1)} fusion(bf16[1024,3,512]{2,1,0:T(4,128)(2,1)} %bitcast.251, bf16[1,256,1024]{2,1,0:T(8,128)(2,1)} %param.20, f32[256]{0:T(256)S(1)} %add_rsqrt_fusion), kind=kOutput, calls=%fused_computation.68 | convolution fusion | flops 806486016 | bytes 4457472 | tf_op jit(solution)/shard_map/rd,dwh->wrh/dot_general | solution.py:131
  6.5 3.3 %collective-permute-start.3 = (bf16[2,256,512]{2,1,0:T(8,128)(2,1)}, bf16[2,256,512]{2,1,0:T(8,128)(2,1)}, u32[]{:S(2)}, u32[]{:S(2)}) collective-permute-start(bf16[2,256,512]{2,1,0:T(8,128)(2,1)} %slice.208), channel_id=1, source_target_pairs={{0,4},{4,8},{8,12},{12,16},{16,20},{20,24},{24,28},{1,5},{5,9},{9,... | collective-permute-start | bytes 1572872 | tf_op jit(solution)/shard_map/ppermute | solution.py:16
  9.7 4.4 %collective-permute-start.2 = (bf16[2,256,512]{2,1,0:T(8,128)(2,1)}, bf16[2,256,512]{2,1,0:T(8,128)(2,1)}, u32[]{:S(2)}, u32[]{:S(2)}) collective-permute-start(bf16[2,256,512]{2,1,0:T(8,128)(2,1)} %slice.208), channel_id=1, source_target_pairs={{0,8},{4,12},{8,16},{12,20},{16,24},{20,28},{1,9},{5,13},{9,17},{1... | collective-permute-start | bytes 1572872 | tf_op jit(solution)/shard_map/ppermute | solution.py:16
  14.2 4.3 %collective-permute-start.1 = (bf16[2,256,512]{2,1,0:T(8,128)(2,1)}, bf16[2,256,512]{2,1,0:T(8,128)(2,1)}, u32[]{:S(2)}, u32[]{:S(2)}) collective-permute-start(bf16[2,256,512]{2,1,0:T(8,128)(2,1)} %slice.208), channel_id=1, source_target_pairs={{0,12},{4,16},{8,20},{12,24},{16,28},{1,13},{5,17},{9,21},{13,25},... | collective-permute-start | bytes 1572872 | tf_op jit(solution)/shard_map/ppermute | solution.py:16
  31.2 15.7 %collective-permute-done = bf16[2,256,512]{2,1,0:T(8,128)(2,1)} collective-permute-done((bf16[2,256,512]{2,1,0:T(8,128)(2,1)}, bf16[2,256,512]{2,1,0:T(8,128)(2,1)}, u32[]{:S(2)}, u32[]{:S(2)}) %collective-permute-start) | collective-permute-done | bytes 524320 | tf_op jit(solution)/shard_map/ppermute | solution.py:16
  53.8 2.3 fusion.45
  62.9 2.3 fusion.43
  72.0 2.3 fusion.41
  114.2 2.9 %collective-permute-done.4 = bf16[2,256,512]{2,1,0:T(8,128)(2,1)S(1)} collective-permute-done((bf16[2,256,512]{2,1,0:T(8,128)(2,1)S(1)}, bf16[2,256,512]{2,1,0:T(8,128)(2,1)S(1)}, u32[]{:S(2)}, u32[]{:S(2)}) %collective-permute-start.4) | collective-permute-done | bytes 524320 | tf_op jit(solution)/shard_map/ppermute | solution.py:16
  117.1 4.6 %collective-permute-done.7 = bf16[2,256,512]{2,1,0:T(8,128)(2,1)S(1)} collective-permute-done((bf16[2,256,512]{2,1,0:T(8,128)(2,1)S(1)}, bf16[2,256,512]{2,1,0:T(8,128)(2,1)S(1)}, u32[]{:S(2)}, u32[]{:S(2)}) %collective-permute-start.7) | collective-permute-done | bytes 524320 | tf_op jit(solution)/shard_map/ppermute | solution.py:16
  123.6 14.5 %collective-permute-done.5 = bf16[2,256,512]{2,1,0:T(8,128)(2,1)S(1)} collective-permute-done((bf16[2,256,512]{2,1,0:T(8,128)(2,1)S(1)}, bf16[2,256,512]{2,1,0:T(8,128)(2,1)S(1)}, u32[]{:S(2)}, u32[]{:S(2)}) %collective-permute-start.5) | collective-permute-done | bytes 524320 | tf_op jit(solution)/shard_map/ppermute | solution.py:16
  144.3 2.9 %fusion.1 = f32[2,2,2,2,32,4,512]{6,4,5,3,2,1,0:T(8,128)} fusion(s32[]{:T(128)S(6)} %select_n.95, f32[2,2,2,2,2,32,3,512]{7,5,6,4,3,2,1,0:T(8,128)S(1)} %fusion.64, f32[2,2,2,2,2,32,1,512]{7,5,6,4,3,2,1,0:T(8,128)S(1)} %convolution_bitcast_fusion), kind=kLoop, calls=%fused_computation.6 | loop fusion | flops 1048576 | bytes 12582916 | tf_op jit(solution)/shard_map/jit(dynamic_index_in_dim)/squeeze | solution.py:27
  148.8 6.9 %collective-permute-done.8 = f32[2,2,2,2,32,4,512]{6,4,5,3,2,1,0:T(8,128)} collective-permute-done((f32[2,2,2,2,32,4,512]{6,4,5,3,2,1,0:T(8,128)}, f32[2,2,2,2,32,4,512]{6,4,5,3,2,1,0:T(8,128)}, u32[]{:S(2)}, u32[]{:S(2)}) %collective-permute-start.8) | collective-permute-done | bytes 4194336 | tf_op jit(solution)/shard_map/ppermute | solution.py:29
  155.7 4.2 %fusion.4 = f32[2,2,2,2,32,4,512]{6,4,5,3,2,1,0:T(8,128)S(1)} fusion(f32[2,2,2,2,32,4,512]{6,4,5,3,2,1,0:T(8,128)} %collective-permute-done.8, s32[]{:T(128)S(6)} %select_n.94, f32[2,2,2,2,2,32,3,512]{7,5,6,4,3,2,1,0:T(8,128)} %copy-done, f32[2,2,2,2,2,32,1,512]{7,5,6,4,3,2,1,0:T(8,128)S(1)} %convolution_bitcast_fusion), kind=kLoop, calls=%fused_computation.9 | loop fusion | flops 2097152 | bytes 16777220 | tf_op jit(solution)/shard_map/add | solution.py:29
  163.0 3.1 %collective-permute-start.10 = (f32[2,2,2,32,4,256]{5,3,4,2,1,0:T(8,128)}, f32[2,2,2,32,4,256]{5,3,4,2,1,0:T(8,128)}, u32[]{:S(2)}, u32[]{:S(2)}) collective-permute-start(f32[2,2,2,32,4,256]{5,3,4,2,1,0:T(8,128)} %dynamic-slice_bitcast_fusion.1), channel_id=1, source_target_pairs={{0,16},{4,20},{8,24},{12,28},{16,0},{20,4},{24,8},{28,12},{1,17},{... | collective-permute-start | bytes 3145736 | tf_op jit(solution)/shard_map/ppermute | solution.py:29
  167.1 9.2 %collective-permute-start.14 = (f32[2,2,2,32,4,256]{5,3,4,2,1,0:T(8,128)}, f32[2,2,2,32,4,256]{5,3,4,2,1,0:T(8,128)}, u32[]{:S(2)}, u32[]{:S(2)}) collective-permute-start(f32[2,2,2,32,4,256]{5,3,4,2,1,0:T(8,128)} %dynamic-slice_bitcast_fusion), channel_id=1, source_target_pairs={{0,8},{4,12},{8,0},{12,4},{16,24},{20,28},{24,16},{28,20},{1,9},{5... | collective-permute-start | bytes 3145736 | tf_op jit(solution)/shard_map/ppermute | solution.py:29
  178.8 11.0 %collective-permute-done.10 = f32[2,2,2,32,4,256]{5,3,4,2,1,0:T(8,128)} collective-permute-done((f32[2,2,2,32,4,256]{5,3,4,2,1,0:T(8,128)}, f32[2,2,2,32,4,256]{5,3,4,2,1,0:T(8,128)}, u32[]{:S(2)}, u32[]{:S(2)}) %collective-permute-start.10) | collective-permute-done | bytes 1048608 | tf_op jit(solution)/shard_map/ppermute | solution.py:29
  192.5 11.1 %collective-permute-start.12 = (f32[2,2,32,4,256]{4,2,3,1,0:T(8,128)}, f32[2,2,32,4,256]{4,2,3,1,0:T(8,128)S(1)}, u32[]{:S(2)}, u32[]{:S(2)}) collective-permute-start(f32[2,2,32,4,256]{4,2,3,1,0:T(8,128)} %dynamic-slice_bitcast_fusion.3), channel_id=1, source_target_pairs={{0,8},{4,12},{8,0},{12,4},{16,24},{20,28},{24,16},{28,20},{1,9},{5... | collective-permute-start | bytes 1572872 | tf_op jit(solution)/shard_map/ppermute | solution.py:29
  206.3 10.9 %collective-permute-start.11 = (s32[]{:T(128)}, s32[]{:T(128)}, u32[]{:S(2)}, u32[]{:S(2)}) collective-permute-start(s32[]{:T(128)} %add.184), channel_id=1, source_target_pairs={{0,16},{4,20},{8,24},{12,28},{16,0},{20,4},{24,8},{28,12},{1,17},{... | collective-permute-start | bytes 20 | tf_op jit(solution)/shard_map/ppermute | solution.py:36
  228.7 6.5 %collective-permute-done.16 = f32[2,32,4,512]{3,1,2,0:T(8,128)S(1)} collective-permute-done((f32[2,32,4,512]{3,1,2,0:T(8,128)}, f32[2,32,4,512]{3,1,2,0:T(8,128)S(1)}, u32[]{:S(2)}, u32[]{:S(2)}) %collective-permute-start.16) | collective-permute-done | bytes 524320 | tf_op jit(solution)/shard_map/ppermute | solution.py:29
  235.6 2.7 %collective-permute-start.18 = (f32[32,4,512]{2,1,0:T(4,128)S(1)}, f32[32,4,512]{2,1,0:T(4,128)S(1)}, u32[]{:S(2)}, u32[]{:S(2)}) collective-permute-start(f32[32,4,512]{2,1,0:T(4,128)S(1)} %bitcast.262), channel_id=1, source_target_pairs={{0,2},{1,3},{2,0},{3,1},{4,6},{5,7},{6,4},{7,5},{8,10},{9,11},{10,... | collective-permute-start | bytes 786440 | tf_op jit(solution)/shard_map/ppermute | solution.py:29
  238.2 4.0 %collective-permute-start.17 = (s32[]{:T(128)}, s32[]{:T(128)}, u32[]{:S(2)}, u32[]{:S(2)}) collective-permute-start(s32[]{:T(128)} %add.194), channel_id=1, source_target_pairs={{0,1},{1,0},{2,3},{3,2},{4,5},{5,4},{6,7},{7,6},{8,9},{9,8},{10,11... | collective-permute-start | bytes 20 | tf_op jit(solution)/shard_map/ppermute | solution.py:36
  242.8 4.8 %collective-permute-done.18 = f32[32,4,512]{2,1,0:T(4,128)S(1)} collective-permute-done((f32[32,4,512]{2,1,0:T(4,128)S(1)}, f32[32,4,512]{2,1,0:T(4,128)S(1)}, u32[]{:S(2)}, u32[]{:S(2)}) %collective-permute-start.18) | collective-permute-done | bytes 262176 | tf_op jit(solution)/shard_map/ppermute | solution.py:29
  249.2 3.1 %collective-permute-done.19 = s32[]{:T(128)} collective-permute-done((s32[]{:T(128)}, s32[]{:T(128)}, u32[]{:S(2)}, u32[]{:S(2)}) %collective-permute-start.19) | collective-permute-done | bytes 36 | tf_op jit(solution)/shard_map/ppermute | solution.py:36
  (210 shorter events, 108.9 us)
Async XLA Ops:
  1.9 18.7 %copy-start.29 = (bf16[1024,4,512]{2,1,0:T(4,128)(2,1)S(1)}, bf16[1024,4,512]{2,1,0:T(4,128)(2,1)}, u32[]{:S(2)}) copy-start(bf16[1024,4,512]{2,1,0:T(4,128)(2,1)} %param.21) | copy-start | bytes 12582916
  6.4 16.4 %copy-start.42 = (s32[1,256]{1,0:T(1,128)S(1)}, s32[1,256]{1,0:T(1,128)}, u32[]{:S(2)}) copy-start(s32[1,256]{1,0:T(1,128)} %param.23) | copy-start | bytes 3076
  6.5 43.8 %collective-permute-start.3 = (bf16[2,256,512]{2,1,0:T(8,128)(2,1)}, bf16[2,256,512]{2,1,0:T(8,128)(2,1)}, u32[]{:S(2)}, u32[]{:S(2)}) collective-permute-start(bf16[2,256,512]{2,1,0:T(8,128)(2,1)} %slice.208), channel_id=1, source_target_pairs={{0,4},{4,8},{8,12},{12,16},{16,20},{20,24},{24,28},{1,5},{5,9},{9,... | collective-permute-start | bytes 1572872 | tf_op jit(solution)/shard_map/ppermute | solution.py:16
  9.7 39.4 %collective-permute-start.2 = (bf16[2,256,512]{2,1,0:T(8,128)(2,1)}, bf16[2,256,512]{2,1,0:T(8,128)(2,1)}, u32[]{:S(2)}, u32[]{:S(2)}) collective-permute-start(bf16[2,256,512]{2,1,0:T(8,128)(2,1)} %slice.208), channel_id=1, source_target_pairs={{0,8},{4,12},{8,16},{12,20},{16,24},{20,28},{1,9},{5,13},{9,17},{1... | collective-permute-start | bytes 1572872 | tf_op jit(solution)/shard_map/ppermute | solution.py:16
  14.2 33.9 %collective-permute-start.1 = (bf16[2,256,512]{2,1,0:T(8,128)(2,1)}, bf16[2,256,512]{2,1,0:T(8,128)(2,1)}, u32[]{:S(2)}, u32[]{:S(2)}) collective-permute-start(bf16[2,256,512]{2,1,0:T(8,128)(2,1)} %slice.208), channel_id=1, source_target_pairs={{0,12},{4,16},{8,20},{12,24},{16,28},{1,13},{5,17},{9,21},{13,25},... | collective-permute-start | bytes 1572872 | tf_op jit(solution)/shard_map/ppermute | solution.py:16
  18.5 28.5 %collective-permute-start = (bf16[2,256,512]{2,1,0:T(8,128)(2,1)}, bf16[2,256,512]{2,1,0:T(8,128)(2,1)}, u32[]{:S(2)}, u32[]{:S(2)}) collective-permute-start(bf16[2,256,512]{2,1,0:T(8,128)(2,1)} %slice.208), channel_id=1, source_target_pairs={{0,16},{4,20},{8,24},{12,28},{1,17},{5,21},{9,25},{13,29},{2,18},{... | collective-permute-start | bytes 1572872 | tf_op jit(solution)/shard_map/ppermute | solution.py:16
  108.0 9.1 %collective-permute-start.4 = (bf16[2,256,512]{2,1,0:T(8,128)(2,1)S(1)}, bf16[2,256,512]{2,1,0:T(8,128)(2,1)S(1)}, u32[]{:S(2)}, u32[]{:S(2)}) collective-permute-start(bf16[2,256,512]{2,1,0:T(8,128)(2,1)S(1)} %get-tuple-element.104), channel_id=1, source_target_pairs={{4,0},{8,4},{12,8},{16,12},{20,16},{24,20},{28,24},{5,1},{9,5},{13... | collective-permute-start | bytes 1572872 | tf_op jit(solution)/shard_map/ppermute | solution.py:16
  109.4 12.3 %collective-permute-start.7 = (bf16[2,256,512]{2,1,0:T(8,128)(2,1)S(1)}, bf16[2,256,512]{2,1,0:T(8,128)(2,1)S(1)}, u32[]{:S(2)}, u32[]{:S(2)}) collective-permute-start(bf16[2,256,512]{2,1,0:T(8,128)(2,1)S(1)} %get-tuple-element.105), channel_id=1, source_target_pairs={{16,0},{20,4},{24,8},{28,12},{17,1},{21,5},{25,9},{29,13},{18,2},{... | collective-permute-start | bytes 1572872 | tf_op jit(solution)/shard_map/ppermute | solution.py:16
  110.7 12.8 %collective-permute-start.6 = (bf16[2,256,512]{2,1,0:T(8,128)(2,1)S(1)}, bf16[2,256,512]{2,1,0:T(8,128)(2,1)S(1)}, u32[]{:S(2)}, u32[]{:S(2)}) collective-permute-start(bf16[2,256,512]{2,1,0:T(8,128)(2,1)S(1)} %get-tuple-element.106), channel_id=1, source_target_pairs={{12,0},{16,4},{20,8},{24,12},{28,16},{13,1},{17,5},{21,9},{25,13},... | collective-permute-start | bytes 1572872 | tf_op jit(solution)/shard_map/ppermute | solution.py:16
  112.0 26.1 %collective-permute-start.5 = (bf16[2,256,512]{2,1,0:T(8,128)(2,1)S(1)}, bf16[2,256,512]{2,1,0:T(8,128)(2,1)S(1)}, u32[]{:S(2)}, u32[]{:S(2)}) collective-permute-start(bf16[2,256,512]{2,1,0:T(8,128)(2,1)S(1)} %get-tuple-element.107), channel_id=1, source_target_pairs={{8,0},{12,4},{16,8},{20,12},{24,16},{28,20},{9,1},{13,5},{17,9},{2... | collective-permute-start | bytes 1572872 | tf_op jit(solution)/shard_map/ppermute | solution.py:16
  113.9 24.6 %copy-start.30 = (bf16[1024,4,512]{2,1,0:T(4,128)(2,1)S(1)}, bf16[1024,4,512]{2,1,0:T(4,128)(2,1)}, u32[]{:S(2)}) copy-start(bf16[1024,4,512]{2,1,0:T(4,128)(2,1)} %param.21) | copy-start | bytes 12582916
  148.2 7.5 %collective-permute-start.8 = (f32[2,2,2,2,32,4,512]{6,4,5,3,2,1,0:T(8,128)}, f32[2,2,2,2,32,4,512]{6,4,5,3,2,1,0:T(8,128)}, u32[]{:S(2)}, u32[]{:S(2)}) collective-permute-start(f32[2,2,2,2,32,4,512]{6,4,5,3,2,1,0:T(8,128)} %fusion.1), channel_id=1, source_target_pairs={{0,4},{4,0},{8,12},{12,8},{16,20},{20,16},{24,28},{28,24},{1,5},{5... | collective-permute-start | bytes 12582920 | tf_op jit(solution)/shard_map/ppermute | solution.py:29
  163.0 26.9 %collective-permute-start.10 = (f32[2,2,2,32,4,256]{5,3,4,2,1,0:T(8,128)}, f32[2,2,2,32,4,256]{5,3,4,2,1,0:T(8,128)}, u32[]{:S(2)}, u32[]{:S(2)}) collective-permute-start(f32[2,2,2,32,4,256]{5,3,4,2,1,0:T(8,128)} %dynamic-slice_bitcast_fusion.1), channel_id=1, source_target_pairs={{0,16},{4,20},{8,24},{12,28},{16,0},{20,4},{24,8},{28,12},{1,17},{... | collective-permute-start | bytes 3145736 | tf_op jit(solution)/shard_map/ppermute | solution.py:29
  167.1 36.4 %collective-permute-start.14 = (f32[2,2,2,32,4,256]{5,3,4,2,1,0:T(8,128)}, f32[2,2,2,32,4,256]{5,3,4,2,1,0:T(8,128)}, u32[]{:S(2)}, u32[]{:S(2)}) collective-permute-start(f32[2,2,2,32,4,256]{5,3,4,2,1,0:T(8,128)} %dynamic-slice_bitcast_fusion), channel_id=1, source_target_pairs={{0,8},{4,12},{8,0},{12,4},{16,24},{20,28},{24,16},{28,20},{1,9},{5... | collective-permute-start | bytes 3145736 | tf_op jit(solution)/shard_map/ppermute | solution.py:29
  176.3 1.2 collective-permute-start.9
  192.5 27.4 %collective-permute-start.12 = (f32[2,2,32,4,256]{4,2,3,1,0:T(8,128)}, f32[2,2,32,4,256]{4,2,3,1,0:T(8,128)S(1)}, u32[]{:S(2)}, u32[]{:S(2)}) collective-permute-start(f32[2,2,32,4,256]{4,2,3,1,0:T(8,128)} %dynamic-slice_bitcast_fusion.3), channel_id=1, source_target_pairs={{0,8},{4,12},{8,0},{12,4},{16,24},{20,28},{24,16},{28,20},{1,9},{5... | collective-permute-start | bytes 1572872 | tf_op jit(solution)/shard_map/ppermute | solution.py:29
  206.0 15.1 %collective-permute-start.15 = (f32[2,2,32,4,256]{4,2,3,1,0:T(8,128)S(1)}, f32[2,2,32,4,256]{4,2,3,1,0:T(8,128)S(1)}, u32[]{:S(2)}, u32[]{:S(2)}) collective-permute-start(f32[2,2,32,4,256]{4,2,3,1,0:T(8,128)S(1)} %dynamic-slice_bitcast_fusion.2), channel_id=1, source_target_pairs={{0,16},{4,20},{8,24},{12,28},{16,0},{20,4},{24,8},{28,12},{1,17},{... | collective-permute-start | bytes 1572872 | tf_op jit(solution)/shard_map/ppermute | solution.py:29
  206.3 13.0 %collective-permute-start.11 = (s32[]{:T(128)}, s32[]{:T(128)}, u32[]{:S(2)}, u32[]{:S(2)}) collective-permute-start(s32[]{:T(128)} %add.184), channel_id=1, source_target_pairs={{0,16},{4,20},{8,24},{12,28},{16,0},{20,4},{24,8},{28,12},{1,17},{... | collective-permute-start | bytes 20 | tf_op jit(solution)/shard_map/ppermute | solution.py:36
  223.0 30.0 %copy-start.4 = (f32[256,1024]{1,0:T(8,128)S(1)}, f32[256,1024]{1,0:T(8,128)}, u32[]{:S(2)}) copy-start(f32[256,1024]{1,0:T(8,128)} %copy-done.3) | copy-start | bytes 3145732
  223.0 12.2 %collective-permute-start.16 = (f32[2,32,4,512]{3,1,2,0:T(8,128)}, f32[2,32,4,512]{3,1,2,0:T(8,128)S(1)}, u32[]{:S(2)}, u32[]{:S(2)}) collective-permute-start(f32[2,32,4,512]{3,1,2,0:T(8,128)} %fusion.80), channel_id=1, source_target_pairs={{0,1},{1,0},{2,3},{3,2},{4,5},{5,4},{6,7},{7,6},{8,9},{9,8},{10,11... | collective-permute-start | bytes 1572872 | tf_op jit(solution)/shard_map/ppermute | solution.py:29
  224.6 3.5 %collective-permute-start.13 = (s32[]{:T(128)}, s32[]{:T(128)}, u32[]{:S(2)}, u32[]{:S(2)}) collective-permute-start(s32[]{:T(128)} %add.189), channel_id=1, source_target_pairs={{0,8},{4,12},{8,0},{12,4},{16,24},{20,28},{24,16},{28,20},{1,9},{5... | collective-permute-start | bytes 20 | tf_op jit(solution)/shard_map/ppermute | solution.py:36
  235.6 12.1 %collective-permute-start.18 = (f32[32,4,512]{2,1,0:T(4,128)S(1)}, f32[32,4,512]{2,1,0:T(4,128)S(1)}, u32[]{:S(2)}, u32[]{:S(2)}) collective-permute-start(f32[32,4,512]{2,1,0:T(4,128)S(1)} %bitcast.262), channel_id=1, source_target_pairs={{0,2},{1,3},{2,0},{3,1},{4,6},{5,7},{6,4},{7,5},{8,10},{9,11},{10,... | collective-permute-start | bytes 786440 | tf_op jit(solution)/shard_map/ppermute | solution.py:29
  238.2 4.0 %collective-permute-start.17 = (s32[]{:T(128)}, s32[]{:T(128)}, u32[]{:S(2)}, u32[]{:S(2)}) collective-permute-start(s32[]{:T(128)} %add.194), channel_id=1, source_target_pairs={{0,1},{1,0},{2,3},{3,2},{4,5},{5,4},{6,7},{7,6},{8,9},{9,8},{10,11... | collective-permute-start | bytes 20 | tf_op jit(solution)/shard_map/ppermute | solution.py:36
  247.8 4.5 %collective-permute-start.19 = (s32[]{:T(128)}, s32[]{:T(128)}, u32[]{:S(2)}, u32[]{:S(2)}) collective-permute-start(s32[]{:T(128)} %add.201), channel_id=1, source_target_pairs={{0,2},{1,3},{2,0},{3,1},{4,6},{5,7},{6,4},{7,5},{8,10},{9,11},{10,... | collective-permute-start | bytes 20 | tf_op jit(solution)/shard_map/ppermute | solution.py:36
  (39 other events, 141.6 us)

commit v5 on v4

--- a/solution.py
+++ b/solution.py
@@ -195,7 +195,7 @@
         local_count,
         ("tm", "night"),
         "tm",
-        jnp.float32,
+        jnp.bfloat16,
     )
     total_count = count.astype(jnp.float32)
     loss_scale = jnp.float32(tokens_all) / total_count

time: 256 us -> 222 us (0.87)
  waiting for transfers between devices: 76.9 us -> 53.4 us
  starting transfers between devices: 65.5 us -> 59.8 us
  local copies, waits for them, and re-layouts: 47.7 us -> 43.2 us
    ppermute x7, waiting for transfers between devices: 29.2 us -> 8.27 us  [halve(): lax.ppermute(send.astype(send_type), axis, pairs).astype(keep.dtype)]
    ppermute x5, starting transfers between devices: 18.1 us -> 12.7 us  [swap_add(): return (value + lax.ppermute(value, axis, pairs), anchor)]
    squeeze x4 -> x0, local copies, waits for them, and re-layouts: 3.1 us -> none  [halve(): send = lax.dynamic_index_in_dim(value, 1 - bit, dim, keepdims=False)]
    reshape x4, local copies, waits for them, and re-layouts: 3.03 us -> 0.44 us  [shards(): attended_rows = attended.reshape(block_rows, group_cols)]
    unnamed x91 -> x100, local copies, waits for them, and re-layouts: 13.1 us -> 12.9 us
  transfers between devices with their start and end apart: 20 -> 20, of which waited for: 13 -> 13; matrix products, arithmetic and copies ran while one was open for 8% -> 10% of each run, Pallas kernels for 0% -> 0%
where the time goes in v5:
time: 222 us; the launch traced here: 221 us
  starting transfers between devices  59.8 us (27%)
  waiting for transfers between devices  53.4 us (24%)
  local copies, waits for them, and re-layouts  43.2 us (19%)
  matrix products  38.7 us (17%)
  other arithmetic  20.4 us (9%)
  between operations  5.39 us (2%)
    ppermute x8, waiting for transfers between devices, shifted(): return lax.ppermute(value, axis, pairs)  37.8 us
    ppermute x7, starting transfers between devices, halve(): lax.ppermute(send.astype(send_type), axis, pairs).astype(keep.dtype)  27.7 us
    ppermute x8, starting transfers between devices, shifted(): return lax.ppermute(value, axis, pairs)  19.4 us
    unnamed x100, local copies, waits for them, and re-layouts  12.9 us
    ppermute x5, starting transfers between devices, swap_add(): return (value + lax.ppermute(value, axis, pairs), anchor)  12.7 us
    another operation x8, local copies, waits for them, and re-layouts, shards(): update = jnp.stack([grad_key, grad_value]).reshape(2, key_len, group_cols)  11.1 us
    add x7, other arithmetic, halve(): keep + lax.ppermute(send.astype(send_type), axis, pairs).astype(keep.dtype)  9.3 us
    div x4, matrix products, band_block(): probs = exp_terms / jnp.sum(exp_terms, axis=-1, keepdims=True)  9.09 us
  transfers between devices with their start and end apart: 20, of which 13 were waited for; matrix products, arithmetic and copies ran while one was open for 10% of the time, Pallas kernels for 0%

profile of v5, /device:TPU:0, one launch (start us, length us, event | category | flops | bytes accessed | tf_op | source)
XLA Modules:
  0.0 220.9 jit_solution(7634818541576110806)
XLA Ops:
  1.9 3.7 %fusion.51 = bf16[3,256,512]{2,1,0:T(8,128)(2,1)S(1)} fusion(bf16[1024,3,512]{2,1,0:T(4,128)(2,1)} %bitcast.247, bf16[1,256,1024]{2,1,0:T(8,128)(2,1)} %param.20, f32[256]{0:T(256)S(1)} %add_rsqrt_fusion), kind=kOutput, calls=%fused_computation.68 | convolution fusion | flops 806486016 | bytes 4457472 | tf_op jit(solution)/shard_map/rd,dwh->wrh/dot_general | solution.py:131
  6.5 3.3 %collective-permute-start.3 = (bf16[2,256,512]{2,1,0:T(8,128)(2,1)}, bf16[2,256,512]{2,1,0:T(8,128)(2,1)}, u32[]{:S(2)}, u32[]{:S(2)}) collective-permute-start(bf16[2,256,512]{2,1,0:T(8,128)(2,1)} %slice.208), channel_id=1, source_target_pairs={{0,4},{4,8},{8,12},{12,16},{16,20},{20,24},{24,28},{1,5},{5,9},{9,... | collective-permute-start | bytes 1572872 | tf_op jit(solution)/shard_map/ppermute | solution.py:16
  9.7 4.4 %collective-permute-start.2 = (bf16[2,256,512]{2,1,0:T(8,128)(2,1)}, bf16[2,256,512]{2,1,0:T(8,128)(2,1)}, u32[]{:S(2)}, u32[]{:S(2)}) collective-permute-start(bf16[2,256,512]{2,1,0:T(8,128)(2,1)} %slice.208), channel_id=1, source_target_pairs={{0,8},{4,12},{8,16},{12,20},{16,24},{20,28},{1,9},{5,13},{9,17},{1... | collective-permute-start | bytes 1572872 | tf_op jit(solution)/shard_map/ppermute | solution.py:16
  14.2 4.3 %collective-permute-start.1 = (bf16[2,256,512]{2,1,0:T(8,128)(2,1)}, bf16[2,256,512]{2,1,0:T(8,128)(2,1)}, u32[]{:S(2)}, u32[]{:S(2)}) collective-permute-start(bf16[2,256,512]{2,1,0:T(8,128)(2,1)} %slice.208), channel_id=1, source_target_pairs={{0,12},{4,16},{8,20},{12,24},{16,28},{1,13},{5,17},{9,21},{13,25},... | collective-permute-start | bytes 1572872 | tf_op jit(solution)/shard_map/ppermute | solution.py:16
  20.6 2.2 %slice.186 = bf16[1024,1,512]{2,1,0:T(2,128)(2,1)S(1)} slice(bf16[1024,4,512]{2,1,0:T(4,128)(2,1)S(1)} %copy-done.31), slice={[0:1024], [3:4], [0:512]} | slice | bytes 2097152 | tf_op jit(solution)/shard_map/slice | solution.py:142
  33.0 13.9 %collective-permute-done = bf16[2,256,512]{2,1,0:T(8,128)(2,1)} collective-permute-done((bf16[2,256,512]{2,1,0:T(8,128)(2,1)}, bf16[2,256,512]{2,1,0:T(8,128)(2,1)}, u32[]{:S(2)}, u32[]{:S(2)}) %collective-permute-start) | collective-permute-done | bytes 524320 | tf_op jit(solution)/shard_map/ppermute | solution.py:16
  53.9 2.3 %fusion.45 = f32[2,256,1280]{2,1,0:T(8,128)S(1)} fusion(bf16[256,2,64]{0,2,1:T(8,128)(2,1)S(1)} %bitcast.255, bf16[1280,2,64]{0,2,1:T(8,128)(2,1)} %bitcast.233, f32[256,1280]{1,0:T(8,128)} %fusion.50), kind=kOutput, calls=%fused_computation.61 | convolution fusion | flops 85853952 | bytes 4325376 | tf_op jit(solution)/shard_map/div | solution.py:94
  62.9 2.3 %fusion.43 = f32[2,256,1280]{2,1,0:T(8,128)S(1)} fusion(bf16[256,2,64]{0,2,1:T(8,128)(2,1)S(1)} %bitcast.253, bf16[1280,2,64]{0,2,1:T(8,128)(2,1)} %bitcast.235, f32[256,1280]{1,0:T(8,128)} %fusion.50), kind=kOutput, calls=%fused_computation.59 | convolution fusion | flops 85853952 | bytes 4325376 | tf_op jit(solution)/shard_map/div | solution.py:94
  72.0 2.3 %fusion.41 = f32[2,256,1280]{2,1,0:T(8,128)S(1)} fusion(bf16[256,2,64]{0,2,1:T(8,128)(2,1)S(1)} %bitcast.251, bf16[1280,2,64]{0,2,1:T(8,128)(2,1)} %bitcast.237, f32[256,1280]{1,0:T(8,128)} %fusion.50), kind=kOutput, calls=%fused_computation.57 | convolution fusion | flops 85853952 | bytes 4325376 | tf_op jit(solution)/shard_map/div | solution.py:94
  81.2 2.3 %fusion.39 = f32[2,256,1280]{2,1,0:T(8,128)S(1)} fusion(bf16[256,2,64]{0,2,1:T(8,128)(2,1)S(1)} %bitcast.249, bf16[1280,2,64]{0,2,1:T(8,128)(2,1)} %bitcast.231, f32[256,1280]{1,0:T(8,128)} %fusion.50), kind=kOutput, calls=%fused_computation.55 | convolution fusion | flops 85853952 | bytes 4325376 | tf_op jit(solution)/shard_map/div | solution.py:94
  93.8 2.2 %copy.88 = f32[1,1,1280,128]{3,2,1,0:T(8,128)} copy(f32[1,1,1280,128]{2,3,1,0:T(8,128)} %bitcast.227) | data formatting | bytes 1310720 | tf_op jit(solution)/shard_map/stack | solution.py:170
  110.9 2.9 %collective-permute-done.4 = bf16[2,256,512]{2,1,0:T(8,128)(2,1)S(1)} collective-permute-done((bf16[2,256,512]{2,1,0:T(8,128)(2,1)S(1)}, bf16[2,256,512]{2,1,0:T(8,128)(2,1)S(1)}, u32[]{:S(2)}, u32[]{:S(2)}) %collective-permute-start.4) | collective-permute-done | bytes 524320 | tf_op jit(solution)/shard_map/ppermute | solution.py:16
  113.8 4.6 %collective-permute-done.7 = bf16[2,256,512]{2,1,0:T(8,128)(2,1)S(1)} collective-permute-done((bf16[2,256,512]{2,1,0:T(8,128)(2,1)S(1)}, bf16[2,256,512]{2,1,0:T(8,128)(2,1)S(1)}, u32[]{:S(2)}, u32[]{:S(2)}) %collective-permute-start.7) | collective-permute-done | bytes 524320 | tf_op jit(solution)/shard_map/ppermute | solution.py:16
  120.3 14.5 %collective-permute-done.5 = bf16[2,256,512]{2,1,0:T(8,128)(2,1)S(1)} collective-permute-done((bf16[2,256,512]{2,1,0:T(8,128)(2,1)S(1)}, bf16[2,256,512]{2,1,0:T(8,128)(2,1)S(1)}, u32[]{:S(2)}, u32[]{:S(2)}) %collective-permute-start.5) | collective-permute-done | bytes 524320 | tf_op jit(solution)/shard_map/ppermute | solution.py:16
  141.0 2.9 %fusion.1 = f32[2,2,2,2,32,4,512]{6,4,5,3,2,1,0:T(8,128)} fusion(s32[]{:T(128)S(6)} %select_n.95, f32[2,2,2,2,2,32,3,512]{7,5,6,4,3,2,1,0:T(8,128)S(1)} %fusion.64, f32[2,2,2,2,2,32,1,512]{7,5,6,4,3,2,1,0:T(8,128)S(1)} %convolution_bitcast_fusion), kind=kLoop, calls=%fused_computation.6 | loop fusion | flops 1048576 | bytes 12582916 | tf_op jit(solution)/shard_map/jit(dynamic_index_in_dim)/squeeze | solution.py:27
  145.5 6.9 %collective-permute-done.8 = f32[2,2,2,2,32,4,512]{6,4,5,3,2,1,0:T(8,128)} collective-permute-done((f32[2,2,2,2,32,4,512]{6,4,5,3,2,1,0:T(8,128)}, f32[2,2,2,2,32,4,512]{6,4,5,3,2,1,0:T(8,128)}, u32[]{:S(2)}, u32[]{:S(2)}) %collective-permute-start.8) | collective-permute-done | bytes 4194336 | tf_op jit(solution)/shard_map/ppermute | solution.py:29
  152.4 4.2 %fusion.4 = f32[2,2,2,2,32,4,512]{6,4,5,3,2,1,0:T(8,128)S(1)} fusion(f32[2,2,2,2,32,4,512]{6,4,5,3,2,1,0:T(8,128)} %collective-permute-done.8, s32[]{:T(128)S(6)} %select_n.94, f32[2,2,2,2,2,32,3,512]{7,5,6,4,3,2,1,0:T(8,128)} %copy-done, f32[2,2,2,2,2,32,1,512]{7,5,6,4,3,2,1,0:T(8,128)S(1)} %convolution_bitcast_fusion), kind=kLoop, calls=%fused_computation.9 | loop fusion | flops 2097152 | bytes 16777220 | tf_op jit(solution)/shard_map/add | solution.py:29
  158.7 3.2 %collective-permute-start.10 = (bf16[2,2,2,32,4,256]{5,3,4,2,1,0:T(8,128)(2,1)S(1)}, bf16[2,2,2,32,4,256]{5,3,4,2,1,0:T(8,128)(2,1)}, u32[]{:S(2)}, u32[]{:S(2)}) collective-permute-start(bf16[2,2,2,32,4,256]{5,3,4,2,1,0:T(8,128)(2,1)S(1)} %fusion.78), channel_id=1, source_target_pairs={{0,16},{4,20},{8,24},{12,28},{16,0},{20,4},{24,8},{28,12},{1,17},{... | collective-permute-start | bytes 1572872 | tf_op jit(solution)/shard_map/ppermute | solution.py:29
  162.8 9.2 %collective-permute-start.14 = (bf16[2,2,2,32,4,256]{5,3,4,2,1,0:T(8,128)(2,1)}, bf16[2,2,2,32,4,256]{5,3,4,2,1,0:T(8,128)(2,1)}, u32[]{:S(2)}, u32[]{:S(2)}) collective-permute-start(bf16[2,2,2,32,4,256]{5,3,4,2,1,0:T(8,128)(2,1)} %fusion.79), channel_id=1, source_target_pairs={{0,8},{4,12},{8,0},{12,4},{16,24},{20,28},{24,16},{28,20},{1,9},{5... | collective-permute-start | bytes 1572872 | tf_op jit(solution)/shard_map/ppermute | solution.py:29
  176.2 10.7 %collective-permute-start.12 = (bf16[2,2,32,4,256]{4,2,3,1,0:T(8,128)(2,1)S(1)}, bf16[2,2,32,4,256]{4,2,3,1,0:T(8,128)(2,1)S(1)}, u32[]{:S(2)}, u32[]{:S(2)}) collective-permute-start(bf16[2,2,32,4,256]{4,2,3,1,0:T(8,128)(2,1)S(1)} %fusion.90), channel_id=1, source_target_pairs={{0,8},{4,12},{8,0},{12,4},{16,24},{20,28},{24,16},{28,20},{1,9},{5... | collective-permute-start | bytes 786440 | tf_op jit(solution)/shard_map/ppermute | solution.py:29
  189.5 5.3 %collective-permute-start.11 = (s32[]{:T(128)}, s32[]{:T(128)}, u32[]{:S(2)}, u32[]{:S(2)}) collective-permute-start(s32[]{:T(128)} %add.184), channel_id=1, source_target_pairs={{0,16},{4,20},{8,24},{12,28},{16,0},{20,4},{24,8},{28,12},{1,17},{... | collective-permute-start | bytes 20 | tf_op jit(solution)/shard_map/ppermute | solution.py:36
  206.4 2.7 %collective-permute-start.18 = (bf16[32,4,512]{2,0,1:T(8,128)(2,1)S(1)}, bf16[32,4,512]{2,0,1:T(8,128)(2,1)S(1)}, u32[]{:S(2)}, u32[]{:S(2)}) collective-permute-start(bf16[32,4,512]{2,0,1:T(8,128)(2,1)S(1)} %fusion.102), channel_id=1, source_target_pairs={{0,2},{1,3},{2,0},{3,1},{4,6},{5,7},{6,4},{7,5},{8,10},{9,11},{10,... | collective-permute-start | bytes 393224 | tf_op jit(solution)/shard_map/ppermute | solution.py:29
  209.0 2.9 %collective-permute-start.17 = (s32[]{:T(128)}, s32[]{:T(128)}, u32[]{:S(2)}, u32[]{:S(2)}) collective-permute-start(s32[]{:T(128)} %add.194), channel_id=1, source_target_pairs={{0,1},{1,0},{2,3},{3,2},{4,5},{5,4},{6,7},{7,6},{8,9},{9,8},{10,11... | collective-permute-start | bytes 20 | tf_op jit(solution)/shard_map/ppermute | solution.py:36
  213.7 2.6 %collective-permute-start.19 = (s32[]{:T(128)}, s32[]{:T(128)}, u32[]{:S(2)}, u32[]{:S(2)}) collective-permute-start(s32[]{:T(128)} %add.201), channel_id=1, source_target_pairs={{0,2},{1,3},{2,0},{3,1},{4,6},{5,7},{6,4},{7,5},{8,10},{9,11},{10,... | collective-permute-start | bytes 20 | tf_op jit(solution)/shard_map/ppermute | solution.py:36
  (218 shorter events, 99.8 us)
Async XLA Ops:
  1.9 18.7 %copy-start.31 = (bf16[1024,4,512]{2,1,0:T(4,128)(2,1)S(1)}, bf16[1024,4,512]{2,1,0:T(4,128)(2,1)}, u32[]{:S(2)}) copy-start(bf16[1024,4,512]{2,1,0:T(4,128)(2,1)} %param.21) | copy-start | bytes 12582916
  6.4 16.4 %copy-start.46 = (s32[1,256]{1,0:T(1,128)S(1)}, s32[1,256]{1,0:T(1,128)}, u32[]{:S(2)}) copy-start(s32[1,256]{1,0:T(1,128)} %param.23) | copy-start | bytes 3076
  6.5 43.8 %collective-permute-start.3 = (bf16[2,256,512]{2,1,0:T(8,128)(2,1)}, bf16[2,256,512]{2,1,0:T(8,128)(2,1)}, u32[]{:S(2)}, u32[]{:S(2)}) collective-permute-start(bf16[2,256,512]{2,1,0:T(8,128)(2,1)} %slice.208), channel_id=1, source_target_pairs={{0,4},{4,8},{8,12},{12,16},{16,20},{20,24},{24,28},{1,5},{5,9},{9,... | collective-permute-start | bytes 1572872 | tf_op jit(solution)/shard_map/ppermute | solution.py:16
  9.7 39.4 %collective-permute-start.2 = (bf16[2,256,512]{2,1,0:T(8,128)(2,1)}, bf16[2,256,512]{2,1,0:T(8,128)(2,1)}, u32[]{:S(2)}, u32[]{:S(2)}) collective-permute-start(bf16[2,256,512]{2,1,0:T(8,128)(2,1)} %slice.208), channel_id=1, source_target_pairs={{0,8},{4,12},{8,16},{12,20},{16,24},{20,28},{1,9},{5,13},{9,17},{1... | collective-permute-start | bytes 1572872 | tf_op jit(solution)/shard_map/ppermute | solution.py:16
  14.2 33.9 %collective-permute-start.1 = (bf16[2,256,512]{2,1,0:T(8,128)(2,1)}, bf16[2,256,512]{2,1,0:T(8,128)(2,1)}, u32[]{:S(2)}, u32[]{:S(2)}) collective-permute-start(bf16[2,256,512]{2,1,0:T(8,128)(2,1)} %slice.208), channel_id=1, source_target_pairs={{0,12},{4,16},{8,20},{12,24},{16,28},{1,13},{5,17},{9,21},{13,25},... | collective-permute-start | bytes 1572872 | tf_op jit(solution)/shard_map/ppermute | solution.py:16
  18.5 28.5 %collective-permute-start = (bf16[2,256,512]{2,1,0:T(8,128)(2,1)}, bf16[2,256,512]{2,1,0:T(8,128)(2,1)}, u32[]{:S(2)}, u32[]{:S(2)}) collective-permute-start(bf16[2,256,512]{2,1,0:T(8,128)(2,1)} %slice.208), channel_id=1, source_target_pairs={{0,16},{4,20},{8,24},{12,28},{1,17},{5,21},{9,25},{13,29},{2,18},{... | collective-permute-start | bytes 1572872 | tf_op jit(solution)/shard_map/ppermute | solution.py:16
  104.7 9.1 %collective-permute-start.4 = (bf16[2,256,512]{2,1,0:T(8,128)(2,1)S(1)}, bf16[2,256,512]{2,1,0:T(8,128)(2,1)S(1)}, u32[]{:S(2)}, u32[]{:S(2)}) collective-permute-start(bf16[2,256,512]{2,1,0:T(8,128)(2,1)S(1)} %get-tuple-element.106), channel_id=1, source_target_pairs={{4,0},{8,4},{12,8},{16,12},{20,16},{24,20},{28,24},{5,1},{9,5},{13... | collective-permute-start | bytes 1572872 | tf_op jit(solution)/shard_map/ppermute | solution.py:16
  106.2 12.3 %collective-permute-start.7 = (bf16[2,256,512]{2,1,0:T(8,128)(2,1)S(1)}, bf16[2,256,512]{2,1,0:T(8,128)(2,1)S(1)}, u32[]{:S(2)}, u32[]{:S(2)}) collective-permute-start(bf16[2,256,512]{2,1,0:T(8,128)(2,1)S(1)} %get-tuple-element.107), channel_id=1, source_target_pairs={{16,0},{20,4},{24,8},{28,12},{17,1},{21,5},{25,9},{29,13},{18,2},{... | collective-permute-start | bytes 1572872 | tf_op jit(solution)/shard_map/ppermute | solution.py:16
  107.5 12.8 %collective-permute-start.6 = (bf16[2,256,512]{2,1,0:T(8,128)(2,1)S(1)}, bf16[2,256,512]{2,1,0:T(8,128)(2,1)S(1)}, u32[]{:S(2)}, u32[]{:S(2)}) collective-permute-start(bf16[2,256,512]{2,1,0:T(8,128)(2,1)S(1)} %get-tuple-element.108), channel_id=1, source_target_pairs={{12,0},{16,4},{20,8},{24,12},{28,16},{13,1},{17,5},{21,9},{25,13},... | collective-permute-start | bytes 1572872 | tf_op jit(solution)/shard_map/ppermute | solution.py:16
  108.8 26.1 %collective-permute-start.5 = (bf16[2,256,512]{2,1,0:T(8,128)(2,1)S(1)}, bf16[2,256,512]{2,1,0:T(8,128)(2,1)S(1)}, u32[]{:S(2)}, u32[]{:S(2)}) collective-permute-start(bf16[2,256,512]{2,1,0:T(8,128)(2,1)S(1)} %get-tuple-element.109), channel_id=1, source_target_pairs={{8,0},{12,4},{16,8},{20,12},{24,16},{28,20},{9,1},{13,5},{17,9},{2... | collective-permute-start | bytes 1572872 | tf_op jit(solution)/shard_map/ppermute | solution.py:16
  110.6 24.6 %copy-start.32 = (bf16[1024,4,512]{2,1,0:T(4,128)(2,1)S(1)}, bf16[1024,4,512]{2,1,0:T(4,128)(2,1)}, u32[]{:S(2)}) copy-start(bf16[1024,4,512]{2,1,0:T(4,128)(2,1)} %param.21) | copy-start | bytes 12582916
  144.9 7.5 %collective-permute-start.8 = (f32[2,2,2,2,32,4,512]{6,4,5,3,2,1,0:T(8,128)}, f32[2,2,2,2,32,4,512]{6,4,5,3,2,1,0:T(8,128)}, u32[]{:S(2)}, u32[]{:S(2)}) collective-permute-start(f32[2,2,2,2,32,4,512]{6,4,5,3,2,1,0:T(8,128)} %fusion.1), channel_id=1, source_target_pairs={{0,4},{4,0},{8,12},{12,8},{16,20},{20,16},{24,28},{28,24},{1,5},{5... | collective-permute-start | bytes 12582920 | tf_op jit(solution)/shard_map/ppermute | solution.py:29
  158.7 15.9 %collective-permute-start.10 = (bf16[2,2,2,32,4,256]{5,3,4,2,1,0:T(8,128)(2,1)S(1)}, bf16[2,2,2,32,4,256]{5,3,4,2,1,0:T(8,128)(2,1)}, u32[]{:S(2)}, u32[]{:S(2)}) collective-permute-start(bf16[2,2,2,32,4,256]{5,3,4,2,1,0:T(8,128)(2,1)S(1)} %fusion.78), channel_id=1, source_target_pairs={{0,16},{4,20},{8,24},{12,28},{16,0},{20,4},{24,8},{28,12},{1,17},{... | collective-permute-start | bytes 1572872 | tf_op jit(solution)/shard_map/ppermute | solution.py:29
  162.8 24.2 %collective-permute-start.14 = (bf16[2,2,2,32,4,256]{5,3,4,2,1,0:T(8,128)(2,1)}, bf16[2,2,2,32,4,256]{5,3,4,2,1,0:T(8,128)(2,1)}, u32[]{:S(2)}, u32[]{:S(2)}) collective-permute-start(bf16[2,2,2,32,4,256]{5,3,4,2,1,0:T(8,128)(2,1)} %fusion.79), channel_id=1, source_target_pairs={{0,8},{4,12},{8,0},{12,4},{16,24},{20,28},{24,16},{28,20},{1,9},{5... | collective-permute-start | bytes 1572872 | tf_op jit(solution)/shard_map/ppermute | solution.py:29
  171.9 1.4 collective-permute-start.9
  176.2 21.1 %collective-permute-start.12 = (bf16[2,2,32,4,256]{4,2,3,1,0:T(8,128)(2,1)S(1)}, bf16[2,2,32,4,256]{4,2,3,1,0:T(8,128)(2,1)S(1)}, u32[]{:S(2)}, u32[]{:S(2)}) collective-permute-start(bf16[2,2,32,4,256]{4,2,3,1,0:T(8,128)(2,1)S(1)} %fusion.90), channel_id=1, source_target_pairs={{0,8},{4,12},{8,0},{12,4},{16,24},{20,28},{24,16},{28,20},{1,9},{5... | collective-permute-start | bytes 786440 | tf_op jit(solution)/shard_map/ppermute | solution.py:29
  189.2 9.3 %collective-permute-start.15 = (bf16[2,2,32,4,256]{4,2,3,1,0:T(8,128)(2,1)S(1)}, bf16[2,2,32,4,256]{4,2,3,1,0:T(8,128)(2,1)S(1)}, u32[]{:S(2)}, u32[]{:S(2)}) collective-permute-start(bf16[2,2,32,4,256]{4,2,3,1,0:T(8,128)(2,1)S(1)} %fusion.91), channel_id=1, source_target_pairs={{0,16},{4,20},{8,24},{12,28},{16,0},{20,4},{24,8},{28,12},{1,17},{... | collective-permute-start | bytes 786440 | tf_op jit(solution)/shard_map/ppermute | solution.py:29
  189.5 7.2 %collective-permute-start.11 = (s32[]{:T(128)}, s32[]{:T(128)}, u32[]{:S(2)}, u32[]{:S(2)}) collective-permute-start(s32[]{:T(128)} %add.184), channel_id=1, source_target_pairs={{0,16},{4,20},{8,24},{12,28},{16,0},{20,4},{24,8},{28,12},{1,17},{... | collective-permute-start | bytes 20 | tf_op jit(solution)/shard_map/ppermute | solution.py:36
  199.6 20.2 %copy-start.4 = (f32[256,1024]{1,0:T(8,128)S(1)}, f32[256,1024]{1,0:T(8,128)}, u32[]{:S(2)}) copy-start(f32[256,1024]{1,0:T(8,128)} %copy-done.3) | copy-start | bytes 3145732
  199.6 6.6 %collective-permute-start.16 = (bf16[2,32,4,512]{3,1,2,0:T(8,128)(2,1)S(1)}, bf16[2,32,4,512]{3,1,2,0:T(8,128)(2,1)S(1)}, u32[]{:S(2)}, u32[]{:S(2)}) collective-permute-start(bf16[2,32,4,512]{3,1,2,0:T(8,128)(2,1)S(1)} %fusion.92), channel_id=1, source_target_pairs={{0,1},{1,0},{2,3},{3,2},{4,5},{5,4},{6,7},{7,6},{8,9},{9,8},{10,11... | collective-permute-start | bytes 786440 | tf_op jit(solution)/shard_map/ppermute | solution.py:29
  201.3 3.5 %collective-permute-start.13 = (s32[]{:T(128)}, s32[]{:T(128)}, u32[]{:S(2)}, u32[]{:S(2)}) collective-permute-start(s32[]{:T(128)} %add.189), channel_id=1, source_target_pairs={{0,8},{4,12},{8,0},{12,4},{16,24},{20,28},{24,16},{28,20},{1,9},{5... | collective-permute-start | bytes 20 | tf_op jit(solution)/shard_map/ppermute | solution.py:36
  206.4 7.3 %collective-permute-start.18 = (bf16[32,4,512]{2,0,1:T(8,128)(2,1)S(1)}, bf16[32,4,512]{2,0,1:T(8,128)(2,1)S(1)}, u32[]{:S(2)}, u32[]{:S(2)}) collective-permute-start(bf16[32,4,512]{2,0,1:T(8,128)(2,1)S(1)} %fusion.102), channel_id=1, source_target_pairs={{0,2},{1,3},{2,0},{3,1},{4,6},{5,7},{6,4},{7,5},{8,10},{9,11},{10,... | collective-permute-start | bytes 393224 | tf_op jit(solution)/shard_map/ppermute | solution.py:29
  209.0 3.5 %collective-permute-start.17 = (s32[]{:T(128)}, s32[]{:T(128)}, u32[]{:S(2)}, u32[]{:S(2)}) collective-permute-start(s32[]{:T(128)} %add.194), channel_id=1, source_target_pairs={{0,1},{1,0},{2,3},{3,2},{4,5},{5,4},{6,7},{7,6},{8,9},{9,8},{10,11... | collective-permute-start | bytes 20 | tf_op jit(solution)/shard_map/ppermute | solution.py:36
  213.7 4.5 %collective-permute-start.19 = (s32[]{:T(128)}, s32[]{:T(128)}, u32[]{:S(2)}, u32[]{:S(2)}) collective-permute-start(s32[]{:T(128)} %add.201), channel_id=1, source_target_pairs={{0,2},{1,3},{2,0},{3,1},{4,6},{5,7},{6,4},{7,5},{8,10},{9,11},{10,... | collective-permute-start | bytes 20 | tf_op jit(solution)/shard_map/ppermute | solution.py:36
  (43 other events, 146.3 us)

commit v6 on v5

--- a/solution.py
+++ b/solution.py
@@ -120,7 +120,7 @@
     span = (WIN + rows - 2) // rows
     block_rows = min(512, rows)
     key_len = block_rows + span * rows
-    group = max(1, min(HEADS, 128 // HSIZE))
+    group = HEADS
     group_cols = group * HSIZE
     inv_scale = 1.0 / math.sqrt(HSIZE)
     local_in = patches[0].astype(jnp.float32)

time: 222 us -> 206 us (0.928)
  local copies, waits for them, and re-layouts: 43.2 us -> 29.8 us
  matrix products: 38.7 us -> 29.9 us
  starting transfers between devices: 59.8 us -> 67 us
    div x4 -> x0, matrix products: 9.09 us -> none  [band_block(): probs = exp_terms / jnp.sum(exp_terms, axis=-1, keepdims=True)]
    ppermute x7, starting transfers between devices: 27.7 us -> 35 us  [halve(): lax.ppermute(send.astype(send_type), axis, pairs).astype(keep.dtype)]
    another operation x8 -> x2, local copies, waits for them, and re-layouts: 11.1 us -> 5.44 us  [shards(): update = jnp.stack([grad_key, grad_value]).reshape(2, key_len, group_cols)]
    slice x10 -> x2, local copies, waits for them, and re-layouts: 5.32 us -> 0.15 us  [shards(): queries = projected[0]]
    dot_general x0 -> x1, matrix products: none -> 3.91 us  [band_block(): jnp.einsum('qgc,kgc->gqk', queries, keys_blk, preferred_element_type=jnp....]
    slice x1, local copies, waits for them, and re-layouts: 2.22 us -> 5.74 us  [shards(): weights[:, 3, :]]
    unnamed x100 -> x40, local copies, waits for them, and re-layouts: 12.9 us -> 9.6 us
    dot_general x4 -> x1, matrix products: 5 us -> 2.6 us  [band_block(): jnp.einsum('gqk,qgc->kgc', grad_scores, queries, preferred_element_type=j...]
  transfers between devices with their start and end apart: 20 -> 20, of which waited for: 13 -> 11; matrix products, arithmetic and copies ran while one was open for 10% -> 10% of each run, Pallas kernels for 0% -> 0%
where the time goes in v6:
time: 206 us
  starting transfers between devices  67 us (33%)
  waiting for transfers between devices  53.5 us (26%)
  matrix products  29.9 us (15%)
  local copies, waits for them, and re-layouts  29.8 us (14%)
  other arithmetic  20.1 us (10%)
  between operations  5.15 us (2%)
    ppermute x8, waiting for transfers between devices, shifted(): return lax.ppermute(value, axis, pairs)  38.5 us
    ppermute x7, starting transfers between devices, halve(): lax.ppermute(send.astype(send_type), axis, pairs).astype(keep.dtype)  35 us
    ppermute x8, starting transfers between devices, shifted(): return lax.ppermute(value, axis, pairs)  19.6 us
    ppermute x5, starting transfers between devices, swap_add(): return (value + lax.ppermute(value, axis, pairs), anchor)  12.5 us
    unnamed x40, local copies, waits for them, and re-layouts  9.6 us
    add x7, other arithmetic, halve(): keep + lax.ppermute(send.astype(send_type), axis, pairs).astype(keep.dtype)  9.39 us
    ppermute x7, waiting for transfers between devices, halve(): lax.ppermute(send.astype(send_type), axis, pairs).astype(keep.dtype)  7.65 us
    ppermute x5, waiting for transfers between devices, swap_add(): return (value + lax.ppermute(value, axis, pairs), anchor)  7.44 us
  transfers between devices with their start and end apart: 20, of which 11 were waited for; matrix products, arithmetic and copies ran while one was open for 10% of the time, Pallas kernels for 0%

profile of v6, /device:TPU:0, one launch (start us, length us, event | category | flops | bytes accessed | tf_op | source)
XLA Modules:
  0.0 205.6 jit_solution(6111796749980637235)
XLA Ops:
  1.9 3.7 %fusion.29 = bf16[3,256,512]{2,1,0:T(8,128)(2,1)S(1)} fusion(bf16[1024,3,512]{2,1,0:T(4,128)(2,1)} %bitcast.125, bf16[1,256,1024]{2,1,0:T(8,128)(2,1)} %param.8, f32[256]{0:T(256)S(1)} %add_rsqrt_fusion), kind=kOutput, calls=%fused_computation.36 | convolution fusion | flops 806486016 | bytes 4457472 | tf_op jit(solution)/shard_map/rd,dwh->wrh/dot_general | solution.py:131
  5.6 5.7 %collective-permute-start = (bf16[2,256,512]{2,1,0:T(8,128)(2,1)S(1)}, bf16[2,256,512]{2,1,0:T(8,128)(2,1)}, u32[]{:S(2)}, u32[]{:S(2)}) collective-permute-start(bf16[2,256,512]{2,1,0:T(8,128)(2,1)S(1)} %slice.77), channel_id=1, source_target_pairs={{0,16},{4,20},{8,24},{12,28},{1,17},{5,21},{9,25},{13,29},{2,18},{... | collective-permute-start | bytes 1572872 | tf_op jit(solution)/shard_map/ppermute | solution.py:16
  11.3 3.4 %collective-permute-start.1 = (bf16[2,256,512]{2,1,0:T(8,128)(2,1)S(1)}, bf16[2,256,512]{2,1,0:T(8,128)(2,1)}, u32[]{:S(2)}, u32[]{:S(2)}) collective-permute-start(bf16[2,256,512]{2,1,0:T(8,128)(2,1)S(1)} %slice.77), channel_id=1, source_target_pairs={{0,12},{4,16},{8,20},{12,24},{16,28},{1,13},{5,17},{9,21},{13,25},... | collective-permute-start | bytes 1572872 | tf_op jit(solution)/shard_map/ppermute | solution.py:16
  14.6 2.9 %collective-permute-start.2 = (bf16[2,256,512]{2,1,0:T(8,128)(2,1)S(1)}, bf16[2,256,512]{2,1,0:T(8,128)(2,1)}, u32[]{:S(2)}, u32[]{:S(2)}) collective-permute-start(bf16[2,256,512]{2,1,0:T(8,128)(2,1)S(1)} %slice.77), channel_id=1, source_target_pairs={{0,8},{4,12},{8,16},{12,20},{16,24},{20,28},{1,9},{5,13},{9,17},{1... | collective-permute-start | bytes 1572872 | tf_op jit(solution)/shard_map/ppermute | solution.py:16
  21.2 5.7 %slice.68 = bf16[1024,1,512]{2,1,0:T(2,128)(2,1)} slice(bf16[1024,4,512]{2,1,0:T(4,128)(2,1)} %param.9), slice={[0:1024], [3:4], [0:512]} | slice | bytes 2097152 | tf_op jit(solution)/shard_map/slice | solution.py:142
  29.9 15.3 %collective-permute-done = bf16[2,256,512]{2,1,0:T(8,128)(2,1)} collective-permute-done((bf16[2,256,512]{2,1,0:T(8,128)(2,1)S(1)}, bf16[2,256,512]{2,1,0:T(8,128)(2,1)}, u32[]{:S(2)}, u32[]{:S(2)}) %collective-permute-start) | collective-permute-done | bytes 524320 | tf_op jit(solution)/shard_map/ppermute | solution.py:16
  54.0 3.9 %fusion.1 = (f32[8,256]{1,0:T(8,128)S(1)}, f32[8,256,1280]{2,1,0:T(8,128)S(1)}) fusion(f32[256,1280]{1,0:T(8,128)} %fusion.28, bf16[256,8,64]{0,2,1:T(8,128)(2,1)S(1)} %bitcast.118, bf16[1280,8,64]{0,2,1:T(8,128)(2,1)S(1)} %bitcast.116), kind=kOutput, calls=%fused_computation.7 | convolution fusion | flops 343406592 | bytes 13377536 | tf_op jit(solution)/shard_map/qgc,kgc->gqk/dot_general | solution.py:90
  57.9 3.4 %multiply_reduce_fusion = (f32[256,8]{0,1:T(8,128)S(1)}, bf16[8,64,256]{2,1,0:T(8,128)(2,1)}) fusion(bf16[256,512]{0,1:T(8,128)(2,1)S(1)} %copy-done.14, bf16[1280,8,64]{0,2,1:T(8,128)(2,1)S(1)} %bitcast.123, f32[8,256]{1,0:T(8,128)S(1)} %get-tuple-element.54, f32[256,1280]{1,0:T(8,128)S(1)} %copy-done.4, f32[8,256,1280]{2,1,0:T(8,128)S(1)} %get-tuple-element.55), kind=kOutput, calls=%fused_computation.77 | convolution fusion | flops 346683392 | bytes 13647872 | tf_op jit(solution)/shard_map/gqk,kgc->qgc/dot_general | solution.py:96
  61.3 3.9 %multiply_convert_fusion = bf16[8,256,1280]{2,1,0:T(8,128)(2,1)S(1)} fusion(bf16[256,8,64]{0,2,1:T(8,128)(2,1)S(1)} %bitcast.128, bf16[1280,8,64]{0,2,1:T(8,128)(2,1)S(1)} %bitcast.124, f32[8,256]{1,0:T(8,128)S(1)} %bitcast.131, f32[8,256]{1,0:T(8,128)S(1)} %get-tuple-element.54, f32[256,1280]{1,0:T(8,128)S(1)} %copy-done.4, ...), kind=kOutput, calls=%fused_computation.2 | convolution fusion | flops 353894400 | bytes 18628608 | tf_op jit(solution)/shard_map/qgc,kgc->gqk/dot_general | solution.py:100
  66.9 2.6 %fusion.71 = f32[8,64,1280]{2,1,0:T(8,128)} fusion(bf16[256,8,64]{0,2,1:T(8,128)(2,1)S(1)} %bitcast.119, bf16[8,256,1280]{2,1,0:T(8,128)(2,1)S(1)} %multiply_convert_fusion), kind=kOutput, calls=%fused_computation.102 | convolution fusion | flops 335544320 | bytes 8126464 | tf_op jit(solution)/shard_map/gqk,qgc->kgc/dot_general | solution.py:109
  69.5 3.5 %fusion.7 = f32[8,64,1280]{2,1,0:T(8,128)} fusion(bf16[256,8,64]{0,2,1:T(8,128)(2,1)S(1)} %bitcast.129, f32[8,256,1280]{2,1,0:T(8,128)S(1)} %get-tuple-element.55, f32[8,256]{1,0:T(8,128)S(1)} %get-tuple-element.54, f32[256,1280]{1,0:T(8,128)S(1)} %copy-done.4), kind=kOutput, calls=%fused_computation.14 | convolution fusion | flops 346030080 | bytes 14688256 | tf_op jit(solution)/shard_map/gqk,qgc->kgc/dot_general | solution.py:110
  76.0 3.3 %copy.31 = f32[1,1,1280,512]{3,2,1,0:T(8,128)} copy(f32[1,1,1280,512]{2,3,1,0:T(8,128)} %bitcast.120) | data formatting | bytes 5242880 | tf_op jit(solution)/shard_map/stack | solution.py:170
  79.3 2.2 %fusion.65 = bf16[2,1280,512]{2,1,0:T(8,128)(2,1)S(1)} fusion(f32[1,1,1280,512]{3,2,1,0:T(8,128)} %copy.31, f32[1,1,1280,512]{3,2,1,0:T(8,128)S(1)} %copy.30), kind=kLoop, calls=%fused_computation.98 | loop fusion | flops 1310720 | bytes 7864320 | tf_op jit(solution)/shard_map/convert.4
  89.7 21.7 %collective-permute-done.5 = bf16[2,256,512]{2,1,0:T(8,128)(2,1)S(1)} collective-permute-done((bf16[2,256,512]{2,1,0:T(8,128)(2,1)S(1)}, bf16[2,256,512]{2,1,0:T(8,128)(2,1)S(1)}, u32[]{:S(2)}, u32[]{:S(2)}) %collective-permute-start.5) | collective-permute-done | bytes 524320 | tf_op jit(solution)/shard_map/ppermute | solution.py:16
  116.8 2.2 %fusion.45 = f32[2,2,2,2,2,32,3,512]{7,5,6,4,3,2,1,0:T(8,128)S(1)} fusion(bf16[2,2,2,2,2,32,256,1]{6,5,7,4,3,2,1,0:T(8,128)(2,1)} %bitcast.122, bf16[2,256,512]{2,1,0:T(8,128)(2,1)S(1)} %fusion.44, bf16[1,256,512]{2,1,0:T(8,128)(2,1)S(1)} %copy-done.12), kind=kOutput, calls=%fused_computation.61 | convolution fusion | flops 806879232 | bytes 7602176 | tf_op jit(solution)/shard_map/rd,wrh->dwh/dot_general | solution.py:191
  119.0 3.0 %fusion.3 = f32[2,2,2,2,32,4,512]{6,4,5,3,2,1,0:T(8,128)} fusion(s32[]{:T(128)S(6)} %select_n.93, f32[2,2,2,2,2,32,3,512]{7,5,6,4,3,2,1,0:T(8,128)S(1)} %fusion.45, f32[2,2,2,2,2,32,1,512]{7,5,6,4,3,2,1,0:T(8,128)S(1)} %copy-done.2), kind=kLoop, calls=%fused_computation.10 | loop fusion | flops 1048576 | bytes 12582916 | tf_op jit(solution)/shard_map/jit(dynamic_index_in_dim)/squeeze | solution.py:27
  123.5 6.9 %collective-permute-done.8 = f32[2,2,2,2,32,4,512]{6,4,5,3,2,1,0:T(8,128)} collective-permute-done((f32[2,2,2,2,32,4,512]{6,4,5,3,2,1,0:T(8,128)}, f32[2,2,2,2,32,4,512]{6,4,5,3,2,1,0:T(8,128)}, u32[]{:S(2)}, u32[]{:S(2)}) %collective-permute-start.8) | collective-permute-done | bytes 4194336 | tf_op jit(solution)/shard_map/ppermute | solution.py:29
  130.3 4.2 %fusion.6 = f32[2,2,2,2,32,4,512]{6,4,5,3,2,1,0:T(8,128)S(1)} fusion(f32[2,2,2,2,32,4,512]{6,4,5,3,2,1,0:T(8,128)} %collective-permute-done.8, s32[]{:T(128)S(6)} %select_n.92, f32[2,2,2,2,2,32,3,512]{7,5,6,4,3,2,1,0:T(8,128)} %copy-done, f32[2,2,2,2,2,32,1,512]{7,5,6,4,3,2,1,0:T(8,128)S(1)} %copy-done.2), kind=kLoop, calls=%fused_computation.13 | loop fusion | flops 2097152 | bytes 16777220 | tf_op jit(solution)/shard_map/add | solution.py:29
  137.7 19.0 %collective-permute-start.14 = (bf16[2,2,2,32,4,256]{5,3,4,2,1,0:T(8,128)(2,1)}, bf16[2,2,2,32,4,256]{5,3,4,2,1,0:T(8,128)(2,1)}, u32[]{:S(2)}, u32[]{:S(2)}) collective-permute-start(bf16[2,2,2,32,4,256]{5,3,4,2,1,0:T(8,128)(2,1)} %fusion.48), channel_id=1, source_target_pairs={{0,8},{4,12},{8,0},{12,4},{16,24},{20,28},{24,16},{28,20},{1,9},{5... | collective-permute-start | bytes 1572872 | tf_op jit(solution)/shard_map/ppermute | solution.py:29
  160.9 10.6 %collective-permute-start.12 = (bf16[2,2,32,4,256]{4,2,3,1,0:T(8,128)(2,1)S(1)}, bf16[2,2,32,4,256]{4,2,3,1,0:T(8,128)(2,1)S(1)}, u32[]{:S(2)}, u32[]{:S(2)}) collective-permute-start(bf16[2,2,32,4,256]{4,2,3,1,0:T(8,128)(2,1)S(1)} %fusion.57), channel_id=1, source_target_pairs={{0,8},{4,12},{8,0},{12,4},{16,24},{20,28},{24,16},{28,20},{1,9},{5... | collective-permute-start | bytes 786440 | tf_op jit(solution)/shard_map/ppermute | solution.py:29
  174.1 5.1 %collective-permute-start.11 = (s32[]{:T(128)}, s32[]{:T(128)}, u32[]{:S(2)}, u32[]{:S(2)}) collective-permute-start(s32[]{:T(128)} %add.154), channel_id=1, source_target_pairs={{0,16},{4,20},{8,24},{12,28},{16,0},{20,4},{24,8},{28,12},{1,17},{... | collective-permute-start | bytes 20 | tf_op jit(solution)/shard_map/ppermute | solution.py:36
  190.8 3.1 %collective-permute-start.18 = (bf16[32,4,512]{2,0,1:T(8,128)(2,1)S(1)}, bf16[32,4,512]{2,0,1:T(8,128)(2,1)S(1)}, u32[]{:S(2)}, u32[]{:S(2)}) collective-permute-start(bf16[32,4,512]{2,0,1:T(8,128)(2,1)S(1)} %fusion.62), channel_id=1, source_target_pairs={{0,2},{1,3},{2,0},{3,1},{4,6},{5,7},{6,4},{7,5},{8,10},{9,11},{10,... | collective-permute-start | bytes 393224 | tf_op jit(solution)/shard_map/ppermute | solution.py:29
  193.9 2.6 %collective-permute-start.17 = (s32[]{:T(128)}, s32[]{:T(128)}, u32[]{:S(2)}, u32[]{:S(2)}) collective-permute-start(s32[]{:T(128)} %add.164), channel_id=1, source_target_pairs={{0,1},{1,0},{2,3},{3,2},{4,5},{5,4},{6,7},{7,6},{8,9},{9,8},{10,11... | collective-permute-start | bytes 20 | tf_op jit(solution)/shard_map/ppermute | solution.py:36
  198.3 3.0 %collective-permute-start.19 = (s32[]{:T(128)}, s32[]{:T(128)}, u32[]{:S(2)}, u32[]{:S(2)}) collective-permute-start(s32[]{:T(128)} %add.171), channel_id=1, source_target_pairs={{0,2},{1,3},{2,0},{3,1},{4,6},{5,7},{6,4},{7,5},{8,10},{9,11},{10,... | collective-permute-start | bytes 20 | tf_op jit(solution)/shard_map/ppermute | solution.py:36
  (110 shorter events, 59.6 us)
Async XLA Ops:
  1.9 19.0 %copy-start.13 = (bf16[1,256,1024]{2,1,0:T(8,128)(2,1)S(1)}, bf16[1,256,1024]{2,1,0:T(8,128)(2,1)}, u32[]{:S(2)}) copy-start(bf16[1,256,1024]{2,1,0:T(8,128)(2,1)} %param.10) | copy-start | bytes 1572868
  5.6 39.7 %collective-permute-start = (bf16[2,256,512]{2,1,0:T(8,128)(2,1)S(1)}, bf16[2,256,512]{2,1,0:T(8,128)(2,1)}, u32[]{:S(2)}, u32[]{:S(2)}) collective-permute-start(bf16[2,256,512]{2,1,0:T(8,128)(2,1)S(1)} %slice.77), channel_id=1, source_target_pairs={{0,16},{4,20},{8,24},{12,28},{1,17},{5,21},{9,25},{13,29},{2,18},{... | collective-permute-start | bytes 1572872 | tf_op jit(solution)/shard_map/ppermute | solution.py:16
  11.3 35.1 %collective-permute-start.1 = (bf16[2,256,512]{2,1,0:T(8,128)(2,1)S(1)}, bf16[2,256,512]{2,1,0:T(8,128)(2,1)}, u32[]{:S(2)}, u32[]{:S(2)}) collective-permute-start(bf16[2,256,512]{2,1,0:T(8,128)(2,1)S(1)} %slice.77), channel_id=1, source_target_pairs={{0,12},{4,16},{8,20},{12,24},{16,28},{1,13},{5,17},{9,21},{13,25},... | collective-permute-start | bytes 1572872 | tf_op jit(solution)/shard_map/ppermute | solution.py:16
  14.6 32.8 %collective-permute-start.2 = (bf16[2,256,512]{2,1,0:T(8,128)(2,1)S(1)}, bf16[2,256,512]{2,1,0:T(8,128)(2,1)}, u32[]{:S(2)}, u32[]{:S(2)}) collective-permute-start(bf16[2,256,512]{2,1,0:T(8,128)(2,1)S(1)} %slice.77), channel_id=1, source_target_pairs={{0,8},{4,12},{8,16},{12,20},{16,24},{20,28},{1,9},{5,13},{9,17},{1... | collective-permute-start | bytes 1572872 | tf_op jit(solution)/shard_map/ppermute | solution.py:16
  17.5 31.0 %collective-permute-start.3 = (bf16[2,256,512]{2,1,0:T(8,128)(2,1)S(1)}, bf16[2,256,512]{2,1,0:T(8,128)(2,1)}, u32[]{:S(2)}, u32[]{:S(2)}) collective-permute-start(bf16[2,256,512]{2,1,0:T(8,128)(2,1)S(1)} %slice.77), channel_id=1, source_target_pairs={{0,4},{4,8},{8,12},{12,16},{16,20},{20,24},{24,28},{1,5},{5,9},{9,... | collective-permute-start | bytes 1572872 | tf_op jit(solution)/shard_map/ppermute | solution.py:16
  81.6 8.0 %collective-permute-start.4 = (bf16[2,256,512]{2,1,0:T(8,128)(2,1)S(1)}, bf16[2,256,512]{2,1,0:T(8,128)(2,1)S(1)}, u32[]{:S(2)}, u32[]{:S(2)}) collective-permute-start(bf16[2,256,512]{2,1,0:T(8,128)(2,1)S(1)} %get-tuple-element.46), channel_id=1, source_target_pairs={{4,0},{8,4},{12,8},{16,12},{20,16},{24,20},{28,24},{5,1},{9,5},{13... | collective-permute-start | bytes 1572872 | tf_op jit(solution)/shard_map/ppermute | solution.py:16
  83.1 28.3 %collective-permute-start.5 = (bf16[2,256,512]{2,1,0:T(8,128)(2,1)S(1)}, bf16[2,256,512]{2,1,0:T(8,128)(2,1)S(1)}, u32[]{:S(2)}, u32[]{:S(2)}) collective-permute-start(bf16[2,256,512]{2,1,0:T(8,128)(2,1)S(1)} %get-tuple-element.49), channel_id=1, source_target_pairs={{8,0},{12,4},{16,8},{20,12},{24,16},{28,20},{9,1},{13,5},{17,9},{2... | collective-permute-start | bytes 1572872 | tf_op jit(solution)/shard_map/ppermute | solution.py:16
  84.4 28.4 %collective-permute-start.6 = (bf16[2,256,512]{2,1,0:T(8,128)(2,1)S(1)}, bf16[2,256,512]{2,1,0:T(8,128)(2,1)S(1)}, u32[]{:S(2)}, u32[]{:S(2)}) collective-permute-start(bf16[2,256,512]{2,1,0:T(8,128)(2,1)S(1)} %get-tuple-element.48), channel_id=1, source_target_pairs={{12,0},{16,4},{20,8},{24,12},{28,16},{13,1},{17,5},{21,9},{25,13},... | collective-permute-start | bytes 1572872 | tf_op jit(solution)/shard_map/ppermute | solution.py:16
  85.7 27.1 %collective-permute-start.7 = (bf16[2,256,512]{2,1,0:T(8,128)(2,1)S(1)}, bf16[2,256,512]{2,1,0:T(8,128)(2,1)S(1)}, u32[]{:S(2)}, u32[]{:S(2)}) collective-permute-start(bf16[2,256,512]{2,1,0:T(8,128)(2,1)S(1)} %get-tuple-element.47), channel_id=1, source_target_pairs={{16,0},{20,4},{24,8},{28,12},{17,1},{21,5},{25,9},{29,13},{18,2},{... | collective-permute-start | bytes 1572872 | tf_op jit(solution)/shard_map/ppermute | solution.py:16
  89.0 24.2 %copy-start.11 = (bf16[1024,4,512]{2,1,0:T(4,128)(2,1)S(1)}, bf16[1024,4,512]{2,1,0:T(4,128)(2,1)}, u32[]{:S(2)}) copy-start(bf16[1024,4,512]{2,1,0:T(4,128)(2,1)} %param.9) | copy-start | bytes 12582916
  89.6 23.5 %copy-start.12 = (bf16[1,256,512]{2,1,0:T(8,128)(2,1)S(1)}, bf16[1,256,512]{2,1,0:T(8,128)(2,1)}, u32[]{:S(2)}) copy-start(bf16[1,256,512]{2,1,0:T(8,128)(2,1)} %copy.32) | copy-start | bytes 786436
  122.8 7.5 %collective-permute-start.8 = (f32[2,2,2,2,32,4,512]{6,4,5,3,2,1,0:T(8,128)}, f32[2,2,2,2,32,4,512]{6,4,5,3,2,1,0:T(8,128)}, u32[]{:S(2)}, u32[]{:S(2)}) collective-permute-start(f32[2,2,2,2,32,4,512]{6,4,5,3,2,1,0:T(8,128)} %fusion.3), channel_id=1, source_target_pairs={{0,4},{4,0},{8,12},{12,8},{16,20},{20,16},{24,28},{28,24},{1,5},{5... | collective-permute-start | bytes 12582920 | tf_op jit(solution)/shard_map/ppermute | solution.py:29
  136.6 22.7 %collective-permute-start.10 = (bf16[2,2,2,32,4,256]{5,3,4,2,1,0:T(8,128)(2,1)S(1)}, bf16[2,2,2,32,4,256]{5,3,4,2,1,0:T(8,128)(2,1)}, u32[]{:S(2)}, u32[]{:S(2)}) collective-permute-start(bf16[2,2,2,32,4,256]{5,3,4,2,1,0:T(8,128)(2,1)S(1)} %fusion.47), channel_id=1, source_target_pairs={{0,16},{4,20},{8,24},{12,28},{16,0},{20,4},{24,8},{28,12},{1,17},{... | collective-permute-start | bytes 1572872 | tf_op jit(solution)/shard_map/ppermute | solution.py:29
  137.7 33.8 %collective-permute-start.14 = (bf16[2,2,2,32,4,256]{5,3,4,2,1,0:T(8,128)(2,1)}, bf16[2,2,2,32,4,256]{5,3,4,2,1,0:T(8,128)(2,1)}, u32[]{:S(2)}, u32[]{:S(2)}) collective-permute-start(bf16[2,2,2,32,4,256]{5,3,4,2,1,0:T(8,128)(2,1)} %fusion.48), channel_id=1, source_target_pairs={{0,8},{4,12},{8,0},{12,4},{16,24},{20,28},{24,16},{28,20},{1,9},{5... | collective-permute-start | bytes 1572872 | tf_op jit(solution)/shard_map/ppermute | solution.py:29
  156.7 1.4 collective-permute-start.9
  160.9 20.9 %collective-permute-start.12 = (bf16[2,2,32,4,256]{4,2,3,1,0:T(8,128)(2,1)S(1)}, bf16[2,2,32,4,256]{4,2,3,1,0:T(8,128)(2,1)S(1)}, u32[]{:S(2)}, u32[]{:S(2)}) collective-permute-start(bf16[2,2,32,4,256]{4,2,3,1,0:T(8,128)(2,1)S(1)} %fusion.57), channel_id=1, source_target_pairs={{0,8},{4,12},{8,0},{12,4},{16,24},{20,28},{24,16},{28,20},{1,9},{5... | collective-permute-start | bytes 786440 | tf_op jit(solution)/shard_map/ppermute | solution.py:29
  173.8 9.2 %collective-permute-start.15 = (bf16[2,2,32,4,256]{4,2,3,1,0:T(8,128)(2,1)S(1)}, bf16[2,2,32,4,256]{4,2,3,1,0:T(8,128)(2,1)S(1)}, u32[]{:S(2)}, u32[]{:S(2)}) collective-permute-start(bf16[2,2,32,4,256]{4,2,3,1,0:T(8,128)(2,1)S(1)} %fusion.58), channel_id=1, source_target_pairs={{0,16},{4,20},{8,24},{12,28},{16,0},{20,4},{24,8},{28,12},{1,17},{... | collective-permute-start | bytes 786440 | tf_op jit(solution)/shard_map/ppermute | solution.py:29
  174.1 7.1 %collective-permute-start.11 = (s32[]{:T(128)}, s32[]{:T(128)}, u32[]{:S(2)}, u32[]{:S(2)}) collective-permute-start(s32[]{:T(128)} %add.154), channel_id=1, source_target_pairs={{0,16},{4,20},{8,24},{12,28},{16,0},{20,4},{24,8},{28,12},{1,17},{... | collective-permute-start | bytes 20 | tf_op jit(solution)/shard_map/ppermute | solution.py:36
  183.0 21.5 %copy-start.7 = (f32[256,1024]{1,0:T(8,128)S(1)}, f32[256,1024]{1,0:T(8,128)}, u32[]{:S(2)}) copy-start(f32[256,1024]{1,0:T(8,128)} %copy-done.6) | copy-start | bytes 3145732
  184.2 6.4 %collective-permute-start.16 = (bf16[2,32,4,512]{3,1,2,0:T(8,128)(2,1)S(1)}, bf16[2,32,4,512]{3,1,2,0:T(8,128)(2,1)S(1)}, u32[]{:S(2)}, u32[]{:S(2)}) collective-permute-start(bf16[2,32,4,512]{3,1,2,0:T(8,128)(2,1)S(1)} %fusion.59), channel_id=1, source_target_pairs={{0,1},{1,0},{2,3},{3,2},{4,5},{5,4},{6,7},{7,6},{8,9},{9,8},{10,11... | collective-permute-start | bytes 786440 | tf_op jit(solution)/shard_map/ppermute | solution.py:29
  185.9 3.5 %collective-permute-start.13 = (s32[]{:T(128)}, s32[]{:T(128)}, u32[]{:S(2)}, u32[]{:S(2)}) collective-permute-start(s32[]{:T(128)} %add.159), channel_id=1, source_target_pairs={{0,8},{4,12},{8,0},{12,4},{16,24},{20,28},{24,16},{28,20},{1,9},{5... | collective-permute-start | bytes 20 | tf_op jit(solution)/shard_map/ppermute | solution.py:36
  190.8 7.5 %collective-permute-start.18 = (bf16[32,4,512]{2,0,1:T(8,128)(2,1)S(1)}, bf16[32,4,512]{2,0,1:T(8,128)(2,1)S(1)}, u32[]{:S(2)}, u32[]{:S(2)}) collective-permute-start(bf16[32,4,512]{2,0,1:T(8,128)(2,1)S(1)} %fusion.62), channel_id=1, source_target_pairs={{0,2},{1,3},{2,0},{3,1},{4,6},{5,7},{6,4},{7,5},{8,10},{9,11},{10,... | collective-permute-start | bytes 393224 | tf_op jit(solution)/shard_map/ppermute | solution.py:29
  193.9 3.5 %collective-permute-start.17 = (s32[]{:T(128)}, s32[]{:T(128)}, u32[]{:S(2)}, u32[]{:S(2)}) collective-permute-start(s32[]{:T(128)} %add.164), channel_id=1, source_target_pairs={{0,1},{1,0},{2,3},{3,2},{4,5},{5,4},{6,7},{7,6},{8,9},{9,8},{10,11... | collective-permute-start | bytes 20 | tf_op jit(solution)/shard_map/ppermute | solution.py:36
  198.3 4.5 %collective-permute-start.19 = (s32[]{:T(128)}, s32[]{:T(128)}, u32[]{:S(2)}, u32[]{:S(2)}) collective-permute-start(s32[]{:T(128)} %add.171), channel_id=1, source_target_pairs={{0,2},{1,3},{2,0},{3,1},{4,6},{5,7},{6,4},{7,5},{8,10},{9,11},{10,... | collective-permute-start | bytes 20 | tf_op jit(solution)/shard_map/ppermute | solution.py:36
  (13 other events, 67.6 us)

commit v7 on v6

--- a/solution.py
+++ b/solution.py
@@ -36,14 +36,14 @@
     return value + lax.ppermute(value, axis, pairs), anchor
 
 
-def scatter_rows(value, tally, axes, first_axis, wire_type):
+def scatter_rows(value, tally, axes, first_axis, wire_type, tail_first=False):
     sizes = [lax.axis_size(axis) for axis in axes]
     rows = value.shape[0]
     groups = math.prod(sizes)
     if not all(is_power_of_two(n) for n in sizes) or rows % groups:
         return (
             lax.psum_scatter(value, axes, scatter_dimension=0, tiled=True),
-            lax.psum(tally, axes),
+            None if tally is None else lax.psum(tally, axes),
         )
     stages = [
         (axis, 1 << (n.bit_length() - 2 - i))
@@ -61,27 +61,39 @@
         return halve(part, dim, *stage, send_type), part_names[:dim] + part_names[dim + 1 :]
 
     first = (first_axis, 1) if (first_axis, 1) in stages else stages[-1]
+    def count_along(tally, anchor, stage):
+        if tally is None:
+            return tally, anchor
+        return swap_add(tally, anchor, *stage)
+
+    def run_tail(value, names, tally):
+        for stage in tail:
+            value, names = step(value, names, stage, wire_type)
+            tally, value = count_along(tally, value, stage)
+        return value, names, tally
+
     value, names = step(value, names, first, value.dtype)
-    tally, value = swap_add(tally, value, *first)
+    tally, value = count_along(tally, value, first)
     middle = [s for s in stages if s[0] == first[0] and s != first]
     tail = [s for s in stages if s[0] != first[0]][::-1]
+    if tail_first:
+        value, names, tally = run_tail(value, names, tally)
     if len(middle) > 1 and rest[-1] % 2 == 0:
         cut = rest[-1] // 2
         left, right = value[..., :cut], value[..., cut:]
         left_names, right_names = list(names), list(names)
         for a, b in zip(middle, middle[::-1]):
             left, left_names = step(left, left_names, a, wire_type)
-            tally, left = swap_add(tally, left, *a)
+            tally, left = count_along(tally, left, a)
             right, right_names = step(right, right_names, b, wire_type)
         value = jnp.concatenate([left, right], axis=-1)
         names = left_names
     else:
         for stage in middle:
             value, names = step(value, names, stage, wire_type)
-            tally, value = swap_add(tally, value, *stage)
-    for stage in tail:
-        value, names = step(value, names, stage, wire_type)
-        tally, value = swap_add(tally, value, *stage)
+            tally, value = count_along(tally, value, stage)
+    if not tail_first:
+        value, names, tally = run_tail(value, names, tally)
     return value, tally
 
 
@@ -174,6 +186,16 @@
         grad_kv_cols.append(accum)
     attended_all = jnp.concatenate(attended_cols, axis=1)
     grad_q = jnp.concatenate(grad_q_cols, axis=1)
+    query_part = jnp.einsum("rd,rh->dh", normed, grad_q, preferred_element_type=jnp.float32)
+    out_part = jnp.einsum("rd,rh->dh", grad_out, attended_all, preferred_element_type=jnp.float32)
+    early, count = scatter_rows(
+        jnp.stack([query_part, out_part], axis=1),
+        local_count,
+        ("tm", "night"),
+        "tm",
+        jnp.bfloat16,
+        tail_first=True,
+    )
     grad_kv_ext = jnp.concatenate(grad_kv_cols, axis=2)
     owned = grad_kv_ext[:, span * rows :]
     for offset in range(1, span + 1):
@@ -188,15 +210,11 @@
     )
     along = jnp.sum(grad_normed * normed_full, axis=-1) / width
     unscaled_input = inv_rms[:, None] * (grad_normed - normed_full * along[:, None])
-    proj_part = jnp.einsum("rd,wrh->dwh", normed, grad_proj, preferred_element_type=jnp.float32)
-    out_part = jnp.einsum("rd,rh->dh", grad_out, attended_all, preferred_element_type=jnp.float32)
-    summed, count = scatter_rows(
-        jnp.concatenate([proj_part, out_part[:, None]], axis=1),
-        local_count,
-        ("tm", "night"),
-        "tm",
-        jnp.bfloat16,
-    )
+    key_value_part = jnp.einsum(
+        "rd,wrh->dwh", normed, grad_kv, preferred_element_type=jnp.float32
+    )
+    late, _ = scatter_rows(key_value_part, None, ("tm", "night"), "tm", jnp.bfloat16)
+    summed = jnp.concatenate([early[:, :1], late, early[:, 1:]], axis=1)
     total_count = count.astype(jnp.float32)
     loss_scale = jnp.float32(tokens_all) / total_count
     grad_input = (loss_scale * unscaled_input).astype(jnp.bfloat16)

time: 206 us -> 189 us (0.917)
  starting transfers between devices: 67 us -> 51.7 us
  matrix products: 29.9 us -> 32 us
  local copies, waits for them, and re-layouts: 29.8 us -> 27.7 us
    ppermute x8, waiting for transfers between devices: 38.5 us -> 18.8 us  [shifted(): return lax.ppermute(value, axis, pairs)]
    ppermute x7 -> x14, waiting for transfers between devices: 7.65 us -> 26.6 us  [halve(): lax.ppermute(send.astype(send_type), axis, pairs).astype(keep.dtype)]
    ppermute x7 -> x14, starting transfers between devices: 35 us -> 23.4 us  [halve(): lax.ppermute(send.astype(send_type), axis, pairs).astype(keep.dtype)]
    add x7 -> x14, other arithmetic: 9.39 us -> 4.68 us  [halve(): keep + lax.ppermute(send.astype(send_type), axis, pairs).astype(keep.dtype)]
    ppermute x5, starting transfers between devices: 12.5 us -> 8.59 us  [swap_add(): return (value + lax.ppermute(value, axis, pairs), anchor)]
    squeeze x1 -> x0, other arithmetic: 2.96 us -> none  [halve(): send = lax.dynamic_index_in_dim(value, 1 - bit, dim, keepdims=False)]
    unnamed x40 -> x38, local copies, waits for them, and re-layouts: 9.6 us -> 6.76 us
    dot_general x1, matrix products: 2.6 us -> 5.02 us  [band_block(): jnp.einsum('gqk,qgc->kgc', grad_scores, queries, preferred_element_type=j...]
  transfers between devices with their start and end apart: 20 -> 27, of which waited for: 11 -> 16; matrix products, arithmetic and copies ran while one was open for 10% -> 23% of each run, Pallas kernels for 0% -> 0%
where the time goes in v7:
time: 189 us; the launch traced here: 188 us
  waiting for transfers between devices  53.1 us (28%)
  starting transfers between devices  51.7 us (27%)
  matrix products  32 us (17%)
  local copies, waits for them, and re-layouts  27.7 us (15%)
  other arithmetic  18.7 us (10%)
  between operations  5.17 us (3%)
    ppermute x14, waiting for transfers between devices, halve(): lax.ppermute(send.astype(send_type), axis, pairs).astype(keep.dtype)  26.6 us
    ppermute x14, starting transfers between devices, halve(): lax.ppermute(send.astype(send_type), axis, pairs).astype(keep.dtype)  23.4 us
    ppermute x8, starting transfers between devices, shifted(): return lax.ppermute(value, axis, pairs)  19.7 us
    ppermute x8, waiting for transfers between devices, shifted(): return lax.ppermute(value, axis, pairs)  18.8 us
    ppermute x5, starting transfers between devices, swap_add(): return (value + lax.ppermute(value, axis, pairs), anchor)  8.59 us
    ppermute x5, waiting for transfers between devices, swap_add(): return (value + lax.ppermute(value, axis, pairs), anchor)  7.75 us
    unnamed x38, local copies, waits for them, and re-layouts  6.76 us
    another operation x2, local copies, waits for them, and re-layouts, shards(): update = jnp.stack([grad_key, grad_value]).reshape(2, key_len, group_cols)  5.37 us
  transfers between devices with their start and end apart: 27, of which 16 were waited for; matrix products, arithmetic and copies ran while one was open for 23% of the time, Pallas kernels for 0%

profile of v7, /device:TPU:0, one launch (start us, length us, event | category | flops | bytes accessed | tf_op | source)
XLA Modules:
  0.0 188.4 jit_solution(9670382680706004337)
XLA Ops:
  1.9 3.7 %fusion.28 = bf16[3,256,512]{2,1,0:T(8,128)(2,1)S(1)} fusion(bf16[1024,3,512]{2,1,0:T(4,128)(2,1)} %bitcast.188, bf16[1,256,1024]{2,1,0:T(8,128)(2,1)} %param.8, f32[256]{0:T(256)S(1)} %add_rsqrt_fusion), kind=kOutput, calls=%fused_computation.40 | convolution fusion | flops 806486016 | bytes 4457472 | tf_op jit(solution)/shard_map/rd,dwh->wrh/dot_general | solution.py:143
  5.7 5.8 %collective-permute-start = (bf16[2,256,512]{2,1,0:T(8,128)(2,1)S(1)}, bf16[2,256,512]{2,1,0:T(8,128)(2,1)}, u32[]{:S(2)}, u32[]{:S(2)}) collective-permute-start(bf16[2,256,512]{2,1,0:T(8,128)(2,1)S(1)} %slice.93), channel_id=1, source_target_pairs={{0,16},{4,20},{8,24},{12,28},{1,17},{5,21},{9,25},{13,29},{2,18},{... | collective-permute-start | bytes 1572872 | tf_op jit(solution)/shard_map/ppermute | solution.py:16
  11.5 3.4 %collective-permute-start.1 = (bf16[2,256,512]{2,1,0:T(8,128)(2,1)S(1)}, bf16[2,256,512]{2,1,0:T(8,128)(2,1)}, u32[]{:S(2)}, u32[]{:S(2)}) collective-permute-start(bf16[2,256,512]{2,1,0:T(8,128)(2,1)S(1)} %slice.93), channel_id=1, source_target_pairs={{0,12},{4,16},{8,20},{12,24},{16,28},{1,13},{5,17},{9,21},{13,25},... | collective-permute-start | bytes 1572872 | tf_op jit(solution)/shard_map/ppermute | solution.py:16
  14.9 2.9 %collective-permute-start.2 = (bf16[2,256,512]{2,1,0:T(8,128)(2,1)S(1)}, bf16[2,256,512]{2,1,0:T(8,128)(2,1)}, u32[]{:S(2)}, u32[]{:S(2)}) collective-permute-start(bf16[2,256,512]{2,1,0:T(8,128)(2,1)S(1)} %slice.93), channel_id=1, source_target_pairs={{0,8},{4,12},{8,16},{12,20},{16,24},{20,28},{1,9},{5,13},{9,17},{1... | collective-permute-start | bytes 1572872 | tf_op jit(solution)/shard_map/ppermute | solution.py:16
  19.9 3.5 %slice.80 = bf16[1024,1,512]{2,1,0:T(2,128)(2,1)} slice(bf16[1024,4,512]{2,1,0:T(4,128)(2,1)S(1)} %copy-done.12), slice={[0:1024], [3:4], [0:512]} | slice | bytes 2097152 | tf_op jit(solution)/shard_map/slice | solution.py:154
  30.1 15.4 %collective-permute-done = bf16[2,256,512]{2,1,0:T(8,128)(2,1)} collective-permute-done((bf16[2,256,512]{2,1,0:T(8,128)(2,1)S(1)}, bf16[2,256,512]{2,1,0:T(8,128)(2,1)}, u32[]{:S(2)}, u32[]{:S(2)}) %collective-permute-start) | collective-permute-done | bytes 524320 | tf_op jit(solution)/shard_map/ppermute | solution.py:16
  54.2 3.9 %fusion.1 = (f32[8,256]{1,0:T(8,128)S(1)}, f32[8,256,1280]{2,1,0:T(8,128)S(1)}) fusion(f32[256,1280]{1,0:T(8,128)} %fusion.27, bf16[256,8,64]{0,2,1:T(8,128)(2,1)S(1)} %bitcast.178, bf16[1280,8,64]{0,2,1:T(8,128)(2,1)S(1)} %bitcast.176), kind=kOutput, calls=%fused_computation.3 | convolution fusion | flops 343406592 | bytes 13377536 | tf_op jit(solution)/shard_map/qgc,kgc->gqk/dot_general | solution.py:102
  60.9 3.9 %multiply_convert_fusion = bf16[8,256,1280]{2,1,0:T(8,128)(2,1)S(1)} fusion(bf16[256,8,64]{0,2,1:T(8,128)(2,1)S(1)} %bitcast.190, bf16[1280,8,64]{0,2,1:T(8,128)(2,1)S(1)} %bitcast.187, f32[8,256]{1,0:T(8,128)S(1)} %bitcast.193, f32[8,256]{1,0:T(8,128)S(1)} %get-tuple-element.58, f32[256,1280]{1,0:T(8,128)S(1)} %copy-done.4, ...), kind=kOutput, calls=%fused_computation | convolution fusion | flops 353894400 | bytes 18628608 | tf_op jit(solution)/shard_map/qgc,kgc->gqk/dot_general | solution.py:112
  72.4 3.5 %collective-permute-start.4 = (f32[2,2,2,2,32,2,512]{6,4,5,3,2,1,0:T(8,128)}, f32[2,2,2,2,32,2,512]{6,4,5,3,2,1,0:T(8,128)}, u32[]{:S(2)}, u32[]{:S(2)}) collective-permute-start(f32[2,2,2,2,32,2,512]{6,4,5,3,2,1,0:T(8,128)} %bitcast.173), channel_id=1, source_target_pairs={{0,4},{4,0},{8,12},{12,8},{16,20},{20,16},{24,28},{28,24},{1,5},{5... | collective-permute-start | bytes 6291464 | tf_op jit(solution)/shard_map/ppermute | solution.py:29
  75.9 3.5 %fusion.2 = f32[8,64,1280]{2,1,0:T(8,128)} fusion(bf16[256,8,64]{0,2,1:T(8,128)(2,1)S(1)} %bitcast.191, f32[8,256,1280]{2,1,0:T(8,128)S(1)} %get-tuple-element.59, f32[8,256]{1,0:T(8,128)S(1)} %get-tuple-element.58, f32[256,1280]{1,0:T(8,128)S(1)} %copy-done.4), kind=kOutput, calls=%fused_computation.9 | convolution fusion | flops 346030080 | bytes 14688256 | tf_op jit(solution)/shard_map/gqk,qgc->kgc/dot_general | solution.py:122
  81.5 5.0 %fusion.84 = f32[8,64,1280]{2,1,0:T(8,128)} fusion(bf16[256,8,64]{0,2,1:T(8,128)(2,1)S(1)} %bitcast.179, bf16[8,256,1280]{2,1,0:T(8,128)(2,1)} %copy-done), kind=kOutput, calls=%fused_computation.134 | convolution fusion | flops 335544320 | bytes 8126464 | tf_op jit(solution)/shard_map/gqk,qgc->kgc/dot_general | solution.py:121
  86.5 3.2 %copy.36 = f32[1,1,1280,512]{3,2,1,0:T(8,128)} copy(f32[1,1,1280,512]{2,3,1,0:T(8,128)} %bitcast.175) | data formatting | bytes 5242880 | tf_op jit(solution)/shard_map/stack | solution.py:182
  104.9 3.0 %maximum_bitcast_fusion = f32[2,1280,512]{2,1,0:T(8,128)} fusion(f32[1,1,1280,512]{3,2,1,0:T(8,128)S(1)} %copy.37, f32[1,1,1280,512]{3,2,1,0:T(8,128)S(1)} %copy-done.1), kind=kLoop, calls=%fused_computation.4 | loop fusion | flops 1310720 | bytes 10485760 | tf_op jit(solution)/shard_map/add | solution.py:183
  114.5 3.3 %collective-permute-done.15 = bf16[2,256,512]{2,1,0:T(8,128)(2,1)} collective-permute-done((bf16[2,256,512]{2,1,0:T(8,128)(2,1)}, bf16[2,256,512]{2,1,0:T(8,128)(2,1)}, u32[]{:S(2)}, u32[]{:S(2)}) %collective-permute-start.15) | collective-permute-done | bytes 524320 | tf_op jit(solution)/shard_map/ppermute | solution.py:16
  124.2 3.2 %collective-permute-done.8 = bf16[2,2,32,2,512]{4,2,3,1,0:T(8,128)(2,1)S(1)} collective-permute-done((bf16[2,2,32,2,512]{4,2,3,1,0:T(8,128)(2,1)S(1)}, bf16[2,2,32,2,512]{4,2,3,1,0:T(8,128)(2,1)S(1)}, u32[]{:S(2)}, u32[]{:S(2)}) %collective-permute-start.8) | collective-permute-done | bytes 262176 | tf_op jit(solution)/shard_map/ppermute | solution.py:29
  127.5 6.5 %collective-permute-start.10 = (bf16[2,32,2,256]{3,1,2,0:T(8,128)(2,1)S(1)}, bf16[2,32,2,256]{3,1,2,0:T(8,128)(2,1)S(1)}, u32[]{:S(2)}, u32[]{:S(2)}) collective-permute-start(bf16[2,32,2,256]{3,1,2,0:T(8,128)(2,1)S(1)} %fusion.70), channel_id=1, source_target_pairs={{0,16},{4,20},{8,24},{12,28},{16,0},{20,4},{24,8},{28,12},{1,17},{... | collective-permute-start | bytes 196616 | tf_op jit(solution)/shard_map/ppermute | solution.py:29
  134.0 3.6 %fusion.34 = (f32[256]{0:T(256)S(1)}, f32[256,1024]{1,0:T(8,128)S(1)}) fusion(bf16[1,256,1024]{2,1,0:T(8,128)(2,1)S(1)} %copy-done.5, f32[256]{0:T(256)S(1)} %add_rsqrt_fusion, bf16[1024,3,512]{2,1,0:T(4,128)(2,1)} %bitcast.189, bf16[2,256,512]{2,1,0:T(8,128)(2,1)S(1)} %fusion.44, bf16[1,256,512]{2,1,0:T(8,128)(2,1)} %copy.38), kind=kOutput, calls=%fused_computation.44 | convolution fusion | flops 806747904 | bytes 5507072 | tf_op jit(solution)/shard_map/wrh,dwh->rd/dot_general | solution.py:208
  137.6 4.0 %collective-permute-start.9 = (s32[]{:T(128)}, s32[]{:T(128)}, u32[]{:S(2)}, u32[]{:S(2)}) collective-permute-start(s32[]{:T(128)} %add.201), channel_id=1, source_target_pairs={{0,2},{1,3},{2,0},{3,1},{4,6},{5,7},{6,4},{7,5},{8,10},{9,11},{10,... | collective-permute-start | bytes 20 | tf_op jit(solution)/shard_map/ppermute | solution.py:36
  156.4 4.0 %collective-permute-done.20 = f32[2,2,2,2,32,2,512]{6,4,5,3,2,1,0:T(8,128)S(1)} collective-permute-done((f32[2,2,2,2,32,2,512]{6,4,5,3,2,1,0:T(8,128)S(1)}, f32[2,2,2,2,32,2,512]{6,4,5,3,2,1,0:T(8,128)S(1)}, u32[]{:S(2)}, u32[]{:S(2)}) %collective-permute-start.20) | collective-permute-done | bytes 2097184 | tf_op jit(solution)/shard_map/ppermute | solution.py:29
  163.6 6.4 %collective-permute-done.21 = bf16[2,2,2,32,2,256]{5,3,4,2,1,0:T(8,128)(2,1)S(1)} collective-permute-done((bf16[2,2,2,32,2,256]{5,3,4,2,1,0:T(8,128)(2,1)S(1)}, bf16[2,2,2,32,2,256]{5,3,4,2,1,0:T(8,128)(2,1)S(1)}, u32[]{:S(2)}, u32[]{:S(2)}) %collective-permute-start.21) | collective-permute-done | bytes 262176 | tf_op jit(solution)/shard_map/ppermute | solution.py:29
  171.8 3.3 %collective-permute-done.22 = bf16[2,2,32,2,256]{4,2,3,1,0:T(8,128)(2,1)S(1)} collective-permute-done((bf16[2,2,32,2,256]{4,2,3,1,0:T(8,128)(2,1)S(1)}, bf16[2,2,32,2,256]{4,2,3,1,0:T(8,128)(2,1)S(1)}, u32[]{:S(2)}, u32[]{:S(2)}) %collective-permute-start.22) | collective-permute-done | bytes 131104 | tf_op jit(solution)/shard_map/ppermute | solution.py:29
  177.1 4.5 %collective-permute-done.25 = bf16[2,32,2,512]{3,1,2,0:T(8,128)(2,1)S(1)} collective-permute-done((bf16[2,32,2,512]{3,1,2,0:T(8,128)(2,1)S(1)}, bf16[2,32,2,512]{3,1,2,0:T(8,128)(2,1)S(1)}, u32[]{:S(2)}, u32[]{:S(2)}) %collective-permute-start.25) | collective-permute-done | bytes 131104 | tf_op jit(solution)/shard_map/ppermute | solution.py:29
  181.7 2.9 %collective-permute-start.26 = (bf16[32,2,512]{2,0,1:T(8,128)(2,1)S(1)}, bf16[32,2,512]{2,0,1:T(8,128)(2,1)S(1)}, u32[]{:S(2)}, u32[]{:S(2)}) collective-permute-start(bf16[32,2,512]{2,0,1:T(8,128)(2,1)S(1)} %fusion.72), channel_id=1, source_target_pairs={{0,2},{1,3},{2,0},{3,1},{4,6},{5,7},{6,4},{7,5},{8,10},{9,11},{10,... | collective-permute-start | bytes 196616 | tf_op jit(solution)/shard_map/ppermute | solution.py:29
  184.6 2.9 %collective-permute-done.26 = bf16[32,2,512]{2,0,1:T(8,128)(2,1)S(1)} collective-permute-done((bf16[32,2,512]{2,0,1:T(8,128)(2,1)S(1)}, bf16[32,2,512]{2,0,1:T(8,128)(2,1)S(1)}, u32[]{:S(2)}, u32[]{:S(2)}) %collective-permute-start.26) | collective-permute-done | bytes 65568 | tf_op jit(solution)/shard_map/ppermute | solution.py:29
  (141 shorter events, 78.0 us)
Async XLA Ops:
  5.7 39.8 %collective-permute-start = (bf16[2,256,512]{2,1,0:T(8,128)(2,1)S(1)}, bf16[2,256,512]{2,1,0:T(8,128)(2,1)}, u32[]{:S(2)}, u32[]{:S(2)}) collective-permute-start(bf16[2,256,512]{2,1,0:T(8,128)(2,1)S(1)} %slice.93), channel_id=1, source_target_pairs={{0,16},{4,20},{8,24},{12,28},{1,17},{5,21},{9,25},{13,29},{2,18},{... | collective-permute-start | bytes 1572872 | tf_op jit(solution)/shard_map/ppermute | solution.py:16
  11.5 35.1 %collective-permute-start.1 = (bf16[2,256,512]{2,1,0:T(8,128)(2,1)S(1)}, bf16[2,256,512]{2,1,0:T(8,128)(2,1)}, u32[]{:S(2)}, u32[]{:S(2)}) collective-permute-start(bf16[2,256,512]{2,1,0:T(8,128)(2,1)S(1)} %slice.93), channel_id=1, source_target_pairs={{0,12},{4,16},{8,20},{12,24},{16,28},{1,13},{5,17},{9,21},{13,25},... | collective-permute-start | bytes 1572872 | tf_op jit(solution)/shard_map/ppermute | solution.py:16
  14.9 32.8 %collective-permute-start.2 = (bf16[2,256,512]{2,1,0:T(8,128)(2,1)S(1)}, bf16[2,256,512]{2,1,0:T(8,128)(2,1)}, u32[]{:S(2)}, u32[]{:S(2)}) collective-permute-start(bf16[2,256,512]{2,1,0:T(8,128)(2,1)S(1)} %slice.93), channel_id=1, source_target_pairs={{0,8},{4,12},{8,16},{12,20},{16,24},{20,28},{1,9},{5,13},{9,17},{1... | collective-permute-start | bytes 1572872 | tf_op jit(solution)/shard_map/ppermute | solution.py:16
  17.8 31.0 %collective-permute-start.3 = (bf16[2,256,512]{2,1,0:T(8,128)(2,1)S(1)}, bf16[2,256,512]{2,1,0:T(8,128)(2,1)}, u32[]{:S(2)}, u32[]{:S(2)}) collective-permute-start(bf16[2,256,512]{2,1,0:T(8,128)(2,1)S(1)} %slice.93), channel_id=1, source_target_pairs={{0,4},{4,8},{8,12},{12,16},{16,20},{20,24},{24,28},{1,5},{5,9},{9,... | collective-permute-start | bytes 1572872 | tf_op jit(solution)/shard_map/ppermute | solution.py:16
  72.4 19.7 %collective-permute-start.4 = (f32[2,2,2,2,32,2,512]{6,4,5,3,2,1,0:T(8,128)}, f32[2,2,2,2,32,2,512]{6,4,5,3,2,1,0:T(8,128)}, u32[]{:S(2)}, u32[]{:S(2)}) collective-permute-start(f32[2,2,2,2,32,2,512]{6,4,5,3,2,1,0:T(8,128)} %bitcast.173), channel_id=1, source_target_pairs={{0,4},{4,0},{8,12},{12,8},{16,20},{20,16},{24,28},{28,24},{1,5},{5... | collective-permute-start | bytes 6291464 | tf_op jit(solution)/shard_map/ppermute | solution.py:29
  95.1 14.9 %collective-permute-start.6 = (bf16[2,2,2,32,2,512]{5,3,4,2,1,0:T(8,128)(2,1)}, bf16[2,2,2,32,2,512]{5,3,4,2,1,0:T(8,128)(2,1)}, u32[]{:S(2)}, u32[]{:S(2)}) collective-permute-start(bf16[2,2,2,32,2,512]{5,3,4,2,1,0:T(8,128)(2,1)} %fusion.48), channel_id=1, source_target_pairs={{0,1},{1,0},{2,3},{3,2},{4,5},{5,4},{6,7},{7,6},{8,9},{9,8},{10,11... | collective-permute-start | bytes 1572872 | tf_op jit(solution)/shard_map/ppermute | solution.py:29
  98.1 16.4 %collective-permute-start.17 = (bf16[2,256,512]{2,1,0:T(8,128)(2,1)}, bf16[2,256,512]{2,1,0:T(8,128)(2,1)}, u32[]{:S(2)}, u32[]{:S(2)}) collective-permute-start(bf16[2,256,512]{2,1,0:T(8,128)(2,1)} %get-tuple-element.47), channel_id=1, source_target_pairs={{16,0},{20,4},{24,8},{28,12},{17,1},{21,5},{25,9},{29,13},{18,2},{... | collective-permute-start | bytes 1572872 | tf_op jit(solution)/shard_map/ppermute | solution.py:16
  99.4 15.1 %collective-permute-start.16 = (bf16[2,256,512]{2,1,0:T(8,128)(2,1)}, bf16[2,256,512]{2,1,0:T(8,128)(2,1)}, u32[]{:S(2)}, u32[]{:S(2)}) collective-permute-start(bf16[2,256,512]{2,1,0:T(8,128)(2,1)} %get-tuple-element.48), channel_id=1, source_target_pairs={{12,0},{16,4},{20,8},{24,12},{28,16},{13,1},{17,5},{21,9},{25,13},... | collective-permute-start | bytes 1572872 | tf_op jit(solution)/shard_map/ppermute | solution.py:16
  100.7 17.1 %collective-permute-start.15 = (bf16[2,256,512]{2,1,0:T(8,128)(2,1)}, bf16[2,256,512]{2,1,0:T(8,128)(2,1)}, u32[]{:S(2)}, u32[]{:S(2)}) collective-permute-start(bf16[2,256,512]{2,1,0:T(8,128)(2,1)} %get-tuple-element.49), channel_id=1, source_target_pairs={{8,0},{12,4},{16,8},{20,12},{24,16},{28,20},{9,1},{13,5},{17,9},{2... | collective-permute-start | bytes 1572872 | tf_op jit(solution)/shard_map/ppermute | solution.py:16
  103.2 14.5 %collective-permute-start.14 = (bf16[2,256,512]{2,1,0:T(8,128)(2,1)}, bf16[2,256,512]{2,1,0:T(8,128)(2,1)}, u32[]{:S(2)}, u32[]{:S(2)}) collective-permute-start(bf16[2,256,512]{2,1,0:T(8,128)(2,1)} %get-tuple-element.46), channel_id=1, source_target_pairs={{4,0},{8,4},{12,8},{16,12},{20,16},{24,20},{28,24},{5,1},{9,5},{13... | collective-permute-start | bytes 1572872 | tf_op jit(solution)/shard_map/ppermute | solution.py:16
  111.7 15.6 %collective-permute-start.8 = (bf16[2,2,32,2,512]{4,2,3,1,0:T(8,128)(2,1)S(1)}, bf16[2,2,32,2,512]{4,2,3,1,0:T(8,128)(2,1)S(1)}, u32[]{:S(2)}, u32[]{:S(2)}) collective-permute-start(bf16[2,2,32,2,512]{4,2,3,1,0:T(8,128)(2,1)S(1)} %fusion.55), channel_id=1, source_target_pairs={{0,2},{1,3},{2,0},{3,1},{4,6},{5,7},{6,4},{7,5},{8,10},{9,11},{10,... | collective-permute-start | bytes 786440 | tf_op jit(solution)/shard_map/ppermute | solution.py:29
  119.9 3.6 %collective-permute-start.7 = (s32[]{:T(128)}, s32[]{:T(128)}, u32[]{:S(2)}, u32[]{:S(2)}) collective-permute-start(s32[]{:T(128)} %add.196), channel_id=1, source_target_pairs={{0,1},{1,0},{2,3},{3,2},{4,5},{5,4},{6,7},{7,6},{8,9},{9,8},{10,11... | collective-permute-start | bytes 20 | tf_op jit(solution)/shard_map/ppermute | solution.py:36
  127.5 15.2 %collective-permute-start.10 = (bf16[2,32,2,256]{3,1,2,0:T(8,128)(2,1)S(1)}, bf16[2,32,2,256]{3,1,2,0:T(8,128)(2,1)S(1)}, u32[]{:S(2)}, u32[]{:S(2)}) collective-permute-start(bf16[2,32,2,256]{3,1,2,0:T(8,128)(2,1)S(1)} %fusion.70), channel_id=1, source_target_pairs={{0,16},{4,20},{8,24},{12,28},{16,0},{20,4},{24,8},{28,12},{1,17},{... | collective-permute-start | bytes 196616 | tf_op jit(solution)/shard_map/ppermute | solution.py:29
  137.6 4.5 %collective-permute-start.9 = (s32[]{:T(128)}, s32[]{:T(128)}, u32[]{:S(2)}, u32[]{:S(2)}) collective-permute-start(s32[]{:T(128)} %add.201), channel_id=1, source_target_pairs={{0,2},{1,3},{2,0},{3,1},{4,6},{5,7},{6,4},{7,5},{8,10},{9,11},{10,... | collective-permute-start | bytes 20 | tf_op jit(solution)/shard_map/ppermute | solution.py:36
  142.7 6.8 %collective-permute-start.12 = (bf16[32,2,256]{2,0,1:T(8,128)(2,1)S(1)}, bf16[32,2,256]{2,0,1:T(8,128)(2,1)S(1)}, u32[]{:S(2)}, u32[]{:S(2)}) collective-permute-start(bf16[32,2,256]{2,0,1:T(8,128)(2,1)S(1)} %fusion.74), channel_id=1, source_target_pairs={{0,8},{4,12},{8,0},{12,4},{16,24},{20,28},{24,16},{28,20},{1,9},{5... | collective-permute-start | bytes 98312 | tf_op jit(solution)/shard_map/ppermute | solution.py:29
  156.1 4.2 %collective-permute-start.20 = (f32[2,2,2,2,32,2,512]{6,4,5,3,2,1,0:T(8,128)S(1)}, f32[2,2,2,2,32,2,512]{6,4,5,3,2,1,0:T(8,128)S(1)}, u32[]{:S(2)}, u32[]{:S(2)}) collective-permute-start(f32[2,2,2,2,32,2,512]{6,4,5,3,2,1,0:T(8,128)S(1)} %dynamic-slice_bitcast_fusion), channel_id=1, source_target_pairs={{0,4},{4,0},{8,12},{12,8},{16,20},{20,16},{24,28},{28,24},{1,5},{5... | collective-permute-start | bytes 6291464 | tf_op jit(solution)/shard_map/ppermute | solution.py:29
  156.2 5.1 %collective-permute-start.18 = (bf16[2,32,2,256]{3,1,2,0:T(8,128)(2,1)S(1)}, bf16[2,32,2,256]{3,1,2,0:T(8,128)(2,1)S(1)}, u32[]{:S(2)}, u32[]{:S(2)}) collective-permute-start(bf16[2,32,2,256]{3,1,2,0:T(8,128)(2,1)S(1)} %fusion.71), channel_id=1, source_target_pairs={{0,8},{4,12},{8,0},{12,4},{16,24},{20,28},{24,16},{28,20},{1,9},{5... | collective-permute-start | bytes 196616 | tf_op jit(solution)/shard_map/ppermute | solution.py:29
  161.2 8.8 %collective-permute-start.21 = (bf16[2,2,2,32,2,256]{5,3,4,2,1,0:T(8,128)(2,1)S(1)}, bf16[2,2,2,32,2,256]{5,3,4,2,1,0:T(8,128)(2,1)S(1)}, u32[]{:S(2)}, u32[]{:S(2)}) collective-permute-start(bf16[2,2,2,32,2,256]{5,3,4,2,1,0:T(8,128)(2,1)S(1)} %fusion.56), channel_id=1, source_target_pairs={{0,16},{4,20},{8,24},{12,28},{16,0},{20,4},{24,8},{28,12},{1,17},{... | collective-permute-start | bytes 786440 | tf_op jit(solution)/shard_map/ppermute | solution.py:29
  161.4 15.7 %collective-permute-start.19 = (bf16[32,2,256]{2,0,1:T(8,128)(2,1)S(1)}, bf16[32,2,256]{2,0,1:T(8,128)(2,1)S(1)}, u32[]{:S(2)}, u32[]{:S(2)}) collective-permute-start(bf16[32,2,256]{2,0,1:T(8,128)(2,1)S(1)} %fusion.75), channel_id=1, source_target_pairs={{0,16},{4,20},{8,24},{12,28},{16,0},{20,4},{24,8},{28,12},{1,17},{... | collective-permute-start | bytes 98312 | tf_op jit(solution)/shard_map/ppermute | solution.py:29
  163.5 7.9 %collective-permute-start.23 = (bf16[2,2,2,32,2,256]{5,3,4,2,1,0:T(8,128)(2,1)S(1)}, bf16[2,2,2,32,2,256]{5,3,4,2,1,0:T(8,128)(2,1)S(1)}, u32[]{:S(2)}, u32[]{:S(2)}) collective-permute-start(bf16[2,2,2,32,2,256]{5,3,4,2,1,0:T(8,128)(2,1)S(1)} %fusion.57), channel_id=1, source_target_pairs={{0,8},{4,12},{8,0},{12,4},{16,24},{20,28},{24,16},{28,20},{1,9},{5... | collective-permute-start | bytes 786440 | tf_op jit(solution)/shard_map/ppermute | solution.py:29
  170.1 5.0 %collective-permute-start.22 = (bf16[2,2,32,2,256]{4,2,3,1,0:T(8,128)(2,1)S(1)}, bf16[2,2,32,2,256]{4,2,3,1,0:T(8,128)(2,1)S(1)}, u32[]{:S(2)}, u32[]{:S(2)}) collective-permute-start(bf16[2,2,32,2,256]{4,2,3,1,0:T(8,128)(2,1)S(1)} %fusion.67), channel_id=1, source_target_pairs={{0,8},{4,12},{8,0},{12,4},{16,24},{20,28},{24,16},{28,20},{1,9},{5... | collective-permute-start | bytes 393224 | tf_op jit(solution)/shard_map/ppermute | solution.py:29
  171.5 5.0 %collective-permute-start.24 = (bf16[2,2,32,2,256]{4,2,3,1,0:T(8,128)(2,1)S(1)}, bf16[2,2,32,2,256]{4,2,3,1,0:T(8,128)(2,1)S(1)}, u32[]{:S(2)}, u32[]{:S(2)}) collective-permute-start(bf16[2,2,32,2,256]{4,2,3,1,0:T(8,128)(2,1)S(1)} %fusion.68), channel_id=1, source_target_pairs={{0,16},{4,20},{8,24},{12,28},{16,0},{20,4},{24,8},{28,12},{1,17},{... | collective-permute-start | bytes 393224 | tf_op jit(solution)/shard_map/ppermute | solution.py:29
  176.6 5.0 %collective-permute-start.25 = (bf16[2,32,2,512]{3,1,2,0:T(8,128)(2,1)S(1)}, bf16[2,32,2,512]{3,1,2,0:T(8,128)(2,1)S(1)}, u32[]{:S(2)}, u32[]{:S(2)}) collective-permute-start(bf16[2,32,2,512]{3,1,2,0:T(8,128)(2,1)S(1)} %fusion.69), channel_id=1, source_target_pairs={{0,1},{1,0},{2,3},{3,2},{4,5},{5,4},{6,7},{7,6},{8,9},{9,8},{10,11... | collective-permute-start | bytes 393224 | tf_op jit(solution)/shard_map/ppermute | solution.py:29
  181.7 5.8 %collective-permute-start.26 = (bf16[32,2,512]{2,0,1:T(8,128)(2,1)S(1)}, bf16[32,2,512]{2,0,1:T(8,128)(2,1)S(1)}, u32[]{:S(2)}, u32[]{:S(2)}) collective-permute-start(bf16[32,2,512]{2,0,1:T(8,128)(2,1)S(1)} %fusion.72), channel_id=1, source_target_pairs={{0,2},{1,3},{2,0},{3,1},{4,6},{5,7},{6,4},{7,5},{8,10},{9,11},{10,... | collective-permute-start | bytes 196616 | tf_op jit(solution)/shard_map/ppermute | solution.py:29
  (19 other events, 111.0 us)

commit v8 on v7

--- a/solution.py
+++ b/solution.py
@@ -116,11 +116,11 @@
         jnp.bfloat16
     )
     grad_query = jnp.einsum(
-        "gqk,kgc->qgc", grad_scores, keys_blk, preferred_element_type=jnp.float32
-    )
-    grad_key = jnp.einsum("gqk,qgc->kgc", grad_scores, queries, preferred_element_type=jnp.float32)
+        "gqk,kgc->gcq", grad_scores, keys_blk, preferred_element_type=jnp.float32
+    )
+    grad_key = jnp.einsum("gqk,qgc->gck", grad_scores, queries, preferred_element_type=jnp.float32)
     grad_value = jnp.einsum(
-        "gqk,qgc->kgc", probs_low, grad_attn, preferred_element_type=jnp.float32
+        "gqk,qgc->gck", probs_low, grad_attn, preferred_element_type=jnp.float32
     )
     return (attended, grad_query, grad_key, grad_value)
 
@@ -159,34 +159,20 @@
     key_idx = jnp.arange(key_len, dtype=jnp.int32)[None, :]
     offsets = query_idx - key_idx + span * rows
     band = (offsets >= 0) & (offsets < WIN)
-    attended_cols = []
-    grad_q_cols = []
-    grad_kv_cols = []
-    for first in range(0, inner, group_cols):
-        accum = jnp.zeros((2, (span + 1) * rows, group_cols), jnp.float32)
-        valid = (band & (key_idx >= span * rows - base - 0)).astype(jnp.float32)
-        query_blk = queries[0:block_rows, first : first + group_cols].reshape(
-            block_rows, group, HSIZE
-        )
-        kv_blk = extended[:, 0:key_len, first : first + group_cols].reshape(
-            2, key_len, group, HSIZE
-        )
-        grad_blk = grad_attn[0:block_rows, first : first + group_cols].reshape(
-            block_rows, group, HSIZE
-        )
-        attended, grad_query, grad_key, grad_value = band_block(
-            query_blk, kv_blk[0], kv_blk[1], grad_blk, valid, inv_scale
-        )
-        attended_rows = attended.reshape(block_rows, group_cols)
-        grad_q_rows = grad_query.reshape(block_rows, group_cols).astype(jnp.bfloat16)
-        update = jnp.stack([grad_key, grad_value]).reshape(2, key_len, group_cols)
-        accum = accum.at[:, 0:key_len].add(update)
-        attended_cols.append(attended_rows)
-        grad_q_cols.append(grad_q_rows)
-        grad_kv_cols.append(accum)
-    attended_all = jnp.concatenate(attended_cols, axis=1)
-    grad_q = jnp.concatenate(grad_q_cols, axis=1)
-    query_part = jnp.einsum("rd,rh->dh", normed, grad_q, preferred_element_type=jnp.float32)
+    valid = (band & (key_idx >= span * rows - base)).astype(jnp.float32)
+    attended, grad_query, grad_key, grad_value = band_block(
+        queries.reshape(rows, HEADS, HSIZE),
+        extended[0].reshape(key_len, HEADS, HSIZE),
+        extended[1].reshape(key_len, HEADS, HSIZE),
+        grad_attn.reshape(rows, HEADS, HSIZE),
+        valid,
+        inv_scale,
+    )
+    attended_all = attended.reshape(rows, inner)
+    grad_q = grad_query.astype(jnp.bfloat16)
+    query_part = jnp.einsum(
+        "rd,gcr->dgc", normed, grad_q, preferred_element_type=jnp.float32
+    ).reshape(width, inner)
     out_part = jnp.einsum("rd,rh->dh", grad_out, attended_all, preferred_element_type=jnp.float32)
     early, count = scatter_rows(
         jnp.stack([query_part, out_part], axis=1),
@@ -196,23 +182,24 @@
         jnp.bfloat16,
         tail_first=True,
     )
-    grad_kv_ext = jnp.concatenate(grad_kv_cols, axis=2)
-    owned = grad_kv_ext[:, span * rows :]
+    owned = jnp.stack([grad_key[..., span * rows :], grad_value[..., span * rows :]])
     for offset in range(1, span + 1):
         lower = (span - offset) * rows
-        owned = owned + shifted(
-            grad_kv_ext[:, lower : lower + rows].astype(jnp.bfloat16), "tm", -offset
-        ).astype(jnp.float32)
+        piece = jnp.stack(
+            [grad_key[..., lower : lower + rows], grad_value[..., lower : lower + rows]]
+        )
+        owned = owned + shifted(piece.astype(jnp.bfloat16), "tm", -offset).astype(jnp.float32)
     grad_kv = owned.astype(jnp.bfloat16)
     grad_proj = jnp.concatenate([grad_q[None], grad_kv], axis=0)
+    split_weights = proj_weights.reshape(width, 3, HEADS, HSIZE)
     grad_normed = jnp.einsum(
-        "wrh,dwh->rd", grad_proj, proj_weights, preferred_element_type=jnp.float32
+        "wgcr,dwgc->rd", grad_proj, split_weights, preferred_element_type=jnp.float32
     )
     along = jnp.sum(grad_normed * normed_full, axis=-1) / width
     unscaled_input = inv_rms[:, None] * (grad_normed - normed_full * along[:, None])
     key_value_part = jnp.einsum(
-        "rd,wrh->dwh", normed, grad_kv, preferred_element_type=jnp.float32
-    )
+        "rd,wgcr->dwgc", normed, grad_kv, preferred_element_type=jnp.float32
+    ).reshape(width, 2, inner)
     late, _ = scatter_rows(key_value_part, None, ("tm", "night"), "tm", jnp.bfloat16)
     summed = jnp.concatenate([early[:, :1], late, early[:, 1:]], axis=1)
     total_count = count.astype(jnp.float32)

time: 189 us -> 177 us (0.937)
  matrix products: 32 us -> 25.4 us
  other arithmetic: 18.7 us -> 13.1 us
    unnamed x38 -> x33, local copies, waits for them, and re-layouts: 6.76 us -> 15 us
    dot_general x6, matrix products: 15 us -> 9.21 us  [the longest x1 2.98 us: shards(): jnp.einsum('wgcr,dwgc->rd', grad_proj, split_weights, preferred_element_t...]
    another operation x2, local copies, waits for them, and re-layouts: 5.37 us -> 1.05 us  [the longest x1 0.89 us: shards(): jnp.stack([grad_key[..., span * rows:], grad_value[..., span * rows:]])]
    ppermute x8, waiting for transfers between devices: 18.8 us -> 15.2 us  [shifted(): return lax.ppermute(value, axis, pairs)]
    add x1 -> x0, other arithmetic: 2.97 us -> none  [shards(): accum = accum.at[:, 0:key_len].add(update)]
    add x14, other arithmetic: 4.68 us -> 2.71 us  [halve(): keep + lax.ppermute(send.astype(send_type), axis, pairs).astype(keep.dtype)]
    slice x4 -> x3, local copies, waits for them, and re-layouts: 5.73 us -> 4.29 us  [the longest x2 2.69 us: shards(): extended[1].reshape(key_len, HEADS, HSIZE)]
  transfers between devices with their start and end apart: 27 -> 27, of which waited for: 16 -> 15; matrix products, arithmetic and copies ran while one was open for 23% -> 17% of each run, Pallas kernels for 0% -> 0%
where the time goes in v8:
time: 177 us; the launch traced here: 176 us
  starting transfers between devices  52.9 us (30%)
  waiting for transfers between devices  51.7 us (29%)
  local copies, waits for them, and re-layouts  28 us (16%)
  matrix products  25.4 us (14%)
  other arithmetic  13.1 us (7%)
  between operations  4.98 us (3%)
    ppermute x14, waiting for transfers between devices, halve(): lax.ppermute(send.astype(send_type), axis, pairs).astype(keep.dtype)  28.3 us
    ppermute x14, starting transfers between devices, halve(): lax.ppermute(send.astype(send_type), axis, pairs).astype(keep.dtype)  24.9 us
    ppermute x8, starting transfers between devices, shifted(): return lax.ppermute(value, axis, pairs)  19.6 us
    ppermute x8, waiting for transfers between devices, shifted(): return lax.ppermute(value, axis, pairs)  15.2 us
    unnamed x33, local copies, waits for them, and re-layouts  15 us
    ppermute x5, starting transfers between devices, swap_add(): return (value + lax.ppermute(value, axis, pairs), anchor)  8.48 us
    ppermute x5, waiting for transfers between devices, swap_add(): return (value + lax.ppermute(value, axis, pairs), anchor)  8.2 us
    dot_general x1, matrix products, band_block(): jnp.einsum('qgc,kgc->gqk', grad_attn, values_blk, preferred_element_type=...  3.91 us
  transfers between devices with their start and end apart: 27, of which 15 were waited for; matrix products, arithmetic and copies ran while one was open for 17% of the time, Pallas kernels for 0%

profile of v8, /device:TPU:0, one launch (start us, length us, event | category | flops | bytes accessed | tf_op | source)
XLA Modules:
  0.0 176.1 jit_solution(17579929822896601284)
XLA Ops:
  1.9 7.2 %copy.33 = bf16[1024,3,512]{0,2,1:T(8,128)(2,1)} copy(bf16[1024,3,512]{2,1,0:T(4,128)(2,1)} %bitcast.191) | data formatting | bytes 6291456
  9.1 3.1 %fusion.23 = bf16[3,256,512]{2,1,0:T(8,128)(2,1)S(1)} fusion(bf16[1024,3,512]{0,2,1:T(8,128)(2,1)} %copy.33, bf16[1,256,1024]{2,1,0:T(8,128)(2,1)S(1)} %copy-done.2, f32[256]{0:T(256)S(1)} %add_rsqrt_fusion), kind=kOutput, calls=%fused_computation.37 | convolution fusion | flops 806486016 | bytes 4457472 | tf_op jit(solution)/shard_map/rd,dwh->wrh/dot_general | solution.py:143
  12.2 5.8 %collective-permute-start = (bf16[2,256,512]{2,1,0:T(8,128)(2,1)S(1)}, bf16[2,256,512]{2,1,0:T(8,128)(2,1)}, u32[]{:S(2)}, u32[]{:S(2)}) collective-permute-start(bf16[2,256,512]{2,1,0:T(8,128)(2,1)S(1)} %slice.96), channel_id=1, source_target_pairs={{0,16},{4,20},{8,24},{12,28},{1,17},{5,21},{9,25},{13,29},{2,18},{... | collective-permute-start | bytes 1572872 | tf_op jit(solution)/shard_map/ppermute | solution.py:16
  18.1 3.4 %collective-permute-start.1 = (bf16[2,256,512]{2,1,0:T(8,128)(2,1)S(1)}, bf16[2,256,512]{2,1,0:T(8,128)(2,1)}, u32[]{:S(2)}, u32[]{:S(2)}) collective-permute-start(bf16[2,256,512]{2,1,0:T(8,128)(2,1)S(1)} %slice.96), channel_id=1, source_target_pairs={{0,12},{4,16},{8,20},{12,24},{16,28},{1,13},{5,17},{9,21},{13,25},... | collective-permute-start | bytes 1572872 | tf_op jit(solution)/shard_map/ppermute | solution.py:16
  21.4 3.0 %collective-permute-start.2 = (bf16[2,256,512]{2,1,0:T(8,128)(2,1)S(1)}, bf16[2,256,512]{2,1,0:T(8,128)(2,1)}, u32[]{:S(2)}, u32[]{:S(2)}) collective-permute-start(bf16[2,256,512]{2,1,0:T(8,128)(2,1)S(1)} %slice.96), channel_id=1, source_target_pairs={{0,8},{4,12},{8,16},{12,20},{16,24},{20,28},{1,9},{5,13},{9,17},{1... | collective-permute-start | bytes 1572872 | tf_op jit(solution)/shard_map/ppermute | solution.py:16
  26.5 3.5 %slice.78 = bf16[1024,1,512]{2,1,0:T(2,128)(2,1)} slice(bf16[1024,4,512]{2,1,0:T(4,128)(2,1)S(1)} %copy-done), slice={[0:1024], [3:4], [0:512]} | slice | bytes 2097152 | tf_op jit(solution)/shard_map/slice | solution.py:154
  37.2 14.9 %collective-permute-done = bf16[2,256,512]{2,1,0:T(8,128)(2,1)} collective-permute-done((bf16[2,256,512]{2,1,0:T(8,128)(2,1)S(1)}, bf16[2,256,512]{2,1,0:T(8,128)(2,1)}, u32[]{:S(2)}, u32[]{:S(2)}) %collective-permute-start) | collective-permute-done | bytes 524320 | tf_op jit(solution)/shard_map/ppermute | solution.py:16
  60.7 3.9 %fusion.1 = (f32[8,256]{1,0:T(8,128)S(1)}, f32[8,256,1280]{2,1,0:T(8,128)S(1)}) fusion(f32[256,1280]{1,0:T(8,128)} %fusion.22, bf16[256,8,64]{0,2,1:T(8,128)(2,1)S(1)} %bitcast.192, bf16[1280,8,64]{0,2,1:T(8,128)(2,1)S(1)} %bitcast.189), kind=kOutput, calls=%fused_computation.3 | convolution fusion | flops 343406592 | bytes 13377536 | tf_op jit(solution)/shard_map/qgc,kgc->gqk/dot_general | solution.py:102
  64.7 2.8 %multiply_reduce_fusion = (f32[256,8]{0,1:T(8,128)S(1)}, bf16[8,64,256]{2,1,0:T(8,128)(2,1)S(1)}) fusion(bf16[256,512]{0,1:T(8,128)(2,1)S(1)} %copy-done.11, bf16[1280,8,64]{0,2,1:T(8,128)(2,1)S(1)} %bitcast.200, f32[8,256]{1,0:T(8,128)S(1)} %get-tuple-element.42, f32[256,1280]{1,0:T(8,128)S(1)} %copy-done.1, f32[8,256,1280]{2,1,0:T(8,128)S(1)} %get-tuple-element.43), kind=kOutput, calls=%fused_computation.79 | convolution fusion | flops 346683392 | bytes 13647872 | tf_op jit(solution)/shard_map/gqk,kgc->qgc/dot_general | solution.py:108
  67.4 3.9 %multiply_convert_fusion = bf16[8,256,1280]{2,1,0:T(8,128)(2,1)S(1)} fusion(bf16[256,8,64]{0,2,1:T(8,128)(2,1)S(1)} %bitcast.204, bf16[1280,8,64]{0,2,1:T(8,128)(2,1)S(1)} %bitcast.201, f32[8,256]{1,0:T(8,128)S(1)} %bitcast.207, f32[8,256]{1,0:T(8,128)S(1)} %get-tuple-element.42, f32[256,1280]{1,0:T(8,128)S(1)} %copy-done.1, ...), kind=kOutput, calls=%fused_computation | convolution fusion | flops 353894400 | bytes 18628608 | tf_op jit(solution)/shard_map/qgc,kgc->gqk/dot_general | solution.py:112
  75.4 3.6 %collective-permute-start.4 = (f32[2,2,2,2,32,2,512]{6,4,5,3,2,1,0:T(8,128)S(1)}, f32[2,2,2,2,32,2,512]{6,4,5,3,2,1,0:T(8,128)S(1)}, u32[]{:S(2)}, u32[]{:S(2)}) collective-permute-start(f32[2,2,2,2,32,2,512]{6,4,5,3,2,1,0:T(8,128)S(1)} %bitcast.197), channel_id=1, source_target_pairs={{0,4},{4,0},{8,12},{12,8},{16,20},{20,16},{24,28},{28,24},{1,5},{5... | collective-permute-start | bytes 6291464 | tf_op jit(solution)/shard_map/ppermute | solution.py:29
  97.9 4.4 %collective-permute-done.6 = bf16[2,2,2,32,2,512]{5,3,4,2,1,0:T(8,128)(2,1)} collective-permute-done((bf16[2,2,2,32,2,512]{5,3,4,2,1,0:T(8,128)(2,1)}, bf16[2,2,2,32,2,512]{5,3,4,2,1,0:T(8,128)(2,1)}, u32[]{:S(2)}, u32[]{:S(2)}) %collective-permute-start.6) | collective-permute-done | bytes 524320 | tf_op jit(solution)/shard_map/ppermute | solution.py:29
  104.6 2.7 %collective-permute-start.8 = (bf16[2,2,32,2,512]{4,2,3,1,0:T(8,128)(2,1)S(1)}, bf16[2,2,32,2,512]{4,2,3,1,0:T(8,128)(2,1)S(1)}, u32[]{:S(2)}, u32[]{:S(2)}) collective-permute-start(bf16[2,2,32,2,512]{4,2,3,1,0:T(8,128)(2,1)S(1)} %fusion.44), channel_id=1, source_target_pairs={{0,2},{1,3},{2,0},{3,1},{4,6},{5,7},{6,4},{7,5},{8,10},{9,11},{10,... | collective-permute-start | bytes 786440 | tf_op jit(solution)/shard_map/ppermute | solution.py:29
  109.5 2.7 %collective-permute-start.7 = (s32[]{:T(128)}, s32[]{:T(128)}, u32[]{:S(2)}, u32[]{:S(2)}) collective-permute-start(s32[]{:T(128)} %add.187), channel_id=1, source_target_pairs={{0,1},{1,0},{2,3},{3,2},{4,5},{5,4},{6,7},{7,6},{8,9},{9,8},{10,11... | collective-permute-start | bytes 20 | tf_op jit(solution)/shard_map/ppermute | solution.py:36
  113.8 4.8 %collective-permute-done.8 = bf16[2,2,32,2,512]{4,2,3,1,0:T(8,128)(2,1)S(1)} collective-permute-done((bf16[2,2,32,2,512]{4,2,3,1,0:T(8,128)(2,1)S(1)}, bf16[2,2,32,2,512]{4,2,3,1,0:T(8,128)(2,1)S(1)}, u32[]{:S(2)}, u32[]{:S(2)}) %collective-permute-start.8) | collective-permute-done | bytes 262176 | tf_op jit(solution)/shard_map/ppermute | solution.py:29
  118.7 5.3 %collective-permute-start.10 = (bf16[2,32,2,256]{3,1,2,0:T(8,128)(2,1)S(1)}, bf16[2,32,2,256]{3,1,2,0:T(8,128)(2,1)S(1)}, u32[]{:S(2)}, u32[]{:S(2)}) collective-permute-start(bf16[2,32,2,256]{3,1,2,0:T(8,128)(2,1)S(1)} %fusion.59), channel_id=1, source_target_pairs={{0,16},{4,20},{8,24},{12,28},{16,0},{20,4},{24,8},{28,12},{1,17},{... | collective-permute-start | bytes 196616 | tf_op jit(solution)/shard_map/ppermute | solution.py:29
  124.0 3.0 %fusion.27 = (f32[256]{0:T(256)S(1)}, f32[256,1024]{1,0:T(8,128)S(1)}) fusion(bf16[1,256,1024]{2,1,0:T(8,128)(2,1)S(1)} %copy-done.2, f32[256]{0:T(256)S(1)} %add_rsqrt_fusion, bf16[1024,3,8,64]{0,3,2,1:T(8,128)(2,1)} %bitcast.194, bf16[2,8,64,256]{3,2,1,0:T(8,128)(2,1)S(1)} %fusion.37, bf16[1,8,64,256]{3,2,1,0:T(8,128)(2,1)S(1)} %bitcast.203), kind=kOutput, calls=%fused_computation.41 | convolution fusion | flops 806747904 | bytes 5507072 | tf_op jit(solution)/shard_map/wgcr,dwgc->rd/dot_general | solution.py:195
  128.3 3.1 %collective-permute-done.9 = s32[]{:T(128)} collective-permute-done((s32[]{:T(128)}, s32[]{:T(128)}, u32[]{:S(2)}, u32[]{:S(2)}) %collective-permute-start.9) | collective-permute-done | bytes 36 | tf_op jit(solution)/shard_map/ppermute | solution.py:36
  136.6 3.1 %collective-permute-start.13 = (s32[]{:T(128)}, s32[]{:T(128)}, u32[]{:S(2)}, u32[]{:S(2)}) collective-permute-start(s32[]{:T(128)} %add.202), channel_id=1, source_target_pairs={{0,8},{4,12},{8,0},{12,4},{16,24},{20,28},{24,16},{28,20},{1,9},{5... | collective-permute-start | bytes 20 | tf_op jit(solution)/shard_map/ppermute | solution.py:36
  152.3 4.8 %collective-permute-done.21 = bf16[2,2,2,32,2,256]{5,3,4,2,1,0:T(8,128)(2,1)S(1)} collective-permute-done((bf16[2,2,2,32,2,256]{5,3,4,2,1,0:T(8,128)(2,1)S(1)}, bf16[2,2,2,32,2,256]{5,3,4,2,1,0:T(8,128)(2,1)S(1)}, u32[]{:S(2)}, u32[]{:S(2)}) %collective-permute-start.21) | collective-permute-done | bytes 262176 | tf_op jit(solution)/shard_map/ppermute | solution.py:29
  159.4 2.8 %collective-permute-done.22 = bf16[2,2,32,2,256]{4,2,3,1,0:T(8,128)(2,1)S(1)} collective-permute-done((bf16[2,2,32,2,256]{4,2,3,1,0:T(8,128)(2,1)S(1)}, bf16[2,2,32,2,256]{4,2,3,1,0:T(8,128)(2,1)S(1)}, u32[]{:S(2)}, u32[]{:S(2)}) %collective-permute-start.22) | collective-permute-done | bytes 131104 | tf_op jit(solution)/shard_map/ppermute | solution.py:29
  165.4 3.8 %collective-permute-done.25 = bf16[2,32,2,512]{3,1,2,0:T(8,128)(2,1)S(1)} collective-permute-done((bf16[2,32,2,512]{3,1,2,0:T(8,128)(2,1)S(1)}, bf16[2,32,2,512]{3,1,2,0:T(8,128)(2,1)S(1)}, u32[]{:S(2)}, u32[]{:S(2)}) %collective-permute-start.25) | collective-permute-done | bytes 131104 | tf_op jit(solution)/shard_map/ppermute | solution.py:29
  169.3 2.4 %collective-permute-start.26 = (bf16[32,2,512]{2,0,1:T(8,128)(2,1)S(1)}, bf16[32,2,512]{2,0,1:T(8,128)(2,1)S(1)}, u32[]{:S(2)}, u32[]{:S(2)}) collective-permute-start(bf16[32,2,512]{2,0,1:T(8,128)(2,1)S(1)} %fusion.61), channel_id=1, source_target_pairs={{0,2},{1,3},{2,0},{3,1},{4,6},{5,7},{6,4},{7,5},{8,10},{9,11},{10,... | collective-permute-start | bytes 196616 | tf_op jit(solution)/shard_map/ppermute | solution.py:29
  171.7 3.5 %collective-permute-done.26 = bf16[32,2,512]{2,0,1:T(8,128)(2,1)S(1)} collective-permute-done((bf16[32,2,512]{2,0,1:T(8,128)(2,1)S(1)}, bf16[32,2,512]{2,0,1:T(8,128)(2,1)S(1)}, u32[]{:S(2)}, u32[]{:S(2)}) %collective-permute-start.26) | collective-permute-done | bytes 65568 | tf_op jit(solution)/shard_map/ppermute | solution.py:29
  (136 shorter events, 69.9 us)
Async XLA Ops:
  12.2 39.8 %collective-permute-start = (bf16[2,256,512]{2,1,0:T(8,128)(2,1)S(1)}, bf16[2,256,512]{2,1,0:T(8,128)(2,1)}, u32[]{:S(2)}, u32[]{:S(2)}) collective-permute-start(bf16[2,256,512]{2,1,0:T(8,128)(2,1)S(1)} %slice.96), channel_id=1, source_target_pairs={{0,16},{4,20},{8,24},{12,28},{1,17},{5,21},{9,25},{13,29},{2,18},{... | collective-permute-start | bytes 1572872 | tf_op jit(solution)/shard_map/ppermute | solution.py:16
  18.1 35.1 %collective-permute-start.1 = (bf16[2,256,512]{2,1,0:T(8,128)(2,1)S(1)}, bf16[2,256,512]{2,1,0:T(8,128)(2,1)}, u32[]{:S(2)}, u32[]{:S(2)}) collective-permute-start(bf16[2,256,512]{2,1,0:T(8,128)(2,1)S(1)} %slice.96), channel_id=1, source_target_pairs={{0,12},{4,16},{8,20},{12,24},{16,28},{1,13},{5,17},{9,21},{13,25},... | collective-permute-start | bytes 1572872 | tf_op jit(solution)/shard_map/ppermute | solution.py:16
  21.4 32.8 %collective-permute-start.2 = (bf16[2,256,512]{2,1,0:T(8,128)(2,1)S(1)}, bf16[2,256,512]{2,1,0:T(8,128)(2,1)}, u32[]{:S(2)}, u32[]{:S(2)}) collective-permute-start(bf16[2,256,512]{2,1,0:T(8,128)(2,1)S(1)} %slice.96), channel_id=1, source_target_pairs={{0,8},{4,12},{8,16},{12,20},{16,24},{20,28},{1,9},{5,13},{9,17},{1... | collective-permute-start | bytes 1572872 | tf_op jit(solution)/shard_map/ppermute | solution.py:16
  24.4 30.9 %collective-permute-start.3 = (bf16[2,256,512]{2,1,0:T(8,128)(2,1)S(1)}, bf16[2,256,512]{2,1,0:T(8,128)(2,1)}, u32[]{:S(2)}, u32[]{:S(2)}) collective-permute-start(bf16[2,256,512]{2,1,0:T(8,128)(2,1)S(1)} %slice.96), channel_id=1, source_target_pairs={{0,4},{4,8},{8,12},{12,16},{16,20},{20,24},{24,28},{1,5},{5,9},{9,... | collective-permute-start | bytes 1572872 | tf_op jit(solution)/shard_map/ppermute | solution.py:16
  75.4 11.3 %collective-permute-start.4 = (f32[2,2,2,2,32,2,512]{6,4,5,3,2,1,0:T(8,128)S(1)}, f32[2,2,2,2,32,2,512]{6,4,5,3,2,1,0:T(8,128)S(1)}, u32[]{:S(2)}, u32[]{:S(2)}) collective-permute-start(f32[2,2,2,2,32,2,512]{6,4,5,3,2,1,0:T(8,128)S(1)} %bitcast.197), channel_id=1, source_target_pairs={{0,4},{4,0},{8,12},{12,8},{16,20},{20,16},{24,28},{28,24},{1,5},{5... | collective-permute-start | bytes 6291464 | tf_op jit(solution)/shard_map/ppermute | solution.py:29
  83.4 23.9 %collective-permute-start.17 = (bf16[2,8,64,256]{3,2,1,0:T(8,128)(2,1)}, bf16[2,8,64,256]{3,2,1,0:T(8,128)(2,1)}, u32[]{:S(2)}, u32[]{:S(2)}) collective-permute-start(bf16[2,8,64,256]{3,2,1,0:T(8,128)(2,1)} %pad_maximum_fusion.4), channel_id=1, source_target_pairs={{16,0},{20,4},{24,8},{28,12},{17,1},{21,5},{25,9},{29,13},{18,2},{... | collective-permute-start | bytes 1572872 | tf_op jit(solution)/shard_map/ppermute | solution.py:16
  85.5 21.7 %collective-permute-start.16 = (bf16[2,8,64,256]{3,2,1,0:T(8,128)(2,1)}, bf16[2,8,64,256]{3,2,1,0:T(8,128)(2,1)}, u32[]{:S(2)}, u32[]{:S(2)}) collective-permute-start(bf16[2,8,64,256]{3,2,1,0:T(8,128)(2,1)} %pad_maximum_fusion.3), channel_id=1, source_target_pairs={{12,0},{16,4},{20,8},{24,12},{28,16},{13,1},{17,5},{21,9},{25,13},... | collective-permute-start | bytes 1572872 | tf_op jit(solution)/shard_map/ppermute | solution.py:16
  88.2 14.2 %collective-permute-start.6 = (bf16[2,2,2,32,2,512]{5,3,4,2,1,0:T(8,128)(2,1)}, bf16[2,2,2,32,2,512]{5,3,4,2,1,0:T(8,128)(2,1)}, u32[]{:S(2)}, u32[]{:S(2)}) collective-permute-start(bf16[2,2,2,32,2,512]{5,3,4,2,1,0:T(8,128)(2,1)} %fusion.39), channel_id=1, source_target_pairs={{0,1},{1,0},{2,3},{3,2},{4,5},{5,4},{6,7},{7,6},{8,9},{9,8},{10,11... | collective-permute-start | bytes 1572872 | tf_op jit(solution)/shard_map/ppermute | solution.py:29
  90.6 16.9 %collective-permute-start.15 = (bf16[2,8,64,256]{3,2,1,0:T(8,128)(2,1)}, bf16[2,8,64,256]{3,2,1,0:T(8,128)(2,1)}, u32[]{:S(2)}, u32[]{:S(2)}) collective-permute-start(bf16[2,8,64,256]{3,2,1,0:T(8,128)(2,1)} %pad_maximum_fusion.2), channel_id=1, source_target_pairs={{8,0},{12,4},{16,8},{20,12},{24,16},{28,20},{9,1},{13,5},{17,9},{2... | collective-permute-start | bytes 1572872 | tf_op jit(solution)/shard_map/ppermute | solution.py:16
  94.3 13.3 %collective-permute-start.14 = (bf16[2,8,64,256]{3,2,1,0:T(8,128)(2,1)}, bf16[2,8,64,256]{3,2,1,0:T(8,128)(2,1)}, u32[]{:S(2)}, u32[]{:S(2)}) collective-permute-start(bf16[2,8,64,256]{3,2,1,0:T(8,128)(2,1)} %pad_maximum_fusion.1), channel_id=1, source_target_pairs={{4,0},{8,4},{12,8},{16,12},{20,16},{24,20},{28,24},{5,1},{9,5},{13... | collective-permute-start | bytes 1572872 | tf_op jit(solution)/shard_map/ppermute | solution.py:16
  104.6 14.0 %collective-permute-start.8 = (bf16[2,2,32,2,512]{4,2,3,1,0:T(8,128)(2,1)S(1)}, bf16[2,2,32,2,512]{4,2,3,1,0:T(8,128)(2,1)S(1)}, u32[]{:S(2)}, u32[]{:S(2)}) collective-permute-start(bf16[2,2,32,2,512]{4,2,3,1,0:T(8,128)(2,1)S(1)} %fusion.44), channel_id=1, source_target_pairs={{0,2},{1,3},{2,0},{3,1},{4,6},{5,7},{6,4},{7,5},{8,10},{9,11},{10,... | collective-permute-start | bytes 786440 | tf_op jit(solution)/shard_map/ppermute | solution.py:29
  109.5 3.7 %collective-permute-start.7 = (s32[]{:T(128)}, s32[]{:T(128)}, u32[]{:S(2)}, u32[]{:S(2)}) collective-permute-start(s32[]{:T(128)} %add.187), channel_id=1, source_target_pairs={{0,1},{1,0},{2,3},{3,2},{4,5},{5,4},{6,7},{7,6},{8,9},{9,8},{10,11... | collective-permute-start | bytes 20 | tf_op jit(solution)/shard_map/ppermute | solution.py:36
  118.7 13.3 %collective-permute-start.10 = (bf16[2,32,2,256]{3,1,2,0:T(8,128)(2,1)S(1)}, bf16[2,32,2,256]{3,1,2,0:T(8,128)(2,1)S(1)}, u32[]{:S(2)}, u32[]{:S(2)}) collective-permute-start(bf16[2,32,2,256]{3,1,2,0:T(8,128)(2,1)S(1)} %fusion.59), channel_id=1, source_target_pairs={{0,16},{4,20},{8,24},{12,28},{16,0},{20,4},{24,8},{28,12},{1,17},{... | collective-permute-start | bytes 196616 | tf_op jit(solution)/shard_map/ppermute | solution.py:29
  126.9 4.5 %collective-permute-start.9 = (s32[]{:T(128)}, s32[]{:T(128)}, u32[]{:S(2)}, u32[]{:S(2)}) collective-permute-start(s32[]{:T(128)} %add.192), channel_id=1, source_target_pairs={{0,2},{1,3},{2,0},{3,1},{4,6},{5,7},{6,4},{7,5},{8,10},{9,11},{10,... | collective-permute-start | bytes 20 | tf_op jit(solution)/shard_map/ppermute | solution.py:36
  132.1 4.5 %collective-permute-start.12 = (bf16[32,2,256]{2,0,1:T(8,128)(2,1)S(1)}, bf16[32,2,256]{2,0,1:T(8,128)(2,1)S(1)}, u32[]{:S(2)}, u32[]{:S(2)}) collective-permute-start(bf16[32,2,256]{2,0,1:T(8,128)(2,1)S(1)} %fusion.63), channel_id=1, source_target_pairs={{0,8},{4,12},{8,0},{12,4},{16,24},{20,28},{24,16},{28,20},{1,9},{5... | collective-permute-start | bytes 98312 | tf_op jit(solution)/shard_map/ppermute | solution.py:29
  143.2 4.2 %collective-permute-start.20 = (f32[2,2,2,2,32,2,512]{6,4,5,3,2,1,0:T(8,128)S(1)}, f32[2,2,2,2,32,2,512]{6,4,5,3,2,1,0:T(8,128)S(1)}, u32[]{:S(2)}, u32[]{:S(2)}) collective-permute-start(f32[2,2,2,2,32,2,512]{6,4,5,3,2,1,0:T(8,128)S(1)} %dynamic-slice_bitcast_fusion), channel_id=1, source_target_pairs={{0,4},{4,0},{8,12},{12,8},{16,20},{20,16},{24,28},{28,24},{1,5},{5... | collective-permute-start | bytes 6291464 | tf_op jit(solution)/shard_map/ppermute | solution.py:29
  143.3 5.1 %collective-permute-start.18 = (bf16[2,32,2,256]{3,1,2,0:T(8,128)(2,1)S(1)}, bf16[2,32,2,256]{3,1,2,0:T(8,128)(2,1)S(1)}, u32[]{:S(2)}, u32[]{:S(2)}) collective-permute-start(bf16[2,32,2,256]{3,1,2,0:T(8,128)(2,1)S(1)} %fusion.60), channel_id=1, source_target_pairs={{0,8},{4,12},{8,0},{12,4},{16,24},{20,28},{24,16},{28,20},{1,9},{5... | collective-permute-start | bytes 196616 | tf_op jit(solution)/shard_map/ppermute | solution.py:29
  148.3 8.8 %collective-permute-start.21 = (bf16[2,2,2,32,2,256]{5,3,4,2,1,0:T(8,128)(2,1)S(1)}, bf16[2,2,2,32,2,256]{5,3,4,2,1,0:T(8,128)(2,1)S(1)}, u32[]{:S(2)}, u32[]{:S(2)}) collective-permute-start(bf16[2,2,2,32,2,256]{5,3,4,2,1,0:T(8,128)(2,1)S(1)} %fusion.45), channel_id=1, source_target_pairs={{0,16},{4,20},{8,24},{12,28},{16,0},{20,4},{24,8},{28,12},{1,17},{... | collective-permute-start | bytes 786440 | tf_op jit(solution)/shard_map/ppermute | solution.py:29
  148.5 16.9 %collective-permute-start.19 = (bf16[32,2,256]{2,0,1:T(8,128)(2,1)S(1)}, bf16[32,2,256]{2,0,1:T(8,128)(2,1)S(1)}, u32[]{:S(2)}, u32[]{:S(2)}) collective-permute-start(bf16[32,2,256]{2,0,1:T(8,128)(2,1)S(1)} %fusion.64), channel_id=1, source_target_pairs={{0,16},{4,20},{8,24},{12,28},{16,0},{20,4},{24,8},{28,12},{1,17},{... | collective-permute-start | bytes 98312 | tf_op jit(solution)/shard_map/ppermute | solution.py:29
  150.6 8.4 %collective-permute-start.23 = (bf16[2,2,2,32,2,256]{5,3,4,2,1,0:T(8,128)(2,1)S(1)}, bf16[2,2,2,32,2,256]{5,3,4,2,1,0:T(8,128)(2,1)S(1)}, u32[]{:S(2)}, u32[]{:S(2)}) collective-permute-start(bf16[2,2,2,32,2,256]{5,3,4,2,1,0:T(8,128)(2,1)S(1)} %fusion.46), channel_id=1, source_target_pairs={{0,8},{4,12},{8,0},{12,4},{16,24},{20,28},{24,16},{28,20},{1,9},{5... | collective-permute-start | bytes 786440 | tf_op jit(solution)/shard_map/ppermute | solution.py:29
  157.2 5.0 %collective-permute-start.22 = (bf16[2,2,32,2,256]{4,2,3,1,0:T(8,128)(2,1)S(1)}, bf16[2,2,32,2,256]{4,2,3,1,0:T(8,128)(2,1)S(1)}, u32[]{:S(2)}, u32[]{:S(2)}) collective-permute-start(bf16[2,2,32,2,256]{4,2,3,1,0:T(8,128)(2,1)S(1)} %fusion.56), channel_id=1, source_target_pairs={{0,8},{4,12},{8,0},{12,4},{16,24},{20,28},{24,16},{28,20},{1,9},{5... | collective-permute-start | bytes 393224 | tf_op jit(solution)/shard_map/ppermute | solution.py:29
  159.1 5.0 %collective-permute-start.24 = (bf16[2,2,32,2,256]{4,2,3,1,0:T(8,128)(2,1)S(1)}, bf16[2,2,32,2,256]{4,2,3,1,0:T(8,128)(2,1)S(1)}, u32[]{:S(2)}, u32[]{:S(2)}) collective-permute-start(bf16[2,2,32,2,256]{4,2,3,1,0:T(8,128)(2,1)S(1)} %fusion.57), channel_id=1, source_target_pairs={{0,16},{4,20},{8,24},{12,28},{16,0},{20,4},{24,8},{28,12},{1,17},{... | collective-permute-start | bytes 393224 | tf_op jit(solution)/shard_map/ppermute | solution.py:29
  164.2 5.0 %collective-permute-start.25 = (bf16[2,32,2,512]{3,1,2,0:T(8,128)(2,1)S(1)}, bf16[2,32,2,512]{3,1,2,0:T(8,128)(2,1)S(1)}, u32[]{:S(2)}, u32[]{:S(2)}) collective-permute-start(bf16[2,32,2,512]{3,1,2,0:T(8,128)(2,1)S(1)} %fusion.58), channel_id=1, source_target_pairs={{0,1},{1,0},{2,3},{3,2},{4,5},{5,4},{6,7},{7,6},{8,9},{9,8},{10,11... | collective-permute-start | bytes 393224 | tf_op jit(solution)/shard_map/ppermute | solution.py:29
  169.3 5.9 %collective-permute-start.26 = (bf16[32,2,512]{2,0,1:T(8,128)(2,1)S(1)}, bf16[32,2,512]{2,0,1:T(8,128)(2,1)S(1)}, u32[]{:S(2)}, u32[]{:S(2)}) collective-permute-start(bf16[32,2,512]{2,0,1:T(8,128)(2,1)S(1)} %fusion.61), channel_id=1, source_target_pairs={{0,2},{1,3},{2,0},{3,1},{4,6},{5,7},{6,4},{7,5},{8,10},{9,11},{10,... | collective-permute-start | bytes 196616 | tf_op jit(solution)/shard_map/ppermute | solution.py:29
  (16 other events, 108.9 us)

commit v9 on v8

--- a/solution.py
+++ b/solution.py
@@ -139,21 +139,20 @@
     inv_rms = lax.rsqrt(jnp.mean(local_in * local_in, axis=-1) + 1e-06)
     normed_full = local_in * inv_rms[:, None]
     normed = normed_full.astype(jnp.bfloat16)
-    proj_weights = weights[:, :3, :]
     projected = jnp.einsum(
-        "rd,dwh->wrh", normed, proj_weights, preferred_element_type=jnp.float32
+        "rd,dwh->wrh", normed, weights, preferred_element_type=jnp.float32
     ).astype(jnp.bfloat16)
     queries = projected[0]
-    key_vals = projected[1:]
+    key_vals = projected[1:3]
     earlier = [shifted(key_vals, "tm", offset) for offset in range(span, 0, -1)]
     extended = jnp.concatenate(earlier + [key_vals], axis=1)
     local_count = jnp.sum(loss_mask.astype(jnp.int32))
     tokens_all = rows * lax.axis_size("tm") * lax.axis_size("night")
     local_cot = cotangent[0]
     grad_out = jnp.where(loss_mask[0][:, None] > 0, local_cot, jnp.zeros_like(local_cot))
-    grad_attn = jnp.dot(grad_out, weights[:, 3, :], preferred_element_type=jnp.float32).astype(
-        jnp.bfloat16
-    )
+    grad_attn = jnp.einsum(
+        "rd,dwh->wrh", grad_out, weights, preferred_element_type=jnp.float32
+    )[3].astype(jnp.bfloat16)
     base = lax.axis_index("tm") * rows
     query_idx = jnp.arange(block_rows, dtype=jnp.int32)[:, None]
     key_idx = jnp.arange(key_len, dtype=jnp.int32)[None, :]
@@ -190,15 +189,15 @@
         )
         owned = owned + shifted(piece.astype(jnp.bfloat16), "tm", -offset).astype(jnp.float32)
     grad_kv = owned.astype(jnp.bfloat16)
-    grad_proj = jnp.concatenate([grad_q[None], grad_kv], axis=0)
-    split_weights = proj_weights.reshape(width, 3, HEADS, HSIZE)
+    grad_proj = jnp.concatenate([grad_q[None], grad_kv, jnp.zeros_like(grad_q)[None]], axis=0)
+    split_weights = weights.reshape(width, weights.shape[1], HEADS, HSIZE)
     grad_normed = jnp.einsum(
         "wgcr,dwgc->rd", grad_proj, split_weights, preferred_element_type=jnp.float32
     )
     along = jnp.sum(grad_normed * normed_full, axis=-1) / width
     unscaled_input = inv_rms[:, None] * (grad_normed - normed_full * along[:, None])
     key_value_part = jnp.einsum(
-        "rd,wgcr->dwgc", normed, grad_kv, preferred_element_type=jnp.float32
+        "rd,wgcr->dwgc", normed, grad_proj[1:3], preferred_element_type=jnp.float32
     ).reshape(width, 2, inner)
     late, _ = scatter_rows(key_value_part, None, ("tm", "night"), "tm", jnp.bfloat16)
     summed = jnp.concatenate([early[:, :1], late, early[:, 1:]], axis=1)

time: 177 us -> 180 us (1.017)
  matrix products: 25.4 us -> 29 us
    dot_general x3, matrix products: 5.87 us -> 8.82 us  [the longest x1 4.49 us: shards(): jnp.einsum('rd,dwh->wrh', grad_out, weights, preferred_element_type=jnp.f...]
    slice x2 -> x4, local copies, waits for them, and re-layouts: 3.55 us -> 1.67 us  [the longest x3 0.85 us: shards(): jnp.einsum('rd,dwh->wrh', grad_out, weights, preferred_element_type=jnp.f...]
where the time goes in v9:
time: 180 us; the launch traced here: 179 us
  starting transfers between devices  52.4 us (29%)
  waiting for transfers between devices  52 us (29%)
  matrix products  29 us (16%)
  local copies, waits for them, and re-layouts  26.3 us (15%)
  other arithmetic  13.9 us (8%)
  between operations  5.25 us (3%)
    ppermute x14, waiting for transfers between devices, halve(): lax.ppermute(send.astype(send_type), axis, pairs).astype(keep.dtype)  28.5 us
    ppermute x14, starting transfers between devices, halve(): lax.ppermute(send.astype(send_type), axis, pairs).astype(keep.dtype)  24.5 us
    ppermute x8, starting transfers between devices, shifted(): return lax.ppermute(value, axis, pairs)  19.5 us
    unnamed x33, local copies, waits for them, and re-layouts  15.8 us
    ppermute x8, waiting for transfers between devices, shifted(): return lax.ppermute(value, axis, pairs)  15.2 us
    ppermute x5, starting transfers between devices, swap_add(): return (value + lax.ppermute(value, axis, pairs), anchor)  8.41 us
    ppermute x5, waiting for transfers between devices, swap_add(): return (value + lax.ppermute(value, axis, pairs), anchor)  8.27 us
    dot_general x1, matrix products, shards(): jnp.einsum('rd,dwh->wrh', grad_out, weights, preferred_element_type=jnp.f...  4.49 us
  transfers between devices with their start and end apart: 27, of which 15 were waited for; matrix products, arithmetic and copies ran while one was open for 17% of the time, Pallas kernels for 0%

profile of v9, /device:TPU:0, one launch (start us, length us, event | category | flops | bytes accessed | tf_op | source)
XLA Modules:
  0.0 178.8 jit_solution(3264968590801976313)
XLA Ops:
  1.9 7.6 %copy.34 = bf16[1024,4,512]{0,2,1:T(8,128)(2,1)} copy(bf16[1024,4,512]{2,1,0:T(4,128)(2,1)} %param.5) | data formatting | bytes 8388608 | tf_op args[1]
  9.5 3.6 %fusion.13 = bf16[4,256,512]{2,1,0:T(8,128)(2,1)S(1)} fusion(bf16[1024,4,512]{0,2,1:T(8,128)(2,1)} %copy.34, bf16[1,256,1024]{2,1,0:T(8,128)(2,1)S(1)} %copy-done.1, f32[256]{0:T(256)S(1)} %add_rsqrt_fusion), kind=kOutput, calls=%fused_computation.25 | convolution fusion | flops 1075052544 | bytes 5768192 | tf_op jit(solution)/shard_map/rd,dwh->wrh/dot_general | solution.py:142
  13.9 5.7 %collective-permute-start = (bf16[2,256,512]{2,1,0:T(8,128)(2,1)}, bf16[2,256,512]{2,1,0:T(8,128)(2,1)}, u32[]{:S(2)}, u32[]{:S(2)}) collective-permute-start(bf16[2,256,512]{2,1,0:T(8,128)(2,1)} %slice.93), channel_id=1, source_target_pairs={{0,16},{4,20},{8,24},{12,28},{1,17},{5,21},{9,25},{13,29},{2,18},{... | collective-permute-start | bytes 1572872 | tf_op jit(solution)/shard_map/ppermute | solution.py:16
  19.6 3.4 %collective-permute-start.1 = (bf16[2,256,512]{2,1,0:T(8,128)(2,1)}, bf16[2,256,512]{2,1,0:T(8,128)(2,1)}, u32[]{:S(2)}, u32[]{:S(2)}) collective-permute-start(bf16[2,256,512]{2,1,0:T(8,128)(2,1)} %slice.93), channel_id=1, source_target_pairs={{0,12},{4,16},{8,20},{12,24},{16,28},{1,13},{5,17},{9,21},{13,25},... | collective-permute-start | bytes 1572872 | tf_op jit(solution)/shard_map/ppermute | solution.py:16
  23.0 3.0 %collective-permute-start.2 = (bf16[2,256,512]{2,1,0:T(8,128)(2,1)}, bf16[2,256,512]{2,1,0:T(8,128)(2,1)}, u32[]{:S(2)}, u32[]{:S(2)}) collective-permute-start(bf16[2,256,512]{2,1,0:T(8,128)(2,1)} %slice.93), channel_id=1, source_target_pairs={{0,8},{4,12},{8,16},{12,20},{16,24},{20,28},{1,9},{5,13},{9,17},{1... | collective-permute-start | bytes 1572872 | tf_op jit(solution)/shard_map/ppermute | solution.py:16
  29.3 4.5 %fusion.14 = bf16[4,256,512]{2,1,0:T(8,128)(2,1)} fusion(bf16[1024,4,512]{0,2,1:T(8,128)(2,1)} %copy.34, bf16[1,256,1024]{2,1,0:T(8,128)(2,1)S(1)} %copy-done.10, pred[256]{0:T(512)(128)(4,1)S(1)} %compare_reduce_fusion), kind=kOutput, calls=%fused_computation.26 | convolution fusion | flops 1074528256 | bytes 5767424 | tf_op jit(solution)/shard_map/rd,dwh->wrh/dot_general | solution.py:153
  38.9 15.0 %collective-permute-done = bf16[2,256,512]{2,1,0:T(8,128)(2,1)} collective-permute-done((bf16[2,256,512]{2,1,0:T(8,128)(2,1)}, bf16[2,256,512]{2,1,0:T(8,128)(2,1)}, u32[]{:S(2)}, u32[]{:S(2)}) %collective-permute-start) | collective-permute-done | bytes 524320 | tf_op jit(solution)/shard_map/ppermute | solution.py:16
  62.7 3.9 %fusion.1 = (f32[8,256]{1,0:T(8,128)S(1)}, f32[8,256,1280]{2,1,0:T(8,128)S(1)}) fusion(f32[256,1280]{1,0:T(8,128)} %fusion.24, bf16[256,8,64]{0,2,1:T(8,128)(2,1)S(1)} %bitcast.197, bf16[1280,8,64]{0,2,1:T(8,128)(2,1)S(1)} %bitcast.194), kind=kOutput, calls=%fused_computation.3 | convolution fusion | flops 343406592 | bytes 13377536 | tf_op jit(solution)/shard_map/qgc,kgc->gqk/dot_general | solution.py:102
  66.6 2.8 %multiply_reduce_fusion = (f32[256,8]{0,1:T(8,128)S(1)}, bf16[8,64,256]{2,1,0:T(8,128)(2,1)S(1)}) fusion(bf16[256,8,64]{0,2,1:T(8,128)(2,1)S(1)} %bitcast.208, bf16[1280,8,64]{0,2,1:T(8,128)(2,1)S(1)} %bitcast.204, f32[8,256]{1,0:T(8,128)S(1)} %get-tuple-element.42, f32[256,1280]{1,0:T(8,128)S(1)} %copy-done, f32[8,256,1280]{2,1,0:T(8,128)S(1)} %get-tuple-element.43), kind=kOutput, calls=%fused_computation.80 | convolution fusion | flops 346683392 | bytes 13647872 | tf_op jit(solution)/shard_map/gqk,kgc->qgc/dot_general | solution.py:108
  69.4 3.9 %multiply_convert_fusion = bf16[8,256,1280]{2,1,0:T(8,128)(2,1)S(1)} fusion(bf16[256,8,64]{0,2,1:T(8,128)(2,1)S(1)} %bitcast.209, bf16[1280,8,64]{0,2,1:T(8,128)(2,1)S(1)} %bitcast.205, f32[8,256]{1,0:T(8,128)S(1)} %bitcast.212, f32[8,256]{1,0:T(8,128)S(1)} %get-tuple-element.42, f32[256,1280]{1,0:T(8,128)S(1)} %copy-done, ...), kind=kOutput, calls=%fused_computation | convolution fusion | flops 353894400 | bytes 18628608 | tf_op jit(solution)/shard_map/qgc,kgc->gqk/dot_general | solution.py:112
  77.5 3.6 %collective-permute-start.4 = (f32[2,2,2,2,32,2,512]{6,4,5,3,2,1,0:T(8,128)S(1)}, f32[2,2,2,2,32,2,512]{6,4,5,3,2,1,0:T(8,128)S(1)}, u32[]{:S(2)}, u32[]{:S(2)}) collective-permute-start(f32[2,2,2,2,32,2,512]{6,4,5,3,2,1,0:T(8,128)S(1)} %bitcast.201), channel_id=1, source_target_pairs={{0,4},{4,0},{8,12},{12,8},{16,20},{20,16},{24,28},{28,24},{1,5},{5... | collective-permute-start | bytes 6291464 | tf_op jit(solution)/shard_map/ppermute | solution.py:29
  99.9 4.5 %collective-permute-done.6 = bf16[2,2,2,32,2,512]{5,3,4,2,1,0:T(8,128)(2,1)} collective-permute-done((bf16[2,2,2,32,2,512]{5,3,4,2,1,0:T(8,128)(2,1)}, bf16[2,2,2,32,2,512]{5,3,4,2,1,0:T(8,128)(2,1)}, u32[]{:S(2)}, u32[]{:S(2)}) %collective-permute-start.6) | collective-permute-done | bytes 524320 | tf_op jit(solution)/shard_map/ppermute | solution.py:29
  106.7 2.6 %collective-permute-start.8 = (bf16[2,2,32,2,512]{4,2,3,1,0:T(8,128)(2,1)S(1)}, bf16[2,2,32,2,512]{4,2,3,1,0:T(8,128)(2,1)S(1)}, u32[]{:S(2)}, u32[]{:S(2)}) collective-permute-start(bf16[2,2,32,2,512]{4,2,3,1,0:T(8,128)(2,1)S(1)} %fusion.46), channel_id=1, source_target_pairs={{0,2},{1,3},{2,0},{3,1},{4,6},{5,7},{6,4},{7,5},{8,10},{9,11},{10,... | collective-permute-start | bytes 786440 | tf_op jit(solution)/shard_map/ppermute | solution.py:29
  111.5 2.7 %collective-permute-start.7 = (s32[]{:T(128)}, s32[]{:T(128)}, u32[]{:S(2)}, u32[]{:S(2)}) collective-permute-start(s32[]{:T(128)} %add.187), channel_id=1, source_target_pairs={{0,1},{1,0},{2,3},{3,2},{4,5},{5,4},{6,7},{7,6},{8,9},{9,8},{10,11... | collective-permute-start | bytes 20 | tf_op jit(solution)/shard_map/ppermute | solution.py:36
  115.9 4.8 %collective-permute-done.8 = bf16[2,2,32,2,512]{4,2,3,1,0:T(8,128)(2,1)S(1)} collective-permute-done((bf16[2,2,32,2,512]{4,2,3,1,0:T(8,128)(2,1)S(1)}, bf16[2,2,32,2,512]{4,2,3,1,0:T(8,128)(2,1)S(1)}, u32[]{:S(2)}, u32[]{:S(2)}) %collective-permute-start.8) | collective-permute-done | bytes 262176 | tf_op jit(solution)/shard_map/ppermute | solution.py:29
  120.8 5.0 %collective-permute-start.10 = (bf16[2,32,2,256]{3,1,2,0:T(8,128)(2,1)S(1)}, bf16[2,32,2,256]{3,1,2,0:T(8,128)(2,1)S(1)}, u32[]{:S(2)}, u32[]{:S(2)}) collective-permute-start(bf16[2,32,2,256]{3,1,2,0:T(8,128)(2,1)S(1)} %fusion.62), channel_id=1, source_target_pairs={{0,16},{4,20},{8,24},{12,28},{16,0},{20,4},{24,8},{28,12},{1,17},{... | collective-permute-start | bytes 196616 | tf_op jit(solution)/shard_map/ppermute | solution.py:29
  125.8 3.6 %fusion.28 = (f32[256]{0:T(256)S(1)}, f32[256,1024]{1,0:T(8,128)S(1)}) fusion(bf16[1,256,1024]{2,1,0:T(8,128)(2,1)S(1)} %copy-done.1, f32[256]{0:T(256)S(1)} %add_rsqrt_fusion, bf16[1024,4,8,64]{0,3,2,1:T(8,128)(2,1)} %bitcast.196, bf16[2,8,64,256]{3,2,1,0:T(8,128)(2,1)S(1)} %fusion.38, bf16[1,8,64,256]{3,2,1,0:T(8,128)(2,1)S(1)} %bitcast.207, ...), kind=kOutput, calls=%fused_computation.42 | convolution fusion | flops 1075838720 | bytes 6555656 | tf_op jit(solution)/shard_map/wgcr,dwgc->rd/dot_general | solution.py:194
  130.8 3.1 %collective-permute-done.9 = s32[]{:T(128)} collective-permute-done((s32[]{:T(128)}, s32[]{:T(128)}, u32[]{:S(2)}, u32[]{:S(2)}) %collective-permute-start.9) | collective-permute-done | bytes 36 | tf_op jit(solution)/shard_map/ppermute | solution.py:36
  139.3 3.0 %collective-permute-start.13 = (s32[]{:T(128)}, s32[]{:T(128)}, u32[]{:S(2)}, u32[]{:S(2)}) collective-permute-start(s32[]{:T(128)} %add.202), channel_id=1, source_target_pairs={{0,8},{4,12},{8,0},{12,4},{16,24},{20,28},{24,16},{28,20},{1,9},{5... | collective-permute-start | bytes 20 | tf_op jit(solution)/shard_map/ppermute | solution.py:36
  147.7 2.4 %collective-permute-done.20 = f32[2,2,2,2,32,2,512]{6,4,5,3,2,1,0:T(8,128)S(1)} collective-permute-done((f32[2,2,2,2,32,2,512]{6,4,5,3,2,1,0:T(8,128)S(1)}, f32[2,2,2,2,32,2,512]{6,4,5,3,2,1,0:T(8,128)S(1)}, u32[]{:S(2)}, u32[]{:S(2)}) %collective-permute-start.20) | collective-permute-done | bytes 2097184 | tf_op jit(solution)/shard_map/ppermute | solution.py:29
  155.0 4.9 %collective-permute-done.21 = bf16[2,2,2,32,2,256]{5,3,4,2,1,0:T(8,128)(2,1)S(1)} collective-permute-done((bf16[2,2,2,32,2,256]{5,3,4,2,1,0:T(8,128)(2,1)S(1)}, bf16[2,2,2,32,2,256]{5,3,4,2,1,0:T(8,128)(2,1)S(1)}, u32[]{:S(2)}, u32[]{:S(2)}) %collective-permute-start.21) | collective-permute-done | bytes 262176 | tf_op jit(solution)/shard_map/ppermute | solution.py:29
  162.1 2.9 %collective-permute-done.22 = bf16[2,2,32,2,256]{4,2,3,1,0:T(8,128)(2,1)S(1)} collective-permute-done((bf16[2,2,32,2,256]{4,2,3,1,0:T(8,128)(2,1)S(1)}, bf16[2,2,32,2,256]{4,2,3,1,0:T(8,128)(2,1)S(1)}, u32[]{:S(2)}, u32[]{:S(2)}) %collective-permute-start.22) | collective-permute-done | bytes 131104 | tf_op jit(solution)/shard_map/ppermute | solution.py:29
  168.1 3.8 %collective-permute-done.25 = bf16[2,32,2,512]{3,1,2,0:T(8,128)(2,1)S(1)} collective-permute-done((bf16[2,32,2,512]{3,1,2,0:T(8,128)(2,1)S(1)}, bf16[2,32,2,512]{3,1,2,0:T(8,128)(2,1)S(1)}, u32[]{:S(2)}, u32[]{:S(2)}) %collective-permute-start.25) | collective-permute-done | bytes 131104 | tf_op jit(solution)/shard_map/ppermute | solution.py:29
  174.4 3.5 %collective-permute-done.26 = bf16[32,2,512]{2,0,1:T(8,128)(2,1)S(1)} collective-permute-done((bf16[32,2,512]{2,0,1:T(8,128)(2,1)S(1)}, bf16[32,2,512]{2,0,1:T(8,128)(2,1)S(1)}, u32[]{:S(2)}, u32[]{:S(2)}) %collective-permute-start.26) | collective-permute-done | bytes 65568 | tf_op jit(solution)/shard_map/ppermute | solution.py:29
  (138 shorter events, 69.9 us)
Async XLA Ops:
  13.9 40.0 %collective-permute-start = (bf16[2,256,512]{2,1,0:T(8,128)(2,1)}, bf16[2,256,512]{2,1,0:T(8,128)(2,1)}, u32[]{:S(2)}, u32[]{:S(2)}) collective-permute-start(bf16[2,256,512]{2,1,0:T(8,128)(2,1)} %slice.93), channel_id=1, source_target_pairs={{0,16},{4,20},{8,24},{12,28},{1,17},{5,21},{9,25},{13,29},{2,18},{... | collective-permute-start | bytes 1572872 | tf_op jit(solution)/shard_map/ppermute | solution.py:16
  19.6 35.4 %collective-permute-start.1 = (bf16[2,256,512]{2,1,0:T(8,128)(2,1)}, bf16[2,256,512]{2,1,0:T(8,128)(2,1)}, u32[]{:S(2)}, u32[]{:S(2)}) collective-permute-start(bf16[2,256,512]{2,1,0:T(8,128)(2,1)} %slice.93), channel_id=1, source_target_pairs={{0,12},{4,16},{8,20},{12,24},{16,28},{1,13},{5,17},{9,21},{13,25},... | collective-permute-start | bytes 1572872 | tf_op jit(solution)/shard_map/ppermute | solution.py:16
  23.0 33.1 %collective-permute-start.2 = (bf16[2,256,512]{2,1,0:T(8,128)(2,1)}, bf16[2,256,512]{2,1,0:T(8,128)(2,1)}, u32[]{:S(2)}, u32[]{:S(2)}) collective-permute-start(bf16[2,256,512]{2,1,0:T(8,128)(2,1)} %slice.93), channel_id=1, source_target_pairs={{0,8},{4,12},{8,16},{12,20},{16,24},{20,28},{1,9},{5,13},{9,17},{1... | collective-permute-start | bytes 1572872 | tf_op jit(solution)/shard_map/ppermute | solution.py:16
  25.9 31.2 %collective-permute-start.3 = (bf16[2,256,512]{2,1,0:T(8,128)(2,1)}, bf16[2,256,512]{2,1,0:T(8,128)(2,1)}, u32[]{:S(2)}, u32[]{:S(2)}) collective-permute-start(bf16[2,256,512]{2,1,0:T(8,128)(2,1)} %slice.93), channel_id=1, source_target_pairs={{0,4},{4,8},{8,12},{12,16},{16,20},{20,24},{24,28},{1,5},{5,9},{9,... | collective-permute-start | bytes 1572872 | tf_op jit(solution)/shard_map/ppermute | solution.py:16
  77.5 11.3 %collective-permute-start.4 = (f32[2,2,2,2,32,2,512]{6,4,5,3,2,1,0:T(8,128)S(1)}, f32[2,2,2,2,32,2,512]{6,4,5,3,2,1,0:T(8,128)S(1)}, u32[]{:S(2)}, u32[]{:S(2)}) collective-permute-start(f32[2,2,2,2,32,2,512]{6,4,5,3,2,1,0:T(8,128)S(1)} %bitcast.201), channel_id=1, source_target_pairs={{0,4},{4,0},{8,12},{12,8},{16,20},{20,16},{24,28},{28,24},{1,5},{5... | collective-permute-start | bytes 6291464 | tf_op jit(solution)/shard_map/ppermute | solution.py:29
  85.4 24.0 %collective-permute-start.17 = (bf16[2,8,64,256]{3,2,1,0:T(8,128)(2,1)}, bf16[2,8,64,256]{3,2,1,0:T(8,128)(2,1)}, u32[]{:S(2)}, u32[]{:S(2)}) collective-permute-start(bf16[2,8,64,256]{3,2,1,0:T(8,128)(2,1)} %pad_maximum_fusion.3), channel_id=1, source_target_pairs={{16,0},{20,4},{24,8},{28,12},{17,1},{21,5},{25,9},{29,13},{18,2},{... | collective-permute-start | bytes 1572872 | tf_op jit(solution)/shard_map/ppermute | solution.py:16
  87.5 21.8 %collective-permute-start.16 = (bf16[2,8,64,256]{3,2,1,0:T(8,128)(2,1)}, bf16[2,8,64,256]{3,2,1,0:T(8,128)(2,1)}, u32[]{:S(2)}, u32[]{:S(2)}) collective-permute-start(bf16[2,8,64,256]{3,2,1,0:T(8,128)(2,1)} %pad_maximum_fusion.2), channel_id=1, source_target_pairs={{12,0},{16,4},{20,8},{24,12},{28,16},{13,1},{17,5},{21,9},{25,13},... | collective-permute-start | bytes 1572872 | tf_op jit(solution)/shard_map/ppermute | solution.py:16
  90.2 14.2 %collective-permute-start.6 = (bf16[2,2,2,32,2,512]{5,3,4,2,1,0:T(8,128)(2,1)}, bf16[2,2,2,32,2,512]{5,3,4,2,1,0:T(8,128)(2,1)}, u32[]{:S(2)}, u32[]{:S(2)}) collective-permute-start(bf16[2,2,2,32,2,512]{5,3,4,2,1,0:T(8,128)(2,1)} %fusion.40), channel_id=1, source_target_pairs={{0,1},{1,0},{2,3},{3,2},{4,5},{5,4},{6,7},{7,6},{8,9},{9,8},{10,11... | collective-permute-start | bytes 1572872 | tf_op jit(solution)/shard_map/ppermute | solution.py:29
  92.7 16.9 %collective-permute-start.15 = (bf16[2,8,64,256]{3,2,1,0:T(8,128)(2,1)}, bf16[2,8,64,256]{3,2,1,0:T(8,128)(2,1)}, u32[]{:S(2)}, u32[]{:S(2)}) collective-permute-start(bf16[2,8,64,256]{3,2,1,0:T(8,128)(2,1)} %pad_maximum_fusion.1), channel_id=1, source_target_pairs={{8,0},{12,4},{16,8},{20,12},{24,16},{28,20},{9,1},{13,5},{17,9},{2... | collective-permute-start | bytes 1572872 | tf_op jit(solution)/shard_map/ppermute | solution.py:16
  96.3 13.3 %collective-permute-start.14 = (bf16[2,8,64,256]{3,2,1,0:T(8,128)(2,1)}, bf16[2,8,64,256]{3,2,1,0:T(8,128)(2,1)}, u32[]{:S(2)}, u32[]{:S(2)}) collective-permute-start(bf16[2,8,64,256]{3,2,1,0:T(8,128)(2,1)} %pad_maximum_fusion), channel_id=1, source_target_pairs={{4,0},{8,4},{12,8},{16,12},{20,16},{24,20},{28,24},{5,1},{9,5},{13... | collective-permute-start | bytes 1572872 | tf_op jit(solution)/shard_map/ppermute | solution.py:16
  106.7 14.0 %collective-permute-start.8 = (bf16[2,2,32,2,512]{4,2,3,1,0:T(8,128)(2,1)S(1)}, bf16[2,2,32,2,512]{4,2,3,1,0:T(8,128)(2,1)S(1)}, u32[]{:S(2)}, u32[]{:S(2)}) collective-permute-start(bf16[2,2,32,2,512]{4,2,3,1,0:T(8,128)(2,1)S(1)} %fusion.46), channel_id=1, source_target_pairs={{0,2},{1,3},{2,0},{3,1},{4,6},{5,7},{6,4},{7,5},{8,10},{9,11},{10,... | collective-permute-start | bytes 786440 | tf_op jit(solution)/shard_map/ppermute | solution.py:29
  111.5 3.7 %collective-permute-start.7 = (s32[]{:T(128)}, s32[]{:T(128)}, u32[]{:S(2)}, u32[]{:S(2)}) collective-permute-start(s32[]{:T(128)} %add.187), channel_id=1, source_target_pairs={{0,1},{1,0},{2,3},{3,2},{4,5},{5,4},{6,7},{7,6},{8,9},{9,8},{10,11... | collective-permute-start | bytes 20 | tf_op jit(solution)/shard_map/ppermute | solution.py:36
  120.8 13.8 %collective-permute-start.10 = (bf16[2,32,2,256]{3,1,2,0:T(8,128)(2,1)S(1)}, bf16[2,32,2,256]{3,1,2,0:T(8,128)(2,1)S(1)}, u32[]{:S(2)}, u32[]{:S(2)}) collective-permute-start(bf16[2,32,2,256]{3,1,2,0:T(8,128)(2,1)S(1)} %fusion.62), channel_id=1, source_target_pairs={{0,16},{4,20},{8,24},{12,28},{16,0},{20,4},{24,8},{28,12},{1,17},{... | collective-permute-start | bytes 196616 | tf_op jit(solution)/shard_map/ppermute | solution.py:29
  129.5 4.5 %collective-permute-start.9 = (s32[]{:T(128)}, s32[]{:T(128)}, u32[]{:S(2)}, u32[]{:S(2)}) collective-permute-start(s32[]{:T(128)} %add.192), channel_id=1, source_target_pairs={{0,2},{1,3},{2,0},{3,1},{4,6},{5,7},{6,4},{7,5},{8,10},{9,11},{10,... | collective-permute-start | bytes 20 | tf_op jit(solution)/shard_map/ppermute | solution.py:36
  134.7 4.7 %collective-permute-start.12 = (bf16[32,2,256]{2,0,1:T(8,128)(2,1)S(1)}, bf16[32,2,256]{2,0,1:T(8,128)(2,1)S(1)}, u32[]{:S(2)}, u32[]{:S(2)}) collective-permute-start(bf16[32,2,256]{2,0,1:T(8,128)(2,1)S(1)} %fusion.66), channel_id=1, source_target_pairs={{0,8},{4,12},{8,0},{12,4},{16,24},{20,28},{24,16},{28,20},{1,9},{5... | collective-permute-start | bytes 98312 | tf_op jit(solution)/shard_map/ppermute | solution.py:29
  146.0 4.2 %collective-permute-start.20 = (f32[2,2,2,2,32,2,512]{6,4,5,3,2,1,0:T(8,128)S(1)}, f32[2,2,2,2,32,2,512]{6,4,5,3,2,1,0:T(8,128)S(1)}, u32[]{:S(2)}, u32[]{:S(2)}) collective-permute-start(f32[2,2,2,2,32,2,512]{6,4,5,3,2,1,0:T(8,128)S(1)} %dynamic-slice_bitcast_fusion), channel_id=1, source_target_pairs={{0,4},{4,0},{8,12},{12,8},{16,20},{20,16},{24,28},{28,24},{1,5},{5... | collective-permute-start | bytes 6291464 | tf_op jit(solution)/shard_map/ppermute | solution.py:29
  146.1 5.1 %collective-permute-start.18 = (bf16[2,32,2,256]{3,1,2,0:T(8,128)(2,1)S(1)}, bf16[2,32,2,256]{3,1,2,0:T(8,128)(2,1)S(1)}, u32[]{:S(2)}, u32[]{:S(2)}) collective-permute-start(bf16[2,32,2,256]{3,1,2,0:T(8,128)(2,1)S(1)} %fusion.63), channel_id=1, source_target_pairs={{0,8},{4,12},{8,0},{12,4},{16,24},{20,28},{24,16},{28,20},{1,9},{5... | collective-permute-start | bytes 196616 | tf_op jit(solution)/shard_map/ppermute | solution.py:29
  151.1 8.8 %collective-permute-start.21 = (bf16[2,2,2,32,2,256]{5,3,4,2,1,0:T(8,128)(2,1)S(1)}, bf16[2,2,2,32,2,256]{5,3,4,2,1,0:T(8,128)(2,1)S(1)}, u32[]{:S(2)}, u32[]{:S(2)}) collective-permute-start(bf16[2,2,2,32,2,256]{5,3,4,2,1,0:T(8,128)(2,1)S(1)} %fusion.47), channel_id=1, source_target_pairs={{0,16},{4,20},{8,24},{12,28},{16,0},{20,4},{24,8},{28,12},{1,17},{... | collective-permute-start | bytes 786440 | tf_op jit(solution)/shard_map/ppermute | solution.py:29
  151.2 16.8 %collective-permute-start.19 = (bf16[32,2,256]{2,0,1:T(8,128)(2,1)S(1)}, bf16[32,2,256]{2,0,1:T(8,128)(2,1)S(1)}, u32[]{:S(2)}, u32[]{:S(2)}) collective-permute-start(bf16[32,2,256]{2,0,1:T(8,128)(2,1)S(1)} %fusion.67), channel_id=1, source_target_pairs={{0,16},{4,20},{8,24},{12,28},{16,0},{20,4},{24,8},{28,12},{1,17},{... | collective-permute-start | bytes 98312 | tf_op jit(solution)/shard_map/ppermute | solution.py:29
  153.3 8.3 %collective-permute-start.23 = (bf16[2,2,2,32,2,256]{5,3,4,2,1,0:T(8,128)(2,1)S(1)}, bf16[2,2,2,32,2,256]{5,3,4,2,1,0:T(8,128)(2,1)S(1)}, u32[]{:S(2)}, u32[]{:S(2)}) collective-permute-start(bf16[2,2,2,32,2,256]{5,3,4,2,1,0:T(8,128)(2,1)S(1)} %fusion.48), channel_id=1, source_target_pairs={{0,8},{4,12},{8,0},{12,4},{16,24},{20,28},{24,16},{28,20},{1,9},{5... | collective-permute-start | bytes 786440 | tf_op jit(solution)/shard_map/ppermute | solution.py:29
  160.0 5.0 %collective-permute-start.22 = (bf16[2,2,32,2,256]{4,2,3,1,0:T(8,128)(2,1)S(1)}, bf16[2,2,32,2,256]{4,2,3,1,0:T(8,128)(2,1)S(1)}, u32[]{:S(2)}, u32[]{:S(2)}) collective-permute-start(bf16[2,2,32,2,256]{4,2,3,1,0:T(8,128)(2,1)S(1)} %fusion.59), channel_id=1, source_target_pairs={{0,8},{4,12},{8,0},{12,4},{16,24},{20,28},{24,16},{28,20},{1,9},{5... | collective-permute-start | bytes 393224 | tf_op jit(solution)/shard_map/ppermute | solution.py:29
  161.8 5.0 %collective-permute-start.24 = (bf16[2,2,32,2,256]{4,2,3,1,0:T(8,128)(2,1)S(1)}, bf16[2,2,32,2,256]{4,2,3,1,0:T(8,128)(2,1)S(1)}, u32[]{:S(2)}, u32[]{:S(2)}) collective-permute-start(bf16[2,2,32,2,256]{4,2,3,1,0:T(8,128)(2,1)S(1)} %fusion.60), channel_id=1, source_target_pairs={{0,16},{4,20},{8,24},{12,28},{16,0},{20,4},{24,8},{28,12},{1,17},{... | collective-permute-start | bytes 393224 | tf_op jit(solution)/shard_map/ppermute | solution.py:29
  166.9 5.0 %collective-permute-start.25 = (bf16[2,32,2,512]{3,1,2,0:T(8,128)(2,1)S(1)}, bf16[2,32,2,512]{3,1,2,0:T(8,128)(2,1)S(1)}, u32[]{:S(2)}, u32[]{:S(2)}) collective-permute-start(bf16[2,32,2,512]{3,1,2,0:T(8,128)(2,1)S(1)} %fusion.61), channel_id=1, source_target_pairs={{0,1},{1,0},{2,3},{3,2},{4,5},{5,4},{6,7},{7,6},{8,9},{9,8},{10,11... | collective-permute-start | bytes 393224 | tf_op jit(solution)/shard_map/ppermute | solution.py:29
  172.0 5.9 %collective-permute-start.26 = (bf16[32,2,512]{2,0,1:T(8,128)(2,1)S(1)}, bf16[32,2,512]{2,0,1:T(8,128)(2,1)S(1)}, u32[]{:S(2)}, u32[]{:S(2)}) collective-permute-start(bf16[32,2,512]{2,0,1:T(8,128)(2,1)S(1)} %fusion.64), channel_id=1, source_target_pairs={{0,2},{1,3},{2,0},{3,1},{4,6},{5,7},{6,4},{7,5},{8,10},{9,11},{10,... | collective-permute-start | bytes 196616 | tf_op jit(solution)/shard_map/ppermute | solution.py:29
  (17 other events, 114.0 us)

commit v10 on v9

--- a/solution.py
+++ b/solution.py
@@ -190,9 +190,9 @@
         owned = owned + shifted(piece.astype(jnp.bfloat16), "tm", -offset).astype(jnp.float32)
     grad_kv = owned.astype(jnp.bfloat16)
     grad_proj = jnp.concatenate([grad_q[None], grad_kv, jnp.zeros_like(grad_q)[None]], axis=0)
-    split_weights = weights.reshape(width, weights.shape[1], HEADS, HSIZE)
+    grad_rows = grad_proj.transpose(0, 3, 1, 2).reshape(grad_proj.shape[0], rows, inner)
     grad_normed = jnp.einsum(
-        "wgcr,dwgc->rd", grad_proj, split_weights, preferred_element_type=jnp.float32
+        "wrh,dwh->rd", grad_rows, weights, preferred_element_type=jnp.float32
     )
     along = jnp.sum(grad_normed * normed_full, axis=-1) / width
     unscaled_input = inv_rms[:, None] * (grad_normed - normed_full * along[:, None])

time: 180 us -> 172 us (0.956)
  local copies, waits for them, and re-layouts: 26.3 us -> 17.7 us
    unnamed x33 -> x30, local copies, waits for them, and re-layouts: 15.8 us -> 7.04 us
    ppermute x14, waiting for transfers between devices: 28.5 us -> 26.4 us  [halve(): lax.ppermute(send.astype(send_type), axis, pairs).astype(keep.dtype)]
  transfers between devices with their start and end apart: 27 -> 27, of which waited for: 15 -> 16; matrix products, arithmetic and copies ran while one was open for 17% -> 20% of each run, Pallas kernels for 0% -> 0%
where the time goes in v10:
time: 172 us; the launch traced here: 171 us
  starting transfers between devices  52 us (30%)
  waiting for transfers between devices  50.8 us (30%)
  matrix products  30.4 us (18%)
  local copies, waits for them, and re-layouts  17.7 us (10%)
  other arithmetic  15.1 us (9%)
  between operations  5.06 us (3%)
    ppermute x14, waiting for transfers between devices, halve(): lax.ppermute(send.astype(send_type), axis, pairs).astype(keep.dtype)  26.4 us
    ppermute x14, starting transfers between devices, halve(): lax.ppermute(send.astype(send_type), axis, pairs).astype(keep.dtype)  24.1 us
    ppermute x8, starting transfers between devices, shifted(): return lax.ppermute(value, axis, pairs)  19.4 us
    ppermute x8, waiting for transfers between devices, shifted(): return lax.ppermute(value, axis, pairs)  16.1 us
    ppermute x5, starting transfers between devices, swap_add(): return (value + lax.ppermute(value, axis, pairs), anchor)  8.52 us
    ppermute x5, waiting for transfers between devices, swap_add(): return (value + lax.ppermute(value, axis, pairs), anchor)  8.31 us
    unnamed x30, local copies, waits for them, and re-layouts  7.04 us
    dot_general x1, matrix products, shards(): jnp.einsum('rd,dwh->wrh', grad_out, weights, preferred_element_type=jnp.f...  4.83 us
  transfers between devices with their start and end apart: 27, of which 16 were waited for; matrix products, arithmetic and copies ran while one was open for 20% of the time, Pallas kernels for 0%

profile of v10, /device:TPU:0, one launch (start us, length us, event | category | flops | bytes accessed | tf_op | source)
XLA Modules:
  0.0 171.1 jit_solution(6835312211120049902)
XLA Ops:
  1.9 4.0 %fusion.23 = bf16[4,256,512]{2,1,0:T(8,128)(2,1)S(1)} fusion(bf16[1024,4,512]{2,1,0:T(4,128)(2,1)} %param.5, bf16[1,256,1024]{2,1,0:T(8,128)(2,1)} %param.4, f32[256]{0:T(256)S(1)} %add_rsqrt_fusion), kind=kOutput, calls=%fused_computation.29 | convolution fusion | flops 1075052544 | bytes 5768192 | tf_op jit(solution)/shard_map/rd,dwh->wrh/dot_general | solution.py:142
  6.7 5.7 %collective-permute-start = (bf16[2,256,512]{2,1,0:T(8,128)(2,1)}, bf16[2,256,512]{2,1,0:T(8,128)(2,1)}, u32[]{:S(2)}, u32[]{:S(2)}) collective-permute-start(bf16[2,256,512]{2,1,0:T(8,128)(2,1)} %slice.93), channel_id=1, source_target_pairs={{0,16},{4,20},{8,24},{12,28},{1,17},{5,21},{9,25},{13,29},{2,18},{... | collective-permute-start | bytes 1572872 | tf_op jit(solution)/shard_map/ppermute | solution.py:16
  12.4 3.4 %collective-permute-start.1 = (bf16[2,256,512]{2,1,0:T(8,128)(2,1)}, bf16[2,256,512]{2,1,0:T(8,128)(2,1)}, u32[]{:S(2)}, u32[]{:S(2)}) collective-permute-start(bf16[2,256,512]{2,1,0:T(8,128)(2,1)} %slice.93), channel_id=1, source_target_pairs={{0,12},{4,16},{8,20},{12,24},{16,28},{1,13},{5,17},{9,21},{13,25},... | collective-permute-start | bytes 1572872 | tf_op jit(solution)/shard_map/ppermute | solution.py:16
  15.7 3.0 %collective-permute-start.2 = (bf16[2,256,512]{2,1,0:T(8,128)(2,1)}, bf16[2,256,512]{2,1,0:T(8,128)(2,1)}, u32[]{:S(2)}, u32[]{:S(2)}) collective-permute-start(bf16[2,256,512]{2,1,0:T(8,128)(2,1)} %slice.93), channel_id=1, source_target_pairs={{0,8},{4,12},{8,16},{12,20},{16,24},{20,28},{1,9},{5,13},{9,17},{1... | collective-permute-start | bytes 1572872 | tf_op jit(solution)/shard_map/ppermute | solution.py:16
  22.0 4.8 %fusion.20 = bf16[4,256,512]{2,1,0:T(8,128)(2,1)} fusion(bf16[1024,4,512]{2,1,0:T(4,128)(2,1)} %param.5, bf16[1,256,1024]{2,1,0:T(8,128)(2,1)S(1)} %copy-done.9, pred[256]{0:T(512)(128)(4,1)S(1)} %compare_reduce_fusion), kind=kOutput, calls=%fused_computation.28 | convolution fusion | flops 1074528256 | bytes 5767424 | tf_op jit(solution)/shard_map/rd,dwh->wrh/dot_general | solution.py:153
  31.9 14.8 %collective-permute-done = bf16[2,256,512]{2,1,0:T(8,128)(2,1)} collective-permute-done((bf16[2,256,512]{2,1,0:T(8,128)(2,1)}, bf16[2,256,512]{2,1,0:T(8,128)(2,1)}, u32[]{:S(2)}, u32[]{:S(2)}) %collective-permute-start) | collective-permute-done | bytes 524320 | tf_op jit(solution)/shard_map/ppermute | solution.py:16
  55.4 3.9 %fusion.1 = (f32[8,256]{1,0:T(8,128)S(1)}, f32[8,256,1280]{2,1,0:T(8,128)S(1)}) fusion(f32[256,1280]{1,0:T(8,128)} %fusion.38, bf16[256,8,64]{0,2,1:T(8,128)(2,1)S(1)} %bitcast.196, bf16[1280,8,64]{0,2,1:T(8,128)(2,1)S(1)} %bitcast.193), kind=kOutput, calls=%fused_computation.3 | convolution fusion | flops 343406592 | bytes 13377536 | tf_op jit(solution)/shard_map/qgc,kgc->gqk/dot_general | solution.py:102
  59.3 2.8 %multiply_reduce_fusion = (f32[256,8]{0,1:T(8,128)S(1)}, bf16[8,64,256]{2,1,0:T(8,128)(2,1)S(1)}) fusion(bf16[256,8,64]{0,2,1:T(8,128)(2,1)S(1)} %bitcast.207, bf16[1280,8,64]{0,2,1:T(8,128)(2,1)S(1)} %bitcast.204, f32[8,256]{1,0:T(8,128)S(1)} %get-tuple-element.42, f32[256,1280]{1,0:T(8,128)S(1)} %copy-done, f32[8,256,1280]{2,1,0:T(8,128)S(1)} %get-tuple-element.43), kind=kOutput, calls=%fused_computation.83 | convolution fusion | flops 346683392 | bytes 13647872 | tf_op jit(solution)/shard_map/gqk,kgc->qgc/dot_general | solution.py:108
  62.1 3.9 %multiply_convert_fusion = bf16[8,256,1280]{2,1,0:T(8,128)(2,1)S(1)} fusion(bf16[256,8,64]{0,2,1:T(8,128)(2,1)S(1)} %bitcast.208, bf16[1280,8,64]{0,2,1:T(8,128)(2,1)S(1)} %bitcast.205, f32[8,256]{1,0:T(8,128)S(1)} %bitcast.211, f32[8,256]{1,0:T(8,128)S(1)} %get-tuple-element.42, f32[256,1280]{1,0:T(8,128)S(1)} %copy-done, ...), kind=kOutput, calls=%fused_computation | convolution fusion | flops 353894400 | bytes 18628608 | tf_op jit(solution)/shard_map/qgc,kgc->gqk/dot_general | solution.py:112
  70.0 3.6 %collective-permute-start.4 = (f32[2,2,2,2,32,2,512]{6,4,5,3,2,1,0:T(8,128)S(1)}, f32[2,2,2,2,32,2,512]{6,4,5,3,2,1,0:T(8,128)S(1)}, u32[]{:S(2)}, u32[]{:S(2)}) collective-permute-start(f32[2,2,2,2,32,2,512]{6,4,5,3,2,1,0:T(8,128)S(1)} %bitcast.201), channel_id=1, source_target_pairs={{0,4},{4,0},{8,12},{12,8},{16,20},{20,16},{24,28},{28,24},{1,5},{5... | collective-permute-start | bytes 6291464 | tf_op jit(solution)/shard_map/ppermute | solution.py:29
  74.6 2.3 %fusion.87 = (bf16[8,64,1280]{2,1,0:T(8,128)(2,1)S(1)}, f32[8,64,1280]{2,1,0:T(8,128)S(1)}) fusion(bf16[256,8,64]{0,2,1:T(8,128)(2,1)S(1)} %bitcast.209, f32[8,256]{1,0:T(8,128)S(1)} %get-tuple-element.42, f32[256,1280]{1,0:T(8,128)S(1)} %copy-done, f32[8,256,1280]{2,1,0:T(8,128)S(1)} %get-tuple-element.43), kind=kOutput, calls=%fused_computation.146 | convolution fusion | flops 346685440 | bytes 15998976 | tf_op jit(solution)/shard_map/gqk,qgc->gck/dot_general | solution.py:122
  92.6 4.4 %collective-permute-done.6 = bf16[2,2,2,32,2,512]{5,3,4,2,1,0:T(8,128)(2,1)} collective-permute-done((bf16[2,2,2,32,2,512]{5,3,4,2,1,0:T(8,128)(2,1)}, bf16[2,2,2,32,2,512]{5,3,4,2,1,0:T(8,128)(2,1)}, u32[]{:S(2)}, u32[]{:S(2)}) %collective-permute-start.6) | collective-permute-done | bytes 524320 | tf_op jit(solution)/shard_map/ppermute | solution.py:29
  98.3 2.7 %collective-permute-start.8 = (bf16[2,2,32,2,512]{4,2,3,1,0:T(8,128)(2,1)S(1)}, bf16[2,2,32,2,512]{4,2,3,1,0:T(8,128)(2,1)S(1)}, u32[]{:S(2)}, u32[]{:S(2)}) collective-permute-start(bf16[2,2,32,2,512]{4,2,3,1,0:T(8,128)(2,1)S(1)} %fusion.59), channel_id=1, source_target_pairs={{0,2},{1,3},{2,0},{3,1},{4,6},{5,7},{6,4},{7,5},{8,10},{9,11},{10,... | collective-permute-start | bytes 786440 | tf_op jit(solution)/shard_map/ppermute | solution.py:29
  109.7 2.6 %collective-permute-done.8 = bf16[2,2,32,2,512]{4,2,3,1,0:T(8,128)(2,1)S(1)} collective-permute-done((bf16[2,2,32,2,512]{4,2,3,1,0:T(8,128)(2,1)S(1)}, bf16[2,2,32,2,512]{4,2,3,1,0:T(8,128)(2,1)S(1)}, u32[]{:S(2)}, u32[]{:S(2)}) %collective-permute-start.8) | collective-permute-done | bytes 262176 | tf_op jit(solution)/shard_map/ppermute | solution.py:29
  112.4 4.9 %collective-permute-start.10 = (bf16[2,32,2,256]{3,1,2,0:T(8,128)(2,1)S(1)}, bf16[2,32,2,256]{3,1,2,0:T(8,128)(2,1)S(1)}, u32[]{:S(2)}, u32[]{:S(2)}) collective-permute-start(bf16[2,32,2,256]{3,1,2,0:T(8,128)(2,1)S(1)} %fusion.75), channel_id=1, source_target_pairs={{0,16},{4,20},{8,24},{12,28},{16,0},{20,4},{24,8},{28,12},{1,17},{... | collective-permute-start | bytes 196616 | tf_op jit(solution)/shard_map/ppermute | solution.py:29
  117.3 4.3 %fusion.42 = (f32[256]{0:T(256)S(1)}, f32[256,1024]{1,0:T(8,128)S(1)}) fusion(bf16[1,256,1024]{2,1,0:T(8,128)(2,1)S(1)} %copy-done.1, f32[256]{0:T(256)S(1)} %add_rsqrt_fusion, bf16[4,256,512]{1,2,0:T(8,128)(2,1)} %bitcast.206, bf16[1024,4,512]{2,1,0:T(4,128)(2,1)} %param.5), kind=kOutput, calls=%fused_computation.46 | convolution fusion | flops 1074790144 | bytes 6817792 | tf_op jit(solution)/shard_map/wrh,dwh->rd/dot_general | solution.py:194
  121.7 3.2 %collective-permute-start.9 = (s32[]{:T(128)}, s32[]{:T(128)}, u32[]{:S(2)}, u32[]{:S(2)}) collective-permute-start(s32[]{:T(128)} %add.192), channel_id=1, source_target_pairs={{0,2},{1,3},{2,0},{3,1},{4,6},{5,7},{6,4},{7,5},{8,10},{9,11},{10,... | collective-permute-start | bytes 20 | tf_op jit(solution)/shard_map/ppermute | solution.py:36
  129.5 2.3 %collective-permute-done.11 = s32[]{:T(128)} collective-permute-done((s32[]{:T(128)}, s32[]{:T(128)}, u32[]{:S(2)}, u32[]{:S(2)}) %collective-permute-start.11) | collective-permute-done | bytes 36 | tf_op jit(solution)/shard_map/ppermute | solution.py:36
  140.1 3.2 %collective-permute-done.20 = f32[2,2,2,2,32,2,512]{6,4,5,3,2,1,0:T(8,128)S(1)} collective-permute-done((f32[2,2,2,2,32,2,512]{6,4,5,3,2,1,0:T(8,128)S(1)}, f32[2,2,2,2,32,2,512]{6,4,5,3,2,1,0:T(8,128)S(1)}, u32[]{:S(2)}, u32[]{:S(2)}) %collective-permute-start.20) | collective-permute-done | bytes 2097184 | tf_op jit(solution)/shard_map/ppermute | solution.py:29
  147.3 5.6 %collective-permute-done.21 = bf16[2,2,2,32,2,256]{5,3,4,2,1,0:T(8,128)(2,1)S(1)} collective-permute-done((bf16[2,2,2,32,2,256]{5,3,4,2,1,0:T(8,128)(2,1)S(1)}, bf16[2,2,2,32,2,256]{5,3,4,2,1,0:T(8,128)(2,1)S(1)}, u32[]{:S(2)}, u32[]{:S(2)}) %collective-permute-start.21) | collective-permute-done | bytes 262176 | tf_op jit(solution)/shard_map/ppermute | solution.py:29
  154.8 3.3 %collective-permute-done.22 = bf16[2,2,32,2,256]{4,2,3,1,0:T(8,128)(2,1)S(1)} collective-permute-done((bf16[2,2,32,2,256]{4,2,3,1,0:T(8,128)(2,1)S(1)}, bf16[2,2,32,2,256]{4,2,3,1,0:T(8,128)(2,1)S(1)}, u32[]{:S(2)}, u32[]{:S(2)}) %collective-permute-start.22) | collective-permute-done | bytes 131104 | tf_op jit(solution)/shard_map/ppermute | solution.py:29
  161.1 3.4 %collective-permute-done.25 = bf16[2,32,2,512]{3,1,2,0:T(8,128)(2,1)S(1)} collective-permute-done((bf16[2,32,2,512]{3,1,2,0:T(8,128)(2,1)S(1)}, bf16[2,32,2,512]{3,1,2,0:T(8,128)(2,1)S(1)}, u32[]{:S(2)}, u32[]{:S(2)}) %collective-permute-start.25) | collective-permute-done | bytes 131104 | tf_op jit(solution)/shard_map/ppermute | solution.py:29
  164.6 3.3 %collective-permute-start.26 = (bf16[32,2,512]{2,0,1:T(8,128)(2,1)S(1)}, bf16[32,2,512]{2,0,1:T(8,128)(2,1)S(1)}, u32[]{:S(2)}, u32[]{:S(2)}) collective-permute-start(bf16[32,2,512]{2,0,1:T(8,128)(2,1)S(1)} %fusion.77), channel_id=1, source_target_pairs={{0,2},{1,3},{2,0},{3,1},{4,6},{5,7},{6,4},{7,5},{8,10},{9,11},{10,... | collective-permute-start | bytes 196616 | tf_op jit(solution)/shard_map/ppermute | solution.py:29
  167.9 2.2 %collective-permute-done.26 = bf16[32,2,512]{2,0,1:T(8,128)(2,1)S(1)} collective-permute-done((bf16[32,2,512]{2,0,1:T(8,128)(2,1)S(1)}, bf16[32,2,512]{2,0,1:T(8,128)(2,1)S(1)}, u32[]{:S(2)}, u32[]{:S(2)}) %collective-permute-start.26) | collective-permute-done | bytes 65568 | tf_op jit(solution)/shard_map/ppermute | solution.py:29
  (136 shorter events, 68.5 us)
Async XLA Ops:
  6.7 40.0 %collective-permute-start = (bf16[2,256,512]{2,1,0:T(8,128)(2,1)}, bf16[2,256,512]{2,1,0:T(8,128)(2,1)}, u32[]{:S(2)}, u32[]{:S(2)}) collective-permute-start(bf16[2,256,512]{2,1,0:T(8,128)(2,1)} %slice.93), channel_id=1, source_target_pairs={{0,16},{4,20},{8,24},{12,28},{1,17},{5,21},{9,25},{13,29},{2,18},{... | collective-permute-start | bytes 1572872 | tf_op jit(solution)/shard_map/ppermute | solution.py:16
  12.4 35.4 %collective-permute-start.1 = (bf16[2,256,512]{2,1,0:T(8,128)(2,1)}, bf16[2,256,512]{2,1,0:T(8,128)(2,1)}, u32[]{:S(2)}, u32[]{:S(2)}) collective-permute-start(bf16[2,256,512]{2,1,0:T(8,128)(2,1)} %slice.93), channel_id=1, source_target_pairs={{0,12},{4,16},{8,20},{12,24},{16,28},{1,13},{5,17},{9,21},{13,25},... | collective-permute-start | bytes 1572872 | tf_op jit(solution)/shard_map/ppermute | solution.py:16
  15.7 33.1 %collective-permute-start.2 = (bf16[2,256,512]{2,1,0:T(8,128)(2,1)}, bf16[2,256,512]{2,1,0:T(8,128)(2,1)}, u32[]{:S(2)}, u32[]{:S(2)}) collective-permute-start(bf16[2,256,512]{2,1,0:T(8,128)(2,1)} %slice.93), channel_id=1, source_target_pairs={{0,8},{4,12},{8,16},{12,20},{16,24},{20,28},{1,9},{5,13},{9,17},{1... | collective-permute-start | bytes 1572872 | tf_op jit(solution)/shard_map/ppermute | solution.py:16
  18.7 31.2 %collective-permute-start.3 = (bf16[2,256,512]{2,1,0:T(8,128)(2,1)}, bf16[2,256,512]{2,1,0:T(8,128)(2,1)}, u32[]{:S(2)}, u32[]{:S(2)}) collective-permute-start(bf16[2,256,512]{2,1,0:T(8,128)(2,1)} %slice.93), channel_id=1, source_target_pairs={{0,4},{4,8},{8,12},{12,16},{16,20},{20,24},{24,28},{1,5},{5,9},{9,... | collective-permute-start | bytes 1572872 | tf_op jit(solution)/shard_map/ppermute | solution.py:16
  70.0 11.5 %collective-permute-start.4 = (f32[2,2,2,2,32,2,512]{6,4,5,3,2,1,0:T(8,128)S(1)}, f32[2,2,2,2,32,2,512]{6,4,5,3,2,1,0:T(8,128)S(1)}, u32[]{:S(2)}, u32[]{:S(2)}) collective-permute-start(f32[2,2,2,2,32,2,512]{6,4,5,3,2,1,0:T(8,128)S(1)} %bitcast.201), channel_id=1, source_target_pairs={{0,4},{4,0},{8,12},{12,8},{16,20},{20,16},{24,28},{28,24},{1,5},{5... | collective-permute-start | bytes 6291464 | tf_op jit(solution)/shard_map/ppermute | solution.py:29
  78.1 22.9 %collective-permute-start.17 = (bf16[2,8,64,256]{3,2,1,0:T(8,128)(2,1)}, bf16[2,8,64,256]{3,2,1,0:T(8,128)(2,1)}, u32[]{:S(2)}, u32[]{:S(2)}) collective-permute-start(bf16[2,8,64,256]{3,2,1,0:T(8,128)(2,1)} %pad_maximum_fusion.3), channel_id=1, source_target_pairs={{16,0},{20,4},{24,8},{28,12},{17,1},{21,5},{25,9},{29,13},{18,2},{... | collective-permute-start | bytes 1572872 | tf_op jit(solution)/shard_map/ppermute | solution.py:16
  80.2 20.8 %collective-permute-start.16 = (bf16[2,8,64,256]{3,2,1,0:T(8,128)(2,1)}, bf16[2,8,64,256]{3,2,1,0:T(8,128)(2,1)}, u32[]{:S(2)}, u32[]{:S(2)}) collective-permute-start(bf16[2,8,64,256]{3,2,1,0:T(8,128)(2,1)} %pad_maximum_fusion.2), channel_id=1, source_target_pairs={{12,0},{16,4},{20,8},{24,12},{28,16},{13,1},{17,5},{21,9},{25,13},... | collective-permute-start | bytes 1572872 | tf_op jit(solution)/shard_map/ppermute | solution.py:16
  82.9 14.2 %collective-permute-start.6 = (bf16[2,2,2,32,2,512]{5,3,4,2,1,0:T(8,128)(2,1)}, bf16[2,2,2,32,2,512]{5,3,4,2,1,0:T(8,128)(2,1)}, u32[]{:S(2)}, u32[]{:S(2)}) collective-permute-start(bf16[2,2,2,32,2,512]{5,3,4,2,1,0:T(8,128)(2,1)} %fusion.53), channel_id=1, source_target_pairs={{0,1},{1,0},{2,3},{3,2},{4,5},{5,4},{6,7},{7,6},{8,9},{9,8},{10,11... | collective-permute-start | bytes 1572872 | tf_op jit(solution)/shard_map/ppermute | solution.py:29
  85.3 16.9 %collective-permute-start.15 = (bf16[2,8,64,256]{3,2,1,0:T(8,128)(2,1)}, bf16[2,8,64,256]{3,2,1,0:T(8,128)(2,1)}, u32[]{:S(2)}, u32[]{:S(2)}) collective-permute-start(bf16[2,8,64,256]{3,2,1,0:T(8,128)(2,1)} %pad_maximum_fusion.1), channel_id=1, source_target_pairs={{8,0},{12,4},{16,8},{20,12},{24,16},{28,20},{9,1},{13,5},{17,9},{2... | collective-permute-start | bytes 1572872 | tf_op jit(solution)/shard_map/ppermute | solution.py:16
  88.8 13.5 %collective-permute-start.14 = (bf16[2,8,64,256]{3,2,1,0:T(8,128)(2,1)}, bf16[2,8,64,256]{3,2,1,0:T(8,128)(2,1)}, u32[]{:S(2)}, u32[]{:S(2)}) collective-permute-start(bf16[2,8,64,256]{3,2,1,0:T(8,128)(2,1)} %pad_maximum_fusion), channel_id=1, source_target_pairs={{4,0},{8,4},{12,8},{16,12},{20,16},{24,20},{28,24},{5,1},{9,5},{13... | collective-permute-start | bytes 1572872 | tf_op jit(solution)/shard_map/ppermute | solution.py:16
  98.3 14.0 %collective-permute-start.8 = (bf16[2,2,32,2,512]{4,2,3,1,0:T(8,128)(2,1)S(1)}, bf16[2,2,32,2,512]{4,2,3,1,0:T(8,128)(2,1)S(1)}, u32[]{:S(2)}, u32[]{:S(2)}) collective-permute-start(bf16[2,2,32,2,512]{4,2,3,1,0:T(8,128)(2,1)S(1)} %fusion.59), channel_id=1, source_target_pairs={{0,2},{1,3},{2,0},{3,1},{4,6},{5,7},{6,4},{7,5},{8,10},{9,11},{10,... | collective-permute-start | bytes 786440 | tf_op jit(solution)/shard_map/ppermute | solution.py:29
  112.4 14.4 %collective-permute-start.10 = (bf16[2,32,2,256]{3,1,2,0:T(8,128)(2,1)S(1)}, bf16[2,32,2,256]{3,1,2,0:T(8,128)(2,1)S(1)}, u32[]{:S(2)}, u32[]{:S(2)}) collective-permute-start(bf16[2,32,2,256]{3,1,2,0:T(8,128)(2,1)S(1)} %fusion.75), channel_id=1, source_target_pairs={{0,16},{4,20},{8,24},{12,28},{16,0},{20,4},{24,8},{28,12},{1,17},{... | collective-permute-start | bytes 196616 | tf_op jit(solution)/shard_map/ppermute | solution.py:29
  121.7 4.6 %collective-permute-start.9 = (s32[]{:T(128)}, s32[]{:T(128)}, u32[]{:S(2)}, u32[]{:S(2)}) collective-permute-start(s32[]{:T(128)} %add.192), channel_id=1, source_target_pairs={{0,2},{1,3},{2,0},{3,1},{4,6},{5,7},{6,4},{7,5},{8,10},{9,11},{10,... | collective-permute-start | bytes 20 | tf_op jit(solution)/shard_map/ppermute | solution.py:36
  126.9 5.5 %collective-permute-start.12 = (bf16[32,2,256]{2,0,1:T(8,128)(2,1)S(1)}, bf16[32,2,256]{2,0,1:T(8,128)(2,1)S(1)}, u32[]{:S(2)}, u32[]{:S(2)}) collective-permute-start(bf16[32,2,256]{2,0,1:T(8,128)(2,1)S(1)} %fusion.79), channel_id=1, source_target_pairs={{0,8},{4,12},{8,0},{12,4},{16,24},{20,28},{24,16},{28,20},{1,9},{5... | collective-permute-start | bytes 98312 | tf_op jit(solution)/shard_map/ppermute | solution.py:29
  132.4 3.7 %collective-permute-start.13 = (s32[]{:T(128)}, s32[]{:T(128)}, u32[]{:S(2)}, u32[]{:S(2)}) collective-permute-start(s32[]{:T(128)} %add.202), channel_id=1, source_target_pairs={{0,8},{4,12},{8,0},{12,4},{16,24},{20,28},{24,16},{28,20},{1,9},{5... | collective-permute-start | bytes 20 | tf_op jit(solution)/shard_map/ppermute | solution.py:36
  139.0 4.2 %collective-permute-start.20 = (f32[2,2,2,2,32,2,512]{6,4,5,3,2,1,0:T(8,128)S(1)}, f32[2,2,2,2,32,2,512]{6,4,5,3,2,1,0:T(8,128)S(1)}, u32[]{:S(2)}, u32[]{:S(2)}) collective-permute-start(f32[2,2,2,2,32,2,512]{6,4,5,3,2,1,0:T(8,128)S(1)} %dynamic-slice_bitcast_fusion), channel_id=1, source_target_pairs={{0,4},{4,0},{8,12},{12,8},{16,20},{20,16},{24,28},{28,24},{1,5},{5... | collective-permute-start | bytes 6291464 | tf_op jit(solution)/shard_map/ppermute | solution.py:29
  139.1 5.1 %collective-permute-start.18 = (bf16[2,32,2,256]{3,1,2,0:T(8,128)(2,1)S(1)}, bf16[2,32,2,256]{3,1,2,0:T(8,128)(2,1)S(1)}, u32[]{:S(2)}, u32[]{:S(2)}) collective-permute-start(bf16[2,32,2,256]{3,1,2,0:T(8,128)(2,1)S(1)} %fusion.76), channel_id=1, source_target_pairs={{0,8},{4,12},{8,0},{12,4},{16,24},{20,28},{24,16},{28,20},{1,9},{5... | collective-permute-start | bytes 196616 | tf_op jit(solution)/shard_map/ppermute | solution.py:29
  144.2 8.8 %collective-permute-start.21 = (bf16[2,2,2,32,2,256]{5,3,4,2,1,0:T(8,128)(2,1)S(1)}, bf16[2,2,2,32,2,256]{5,3,4,2,1,0:T(8,128)(2,1)S(1)}, u32[]{:S(2)}, u32[]{:S(2)}) collective-permute-start(bf16[2,2,2,32,2,256]{5,3,4,2,1,0:T(8,128)(2,1)S(1)} %fusion.60), channel_id=1, source_target_pairs={{0,16},{4,20},{8,24},{12,28},{16,0},{20,4},{24,8},{28,12},{1,17},{... | collective-permute-start | bytes 786440 | tf_op jit(solution)/shard_map/ppermute | solution.py:29
  144.3 16.8 %collective-permute-start.19 = (bf16[32,2,256]{2,0,1:T(8,128)(2,1)S(1)}, bf16[32,2,256]{2,0,1:T(8,128)(2,1)S(1)}, u32[]{:S(2)}, u32[]{:S(2)}) collective-permute-start(bf16[32,2,256]{2,0,1:T(8,128)(2,1)S(1)} %fusion.80), channel_id=1, source_target_pairs={{0,16},{4,20},{8,24},{12,28},{16,0},{20,4},{24,8},{28,12},{1,17},{... | collective-permute-start | bytes 98312 | tf_op jit(solution)/shard_map/ppermute | solution.py:29
  146.4 7.9 %collective-permute-start.23 = (bf16[2,2,2,32,2,256]{5,3,4,2,1,0:T(8,128)(2,1)S(1)}, bf16[2,2,2,32,2,256]{5,3,4,2,1,0:T(8,128)(2,1)S(1)}, u32[]{:S(2)}, u32[]{:S(2)}) collective-permute-start(bf16[2,2,2,32,2,256]{5,3,4,2,1,0:T(8,128)(2,1)S(1)} %fusion.61), channel_id=1, source_target_pairs={{0,8},{4,12},{8,0},{12,4},{16,24},{20,28},{24,16},{28,20},{1,9},{5... | collective-permute-start | bytes 786440 | tf_op jit(solution)/shard_map/ppermute | solution.py:29
  153.1 5.0 %collective-permute-start.22 = (bf16[2,2,32,2,256]{4,2,3,1,0:T(8,128)(2,1)S(1)}, bf16[2,2,32,2,256]{4,2,3,1,0:T(8,128)(2,1)S(1)}, u32[]{:S(2)}, u32[]{:S(2)}) collective-permute-start(bf16[2,2,32,2,256]{4,2,3,1,0:T(8,128)(2,1)S(1)} %fusion.72), channel_id=1, source_target_pairs={{0,8},{4,12},{8,0},{12,4},{16,24},{20,28},{24,16},{28,20},{1,9},{5... | collective-permute-start | bytes 393224 | tf_op jit(solution)/shard_map/ppermute | solution.py:29
  154.4 5.0 %collective-permute-start.24 = (bf16[2,2,32,2,256]{4,2,3,1,0:T(8,128)(2,1)S(1)}, bf16[2,2,32,2,256]{4,2,3,1,0:T(8,128)(2,1)S(1)}, u32[]{:S(2)}, u32[]{:S(2)}) collective-permute-start(bf16[2,2,32,2,256]{4,2,3,1,0:T(8,128)(2,1)S(1)} %fusion.73), channel_id=1, source_target_pairs={{0,16},{4,20},{8,24},{12,28},{16,0},{20,4},{24,8},{28,12},{1,17},{... | collective-permute-start | bytes 393224 | tf_op jit(solution)/shard_map/ppermute | solution.py:29
  159.5 5.0 %collective-permute-start.25 = (bf16[2,32,2,512]{3,1,2,0:T(8,128)(2,1)S(1)}, bf16[2,32,2,512]{3,1,2,0:T(8,128)(2,1)S(1)}, u32[]{:S(2)}, u32[]{:S(2)}) collective-permute-start(bf16[2,32,2,512]{3,1,2,0:T(8,128)(2,1)S(1)} %fusion.74), channel_id=1, source_target_pairs={{0,1},{1,0},{2,3},{3,2},{4,5},{5,4},{6,7},{7,6},{8,9},{9,8},{10,11... | collective-permute-start | bytes 393224 | tf_op jit(solution)/shard_map/ppermute | solution.py:29
  164.6 5.5 %collective-permute-start.26 = (bf16[32,2,512]{2,0,1:T(8,128)(2,1)S(1)}, bf16[32,2,512]{2,0,1:T(8,128)(2,1)S(1)}, u32[]{:S(2)}, u32[]{:S(2)}) collective-permute-start(bf16[32,2,512]{2,0,1:T(8,128)(2,1)S(1)} %fusion.77), channel_id=1, source_target_pairs={{0,2},{1,3},{2,0},{3,1},{4,6},{5,7},{6,4},{7,5},{8,10},{9,11},{10,... | collective-permute-start | bytes 196616 | tf_op jit(solution)/shard_map/ppermute | solution.py:29
  (16 other events, 102.4 us)

commit v11 on v10

--- a/solution.py
+++ b/solution.py
@@ -36,7 +36,7 @@
     return value + lax.ppermute(value, axis, pairs), anchor
 
 
-def scatter_rows(value, tally, axes, first_axis, wire_type, tail_first=False):
+def scatter_rows(value, tally, axes, first_axis, wire_type, tail_first=False, balance=True):
     sizes = [lax.axis_size(axis) for axis in axes]
     rows = value.shape[0]
     groups = math.prod(sizes)
@@ -78,7 +78,7 @@
     tail = [s for s in stages if s[0] != first[0]][::-1]
     if tail_first:
         value, names, tally = run_tail(value, names, tally)
-    if len(middle) > 1 and rest[-1] % 2 == 0:
+    if balance and len(middle) > 1 and rest[-1] % 2 == 0:
         cut = rest[-1] // 2
         left, right = value[..., :cut], value[..., cut:]
         left_names, right_names = list(names), list(names)
@@ -180,6 +180,7 @@
         "tm",
         jnp.bfloat16,
         tail_first=True,
+        balance=False,
     )
     owned = jnp.stack([grad_key[..., span * rows :], grad_value[..., span * rows :]])
     for offset in range(1, span + 1):

time: 172 us -> 174 us (1.012)
  starting transfers between devices: 52 us -> 48 us
  waiting for transfers between devices: 50.8 us -> 54.6 us
    ppermute x14 -> x12, starting transfers between devices: 24.1 us -> 20.1 us  [halve(): lax.ppermute(send.astype(send_type), axis, pairs).astype(keep.dtype)]
    ppermute x14 -> x12, waiting for transfers between devices: 26.4 us -> 30.2 us  [halve(): lax.ppermute(send.astype(send_type), axis, pairs).astype(keep.dtype)]
  transfers between devices with their start and end apart: 27 -> 25, of which waited for: 16 -> 15; matrix products, arithmetic and copies ran while one was open for 20% -> 19% of each run, Pallas kernels for 0% -> 0%
where the time goes in v11:
time: 174 us; the launch traced here: 173 us
  waiting for transfers between devices  54.6 us (31%)
  starting transfers between devices  48 us (28%)
  matrix products  31.3 us (18%)
  local copies, waits for them, and re-layouts  17.6 us (10%)
  other arithmetic  16.4 us (9%)
  between operations  5.12 us (3%)
    ppermute x12, waiting for transfers between devices, halve(): lax.ppermute(send.astype(send_type), axis, pairs).astype(keep.dtype)  30.2 us
    ppermute x12, starting transfers between devices, halve(): lax.ppermute(send.astype(send_type), axis, pairs).astype(keep.dtype)  20.1 us
    ppermute x8, starting transfers between devices, shifted(): return lax.ppermute(value, axis, pairs)  19.4 us
    ppermute x8, waiting for transfers between devices, shifted(): return lax.ppermute(value, axis, pairs)  16 us
    ppermute x5, starting transfers between devices, swap_add(): return (value + lax.ppermute(value, axis, pairs), anchor)  8.48 us
    ppermute x5, waiting for transfers between devices, swap_add(): return (value + lax.ppermute(value, axis, pairs), anchor)  8.43 us
    unnamed x30, local copies, waits for them, and re-layouts  7.04 us
    dot_general x1, matrix products, shards(): jnp.einsum('wrh,dwh->rd', grad_rows, weights, preferred_element_type=jnp....  5.2 us
  transfers between devices with their start and end apart: 25, of which 15 were waited for; matrix products, arithmetic and copies ran while one was open for 19% of the time, Pallas kernels for 0%

profile of v11, /device:TPU:0, one launch (start us, length us, event | category | flops | bytes accessed | tf_op | source)
XLA Modules:
  0.0 173.1 jit_solution(12110701133967212138)
XLA Ops:
  1.9 4.0 %fusion.23 = bf16[4,256,512]{2,1,0:T(8,128)(2,1)S(1)} fusion(bf16[1024,4,512]{2,1,0:T(4,128)(2,1)} %param.5, bf16[1,256,1024]{2,1,0:T(8,128)(2,1)} %param.4, f32[256]{0:T(256)S(1)} %add_rsqrt_fusion), kind=kOutput, calls=%fused_computation.29 | convolution fusion | flops 1075052544 | bytes 5768192 | tf_op jit(solution)/shard_map/rd,dwh->wrh/dot_general | solution.py:142
  6.7 5.7 %collective-permute-start = (bf16[2,256,512]{2,1,0:T(8,128)(2,1)}, bf16[2,256,512]{2,1,0:T(8,128)(2,1)}, u32[]{:S(2)}, u32[]{:S(2)}) collective-permute-start(bf16[2,256,512]{2,1,0:T(8,128)(2,1)} %slice.85), channel_id=1, source_target_pairs={{0,16},{4,20},{8,24},{12,28},{1,17},{5,21},{9,25},{13,29},{2,18},{... | collective-permute-start | bytes 1572872 | tf_op jit(solution)/shard_map/ppermute | solution.py:16
  12.4 3.4 %collective-permute-start.1 = (bf16[2,256,512]{2,1,0:T(8,128)(2,1)}, bf16[2,256,512]{2,1,0:T(8,128)(2,1)}, u32[]{:S(2)}, u32[]{:S(2)}) collective-permute-start(bf16[2,256,512]{2,1,0:T(8,128)(2,1)} %slice.85), channel_id=1, source_target_pairs={{0,12},{4,16},{8,20},{12,24},{16,28},{1,13},{5,17},{9,21},{13,25},... | collective-permute-start | bytes 1572872 | tf_op jit(solution)/shard_map/ppermute | solution.py:16
  15.7 2.9 %collective-permute-start.2 = (bf16[2,256,512]{2,1,0:T(8,128)(2,1)}, bf16[2,256,512]{2,1,0:T(8,128)(2,1)}, u32[]{:S(2)}, u32[]{:S(2)}) collective-permute-start(bf16[2,256,512]{2,1,0:T(8,128)(2,1)} %slice.85), channel_id=1, source_target_pairs={{0,8},{4,12},{8,16},{12,20},{16,24},{20,28},{1,9},{5,13},{9,17},{1... | collective-permute-start | bytes 1572872 | tf_op jit(solution)/shard_map/ppermute | solution.py:16
  22.0 4.8 %fusion.20 = bf16[4,256,512]{2,1,0:T(8,128)(2,1)} fusion(bf16[1024,4,512]{2,1,0:T(4,128)(2,1)} %param.5, bf16[1,256,1024]{2,1,0:T(8,128)(2,1)S(1)} %copy-done.9, pred[256]{0:T(512)(128)(4,1)S(1)} %compare_reduce_fusion), kind=kOutput, calls=%fused_computation.28 | convolution fusion | flops 1074528256 | bytes 5767424 | tf_op jit(solution)/shard_map/rd,dwh->wrh/dot_general | solution.py:153
  32.0 14.7 %collective-permute-done = bf16[2,256,512]{2,1,0:T(8,128)(2,1)} collective-permute-done((bf16[2,256,512]{2,1,0:T(8,128)(2,1)}, bf16[2,256,512]{2,1,0:T(8,128)(2,1)}, u32[]{:S(2)}, u32[]{:S(2)}) %collective-permute-start) | collective-permute-done | bytes 524320 | tf_op jit(solution)/shard_map/ppermute | solution.py:16
  55.4 3.9 %fusion.1 = (f32[8,256]{1,0:T(8,128)S(1)}, f32[8,256,1280]{2,1,0:T(8,128)S(1)}) fusion(f32[256,1280]{1,0:T(8,128)} %fusion.38, bf16[256,8,64]{0,2,1:T(8,128)(2,1)S(1)} %bitcast.188, bf16[1280,8,64]{0,2,1:T(8,128)(2,1)S(1)} %bitcast.185), kind=kOutput, calls=%fused_computation.3 | convolution fusion | flops 343406592 | bytes 13377536 | tf_op jit(solution)/shard_map/qgc,kgc->gqk/dot_general | solution.py:102
  59.3 2.8 %multiply_reduce_fusion = (f32[256,8]{0,1:T(8,128)S(1)}, bf16[8,64,256]{2,1,0:T(8,128)(2,1)S(1)}) fusion(bf16[256,8,64]{0,2,1:T(8,128)(2,1)S(1)} %bitcast.199, bf16[1280,8,64]{0,2,1:T(8,128)(2,1)S(1)} %bitcast.196, f32[8,256]{1,0:T(8,128)S(1)} %get-tuple-element.42, f32[256,1280]{1,0:T(8,128)S(1)} %copy-done, f32[8,256,1280]{2,1,0:T(8,128)S(1)} %get-tuple-element.43), kind=kOutput, calls=%fused_computation.83 | convolution fusion | flops 346683392 | bytes 13647872 | tf_op jit(solution)/shard_map/gqk,kgc->qgc/dot_general | solution.py:108
  62.1 3.9 %multiply_convert_fusion = bf16[8,256,1280]{2,1,0:T(8,128)(2,1)S(1)} fusion(bf16[256,8,64]{0,2,1:T(8,128)(2,1)S(1)} %bitcast.200, bf16[1280,8,64]{0,2,1:T(8,128)(2,1)S(1)} %bitcast.197, f32[8,256]{1,0:T(8,128)S(1)} %bitcast.203, f32[8,256]{1,0:T(8,128)S(1)} %get-tuple-element.42, f32[256,1280]{1,0:T(8,128)S(1)} %copy-done, ...), kind=kOutput, calls=%fused_computation | convolution fusion | flops 353894400 | bytes 18628608 | tf_op jit(solution)/shard_map/qgc,kgc->gqk/dot_general | solution.py:112
  70.0 3.6 %collective-permute-start.4 = (f32[2,2,2,2,32,2,512]{6,4,5,3,2,1,0:T(8,128)S(1)}, f32[2,2,2,2,32,2,512]{6,4,5,3,2,1,0:T(8,128)S(1)}, u32[]{:S(2)}, u32[]{:S(2)}) collective-permute-start(f32[2,2,2,2,32,2,512]{6,4,5,3,2,1,0:T(8,128)S(1)} %bitcast.193), channel_id=1, source_target_pairs={{0,4},{4,0},{8,12},{12,8},{16,20},{20,16},{24,28},{28,24},{1,5},{5... | collective-permute-start | bytes 6291464 | tf_op jit(solution)/shard_map/ppermute | solution.py:29
  74.6 2.3 %fusion.82 = (bf16[8,64,1280]{2,1,0:T(8,128)(2,1)S(1)}, f32[8,64,1280]{2,1,0:T(8,128)S(1)}) fusion(bf16[256,8,64]{0,2,1:T(8,128)(2,1)S(1)} %bitcast.201, f32[8,256]{1,0:T(8,128)S(1)} %get-tuple-element.42, f32[256,1280]{1,0:T(8,128)S(1)} %copy-done, f32[8,256,1280]{2,1,0:T(8,128)S(1)} %get-tuple-element.43), kind=kOutput, calls=%fused_computation.134 | convolution fusion | flops 346685440 | bytes 15998976 | tf_op jit(solution)/shard_map/gqk,qgc->gck/dot_general | solution.py:122
  92.6 4.4 %collective-permute-done.6 = bf16[2,2,2,32,2,512]{5,3,4,2,1,0:T(8,128)(2,1)} collective-permute-done((bf16[2,2,2,32,2,512]{5,3,4,2,1,0:T(8,128)(2,1)}, bf16[2,2,2,32,2,512]{5,3,4,2,1,0:T(8,128)(2,1)}, u32[]{:S(2)}, u32[]{:S(2)}) %collective-permute-start.6) | collective-permute-done | bytes 524320 | tf_op jit(solution)/shard_map/ppermute | solution.py:29
  98.3 2.7 %collective-permute-start.8 = (bf16[2,2,32,2,512]{4,2,3,1,0:T(8,128)(2,1)S(1)}, bf16[2,2,32,2,512]{4,2,3,1,0:T(8,128)(2,1)S(1)}, u32[]{:S(2)}, u32[]{:S(2)}) collective-permute-start(bf16[2,2,32,2,512]{4,2,3,1,0:T(8,128)(2,1)S(1)} %fusion.59), channel_id=1, source_target_pairs={{0,2},{1,3},{2,0},{3,1},{4,6},{5,7},{6,4},{7,5},{8,10},{9,11},{10,... | collective-permute-start | bytes 786440 | tf_op jit(solution)/shard_map/ppermute | solution.py:29
  109.7 2.6 %collective-permute-done.8 = bf16[2,2,32,2,512]{4,2,3,1,0:T(8,128)(2,1)S(1)} collective-permute-done((bf16[2,2,32,2,512]{4,2,3,1,0:T(8,128)(2,1)S(1)}, bf16[2,2,32,2,512]{4,2,3,1,0:T(8,128)(2,1)S(1)}, u32[]{:S(2)}, u32[]{:S(2)}) %collective-permute-start.8) | collective-permute-done | bytes 262176 | tf_op jit(solution)/shard_map/ppermute | solution.py:29
  112.4 4.9 %collective-permute-start.10 = (bf16[2,32,2,512]{3,1,2,0:T(8,128)(2,1)S(1)}, bf16[2,32,2,512]{3,1,2,0:T(8,128)(2,1)S(1)}, u32[]{:S(2)}, u32[]{:S(2)}) collective-permute-start(bf16[2,32,2,512]{3,1,2,0:T(8,128)(2,1)S(1)} %fusion.70), channel_id=1, source_target_pairs={{0,16},{4,20},{8,24},{12,28},{16,0},{20,4},{24,8},{28,12},{1,17},{... | collective-permute-start | bytes 393224 | tf_op jit(solution)/shard_map/ppermute | solution.py:29
  117.3 5.2 %fusion.42 = (f32[256]{0:T(256)S(1)}, f32[256,1024]{1,0:T(8,128)}) fusion(bf16[1,256,1024]{2,1,0:T(8,128)(2,1)S(1)} %copy-done.1, f32[256]{0:T(256)S(1)} %add_rsqrt_fusion, bf16[4,256,512]{1,2,0:T(8,128)(2,1)} %bitcast.198, bf16[1024,4,512]{2,1,0:T(4,128)(2,1)} %param.5), kind=kOutput, calls=%fused_computation.46 | convolution fusion | flops 1074790144 | bytes 6817792 | tf_op jit(solution)/shard_map/wrh,dwh->rd/dot_general | solution.py:195
  122.5 3.1 %collective-permute-start.9 = (s32[]{:T(128)}, s32[]{:T(128)}, u32[]{:S(2)}, u32[]{:S(2)}) collective-permute-start(s32[]{:T(128)} %add.178), channel_id=1, source_target_pairs={{0,2},{1,3},{2,0},{3,1},{4,6},{5,7},{6,4},{7,5},{8,10},{9,11},{10,... | collective-permute-start | bytes 20 | tf_op jit(solution)/shard_map/ppermute | solution.py:36
  130.4 2.3 %collective-permute-done.11 = s32[]{:T(128)} collective-permute-done((s32[]{:T(128)}, s32[]{:T(128)}, u32[]{:S(2)}, u32[]{:S(2)}) %collective-permute-start.11) | collective-permute-done | bytes 36 | tf_op jit(solution)/shard_map/ppermute | solution.py:36
  137.8 2.3 %fusion.68 = (bf16[1024,256]{0,1:T(8,128)(2,1)S(1)}, bf16[1,256,1024]{2,1,0:T(8,128)(2,1)}) fusion(f32[256]{0:T(256)S(1)} %add_rsqrt_fusion, bf16[1,256,1024]{2,1,0:T(8,128)(2,1)S(1)} %copy-done.1, f32[256,1024]{1,0:T(8,128)} %get-tuple-element.51, f32[256]{0:T(256)S(1)} %broadcast_multiply_fusion, f32[]{:T(128)S(6)} %div.63), kind=kLoop, calls=%fused_computation.110 | loop fusion | flops 2097152 | bytes 2623492 | tf_op jit(solution)/shard_map/rd,wgcr->dwgc/dot_general | solution.py:200
  141.4 4.1 %collective-permute-done.18 = f32[2,2,2,2,32,2,512]{6,4,5,3,2,1,0:T(8,128)S(1)} collective-permute-done((f32[2,2,2,2,32,2,512]{6,4,5,3,2,1,0:T(8,128)S(1)}, f32[2,2,2,2,32,2,512]{6,4,5,3,2,1,0:T(8,128)S(1)}, u32[]{:S(2)}, u32[]{:S(2)}) %collective-permute-start.18) | collective-permute-done | bytes 2097184 | tf_op jit(solution)/shard_map/ppermute | solution.py:29
  147.5 7.4 %collective-permute-done.19 = bf16[2,2,2,32,2,256]{5,3,4,2,1,0:T(8,128)(2,1)S(1)} collective-permute-done((bf16[2,2,2,32,2,256]{5,3,4,2,1,0:T(8,128)(2,1)S(1)}, bf16[2,2,2,32,2,256]{5,3,4,2,1,0:T(8,128)(2,1)S(1)}, u32[]{:S(2)}, u32[]{:S(2)}) %collective-permute-start.19) | collective-permute-done | bytes 262176 | tf_op jit(solution)/shard_map/ppermute | solution.py:29
  156.9 3.1 %collective-permute-done.20 = bf16[2,2,32,2,256]{4,2,3,1,0:T(8,128)(2,1)S(1)} collective-permute-done((bf16[2,2,32,2,256]{4,2,3,1,0:T(8,128)(2,1)S(1)}, bf16[2,2,32,2,256]{4,2,3,1,0:T(8,128)(2,1)S(1)}, u32[]{:S(2)}, u32[]{:S(2)}) %collective-permute-start.20) | collective-permute-done | bytes 131104 | tf_op jit(solution)/shard_map/ppermute | solution.py:29
  162.3 3.8 %collective-permute-done.23 = bf16[2,32,2,512]{3,1,2,0:T(8,128)(2,1)S(1)} collective-permute-done((bf16[2,32,2,512]{3,1,2,0:T(8,128)(2,1)S(1)}, bf16[2,32,2,512]{3,1,2,0:T(8,128)(2,1)S(1)}, u32[]{:S(2)}, u32[]{:S(2)}) %collective-permute-start.23) | collective-permute-done | bytes 131104 | tf_op jit(solution)/shard_map/ppermute | solution.py:29
  168.4 3.8 %collective-permute-done.24 = bf16[32,2,512]{2,0,1:T(8,128)(2,1)S(1)} collective-permute-done((bf16[32,2,512]{2,0,1:T(8,128)(2,1)S(1)}, bf16[32,2,512]{2,0,1:T(8,128)(2,1)S(1)}, u32[]{:S(2)}, u32[]{:S(2)}) %collective-permute-start.24) | collective-permute-done | bytes 65568 | tf_op jit(solution)/shard_map/ppermute | solution.py:29
  (127 shorter events, 66.3 us)
Async XLA Ops:
  6.7 40.0 %collective-permute-start = (bf16[2,256,512]{2,1,0:T(8,128)(2,1)}, bf16[2,256,512]{2,1,0:T(8,128)(2,1)}, u32[]{:S(2)}, u32[]{:S(2)}) collective-permute-start(bf16[2,256,512]{2,1,0:T(8,128)(2,1)} %slice.85), channel_id=1, source_target_pairs={{0,16},{4,20},{8,24},{12,28},{1,17},{5,21},{9,25},{13,29},{2,18},{... | collective-permute-start | bytes 1572872 | tf_op jit(solution)/shard_map/ppermute | solution.py:16
  12.4 35.4 %collective-permute-start.1 = (bf16[2,256,512]{2,1,0:T(8,128)(2,1)}, bf16[2,256,512]{2,1,0:T(8,128)(2,1)}, u32[]{:S(2)}, u32[]{:S(2)}) collective-permute-start(bf16[2,256,512]{2,1,0:T(8,128)(2,1)} %slice.85), channel_id=1, source_target_pairs={{0,12},{4,16},{8,20},{12,24},{16,28},{1,13},{5,17},{9,21},{13,25},... | collective-permute-start | bytes 1572872 | tf_op jit(solution)/shard_map/ppermute | solution.py:16
  15.7 33.1 %collective-permute-start.2 = (bf16[2,256,512]{2,1,0:T(8,128)(2,1)}, bf16[2,256,512]{2,1,0:T(8,128)(2,1)}, u32[]{:S(2)}, u32[]{:S(2)}) collective-permute-start(bf16[2,256,512]{2,1,0:T(8,128)(2,1)} %slice.85), channel_id=1, source_target_pairs={{0,8},{4,12},{8,16},{12,20},{16,24},{20,28},{1,9},{5,13},{9,17},{1... | collective-permute-start | bytes 1572872 | tf_op jit(solution)/shard_map/ppermute | solution.py:16
  18.7 31.3 %collective-permute-start.3 = (bf16[2,256,512]{2,1,0:T(8,128)(2,1)}, bf16[2,256,512]{2,1,0:T(8,128)(2,1)}, u32[]{:S(2)}, u32[]{:S(2)}) collective-permute-start(bf16[2,256,512]{2,1,0:T(8,128)(2,1)} %slice.85), channel_id=1, source_target_pairs={{0,4},{4,8},{8,12},{12,16},{16,20},{20,24},{24,28},{1,5},{5,9},{9,... | collective-permute-start | bytes 1572872 | tf_op jit(solution)/shard_map/ppermute | solution.py:16
  70.0 11.5 %collective-permute-start.4 = (f32[2,2,2,2,32,2,512]{6,4,5,3,2,1,0:T(8,128)S(1)}, f32[2,2,2,2,32,2,512]{6,4,5,3,2,1,0:T(8,128)S(1)}, u32[]{:S(2)}, u32[]{:S(2)}) collective-permute-start(f32[2,2,2,2,32,2,512]{6,4,5,3,2,1,0:T(8,128)S(1)} %bitcast.193), channel_id=1, source_target_pairs={{0,4},{4,0},{8,12},{12,8},{16,20},{20,16},{24,28},{28,24},{1,5},{5... | collective-permute-start | bytes 6291464 | tf_op jit(solution)/shard_map/ppermute | solution.py:29
  78.1 22.9 %collective-permute-start.17 = (bf16[2,8,64,256]{3,2,1,0:T(8,128)(2,1)}, bf16[2,8,64,256]{3,2,1,0:T(8,128)(2,1)}, u32[]{:S(2)}, u32[]{:S(2)}) collective-permute-start(bf16[2,8,64,256]{3,2,1,0:T(8,128)(2,1)} %pad_maximum_fusion.3), channel_id=1, source_target_pairs={{16,0},{20,4},{24,8},{28,12},{17,1},{21,5},{25,9},{29,13},{18,2},{... | collective-permute-start | bytes 1572872 | tf_op jit(solution)/shard_map/ppermute | solution.py:16
  80.2 20.8 %collective-permute-start.16 = (bf16[2,8,64,256]{3,2,1,0:T(8,128)(2,1)}, bf16[2,8,64,256]{3,2,1,0:T(8,128)(2,1)}, u32[]{:S(2)}, u32[]{:S(2)}) collective-permute-start(bf16[2,8,64,256]{3,2,1,0:T(8,128)(2,1)} %pad_maximum_fusion.2), channel_id=1, source_target_pairs={{12,0},{16,4},{20,8},{24,12},{28,16},{13,1},{17,5},{21,9},{25,13},... | collective-permute-start | bytes 1572872 | tf_op jit(solution)/shard_map/ppermute | solution.py:16
  82.9 14.2 %collective-permute-start.6 = (bf16[2,2,2,32,2,512]{5,3,4,2,1,0:T(8,128)(2,1)}, bf16[2,2,2,32,2,512]{5,3,4,2,1,0:T(8,128)(2,1)}, u32[]{:S(2)}, u32[]{:S(2)}) collective-permute-start(bf16[2,2,2,32,2,512]{5,3,4,2,1,0:T(8,128)(2,1)} %fusion.53), channel_id=1, source_target_pairs={{0,1},{1,0},{2,3},{3,2},{4,5},{5,4},{6,7},{7,6},{8,9},{9,8},{10,11... | collective-permute-start | bytes 1572872 | tf_op jit(solution)/shard_map/ppermute | solution.py:29
  85.3 17.0 %collective-permute-start.15 = (bf16[2,8,64,256]{3,2,1,0:T(8,128)(2,1)}, bf16[2,8,64,256]{3,2,1,0:T(8,128)(2,1)}, u32[]{:S(2)}, u32[]{:S(2)}) collective-permute-start(bf16[2,8,64,256]{3,2,1,0:T(8,128)(2,1)} %pad_maximum_fusion.1), channel_id=1, source_target_pairs={{8,0},{12,4},{16,8},{20,12},{24,16},{28,20},{9,1},{13,5},{17,9},{2... | collective-permute-start | bytes 1572872 | tf_op jit(solution)/shard_map/ppermute | solution.py:16
  88.8 13.5 %collective-permute-start.14 = (bf16[2,8,64,256]{3,2,1,0:T(8,128)(2,1)}, bf16[2,8,64,256]{3,2,1,0:T(8,128)(2,1)}, u32[]{:S(2)}, u32[]{:S(2)}) collective-permute-start(bf16[2,8,64,256]{3,2,1,0:T(8,128)(2,1)} %pad_maximum_fusion), channel_id=1, source_target_pairs={{4,0},{8,4},{12,8},{16,12},{20,16},{24,20},{28,24},{5,1},{9,5},{13... | collective-permute-start | bytes 1572872 | tf_op jit(solution)/shard_map/ppermute | solution.py:16
  98.3 14.0 %collective-permute-start.8 = (bf16[2,2,32,2,512]{4,2,3,1,0:T(8,128)(2,1)S(1)}, bf16[2,2,32,2,512]{4,2,3,1,0:T(8,128)(2,1)S(1)}, u32[]{:S(2)}, u32[]{:S(2)}) collective-permute-start(bf16[2,2,32,2,512]{4,2,3,1,0:T(8,128)(2,1)S(1)} %fusion.59), channel_id=1, source_target_pairs={{0,2},{1,3},{2,0},{3,1},{4,6},{5,7},{6,4},{7,5},{8,10},{9,11},{10,... | collective-permute-start | bytes 786440 | tf_op jit(solution)/shard_map/ppermute | solution.py:29
  105.4 3.7 %collective-permute-start.7 = (s32[]{:T(128)}, s32[]{:T(128)}, u32[]{:S(2)}, u32[]{:S(2)}) collective-permute-start(s32[]{:T(128)} %add.173), channel_id=1, source_target_pairs={{0,1},{1,0},{2,3},{3,2},{4,5},{5,4},{6,7},{7,6},{8,9},{9,8},{10,11... | collective-permute-start | bytes 20 | tf_op jit(solution)/shard_map/ppermute | solution.py:36
  112.4 15.3 %collective-permute-start.10 = (bf16[2,32,2,512]{3,1,2,0:T(8,128)(2,1)S(1)}, bf16[2,32,2,512]{3,1,2,0:T(8,128)(2,1)S(1)}, u32[]{:S(2)}, u32[]{:S(2)}) collective-permute-start(bf16[2,32,2,512]{3,1,2,0:T(8,128)(2,1)S(1)} %fusion.70), channel_id=1, source_target_pairs={{0,16},{4,20},{8,24},{12,28},{16,0},{20,4},{24,8},{28,12},{1,17},{... | collective-permute-start | bytes 393224 | tf_op jit(solution)/shard_map/ppermute | solution.py:29
  122.5 4.5 %collective-permute-start.9 = (s32[]{:T(128)}, s32[]{:T(128)}, u32[]{:S(2)}, u32[]{:S(2)}) collective-permute-start(s32[]{:T(128)} %add.178), channel_id=1, source_target_pairs={{0,2},{1,3},{2,0},{3,1},{4,6},{5,7},{6,4},{7,5},{8,10},{9,11},{10,... | collective-permute-start | bytes 20 | tf_op jit(solution)/shard_map/ppermute | solution.py:36
  127.8 5.6 %collective-permute-start.12 = (bf16[32,2,512]{2,0,1:T(8,128)(2,1)S(1)}, bf16[32,2,512]{2,0,1:T(8,128)(2,1)S(1)}, u32[]{:S(2)}, u32[]{:S(2)}) collective-permute-start(bf16[32,2,512]{2,0,1:T(8,128)(2,1)S(1)} %fusion.74), channel_id=1, source_target_pairs={{0,8},{4,12},{8,0},{12,4},{16,24},{20,28},{24,16},{28,20},{1,9},{5... | collective-permute-start | bytes 196616 | tf_op jit(solution)/shard_map/ppermute | solution.py:29
  129.0 3.6 %collective-permute-start.11 = (s32[]{:T(128)}, s32[]{:T(128)}, u32[]{:S(2)}, u32[]{:S(2)}) collective-permute-start(s32[]{:T(128)} %add.183), channel_id=1, source_target_pairs={{0,16},{4,20},{8,24},{12,28},{16,0},{20,4},{24,8},{28,12},{1,17},{... | collective-permute-start | bytes 20 | tf_op jit(solution)/shard_map/ppermute | solution.py:36
  133.4 3.7 %collective-permute-start.13 = (s32[]{:T(128)}, s32[]{:T(128)}, u32[]{:S(2)}, u32[]{:S(2)}) collective-permute-start(s32[]{:T(128)} %add.188), channel_id=1, source_target_pairs={{0,8},{4,12},{8,0},{12,4},{16,24},{20,28},{24,16},{28,20},{1,9},{5... | collective-permute-start | bytes 20 | tf_op jit(solution)/shard_map/ppermute | solution.py:36
  141.3 4.2 %collective-permute-start.18 = (f32[2,2,2,2,32,2,512]{6,4,5,3,2,1,0:T(8,128)S(1)}, f32[2,2,2,2,32,2,512]{6,4,5,3,2,1,0:T(8,128)S(1)}, u32[]{:S(2)}, u32[]{:S(2)}) collective-permute-start(f32[2,2,2,2,32,2,512]{6,4,5,3,2,1,0:T(8,128)S(1)} %dynamic-slice_bitcast_fusion), channel_id=1, source_target_pairs={{0,4},{4,0},{8,12},{12,8},{16,20},{20,16},{24,28},{28,24},{1,5},{5... | collective-permute-start | bytes 6291464 | tf_op jit(solution)/shard_map/ppermute | solution.py:29
  146.5 8.4 %collective-permute-start.19 = (bf16[2,2,2,32,2,256]{5,3,4,2,1,0:T(8,128)(2,1)S(1)}, bf16[2,2,2,32,2,256]{5,3,4,2,1,0:T(8,128)(2,1)S(1)}, u32[]{:S(2)}, u32[]{:S(2)}) collective-permute-start(bf16[2,2,2,32,2,256]{5,3,4,2,1,0:T(8,128)(2,1)S(1)} %fusion.60), channel_id=1, source_target_pairs={{0,16},{4,20},{8,24},{12,28},{16,0},{20,4},{24,8},{28,12},{1,17},{... | collective-permute-start | bytes 786440 | tf_op jit(solution)/shard_map/ppermute | solution.py:29
  146.6 9.3 %collective-permute-start.21 = (bf16[2,2,2,32,2,256]{5,3,4,2,1,0:T(8,128)(2,1)S(1)}, bf16[2,2,2,32,2,256]{5,3,4,2,1,0:T(8,128)(2,1)S(1)}, u32[]{:S(2)}, u32[]{:S(2)}) collective-permute-start(bf16[2,2,2,32,2,256]{5,3,4,2,1,0:T(8,128)(2,1)S(1)} %fusion.61), channel_id=1, source_target_pairs={{0,8},{4,12},{8,0},{12,4},{16,24},{20,28},{24,16},{28,20},{1,9},{5... | collective-permute-start | bytes 786440 | tf_op jit(solution)/shard_map/ppermute | solution.py:29
  155.0 5.0 %collective-permute-start.20 = (bf16[2,2,32,2,256]{4,2,3,1,0:T(8,128)(2,1)S(1)}, bf16[2,2,32,2,256]{4,2,3,1,0:T(8,128)(2,1)S(1)}, u32[]{:S(2)}, u32[]{:S(2)}) collective-permute-start(bf16[2,2,32,2,256]{4,2,3,1,0:T(8,128)(2,1)S(1)} %fusion.71), channel_id=1, source_target_pairs={{0,8},{4,12},{8,0},{12,4},{16,24},{20,28},{24,16},{28,20},{1,9},{5... | collective-permute-start | bytes 393224 | tf_op jit(solution)/shard_map/ppermute | solution.py:29
  156.0 5.0 %collective-permute-start.22 = (bf16[2,2,32,2,256]{4,2,3,1,0:T(8,128)(2,1)S(1)}, bf16[2,2,32,2,256]{4,2,3,1,0:T(8,128)(2,1)S(1)}, u32[]{:S(2)}, u32[]{:S(2)}) collective-permute-start(bf16[2,2,32,2,256]{4,2,3,1,0:T(8,128)(2,1)S(1)} %fusion.72), channel_id=1, source_target_pairs={{0,16},{4,20},{8,24},{12,28},{16,0},{20,4},{24,8},{28,12},{1,17},{... | collective-permute-start | bytes 393224 | tf_op jit(solution)/shard_map/ppermute | solution.py:29
  161.1 5.0 %collective-permute-start.23 = (bf16[2,32,2,512]{3,1,2,0:T(8,128)(2,1)S(1)}, bf16[2,32,2,512]{3,1,2,0:T(8,128)(2,1)S(1)}, u32[]{:S(2)}, u32[]{:S(2)}) collective-permute-start(bf16[2,32,2,512]{3,1,2,0:T(8,128)(2,1)S(1)} %fusion.73), channel_id=1, source_target_pairs={{0,1},{1,0},{2,3},{3,2},{4,5},{5,4},{6,7},{7,6},{8,9},{9,8},{10,11... | collective-permute-start | bytes 393224 | tf_op jit(solution)/shard_map/ppermute | solution.py:29
  166.2 5.9 %collective-permute-start.24 = (bf16[32,2,512]{2,0,1:T(8,128)(2,1)S(1)}, bf16[32,2,512]{2,0,1:T(8,128)(2,1)S(1)}, u32[]{:S(2)}, u32[]{:S(2)}) collective-permute-start(bf16[32,2,512]{2,0,1:T(8,128)(2,1)S(1)} %fusion.75), channel_id=1, source_target_pairs={{0,2},{1,3},{2,0},{3,1},{4,6},{5,7},{6,4},{7,5},{8,10},{9,11},{10,... | collective-permute-start | bytes 196616 | tf_op jit(solution)/shard_map/ppermute | solution.py:29
  (14 other events, 95.3 us)

commit v12 on v10

--- a/solution.py
+++ b/solution.py
@@ -29,6 +29,22 @@
     return keep + lax.ppermute(send.astype(send_type), axis, pairs).astype(keep.dtype)
 
 
+def exchange_all(value, dims, axis, flips, send_type):
+    peers = lax.axis_size(axis)
+    me = lax.axis_index(axis)
+    count = len(flips)
+    code = sum(((me // f) % 2) * (1 << (count - 1 - j)) for j, f in enumerate(flips))
+    lead = value.shape[:count]
+    merged = value.reshape((math.prod(lead),) + value.shape[count:])
+    total = lax.dynamic_index_in_dim(merged, code, 0, keepdims=False)
+    for m in range(1, 1 << count):
+        mask = sum(f for j, f in enumerate(flips) if (m >> (count - 1 - j)) & 1)
+        send = lax.dynamic_index_in_dim(merged, code ^ m, 0, keepdims=False)
+        pairs = [(i, i ^ mask) for i in range(peers)]
+        total = total + lax.ppermute(send.astype(send_type), axis, pairs).astype(total.dtype)
+    return total
+
+
 def swap_add(value, anchor, axis, flip):
     value, anchor = lax.optimization_barrier((value, anchor))
     peers = lax.axis_size(axis)
@@ -36,7 +52,7 @@
     return value + lax.ppermute(value, axis, pairs), anchor
 
 
-def scatter_rows(value, tally, axes, first_axis, wire_type, tail_first=False):
+def scatter_rows(value, tally, axes, first_axis, wire_type, tail_first=False, direct=True):
     sizes = [lax.axis_size(axis) for axis in axes]
     rows = value.shape[0]
     groups = math.prod(sizes)
@@ -66,7 +82,19 @@
             return tally, anchor
         return swap_add(tally, anchor, *stage)
 
+    def run_group(value, names, tally, group):
+        dim = names.index(group[0])
+        assert names[dim : dim + len(group)] == list(group)
+        moved = jnp.moveaxis(value, list(range(dim, dim + len(group))), list(range(len(group))))
+        value = exchange_all(moved, None, group[0][0], [s[1] for s in group], wire_type)
+        names = names[:dim] + names[dim + len(group) :]
+        for stage in group:
+            tally, value = count_along(tally, value, stage)
+        return value, names, tally
+
     def run_tail(value, names, tally):
+        if direct and len(tail) > 1:
+            return run_group(value, names, tally, sorted(tail, key=names.index))
         for stage in tail:
             value, names = step(value, names, stage, wire_type)
             tally, value = count_along(tally, value, stage)
@@ -78,7 +106,9 @@
     tail = [s for s in stages if s[0] != first[0]][::-1]
     if tail_first:
         value, names, tally = run_tail(value, names, tally)
-    if len(middle) > 1 and rest[-1] % 2 == 0:
+    if direct and len(middle) > 1:
+        value, names, tally = run_group(value, names, tally, sorted(middle, key=names.index))
+    elif len(middle) > 1 and rest[-1] % 2 == 0:
         cut = rest[-1] // 2
         left, right = value[..., :cut], value[..., cut:]
         left_names, right_names = list(names), list(names)

time: 172 us -> 205 us (1.19)
  waiting for transfers between devices: 50.8 us -> 64.8 us
  starting transfers between devices: 52 us -> 61.7 us
  other arithmetic: 15.1 us -> 21.1 us
  local copies, waits for them, and re-layouts: 17.7 us -> 20.7 us
    ppermute x0 -> x12, waiting for transfers between devices: none -> 26.8 us  [exchange_all(): lax.ppermute(send.astype(send_type), axis, pairs).astype(total.dtype)]
    ppermute x0 -> x12, starting transfers between devices: none -> 24 us  [exchange_all(): lax.ppermute(send.astype(send_type), axis, pairs).astype(total.dtype)]
    ppermute x14 -> x2, waiting for transfers between devices: 26.4 us -> 4.15 us  [halve(): lax.ppermute(send.astype(send_type), axis, pairs).astype(keep.dtype)]
    ppermute x14 -> x2, starting transfers between devices: 24.1 us -> 3.56 us  [halve(): lax.ppermute(send.astype(send_type), axis, pairs).astype(keep.dtype)]
    ppermute x8, waiting for transfers between devices: 16.1 us -> 27.3 us  [shifted(): return lax.ppermute(value, axis, pairs)]
    ppermute x5, starting transfers between devices: 8.52 us -> 14.8 us  [swap_add(): return (value + lax.ppermute(value, axis, pairs), anchor)]
    add x0 -> x4, other arithmetic: none -> 3.57 us  [exchange_all(): total + lax.ppermute(send.astype(send_type), axis, pairs).astype(total.dt...]
    unnamed x30 -> x35, local copies, waits for them, and re-layouts: 7.04 us -> 6.67 us
  transfers between devices with their start and end apart: 27 -> 27, of which waited for: 16 -> 14; matrix products, arithmetic and copies ran while one was open for 20% -> 13% of each run, Pallas kernels for 0% -> 0%
where the time goes in v12:
time: 205 us; the launch traced here: 204 us
  waiting for transfers between devices  64.8 us (32%)
  starting transfers between devices  61.7 us (30%)
  matrix products  30.9 us (15%)
  other arithmetic  21.1 us (10%)
  local copies, waits for them, and re-layouts  20.7 us (10%)
  between operations  5.04 us (2%)
    ppermute x8, waiting for transfers between devices, shifted(): return lax.ppermute(value, axis, pairs)  27.3 us
    ppermute x12, waiting for transfers between devices, exchange_all(): lax.ppermute(send.astype(send_type), axis, pairs).astype(total.dtype)  26.8 us
    ppermute x12, starting transfers between devices, exchange_all(): lax.ppermute(send.astype(send_type), axis, pairs).astype(total.dtype)  24 us
    ppermute x8, starting transfers between devices, shifted(): return lax.ppermute(value, axis, pairs)  19.3 us
    ppermute x5, starting transfers between devices, swap_add(): return (value + lax.ppermute(value, axis, pairs), anchor)  14.8 us
    unnamed x35, local copies, waits for them, and re-layouts  6.67 us
    ppermute x5, waiting for transfers between devices, swap_add(): return (value + lax.ppermute(value, axis, pairs), anchor)  6.55 us
    dot_general x1, matrix products, shards(): jnp.einsum('rd,dwh->wrh', grad_out, weights, preferred_element_type=jnp.f...  4.81 us
  transfers between devices with their start and end apart: 27, of which 14 were waited for; matrix products, arithmetic and copies ran while one was open for 13% of the time, Pallas kernels for 0%

profile of v12, /device:TPU:0, one launch (start us, length us, event | category | flops | bytes accessed | tf_op | source)
XLA Modules:
  0.0 204.2 jit_solution(12719759926084609726)
XLA Ops:
  1.9 4.0 %fusion.23 = bf16[4,256,512]{2,1,0:T(8,128)(2,1)S(1)} fusion(bf16[1024,4,512]{2,1,0:T(4,128)(2,1)} %param.5, bf16[1,256,1024]{2,1,0:T(8,128)(2,1)} %param.4, f32[256]{0:T(256)S(1)} %add_rsqrt_fusion), kind=kOutput, calls=%fused_computation.29 | convolution fusion | flops 1075052544 | bytes 5768192 | tf_op jit(solution)/shard_map/rd,dwh->wrh/dot_general | solution.py:172
  6.7 5.7 %collective-permute-start = (bf16[2,256,512]{2,1,0:T(8,128)(2,1)}, bf16[2,256,512]{2,1,0:T(8,128)(2,1)}, u32[]{:S(2)}, u32[]{:S(2)}) collective-permute-start(bf16[2,256,512]{2,1,0:T(8,128)(2,1)} %slice.77), channel_id=1, source_target_pairs={{0,16},{4,20},{8,24},{12,28},{1,17},{5,21},{9,25},{13,29},{2,18},{... | collective-permute-start | bytes 1572872 | tf_op jit(solution)/shard_map/ppermute | solution.py:16
  12.4 3.4 %collective-permute-start.1 = (bf16[2,256,512]{2,1,0:T(8,128)(2,1)}, bf16[2,256,512]{2,1,0:T(8,128)(2,1)}, u32[]{:S(2)}, u32[]{:S(2)}) collective-permute-start(bf16[2,256,512]{2,1,0:T(8,128)(2,1)} %slice.77), channel_id=1, source_target_pairs={{0,12},{4,16},{8,20},{12,24},{16,28},{1,13},{5,17},{9,21},{13,25},... | collective-permute-start | bytes 1572872 | tf_op jit(solution)/shard_map/ppermute | solution.py:16
  15.7 2.9 %collective-permute-start.2 = (bf16[2,256,512]{2,1,0:T(8,128)(2,1)}, bf16[2,256,512]{2,1,0:T(8,128)(2,1)}, u32[]{:S(2)}, u32[]{:S(2)}) collective-permute-start(bf16[2,256,512]{2,1,0:T(8,128)(2,1)} %slice.77), channel_id=1, source_target_pairs={{0,8},{4,12},{8,16},{12,20},{16,24},{20,28},{1,9},{5,13},{9,17},{1... | collective-permute-start | bytes 1572872 | tf_op jit(solution)/shard_map/ppermute | solution.py:16
  22.0 4.8 %fusion.20 = bf16[4,256,512]{2,1,0:T(8,128)(2,1)} fusion(bf16[1024,4,512]{2,1,0:T(4,128)(2,1)} %param.5, bf16[1,256,1024]{2,1,0:T(8,128)(2,1)S(1)} %copy-done.8, pred[256]{0:T(512)(128)(4,1)S(1)} %compare_reduce_fusion), kind=kOutput, calls=%fused_computation.28 | convolution fusion | flops 1074528256 | bytes 5767424 | tf_op jit(solution)/shard_map/rd,dwh->wrh/dot_general | solution.py:183
  31.1 15.6 %collective-permute-done = bf16[2,256,512]{2,1,0:T(8,128)(2,1)} collective-permute-done((bf16[2,256,512]{2,1,0:T(8,128)(2,1)}, bf16[2,256,512]{2,1,0:T(8,128)(2,1)}, u32[]{:S(2)}, u32[]{:S(2)}) %collective-permute-start) | collective-permute-done | bytes 524320 | tf_op jit(solution)/shard_map/ppermute | solution.py:16
  55.4 4.1 %fusion.1 = (f32[8,256]{1,0:T(8,128)S(1)}, f32[8,256,1280]{2,1,0:T(8,128)S(1)}) fusion(f32[256,1280]{1,0:T(8,128)} %fusion.38, bf16[256,8,64]{0,2,1:T(8,128)(2,1)S(1)} %bitcast.210, bf16[1280,8,64]{0,2,1:T(8,128)(2,1)S(1)} %bitcast.202), kind=kOutput, calls=%fused_computation.3 | convolution fusion | flops 343406592 | bytes 13377536 | tf_op jit(solution)/shard_map/qgc,kgc->gqk/dot_general | solution.py:132
  59.5 3.9 %fusion.80 = (bf16[8,64,1280]{2,1,0:T(8,128)(2,1)S(1)}, f32[8,64,1280]{2,1,0:T(8,128)}) fusion(bf16[256,8,64]{0,2,1:T(8,128)(2,1)S(1)} %bitcast.224, f32[8,256]{1,0:T(8,128)S(1)} %get-tuple-element.50, f32[256,1280]{1,0:T(8,128)S(1)} %copy-done.1, f32[8,256,1280]{2,1,0:T(8,128)S(1)} %get-tuple-element.51), kind=kOutput, calls=%fused_computation.134 | convolution fusion | flops 346685440 | bytes 15998976 | tf_op jit(solution)/shard_map/gqk,qgc->gck/dot_general | solution.py:152
  63.4 2.9 %multiply_reduce_fusion = (f32[256,8]{0,1:T(8,128)S(1)}, bf16[8,64,256]{2,1,0:T(8,128)(2,1)S(1)}) fusion(bf16[256,8,64]{0,2,1:T(8,128)(2,1)S(1)} %bitcast.225, bf16[1280,8,64]{0,2,1:T(8,128)(2,1)S(1)} %bitcast.221, f32[8,256]{1,0:T(8,128)S(1)} %get-tuple-element.50, f32[256,1280]{1,0:T(8,128)S(1)} %copy-done.1, f32[8,256,1280]{2,1,0:T(8,128)S(1)} %get-tuple-element.51), kind=kOutput, calls=%fused_computation.82 | convolution fusion | flops 346683392 | bytes 13647872 | tf_op jit(solution)/shard_map/gqk,kgc->qgc/dot_general | solution.py:138
  66.3 4.1 %multiply_convert_fusion = bf16[8,256,1280]{2,1,0:T(8,128)(2,1)S(1)} fusion(bf16[256,8,64]{0,2,1:T(8,128)(2,1)S(1)} %bitcast.226, bf16[1280,8,64]{0,2,1:T(8,128)(2,1)S(1)} %bitcast.222, f32[8,256]{1,0:T(8,128)S(1)} %bitcast.234, f32[8,256]{1,0:T(8,128)S(1)} %get-tuple-element.50, f32[256,1280]{1,0:T(8,128)S(1)} %copy-done.1, ...), kind=kOutput, calls=%fused_computation | convolution fusion | flops 353894400 | bytes 18628608 | tf_op jit(solution)/shard_map/qgc,kgc->gqk/dot_general | solution.py:142
  77.4 3.5 %collective-permute-start.4 = (f32[2,2,2,2,32,2,512]{6,4,5,3,2,1,0:T(8,128)}, f32[2,2,2,2,32,2,512]{6,4,5,3,2,1,0:T(8,128)}, u32[]{:S(2)}, u32[]{:S(2)}) collective-permute-start(f32[2,2,2,2,32,2,512]{6,4,5,3,2,1,0:T(8,128)} %bitcast.195), channel_id=1, source_target_pairs={{0,4},{4,0},{8,12},{12,8},{16,20},{20,16},{24,28},{28,24},{1,5},{5... | collective-permute-start | bytes 6291464 | tf_op jit(solution)/shard_map/ppermute | solution.py:29
  92.8 6.9 %collective-permute-done.19 = bf16[2,8,64,256]{3,2,1,0:T(8,128)(2,1)} collective-permute-done((bf16[2,8,64,256]{3,2,1,0:T(8,128)(2,1)}, bf16[2,8,64,256]{3,2,1,0:T(8,128)(2,1)}, u32[]{:S(2)}, u32[]{:S(2)}) %collective-permute-start.19) | collective-permute-done | bytes 524320 | tf_op jit(solution)/shard_map/ppermute | solution.py:16
  99.7 4.8 %collective-permute-done.17 = bf16[2,8,64,256]{3,2,1,0:T(8,128)(2,1)} collective-permute-done((bf16[2,8,64,256]{3,2,1,0:T(8,128)(2,1)}, bf16[2,8,64,256]{3,2,1,0:T(8,128)(2,1)}, u32[]{:S(2)}, u32[]{:S(2)}) %collective-permute-start.17) | collective-permute-done | bytes 524320 | tf_op jit(solution)/shard_map/ppermute | solution.py:16
  109.9 3.6 %collective-permute-start.8 = (bf16[2,2,32,2,512]{4,2,3,1,0:T(8,128)(2,1)}, bf16[2,2,32,2,512]{4,2,3,1,0:T(8,128)(2,1)}, u32[]{:S(2)}, u32[]{:S(2)}) collective-permute-start(bf16[2,2,32,2,512]{4,2,3,1,0:T(8,128)(2,1)} %get-tuple-element.30), channel_id=1, source_target_pairs={{0,3},{1,2},{2,1},{3,0},{4,7},{5,6},{6,5},{7,4},{8,11},{9,10},{10,... | collective-permute-start | bytes 786440 | tf_op jit(solution)/shard_map/ppermute | solution.py:44
  114.3 2.7 %fusion.42 = (f32[256]{0:T(256)S(1)}, f32[256,1024]{1,0:T(8,128)}) fusion(bf16[1,256,1024]{2,1,0:T(8,128)(2,1)S(1)} %copy-done.2, f32[256]{0:T(256)S(1)} %add_rsqrt_fusion, bf16[4,256,512]{1,2,0:T(8,128)(2,1)S(1)} %bitcast.223, bf16[1024,4,512]{2,1,0:T(4,128)(2,1)S(1)} %copy-done.11), kind=kOutput, calls=%fused_computation.46 | convolution fusion | flops 1074790144 | bytes 6817792 | tf_op jit(solution)/shard_map/wrh,dwh->rd/dot_general | solution.py:224
  117.0 7.5 %collective-permute-start.5 = (s32[]{:T(128)}, s32[]{:T(128)}, u32[]{:S(2)}, u32[]{:S(2)}) collective-permute-start(s32[]{:T(128)} %reduce_sum.45), channel_id=1, source_target_pairs={{0,4},{4,0},{8,12},{12,8},{16,20},{20,16},{24,28},{28,24},{1,5},{5... | collective-permute-start | bytes 20 | tf_op jit(solution)/shard_map/ppermute | solution.py:52
  126.9 8.7 %collective-permute-done.7 = bf16[2,2,32,2,512]{4,2,3,1,0:T(8,128)(2,1)} collective-permute-done((bf16[2,2,32,2,512]{4,2,3,1,0:T(8,128)(2,1)}, bf16[2,2,32,2,512]{4,2,3,1,0:T(8,128)(2,1)}, u32[]{:S(2)}, u32[]{:S(2)}) %collective-permute-start.7) | collective-permute-done | bytes 262176 | tf_op jit(solution)/shard_map/ppermute | solution.py:44
  138.9 3.1 %collective-permute-done.9 = s32[]{:T(128)} collective-permute-done((s32[]{:T(128)}, s32[]{:T(128)}, u32[]{:S(2)}, u32[]{:S(2)}) %collective-permute-start.9) | collective-permute-done | bytes 36 | tf_op jit(solution)/shard_map/ppermute | solution.py:52
  145.1 8.3 %collective-permute-start.13 = (bf16[32,2,512]{2,1,0:T(2,128)(2,1)S(1)}, bf16[32,2,512]{2,1,0:T(2,128)(2,1)S(1)}, u32[]{:S(2)}, u32[]{:S(2)}) collective-permute-start(bf16[32,2,512]{2,1,0:T(2,128)(2,1)S(1)} %bitcast.228), channel_id=1, source_target_pairs={{0,24},{4,28},{8,16},{12,20},{16,8},{20,12},{24,0},{28,4},{1,25},{... | collective-permute-start | bytes 196616 | tf_op jit(solution)/shard_map/ppermute | solution.py:44
  172.2 4.1 %collective-permute-done.20 = f32[2,2,2,2,32,2,512]{6,4,5,3,2,1,0:T(8,128)S(1)} collective-permute-done((f32[2,2,2,2,32,2,512]{6,4,5,3,2,1,0:T(8,128)S(1)}, f32[2,2,2,2,32,2,512]{6,4,5,3,2,1,0:T(8,128)S(1)}, u32[]{:S(2)}, u32[]{:S(2)}) %collective-permute-start.20) | collective-permute-done | bytes 2097184 | tf_op jit(solution)/shard_map/ppermute | solution.py:29
  177.0 2.5 %collective-permute-start.23 = (bf16[2,2,32,2,512]{4,2,3,1,0:T(8,128)(2,1)S(1)}, bf16[2,2,32,2,512]{4,2,3,1,0:T(8,128)(2,1)S(1)}, u32[]{:S(2)}, u32[]{:S(2)}) collective-permute-start(bf16[2,2,32,2,512]{4,2,3,1,0:T(8,128)(2,1)S(1)} %get-tuple-element.27), channel_id=1, source_target_pairs={{0,24},{4,28},{8,16},{12,20},{16,8},{20,12},{24,0},{28,4},{1,25},{... | collective-permute-start | bytes 786440 | tf_op jit(solution)/shard_map/ppermute | solution.py:44
  180.7 6.5 %collective-permute-done.23 = bf16[2,2,32,2,512]{4,2,3,1,0:T(8,128)(2,1)S(1)} collective-permute-done((bf16[2,2,32,2,512]{4,2,3,1,0:T(8,128)(2,1)S(1)}, bf16[2,2,32,2,512]{4,2,3,1,0:T(8,128)(2,1)S(1)}, u32[]{:S(2)}, u32[]{:S(2)}) %collective-permute-start.23) | collective-permute-done | bytes 262176 | tf_op jit(solution)/shard_map/ppermute | solution.py:44
  187.2 4.9 %collective-permute-done.22 = bf16[2,2,32,2,512]{4,2,3,1,0:T(8,128)(2,1)} collective-permute-done((bf16[2,2,32,2,512]{4,2,3,1,0:T(8,128)(2,1)S(1)}, bf16[2,2,32,2,512]{4,2,3,1,0:T(8,128)(2,1)}, u32[]{:S(2)}, u32[]{:S(2)}) %collective-permute-start.22) | collective-permute-done | bytes 262176 | tf_op jit(solution)/shard_map/ppermute | solution.py:44
  200.1 3.0 %collective-permute-done.25 = bf16[32,2,512]{2,1,0:T(2,128)(2,1)S(1)} collective-permute-done((bf16[32,2,512]{2,1,0:T(2,128)(2,1)S(1)}, bf16[32,2,512]{2,1,0:T(2,128)(2,1)S(1)}, u32[]{:S(2)}, u32[]{:S(2)}) %collective-permute-start.25) | collective-permute-done | bytes 65568 | tf_op jit(solution)/shard_map/ppermute | solution.py:44
  (126 shorter events, 77.8 us)
Async XLA Ops:
  6.7 40.0 %collective-permute-start = (bf16[2,256,512]{2,1,0:T(8,128)(2,1)}, bf16[2,256,512]{2,1,0:T(8,128)(2,1)}, u32[]{:S(2)}, u32[]{:S(2)}) collective-permute-start(bf16[2,256,512]{2,1,0:T(8,128)(2,1)} %slice.77), channel_id=1, source_target_pairs={{0,16},{4,20},{8,24},{12,28},{1,17},{5,21},{9,25},{13,29},{2,18},{... | collective-permute-start | bytes 1572872 | tf_op jit(solution)/shard_map/ppermute | solution.py:16
  12.4 35.4 %collective-permute-start.1 = (bf16[2,256,512]{2,1,0:T(8,128)(2,1)}, bf16[2,256,512]{2,1,0:T(8,128)(2,1)}, u32[]{:S(2)}, u32[]{:S(2)}) collective-permute-start(bf16[2,256,512]{2,1,0:T(8,128)(2,1)} %slice.77), channel_id=1, source_target_pairs={{0,12},{4,16},{8,20},{12,24},{16,28},{1,13},{5,17},{9,21},{13,25},... | collective-permute-start | bytes 1572872 | tf_op jit(solution)/shard_map/ppermute | solution.py:16
  15.7 33.1 %collective-permute-start.2 = (bf16[2,256,512]{2,1,0:T(8,128)(2,1)}, bf16[2,256,512]{2,1,0:T(8,128)(2,1)}, u32[]{:S(2)}, u32[]{:S(2)}) collective-permute-start(bf16[2,256,512]{2,1,0:T(8,128)(2,1)} %slice.77), channel_id=1, source_target_pairs={{0,8},{4,12},{8,16},{12,20},{16,24},{20,28},{1,9},{5,13},{9,17},{1... | collective-permute-start | bytes 1572872 | tf_op jit(solution)/shard_map/ppermute | solution.py:16
  18.7 31.3 %collective-permute-start.3 = (bf16[2,256,512]{2,1,0:T(8,128)(2,1)}, bf16[2,256,512]{2,1,0:T(8,128)(2,1)}, u32[]{:S(2)}, u32[]{:S(2)}) collective-permute-start(bf16[2,256,512]{2,1,0:T(8,128)(2,1)} %slice.77), channel_id=1, source_target_pairs={{0,4},{4,8},{8,12},{12,16},{16,20},{20,24},{24,28},{1,5},{5,9},{9,... | collective-permute-start | bytes 1572872 | tf_op jit(solution)/shard_map/ppermute | solution.py:16
  77.4 29.4 %collective-permute-start.4 = (f32[2,2,2,2,32,2,512]{6,4,5,3,2,1,0:T(8,128)}, f32[2,2,2,2,32,2,512]{6,4,5,3,2,1,0:T(8,128)}, u32[]{:S(2)}, u32[]{:S(2)}) collective-permute-start(f32[2,2,2,2,32,2,512]{6,4,5,3,2,1,0:T(8,128)} %bitcast.195), channel_id=1, source_target_pairs={{0,4},{4,0},{8,12},{12,8},{16,20},{20,16},{24,28},{28,24},{1,5},{5... | collective-permute-start | bytes 6291464 | tf_op jit(solution)/shard_map/ppermute | solution.py:29
  83.0 16.7 %collective-permute-start.19 = (bf16[2,8,64,256]{3,2,1,0:T(8,128)(2,1)}, bf16[2,8,64,256]{3,2,1,0:T(8,128)(2,1)}, u32[]{:S(2)}, u32[]{:S(2)}) collective-permute-start(bf16[2,8,64,256]{3,2,1,0:T(8,128)(2,1)} %pad_maximum_fusion.3), channel_id=1, source_target_pairs={{16,0},{20,4},{24,8},{28,12},{17,1},{21,5},{25,9},{29,13},{18,2},{... | collective-permute-start | bytes 1572872 | tf_op jit(solution)/shard_map/ppermute | solution.py:16
  85.3 14.4 %collective-permute-start.18 = (bf16[2,8,64,256]{3,2,1,0:T(8,128)(2,1)}, bf16[2,8,64,256]{3,2,1,0:T(8,128)(2,1)}, u32[]{:S(2)}, u32[]{:S(2)}) collective-permute-start(bf16[2,8,64,256]{3,2,1,0:T(8,128)(2,1)} %pad_maximum_fusion.2), channel_id=1, source_target_pairs={{12,0},{16,4},{20,8},{24,12},{28,16},{13,1},{17,5},{21,9},{25,13},... | collective-permute-start | bytes 1572872 | tf_op jit(solution)/shard_map/ppermute | solution.py:16
  87.4 17.1 %collective-permute-start.17 = (bf16[2,8,64,256]{3,2,1,0:T(8,128)(2,1)}, bf16[2,8,64,256]{3,2,1,0:T(8,128)(2,1)}, u32[]{:S(2)}, u32[]{:S(2)}) collective-permute-start(bf16[2,8,64,256]{3,2,1,0:T(8,128)(2,1)} %pad_maximum_fusion.1), channel_id=1, source_target_pairs={{8,0},{12,4},{16,8},{20,12},{24,16},{28,20},{9,1},{13,5},{17,9},{2... | collective-permute-start | bytes 1572872 | tf_op jit(solution)/shard_map/ppermute | solution.py:16
  89.5 14.9 %collective-permute-start.16 = (bf16[2,8,64,256]{3,2,1,0:T(8,128)(2,1)}, bf16[2,8,64,256]{3,2,1,0:T(8,128)(2,1)}, u32[]{:S(2)}, u32[]{:S(2)}) collective-permute-start(bf16[2,8,64,256]{3,2,1,0:T(8,128)(2,1)} %pad_maximum_fusion), channel_id=1, source_target_pairs={{4,0},{8,4},{12,8},{16,12},{20,16},{24,20},{28,24},{5,1},{9,5},{13... | collective-permute-start | bytes 1572872 | tf_op jit(solution)/shard_map/ppermute | solution.py:16
  109.9 16.9 %collective-permute-start.8 = (bf16[2,2,32,2,512]{4,2,3,1,0:T(8,128)(2,1)}, bf16[2,2,32,2,512]{4,2,3,1,0:T(8,128)(2,1)}, u32[]{:S(2)}, u32[]{:S(2)}) collective-permute-start(bf16[2,2,32,2,512]{4,2,3,1,0:T(8,128)(2,1)} %get-tuple-element.30), channel_id=1, source_target_pairs={{0,3},{1,2},{2,1},{3,0},{4,7},{5,6},{6,5},{7,4},{8,11},{9,10},{10,... | collective-permute-start | bytes 786440 | tf_op jit(solution)/shard_map/ppermute | solution.py:44
  113.5 22.0 %collective-permute-start.7 = (bf16[2,2,32,2,512]{4,2,3,1,0:T(8,128)(2,1)}, bf16[2,2,32,2,512]{4,2,3,1,0:T(8,128)(2,1)}, u32[]{:S(2)}, u32[]{:S(2)}) collective-permute-start(bf16[2,2,32,2,512]{4,2,3,1,0:T(8,128)(2,1)} %get-tuple-element.31), channel_id=1, source_target_pairs={{0,2},{1,3},{2,0},{3,1},{4,6},{5,7},{6,4},{7,5},{8,10},{9,11},{10,... | collective-permute-start | bytes 786440 | tf_op jit(solution)/shard_map/ppermute | solution.py:44
  113.5 22.0 %collective-permute-start.6 = (bf16[2,2,32,2,512]{4,2,3,1,0:T(8,128)(2,1)S(1)}, bf16[2,2,32,2,512]{4,2,3,1,0:T(8,128)(2,1)}, u32[]{:S(2)}, u32[]{:S(2)}) collective-permute-start(bf16[2,2,32,2,512]{4,2,3,1,0:T(8,128)(2,1)S(1)} %get-tuple-element.29), channel_id=1, source_target_pairs={{0,1},{1,0},{2,3},{3,2},{4,5},{5,4},{6,7},{7,6},{8,9},{9,8},{10,11... | collective-permute-start | bytes 786440 | tf_op jit(solution)/shard_map/ppermute | solution.py:44
  117.0 8.5 %collective-permute-start.5 = (s32[]{:T(128)}, s32[]{:T(128)}, u32[]{:S(2)}, u32[]{:S(2)}) collective-permute-start(s32[]{:T(128)} %reduce_sum.45), channel_id=1, source_target_pairs={{0,4},{4,0},{8,12},{12,8},{16,20},{20,16},{24,28},{28,24},{1,5},{5... | collective-permute-start | bytes 20 | tf_op jit(solution)/shard_map/ppermute | solution.py:52
  137.6 4.4 %collective-permute-start.9 = (s32[]{:T(128)}, s32[]{:T(128)}, u32[]{:S(2)}, u32[]{:S(2)}) collective-permute-start(s32[]{:T(128)} %add.171), channel_id=1, source_target_pairs={{0,2},{1,3},{2,0},{3,1},{4,6},{5,7},{6,4},{7,5},{8,10},{9,11},{10,... | collective-permute-start | bytes 20 | tf_op jit(solution)/shard_map/ppermute | solution.py:52
  142.6 15.0 %collective-permute-start.10 = (s32[]{:T(128)}, s32[]{:T(128)}, u32[]{:S(2)}, u32[]{:S(2)}) collective-permute-start(s32[]{:T(128)} %add.182), channel_id=1, source_target_pairs={{0,1},{1,0},{2,3},{3,2},{4,5},{5,4},{6,7},{7,6},{8,9},{9,8},{10,11... | collective-permute-start | bytes 20 | tf_op jit(solution)/shard_map/ppermute | solution.py:52
  145.1 13.1 %collective-permute-start.13 = (bf16[32,2,512]{2,1,0:T(2,128)(2,1)S(1)}, bf16[32,2,512]{2,1,0:T(2,128)(2,1)S(1)}, u32[]{:S(2)}, u32[]{:S(2)}) collective-permute-start(bf16[32,2,512]{2,1,0:T(2,128)(2,1)S(1)} %bitcast.228), channel_id=1, source_target_pairs={{0,24},{4,28},{8,16},{12,20},{16,8},{20,12},{24,0},{28,4},{1,25},{... | collective-permute-start | bytes 196616 | tf_op jit(solution)/shard_map/ppermute | solution.py:44
  153.5 4.7 %collective-permute-start.12 = (bf16[32,2,512]{2,1,0:T(2,128)(2,1)S(1)}, bf16[32,2,512]{2,1,0:T(2,128)(2,1)S(1)}, u32[]{:S(2)}, u32[]{:S(2)}) collective-permute-start(bf16[32,2,512]{2,1,0:T(2,128)(2,1)S(1)} %bitcast.229), channel_id=1, source_target_pairs={{0,16},{4,20},{8,24},{12,28},{16,0},{20,4},{24,8},{28,12},{1,17},{... | collective-permute-start | bytes 196616 | tf_op jit(solution)/shard_map/ppermute | solution.py:44
  155.7 4.3 %collective-permute-start.11 = (bf16[32,2,512]{2,1,0:T(2,128)(2,1)S(1)}, bf16[32,2,512]{2,1,0:T(2,128)(2,1)S(1)}, u32[]{:S(2)}, u32[]{:S(2)}) collective-permute-start(bf16[32,2,512]{2,1,0:T(2,128)(2,1)S(1)} %bitcast.230), channel_id=1, source_target_pairs={{0,8},{4,12},{8,0},{12,4},{16,24},{20,28},{24,16},{28,20},{1,9},{5... | collective-permute-start | bytes 196616 | tf_op jit(solution)/shard_map/ppermute | solution.py:44
  177.0 10.2 %collective-permute-start.23 = (bf16[2,2,32,2,512]{4,2,3,1,0:T(8,128)(2,1)S(1)}, bf16[2,2,32,2,512]{4,2,3,1,0:T(8,128)(2,1)S(1)}, u32[]{:S(2)}, u32[]{:S(2)}) collective-permute-start(bf16[2,2,32,2,512]{4,2,3,1,0:T(8,128)(2,1)S(1)} %get-tuple-element.27), channel_id=1, source_target_pairs={{0,24},{4,28},{8,16},{12,20},{16,8},{20,12},{24,0},{28,4},{1,25},{... | collective-permute-start | bytes 786440 | tf_op jit(solution)/shard_map/ppermute | solution.py:44
  179.5 12.5 %collective-permute-start.22 = (bf16[2,2,32,2,512]{4,2,3,1,0:T(8,128)(2,1)S(1)}, bf16[2,2,32,2,512]{4,2,3,1,0:T(8,128)(2,1)}, u32[]{:S(2)}, u32[]{:S(2)}) collective-permute-start(bf16[2,2,32,2,512]{4,2,3,1,0:T(8,128)(2,1)S(1)} %get-tuple-element.28), channel_id=1, source_target_pairs={{0,16},{4,20},{8,24},{12,28},{16,0},{20,4},{24,8},{28,12},{1,17},{... | collective-permute-start | bytes 786440 | tf_op jit(solution)/shard_map/ppermute | solution.py:44
  179.5 12.5 %collective-permute-start.21 = (bf16[2,2,32,2,512]{4,2,3,1,0:T(8,128)(2,1)S(1)}, bf16[2,2,32,2,512]{4,2,3,1,0:T(8,128)(2,1)}, u32[]{:S(2)}, u32[]{:S(2)}) collective-permute-start(bf16[2,2,32,2,512]{4,2,3,1,0:T(8,128)(2,1)S(1)} %get-tuple-element.26), channel_id=1, source_target_pairs={{0,8},{4,12},{8,0},{12,4},{16,24},{20,28},{24,16},{28,20},{1,9},{5... | collective-permute-start | bytes 786440 | tf_op jit(solution)/shard_map/ppermute | solution.py:44
  193.3 6.8 %collective-permute-start.26 = (bf16[32,2,512]{2,1,0:T(2,128)(2,1)S(1)}, bf16[32,2,512]{2,1,0:T(2,128)(2,1)S(1)}, u32[]{:S(2)}, u32[]{:S(2)}) collective-permute-start(bf16[32,2,512]{2,1,0:T(2,128)(2,1)S(1)} %bitcast.231), channel_id=1, source_target_pairs={{0,3},{1,2},{2,1},{3,0},{4,7},{5,6},{6,5},{7,4},{8,11},{9,10},{10,... | collective-permute-start | bytes 196616 | tf_op jit(solution)/shard_map/ppermute | solution.py:44
  195.0 8.1 %collective-permute-start.25 = (bf16[32,2,512]{2,1,0:T(2,128)(2,1)S(1)}, bf16[32,2,512]{2,1,0:T(2,128)(2,1)S(1)}, u32[]{:S(2)}, u32[]{:S(2)}) collective-permute-start(bf16[32,2,512]{2,1,0:T(2,128)(2,1)S(1)} %bitcast.232), channel_id=1, source_target_pairs={{0,2},{1,3},{2,0},{3,1},{4,6},{5,7},{6,4},{7,5},{8,10},{9,11},{10,... | collective-permute-start | bytes 196616 | tf_op jit(solution)/shard_map/ppermute | solution.py:44
  197.1 6.0 %collective-permute-start.24 = (bf16[32,2,512]{2,1,0:T(2,128)(2,1)S(1)}, bf16[32,2,512]{2,1,0:T(2,128)(2,1)S(1)}, u32[]{:S(2)}, u32[]{:S(2)}) collective-permute-start(bf16[32,2,512]{2,1,0:T(2,128)(2,1)S(1)} %bitcast.233), channel_id=1, source_target_pairs={{0,1},{1,0},{2,3},{3,2},{4,5},{5,4},{6,7},{7,6},{8,9},{9,8},{10,11... | collective-permute-start | bytes 196616 | tf_op jit(solution)/shard_map/ppermute | solution.py:44
  (16 other events, 95.9 us)

commit v13 on v10

--- a/solution.py
+++ b/solution.py
@@ -72,7 +72,7 @@
             tally, value = count_along(tally, value, stage)
         return value, names, tally
 
-    value, names = step(value, names, first, value.dtype)
+    value, names = step(value, names, first, wire_type)
     tally, value = count_along(tally, value, first)
     middle = [s for s in stages if s[0] == first[0] and s != first]
     tail = [s for s in stages if s[0] != first[0]][::-1]

time: 172 us -> 169 us (0.983)
  waiting for transfers between devices: 50.8 us -> 48 us
    ppermute x14, waiting for transfers between devices: 26.4 us -> 24.6 us  [halve(): lax.ppermute(send.astype(send_type), axis, pairs).astype(keep.dtype)]
    unnamed x30 -> x32, local copies, waits for them, and re-layouts: 7.04 us -> 7.04 us
  transfers between devices with their start and end apart: 27 -> 27, of which waited for: 16 -> 17; matrix products, arithmetic and copies ran while one was open for 20% -> 20% of each run, Pallas kernels for 0% -> 0%
where the time goes in v13:
time: 169 us; the launch traced here: 168 us
  starting transfers between devices  53 us (31%)
  waiting for transfers between devices  48 us (28%)
  matrix products  30 us (18%)
  local copies, waits for them, and re-layouts  17.3 us (10%)
  other arithmetic  14.4 us (9%)
  between operations  5.13 us (3%)
    ppermute x14, waiting for transfers between devices, halve(): lax.ppermute(send.astype(send_type), axis, pairs).astype(keep.dtype)  24.6 us
    ppermute x14, starting transfers between devices, halve(): lax.ppermute(send.astype(send_type), axis, pairs).astype(keep.dtype)  24.3 us
    ppermute x8, starting transfers between devices, shifted(): return lax.ppermute(value, axis, pairs)  19.4 us
    ppermute x8, waiting for transfers between devices, shifted(): return lax.ppermute(value, axis, pairs)  16.1 us
    ppermute x5, starting transfers between devices, swap_add(): return (value + lax.ppermute(value, axis, pairs), anchor)  9.27 us
    ppermute x5, waiting for transfers between devices, swap_add(): return (value + lax.ppermute(value, axis, pairs), anchor)  7.25 us
    unnamed x32, local copies, waits for them, and re-layouts  7.04 us
    dot_general x1, matrix products, shards(): jnp.einsum('rd,dwh->wrh', grad_out, weights, preferred_element_type=jnp.f...  4.83 us
  transfers between devices with their start and end apart: 27, of which 17 were waited for; matrix products, arithmetic and copies ran while one was open for 20% of the time, Pallas kernels for 0%

profile of v13, /device:TPU:0, one launch (start us, length us, event | category | flops | bytes accessed | tf_op | source)
XLA Modules:
  0.0 167.8 jit_solution(645144420118556329)
XLA Ops:
  1.9 4.0 %fusion.26 = bf16[4,256,512]{2,1,0:T(8,128)(2,1)S(1)} fusion(bf16[1024,4,512]{2,1,0:T(4,128)(2,1)} %param.5, bf16[1,256,1024]{2,1,0:T(8,128)(2,1)} %param.4, f32[256]{0:T(256)S(1)} %add_rsqrt_fusion), kind=kOutput, calls=%fused_computation.30 | convolution fusion | flops 1075052544 | bytes 5768192 | tf_op jit(solution)/shard_map/rd,dwh->wrh/dot_general | solution.py:142
  6.7 5.7 %collective-permute-start = (bf16[2,256,512]{2,1,0:T(8,128)(2,1)}, bf16[2,256,512]{2,1,0:T(8,128)(2,1)}, u32[]{:S(2)}, u32[]{:S(2)}) collective-permute-start(bf16[2,256,512]{2,1,0:T(8,128)(2,1)} %slice.93), channel_id=1, source_target_pairs={{0,16},{4,20},{8,24},{12,28},{1,17},{5,21},{9,25},{13,29},{2,18},{... | collective-permute-start | bytes 1572872 | tf_op jit(solution)/shard_map/ppermute | solution.py:16
  12.4 3.4 %collective-permute-start.1 = (bf16[2,256,512]{2,1,0:T(8,128)(2,1)}, bf16[2,256,512]{2,1,0:T(8,128)(2,1)}, u32[]{:S(2)}, u32[]{:S(2)}) collective-permute-start(bf16[2,256,512]{2,1,0:T(8,128)(2,1)} %slice.93), channel_id=1, source_target_pairs={{0,12},{4,16},{8,20},{12,24},{16,28},{1,13},{5,17},{9,21},{13,25},... | collective-permute-start | bytes 1572872 | tf_op jit(solution)/shard_map/ppermute | solution.py:16
  15.7 3.0 %collective-permute-start.2 = (bf16[2,256,512]{2,1,0:T(8,128)(2,1)}, bf16[2,256,512]{2,1,0:T(8,128)(2,1)}, u32[]{:S(2)}, u32[]{:S(2)}) collective-permute-start(bf16[2,256,512]{2,1,0:T(8,128)(2,1)} %slice.93), channel_id=1, source_target_pairs={{0,8},{4,12},{8,16},{12,20},{16,24},{20,28},{1,9},{5,13},{9,17},{1... | collective-permute-start | bytes 1572872 | tf_op jit(solution)/shard_map/ppermute | solution.py:16
  18.7 2.1 %collective-permute-start.3 = (bf16[2,256,512]{2,1,0:T(8,128)(2,1)}, bf16[2,256,512]{2,1,0:T(8,128)(2,1)}, u32[]{:S(2)}, u32[]{:S(2)}) collective-permute-start(bf16[2,256,512]{2,1,0:T(8,128)(2,1)} %slice.93), channel_id=1, source_target_pairs={{0,4},{4,8},{8,12},{12,16},{16,20},{20,24},{24,28},{1,5},{5,9},{9,... | collective-permute-start | bytes 1572872 | tf_op jit(solution)/shard_map/ppermute | solution.py:16
  22.0 4.8 %fusion.23 = bf16[4,256,512]{2,1,0:T(8,128)(2,1)} fusion(bf16[1024,4,512]{2,1,0:T(4,128)(2,1)} %param.5, bf16[1,256,1024]{2,1,0:T(8,128)(2,1)S(1)} %copy-done.10, pred[256]{0:T(512)(128)(4,1)S(1)} %compare_reduce_fusion), kind=kOutput, calls=%fused_computation.29 | convolution fusion | flops 1074528256 | bytes 5767424 | tf_op jit(solution)/shard_map/rd,dwh->wrh/dot_general | solution.py:153
  31.9 14.7 %collective-permute-done = bf16[2,256,512]{2,1,0:T(8,128)(2,1)} collective-permute-done((bf16[2,256,512]{2,1,0:T(8,128)(2,1)}, bf16[2,256,512]{2,1,0:T(8,128)(2,1)}, u32[]{:S(2)}, u32[]{:S(2)}) %collective-permute-start) | collective-permute-done | bytes 524320 | tf_op jit(solution)/shard_map/ppermute | solution.py:16
  55.4 3.9 %fusion.1 = (f32[8,256]{1,0:T(8,128)S(1)}, f32[8,256,1280]{2,1,0:T(8,128)S(1)}) fusion(f32[256,1280]{1,0:T(8,128)} %fusion.41, bf16[256,8,64]{0,2,1:T(8,128)(2,1)S(1)} %bitcast.197, bf16[1280,8,64]{0,2,1:T(8,128)(2,1)S(1)} %bitcast.194), kind=kOutput, calls=%fused_computation.3 | convolution fusion | flops 343406592 | bytes 13377536 | tf_op jit(solution)/shard_map/qgc,kgc->gqk/dot_general | solution.py:102
  59.3 2.8 %multiply_reduce_fusion = (f32[256,8]{0,1:T(8,128)S(1)}, bf16[8,64,256]{2,1,0:T(8,128)(2,1)S(1)}) fusion(bf16[256,8,64]{0,2,1:T(8,128)(2,1)S(1)} %bitcast.207, bf16[1280,8,64]{0,2,1:T(8,128)(2,1)S(1)} %bitcast.204, f32[8,256]{1,0:T(8,128)S(1)} %get-tuple-element.40, f32[256,1280]{1,0:T(8,128)S(1)} %copy-done, f32[8,256,1280]{2,1,0:T(8,128)S(1)} %get-tuple-element.41), kind=kOutput, calls=%fused_computation.86 | convolution fusion | flops 346683392 | bytes 13647872 | tf_op jit(solution)/shard_map/gqk,kgc->qgc/dot_general | solution.py:108
  62.1 3.9 %multiply_convert_fusion = bf16[8,256,1280]{2,1,0:T(8,128)(2,1)S(1)} fusion(bf16[256,8,64]{0,2,1:T(8,128)(2,1)S(1)} %bitcast.208, bf16[1280,8,64]{0,2,1:T(8,128)(2,1)S(1)} %bitcast.205, f32[8,256]{1,0:T(8,128)S(1)} %bitcast.211, f32[8,256]{1,0:T(8,128)S(1)} %get-tuple-element.40, f32[256,1280]{1,0:T(8,128)S(1)} %copy-done, ...), kind=kOutput, calls=%fused_computation | convolution fusion | flops 353894400 | bytes 18628608 | tf_op jit(solution)/shard_map/qgc,kgc->gqk/dot_general | solution.py:112
  69.4 3.6 %collective-permute-start.4 = (bf16[2,2,2,2,32,2,512]{6,4,3,2,1,0,5:T(8,128)(2,1)S(1)}, bf16[2,2,2,2,32,2,512]{6,4,3,2,1,0,5:T(8,128)(2,1)S(1)}, u32[]{:S(2)}, u32[]{:S(2)}) collective-permute-start(bf16[2,2,2,2,32,2,512]{6,4,3,2,1,0,5:T(8,128)(2,1)S(1)} %fusion.53), channel_id=1, source_target_pairs={{0,4},{4,0},{8,12},{12,8},{16,20},{20,16},{24,28},{28,24},{1,5},{5... | collective-permute-start | bytes 3145736 | tf_op jit(solution)/shard_map/ppermute | solution.py:29
  73.0 2.3 %fusion.91 = (bf16[8,64,1280]{2,1,0:T(8,128)(2,1)S(1)}, f32[8,64,1280]{2,1,0:T(8,128)S(1)}) fusion(bf16[256,8,64]{0,2,1:T(8,128)(2,1)S(1)} %bitcast.209, f32[8,256]{1,0:T(8,128)S(1)} %get-tuple-element.40, f32[256,1280]{1,0:T(8,128)S(1)} %copy-done, f32[8,256,1280]{2,1,0:T(8,128)S(1)} %get-tuple-element.41), kind=kOutput, calls=%fused_computation.148 | convolution fusion | flops 346685440 | bytes 15998976 | tf_op jit(solution)/shard_map/gqk,qgc->gck/dot_general | solution.py:122
  91.8 4.3 %collective-permute-done.6 = bf16[2,2,2,32,2,512]{5,3,2,1,0,4:T(8,128)(2,1)} collective-permute-done((bf16[2,2,2,32,2,512]{5,3,2,1,0,4:T(8,128)(2,1)}, bf16[2,2,2,32,2,512]{5,3,2,1,0,4:T(8,128)(2,1)}, u32[]{:S(2)}, u32[]{:S(2)}) %collective-permute-start.6) | collective-permute-done | bytes 524320 | tf_op jit(solution)/shard_map/ppermute | solution.py:29
  97.4 2.7 %collective-permute-start.8 = (bf16[2,2,32,2,512]{4,2,1,0,3:T(8,128)(2,1)S(1)}, bf16[2,2,32,2,512]{4,2,1,0,3:T(8,128)(2,1)S(1)}, u32[]{:S(2)}, u32[]{:S(2)}) collective-permute-start(bf16[2,2,32,2,512]{4,2,1,0,3:T(8,128)(2,1)S(1)} %fusion.64), channel_id=1, source_target_pairs={{0,2},{1,3},{2,0},{3,1},{4,6},{5,7},{6,4},{7,5},{8,10},{9,11},{10,... | collective-permute-start | bytes 786440 | tf_op jit(solution)/shard_map/ppermute | solution.py:29
  108.9 2.5 %collective-permute-done.8 = bf16[2,2,32,2,512]{4,2,1,0,3:T(8,128)(2,1)S(1)} collective-permute-done((bf16[2,2,32,2,512]{4,2,1,0,3:T(8,128)(2,1)S(1)}, bf16[2,2,32,2,512]{4,2,1,0,3:T(8,128)(2,1)S(1)}, u32[]{:S(2)}, u32[]{:S(2)}) %collective-permute-start.8) | collective-permute-done | bytes 262176 | tf_op jit(solution)/shard_map/ppermute | solution.py:29
  111.5 4.9 %collective-permute-start.10 = (bf16[2,32,2,256]{3,1,2,0:T(8,128)(2,1)S(1)}, bf16[2,32,2,256]{3,1,2,0:T(8,128)(2,1)S(1)}, u32[]{:S(2)}, u32[]{:S(2)}) collective-permute-start(bf16[2,32,2,256]{3,1,2,0:T(8,128)(2,1)S(1)} %fusion.80), channel_id=1, source_target_pairs={{0,16},{4,20},{8,24},{12,28},{16,0},{20,4},{24,8},{28,12},{1,17},{... | collective-permute-start | bytes 196616 | tf_op jit(solution)/shard_map/ppermute | solution.py:29
  116.4 3.9 %fusion.45 = (f32[256]{0:T(256)S(1)}, f32[256,1024]{1,0:T(8,128)S(1)}) fusion(bf16[1,256,1024]{2,1,0:T(8,128)(2,1)S(1)} %copy-done.1, f32[256]{0:T(256)S(1)} %add_rsqrt_fusion, bf16[4,256,512]{1,2,0:T(8,128)(2,1)S(1)} %bitcast.206, bf16[1024,4,512]{2,1,0:T(4,128)(2,1)} %param.5), kind=kOutput, calls=%fused_computation.47 | convolution fusion | flops 1074790144 | bytes 6817792 | tf_op jit(solution)/shard_map/wrh,dwh->rd/dot_general | solution.py:194
  120.4 3.2 %collective-permute-start.9 = (s32[]{:T(128)}, s32[]{:T(128)}, u32[]{:S(2)}, u32[]{:S(2)}) collective-permute-start(s32[]{:T(128)} %add.192), channel_id=1, source_target_pairs={{0,2},{1,3},{2,0},{3,1},{4,6},{5,7},{6,4},{7,5},{8,10},{9,11},{10,... | collective-permute-start | bytes 20 | tf_op jit(solution)/shard_map/ppermute | solution.py:36
  126.9 2.3 %collective-permute-start.11 = (s32[]{:T(128)}, s32[]{:T(128)}, u32[]{:S(2)}, u32[]{:S(2)}) collective-permute-start(s32[]{:T(128)} %add.197), channel_id=1, source_target_pairs={{0,16},{4,20},{8,24},{12,28},{16,0},{20,4},{24,8},{28,12},{1,17},{... | collective-permute-start | bytes 20 | tf_op jit(solution)/shard_map/ppermute | solution.py:36
  144.0 5.8 %collective-permute-done.21 = bf16[2,2,2,32,2,256]{5,3,4,2,1,0:T(8,128)(2,1)S(1)} collective-permute-done((bf16[2,2,2,32,2,256]{5,3,4,2,1,0:T(8,128)(2,1)S(1)}, bf16[2,2,2,32,2,256]{5,3,4,2,1,0:T(8,128)(2,1)S(1)}, u32[]{:S(2)}, u32[]{:S(2)}) %collective-permute-start.21) | collective-permute-done | bytes 262176 | tf_op jit(solution)/shard_map/ppermute | solution.py:29
  152.2 2.6 %collective-permute-done.22 = bf16[2,2,32,2,256]{4,2,3,1,0:T(8,128)(2,1)S(1)} collective-permute-done((bf16[2,2,32,2,256]{4,2,3,1,0:T(8,128)(2,1)S(1)}, bf16[2,2,32,2,256]{4,2,3,1,0:T(8,128)(2,1)S(1)}, u32[]{:S(2)}, u32[]{:S(2)}) %collective-permute-start.22) | collective-permute-done | bytes 131104 | tf_op jit(solution)/shard_map/ppermute | solution.py:29
  157.8 3.4 %collective-permute-done.25 = bf16[2,32,2,512]{3,1,2,0:T(8,128)(2,1)S(1)} collective-permute-done((bf16[2,32,2,512]{3,1,2,0:T(8,128)(2,1)S(1)}, bf16[2,32,2,512]{3,1,2,0:T(8,128)(2,1)S(1)}, u32[]{:S(2)}, u32[]{:S(2)}) %collective-permute-start.25) | collective-permute-done | bytes 131104 | tf_op jit(solution)/shard_map/ppermute | solution.py:29
  161.4 3.3 %collective-permute-start.26 = (bf16[32,2,512]{2,0,1:T(8,128)(2,1)S(1)}, bf16[32,2,512]{2,0,1:T(8,128)(2,1)S(1)}, u32[]{:S(2)}, u32[]{:S(2)}) collective-permute-start(bf16[32,2,512]{2,0,1:T(8,128)(2,1)S(1)} %fusion.82), channel_id=1, source_target_pairs={{0,2},{1,3},{2,0},{3,1},{4,6},{5,7},{6,4},{7,5},{8,10},{9,11},{10,... | collective-permute-start | bytes 196616 | tf_op jit(solution)/shard_map/ppermute | solution.py:29
  164.7 2.2 %collective-permute-done.26 = bf16[32,2,512]{2,0,1:T(8,128)(2,1)S(1)} collective-permute-done((bf16[32,2,512]{2,0,1:T(8,128)(2,1)S(1)}, bf16[32,2,512]{2,0,1:T(8,128)(2,1)S(1)}, u32[]{:S(2)}, u32[]{:S(2)}) %collective-permute-start.26) | collective-permute-done | bytes 65568 | tf_op jit(solution)/shard_map/ppermute | solution.py:29
  (139 shorter events, 67.6 us)
Async XLA Ops:
  6.7 40.0 %collective-permute-start = (bf16[2,256,512]{2,1,0:T(8,128)(2,1)}, bf16[2,256,512]{2,1,0:T(8,128)(2,1)}, u32[]{:S(2)}, u32[]{:S(2)}) collective-permute-start(bf16[2,256,512]{2,1,0:T(8,128)(2,1)} %slice.93), channel_id=1, source_target_pairs={{0,16},{4,20},{8,24},{12,28},{1,17},{5,21},{9,25},{13,29},{2,18},{... | collective-permute-start | bytes 1572872 | tf_op jit(solution)/shard_map/ppermute | solution.py:16
  12.4 35.4 %collective-permute-start.1 = (bf16[2,256,512]{2,1,0:T(8,128)(2,1)}, bf16[2,256,512]{2,1,0:T(8,128)(2,1)}, u32[]{:S(2)}, u32[]{:S(2)}) collective-permute-start(bf16[2,256,512]{2,1,0:T(8,128)(2,1)} %slice.93), channel_id=1, source_target_pairs={{0,12},{4,16},{8,20},{12,24},{16,28},{1,13},{5,17},{9,21},{13,25},... | collective-permute-start | bytes 1572872 | tf_op jit(solution)/shard_map/ppermute | solution.py:16
  15.7 33.1 %collective-permute-start.2 = (bf16[2,256,512]{2,1,0:T(8,128)(2,1)}, bf16[2,256,512]{2,1,0:T(8,128)(2,1)}, u32[]{:S(2)}, u32[]{:S(2)}) collective-permute-start(bf16[2,256,512]{2,1,0:T(8,128)(2,1)} %slice.93), channel_id=1, source_target_pairs={{0,8},{4,12},{8,16},{12,20},{16,24},{20,28},{1,9},{5,13},{9,17},{1... | collective-permute-start | bytes 1572872 | tf_op jit(solution)/shard_map/ppermute | solution.py:16
  18.7 31.2 %collective-permute-start.3 = (bf16[2,256,512]{2,1,0:T(8,128)(2,1)}, bf16[2,256,512]{2,1,0:T(8,128)(2,1)}, u32[]{:S(2)}, u32[]{:S(2)}) collective-permute-start(bf16[2,256,512]{2,1,0:T(8,128)(2,1)} %slice.93), channel_id=1, source_target_pairs={{0,4},{4,8},{8,12},{12,16},{16,20},{20,24},{24,28},{1,5},{5,9},{9,... | collective-permute-start | bytes 1572872 | tf_op jit(solution)/shard_map/ppermute | solution.py:16
  69.4 11.3 %collective-permute-start.4 = (bf16[2,2,2,2,32,2,512]{6,4,3,2,1,0,5:T(8,128)(2,1)S(1)}, bf16[2,2,2,2,32,2,512]{6,4,3,2,1,0,5:T(8,128)(2,1)S(1)}, u32[]{:S(2)}, u32[]{:S(2)}) collective-permute-start(bf16[2,2,2,2,32,2,512]{6,4,3,2,1,0,5:T(8,128)(2,1)S(1)} %fusion.53), channel_id=1, source_target_pairs={{0,4},{4,0},{8,12},{12,8},{16,20},{20,16},{24,28},{28,24},{1,5},{5... | collective-permute-start | bytes 3145736 | tf_op jit(solution)/shard_map/ppermute | solution.py:29
  77.3 22.8 %collective-permute-start.17 = (bf16[2,8,64,256]{3,2,1,0:T(8,128)(2,1)}, bf16[2,8,64,256]{3,2,1,0:T(8,128)(2,1)}, u32[]{:S(2)}, u32[]{:S(2)}) collective-permute-start(bf16[2,8,64,256]{3,2,1,0:T(8,128)(2,1)} %pad_maximum_fusion.3), channel_id=1, source_target_pairs={{16,0},{20,4},{24,8},{28,12},{17,1},{21,5},{25,9},{29,13},{18,2},{... | collective-permute-start | bytes 1572872 | tf_op jit(solution)/shard_map/ppermute | solution.py:16
  79.4 20.6 %collective-permute-start.16 = (bf16[2,8,64,256]{3,2,1,0:T(8,128)(2,1)}, bf16[2,8,64,256]{3,2,1,0:T(8,128)(2,1)}, u32[]{:S(2)}, u32[]{:S(2)}) collective-permute-start(bf16[2,8,64,256]{3,2,1,0:T(8,128)(2,1)} %pad_maximum_fusion.2), channel_id=1, source_target_pairs={{12,0},{16,4},{20,8},{24,12},{28,16},{13,1},{17,5},{21,9},{25,13},... | collective-permute-start | bytes 1572872 | tf_op jit(solution)/shard_map/ppermute | solution.py:16
  81.9 14.2 %collective-permute-start.6 = (bf16[2,2,2,32,2,512]{5,3,2,1,0,4:T(8,128)(2,1)}, bf16[2,2,2,32,2,512]{5,3,2,1,0,4:T(8,128)(2,1)}, u32[]{:S(2)}, u32[]{:S(2)}) collective-permute-start(bf16[2,2,2,32,2,512]{5,3,2,1,0,4:T(8,128)(2,1)} %fusion.58), channel_id=1, source_target_pairs={{0,1},{1,0},{2,3},{3,2},{4,5},{5,4},{6,7},{7,6},{8,9},{9,8},{10,11... | collective-permute-start | bytes 1572872 | tf_op jit(solution)/shard_map/ppermute | solution.py:29
  84.4 17.1 %collective-permute-start.15 = (bf16[2,8,64,256]{3,2,1,0:T(8,128)(2,1)}, bf16[2,8,64,256]{3,2,1,0:T(8,128)(2,1)}, u32[]{:S(2)}, u32[]{:S(2)}) collective-permute-start(bf16[2,8,64,256]{3,2,1,0:T(8,128)(2,1)} %pad_maximum_fusion.1), channel_id=1, source_target_pairs={{8,0},{12,4},{16,8},{20,12},{24,16},{28,20},{9,1},{13,5},{17,9},{2... | collective-permute-start | bytes 1572872 | tf_op jit(solution)/shard_map/ppermute | solution.py:16
  88.0 13.4 %collective-permute-start.14 = (bf16[2,8,64,256]{3,2,1,0:T(8,128)(2,1)}, bf16[2,8,64,256]{3,2,1,0:T(8,128)(2,1)}, u32[]{:S(2)}, u32[]{:S(2)}) collective-permute-start(bf16[2,8,64,256]{3,2,1,0:T(8,128)(2,1)} %pad_maximum_fusion), channel_id=1, source_target_pairs={{4,0},{8,4},{12,8},{16,12},{20,16},{24,20},{28,24},{5,1},{9,5},{13... | collective-permute-start | bytes 1572872 | tf_op jit(solution)/shard_map/ppermute | solution.py:16
  97.4 14.0 %collective-permute-start.8 = (bf16[2,2,32,2,512]{4,2,1,0,3:T(8,128)(2,1)S(1)}, bf16[2,2,32,2,512]{4,2,1,0,3:T(8,128)(2,1)S(1)}, u32[]{:S(2)}, u32[]{:S(2)}) collective-permute-start(bf16[2,2,32,2,512]{4,2,1,0,3:T(8,128)(2,1)S(1)} %fusion.64), channel_id=1, source_target_pairs={{0,2},{1,3},{2,0},{3,1},{4,6},{5,7},{6,4},{7,5},{8,10},{9,11},{10,... | collective-permute-start | bytes 786440 | tf_op jit(solution)/shard_map/ppermute | solution.py:29
  104.6 3.5 %collective-permute-start.7 = (s32[]{:T(128)}, s32[]{:T(128)}, u32[]{:S(2)}, u32[]{:S(2)}) collective-permute-start(s32[]{:T(128)} %add.187), channel_id=1, source_target_pairs={{0,1},{1,0},{2,3},{3,2},{4,5},{5,4},{6,7},{7,6},{8,9},{9,8},{10,11... | collective-permute-start | bytes 20 | tf_op jit(solution)/shard_map/ppermute | solution.py:36
  111.5 13.9 %collective-permute-start.10 = (bf16[2,32,2,256]{3,1,2,0:T(8,128)(2,1)S(1)}, bf16[2,32,2,256]{3,1,2,0:T(8,128)(2,1)S(1)}, u32[]{:S(2)}, u32[]{:S(2)}) collective-permute-start(bf16[2,32,2,256]{3,1,2,0:T(8,128)(2,1)S(1)} %fusion.80), channel_id=1, source_target_pairs={{0,16},{4,20},{8,24},{12,28},{16,0},{20,4},{24,8},{28,12},{1,17},{... | collective-permute-start | bytes 196616 | tf_op jit(solution)/shard_map/ppermute | solution.py:29
  120.4 4.5 %collective-permute-start.9 = (s32[]{:T(128)}, s32[]{:T(128)}, u32[]{:S(2)}, u32[]{:S(2)}) collective-permute-start(s32[]{:T(128)} %add.192), channel_id=1, source_target_pairs={{0,2},{1,3},{2,0},{3,1},{4,6},{5,7},{6,4},{7,5},{8,10},{9,11},{10,... | collective-permute-start | bytes 20 | tf_op jit(solution)/shard_map/ppermute | solution.py:36
  125.5 5.5 %collective-permute-start.12 = (bf16[32,2,256]{2,0,1:T(8,128)(2,1)S(1)}, bf16[32,2,256]{2,0,1:T(8,128)(2,1)S(1)}, u32[]{:S(2)}, u32[]{:S(2)}) collective-permute-start(bf16[32,2,256]{2,0,1:T(8,128)(2,1)S(1)} %fusion.84), channel_id=1, source_target_pairs={{0,8},{4,12},{8,0},{12,4},{16,24},{20,28},{24,16},{28,20},{1,9},{5... | collective-permute-start | bytes 98312 | tf_op jit(solution)/shard_map/ppermute | solution.py:29
  131.0 3.6 %collective-permute-start.13 = (s32[]{:T(128)}, s32[]{:T(128)}, u32[]{:S(2)}, u32[]{:S(2)}) collective-permute-start(s32[]{:T(128)} %add.202), channel_id=1, source_target_pairs={{0,8},{4,12},{8,0},{12,4},{16,24},{20,28},{24,16},{28,20},{1,9},{5... | collective-permute-start | bytes 20 | tf_op jit(solution)/shard_map/ppermute | solution.py:36
  137.6 4.6 %collective-permute-start.18 = (bf16[2,32,2,256]{3,1,0,2:T(8,128)(2,1)S(1)}, bf16[2,32,2,256]{3,1,0,2:T(8,128)(2,1)S(1)}, u32[]{:S(2)}, u32[]{:S(2)}) collective-permute-start(bf16[2,32,2,256]{3,1,0,2:T(8,128)(2,1)S(1)} %fusion.81), channel_id=1, source_target_pairs={{0,8},{4,12},{8,0},{12,4},{16,24},{20,28},{24,16},{28,20},{1,9},{5... | collective-permute-start | bytes 196616 | tf_op jit(solution)/shard_map/ppermute | solution.py:29
  141.0 8.8 %collective-permute-start.21 = (bf16[2,2,2,32,2,256]{5,3,4,2,1,0:T(8,128)(2,1)S(1)}, bf16[2,2,2,32,2,256]{5,3,4,2,1,0:T(8,128)(2,1)S(1)}, u32[]{:S(2)}, u32[]{:S(2)}) collective-permute-start(bf16[2,2,2,32,2,256]{5,3,4,2,1,0:T(8,128)(2,1)S(1)} %fusion.65), channel_id=1, source_target_pairs={{0,16},{4,20},{8,24},{12,28},{16,0},{20,4},{24,8},{28,12},{1,17},{... | collective-permute-start | bytes 786440 | tf_op jit(solution)/shard_map/ppermute | solution.py:29
  142.2 15.6 %collective-permute-start.19 = (bf16[32,2,256]{2,0,1:T(8,128)(2,1)S(1)}, bf16[32,2,256]{2,0,1:T(8,128)(2,1)S(1)}, u32[]{:S(2)}, u32[]{:S(2)}) collective-permute-start(bf16[32,2,256]{2,0,1:T(8,128)(2,1)S(1)} %fusion.85), channel_id=1, source_target_pairs={{0,16},{4,20},{8,24},{12,28},{16,0},{20,4},{24,8},{28,12},{1,17},{... | collective-permute-start | bytes 98312 | tf_op jit(solution)/shard_map/ppermute | solution.py:29
  143.3 7.8 %collective-permute-start.23 = (bf16[2,2,2,32,2,256]{5,3,4,2,1,0:T(8,128)(2,1)S(1)}, bf16[2,2,2,32,2,256]{5,3,4,2,1,0:T(8,128)(2,1)S(1)}, u32[]{:S(2)}, u32[]{:S(2)}) collective-permute-start(bf16[2,2,2,32,2,256]{5,3,4,2,1,0:T(8,128)(2,1)S(1)} %fusion.66), channel_id=1, source_target_pairs={{0,8},{4,12},{8,0},{12,4},{16,24},{20,28},{24,16},{28,20},{1,9},{5... | collective-permute-start | bytes 786440 | tf_op jit(solution)/shard_map/ppermute | solution.py:29
  149.8 5.0 %collective-permute-start.22 = (bf16[2,2,32,2,256]{4,2,3,1,0:T(8,128)(2,1)S(1)}, bf16[2,2,32,2,256]{4,2,3,1,0:T(8,128)(2,1)S(1)}, u32[]{:S(2)}, u32[]{:S(2)}) collective-permute-start(bf16[2,2,32,2,256]{4,2,3,1,0:T(8,128)(2,1)S(1)} %fusion.77), channel_id=1, source_target_pairs={{0,8},{4,12},{8,0},{12,4},{16,24},{20,28},{24,16},{28,20},{1,9},{5... | collective-permute-start | bytes 393224 | tf_op jit(solution)/shard_map/ppermute | solution.py:29
  151.2 5.0 %collective-permute-start.24 = (bf16[2,2,32,2,256]{4,2,3,1,0:T(8,128)(2,1)S(1)}, bf16[2,2,32,2,256]{4,2,3,1,0:T(8,128)(2,1)S(1)}, u32[]{:S(2)}, u32[]{:S(2)}) collective-permute-start(bf16[2,2,32,2,256]{4,2,3,1,0:T(8,128)(2,1)S(1)} %fusion.78), channel_id=1, source_target_pairs={{0,16},{4,20},{8,24},{12,28},{16,0},{20,4},{24,8},{28,12},{1,17},{... | collective-permute-start | bytes 393224 | tf_op jit(solution)/shard_map/ppermute | solution.py:29
  156.3 5.0 %collective-permute-start.25 = (bf16[2,32,2,512]{3,1,2,0:T(8,128)(2,1)S(1)}, bf16[2,32,2,512]{3,1,2,0:T(8,128)(2,1)S(1)}, u32[]{:S(2)}, u32[]{:S(2)}) collective-permute-start(bf16[2,32,2,512]{3,1,2,0:T(8,128)(2,1)S(1)} %fusion.79), channel_id=1, source_target_pairs={{0,1},{1,0},{2,3},{3,2},{4,5},{5,4},{6,7},{7,6},{8,9},{9,8},{10,11... | collective-permute-start | bytes 393224 | tf_op jit(solution)/shard_map/ppermute | solution.py:29
  161.4 5.5 %collective-permute-start.26 = (bf16[32,2,512]{2,0,1:T(8,128)(2,1)S(1)}, bf16[32,2,512]{2,0,1:T(8,128)(2,1)S(1)}, u32[]{:S(2)}, u32[]{:S(2)}) collective-permute-start(bf16[32,2,512]{2,0,1:T(8,128)(2,1)S(1)} %fusion.82), channel_id=1, source_target_pairs={{0,2},{1,3},{2,0},{3,1},{4,6},{5,7},{6,4},{7,5},{8,10},{9,11},{10,... | collective-permute-start | bytes 196616 | tf_op jit(solution)/shard_map/ppermute | solution.py:29
  (17 other events, 109.2 us)

commit v14 on v13

--- a/solution.py
+++ b/solution.py
@@ -173,14 +173,28 @@
         "rd,gcr->dgc", normed, grad_q, preferred_element_type=jnp.float32
     ).reshape(width, inner)
     out_part = jnp.einsum("rd,rh->dh", grad_out, attended_all, preferred_element_type=jnp.float32)
-    early, count = scatter_rows(
-        jnp.stack([query_part, out_part], axis=1),
-        local_count,
-        ("tm", "night"),
-        "tm",
-        jnp.bfloat16,
-        tail_first=True,
-    )
+    early_terms = jnp.stack([query_part, out_part], axis=1)
+    blocks = lax.axis_size("tm") * lax.axis_size("night")
+    block_rows_out = width // blocks
+    bits = rows.bit_length()
+    if width % blocks == 0 and block_rows_out % 8 == 0 and blocks <= 256 and bits <= inner:
+        digits = (local_count // (2 ** jnp.arange(bits, dtype=jnp.int32))) % 2
+        count_rows = jnp.zeros((blocks, 8) + early_terms.shape[1:], jnp.float32)
+        count_rows = count_rows.at[:, 0, 0, :bits].set(digits.astype(jnp.float32))
+        payload = jnp.concatenate(
+            [early_terms.reshape((blocks, block_rows_out) + early_terms.shape[1:]), count_rows],
+            axis=1,
+        ).reshape((-1,) + early_terms.shape[1:])
+        early, _ = scatter_rows(
+            payload, None, ("tm", "night"), "tm", jnp.bfloat16, tail_first=True
+        )
+        digit_sums = early[block_rows_out, 0, :bits].astype(jnp.int32)
+        count = jnp.sum(digit_sums * (2 ** jnp.arange(bits, dtype=jnp.int32)))
+        early = early[:block_rows_out]
+    else:
+        early, count = scatter_rows(
+            early_terms, local_count, ("tm", "night"), "tm", jnp.bfloat16, tail_first=True
+        )
     owned = jnp.stack([grad_key[..., span * rows :], grad_value[..., span * rows :]])
     for offset in range(1, span + 1):
         lower = (span - offset) * rows

time: 169 us -> 159 us (0.941)
  waiting for transfers between devices: 48 us -> 64.9 us
  starting transfers between devices: 53 us -> 37.5 us
  other arithmetic: 14.4 us -> 9.67 us
  between operations: 5.13 us -> 2.72 us
  matrix products: 30 us -> 27.9 us
    ppermute x14, waiting for transfers between devices: 24.6 us -> 50.4 us  [halve(): lax.ppermute(send.astype(send_type), axis, pairs).astype(keep.dtype)]
    ppermute x5 -> x0, starting transfers between devices: 9.27 us -> none  [swap_add(): return (value + lax.ppermute(value, axis, pairs), anchor)]
    ppermute x5 -> x0, waiting for transfers between devices: 7.25 us -> none  [swap_add(): return (value + lax.ppermute(value, axis, pairs), anchor)]
    ppermute x14, starting transfers between devices: 24.3 us -> 18.1 us  [halve(): lax.ppermute(send.astype(send_type), axis, pairs).astype(keep.dtype)]
    another operation x4, other arithmetic: 3.43 us -> 0.2 us  [shards(): jnp.stack([grad_key[..., lower:lower + rows], grad_value[..., lower:lower...]
    dot_general x1, matrix products: 3.93 us -> 1.81 us  [shards(): jnp.einsum('wrh,dwh->rd', grad_rows, weights, preferred_element_type=jnp....]
    unnamed x32 -> x24, local copies, waits for them, and re-layouts: 7.04 us -> 7.03 us
  transfers between devices with their start and end apart: 27 -> 22, of which waited for: 17 -> 14; matrix products, arithmetic and copies ran while one was open for 20% -> 13% of each run, Pallas kernels for 0% -> 0%
where the time goes in v14:
time: 159 us
  waiting for transfers between devices  64.9 us (41%)
  starting transfers between devices  37.5 us (24%)
  matrix products  27.9 us (18%)
  local copies, waits for them, and re-layouts  15.9 us (10%)
  other arithmetic  9.67 us (6%)
  between operations  2.72 us (2%)
    ppermute x14, waiting for transfers between devices, halve(): lax.ppermute(send.astype(send_type), axis, pairs).astype(keep.dtype)  50.4 us
    ppermute x8, starting transfers between devices, shifted(): return lax.ppermute(value, axis, pairs)  19.4 us
    ppermute x14, starting transfers between devices, halve(): lax.ppermute(send.astype(send_type), axis, pairs).astype(keep.dtype)  18.1 us
    ppermute x8, waiting for transfers between devices, shifted(): return lax.ppermute(value, axis, pairs)  14.6 us
    unnamed x24, local copies, waits for them, and re-layouts  7.03 us
    dot_general x1, matrix products, shards(): jnp.einsum('rd,dwh->wrh', grad_out, weights, preferred_element_type=jnp.f...  4.81 us
    dot_general x1, matrix products, shards(): jnp.einsum('rd,dwh->wrh', normed, weights, preferred_element_type=jnp.flo...  3.98 us
    dot_general x1, matrix products, band_block(): jnp.einsum('qgc,kgc->gqk', grad_attn, values_blk, preferred_element_type=...  3.92 us
  transfers between devices with their start and end apart: 22, of which 14 were waited for; matrix products, arithmetic and copies ran while one was open for 13% of the time, Pallas kernels for 0%

profile of v14, /device:TPU:0, one launch (start us, length us, event | category | flops | bytes accessed | tf_op | source)
XLA Modules:
  0.0 158.7 jit_solution(17596671509240231237)
XLA Ops:
  1.9 4.0 %fusion.21 = bf16[4,256,512]{2,1,0:T(8,128)(2,1)S(1)} fusion(bf16[1024,4,512]{2,1,0:T(4,128)(2,1)} %param.7, bf16[1,256,1024]{2,1,0:T(8,128)(2,1)} %param.6, f32[256]{0:T(256)S(1)} %add_rsqrt_fusion), kind=kOutput, calls=%fused_computation.24 | convolution fusion | flops 1075052544 | bytes 5768192 | tf_op jit(solution)/shard_map/rd,dwh->wrh/dot_general | solution.py:142
  6.7 5.7 %collective-permute-start = (bf16[2,256,512]{2,1,0:T(8,128)(2,1)}, bf16[2,256,512]{2,1,0:T(8,128)(2,1)}, u32[]{:S(2)}, u32[]{:S(2)}) collective-permute-start(bf16[2,256,512]{2,1,0:T(8,128)(2,1)} %slice.128), channel_id=1, source_target_pairs={{0,16},{4,20},{8,24},{12,28},{1,17},{5,21},{9,25},{13,29},{2,18},{... | collective-permute-start | bytes 1572872 | tf_op jit(solution)/shard_map/ppermute | solution.py:16
  12.4 3.3 %collective-permute-start.1 = (bf16[2,256,512]{2,1,0:T(8,128)(2,1)}, bf16[2,256,512]{2,1,0:T(8,128)(2,1)}, u32[]{:S(2)}, u32[]{:S(2)}) collective-permute-start(bf16[2,256,512]{2,1,0:T(8,128)(2,1)} %slice.128), channel_id=1, source_target_pairs={{0,12},{4,16},{8,20},{12,24},{16,28},{1,13},{5,17},{9,21},{13,25},... | collective-permute-start | bytes 1572872 | tf_op jit(solution)/shard_map/ppermute | solution.py:16
  15.7 2.9 %collective-permute-start.2 = (bf16[2,256,512]{2,1,0:T(8,128)(2,1)}, bf16[2,256,512]{2,1,0:T(8,128)(2,1)}, u32[]{:S(2)}, u32[]{:S(2)}) collective-permute-start(bf16[2,256,512]{2,1,0:T(8,128)(2,1)} %slice.128), channel_id=1, source_target_pairs={{0,8},{4,12},{8,16},{12,20},{16,24},{20,28},{1,9},{5,13},{9,17},{1... | collective-permute-start | bytes 1572872 | tf_op jit(solution)/shard_map/ppermute | solution.py:16
  18.6 2.1 %collective-permute-start.3 = (bf16[2,256,512]{2,1,0:T(8,128)(2,1)}, bf16[2,256,512]{2,1,0:T(8,128)(2,1)}, u32[]{:S(2)}, u32[]{:S(2)}) collective-permute-start(bf16[2,256,512]{2,1,0:T(8,128)(2,1)} %slice.128), channel_id=1, source_target_pairs={{0,4},{4,8},{8,12},{12,16},{16,20},{20,24},{24,28},{1,5},{5,9},{9,... | collective-permute-start | bytes 1572872 | tf_op jit(solution)/shard_map/ppermute | solution.py:16
  21.9 4.8 %fusion.18 = bf16[4,256,512]{2,1,0:T(8,128)(2,1)} fusion(bf16[1024,4,512]{2,1,0:T(4,128)(2,1)} %param.7, bf16[1,256,1024]{2,1,0:T(8,128)(2,1)S(1)} %copy-done.5, pred[256]{0:T(512)(128)(4,1)S(1)} %compare_reduce_fusion), kind=kOutput, calls=%fused_computation.23 | convolution fusion | flops 1074528256 | bytes 5767424 | tf_op jit(solution)/shard_map/rd,dwh->wrh/dot_general | solution.py:153
  33.3 13.4 %collective-permute-done = bf16[2,256,512]{2,1,0:T(8,128)(2,1)} collective-permute-done((bf16[2,256,512]{2,1,0:T(8,128)(2,1)}, bf16[2,256,512]{2,1,0:T(8,128)(2,1)}, u32[]{:S(2)}, u32[]{:S(2)}) %collective-permute-start) | collective-permute-done | bytes 524320 | tf_op jit(solution)/shard_map/ppermute | solution.py:16
  55.3 3.9 %fusion.1 = (f32[8,256]{1,0:T(8,128)S(1)}, f32[8,256,1280]{2,1,0:T(8,128)S(1)}) fusion(f32[256,1280]{1,0:T(8,128)} %fusion.37, bf16[256,8,64]{0,2,1:T(8,128)(2,1)S(1)} %bitcast.202, bf16[1280,8,64]{0,2,1:T(8,128)(2,1)S(1)} %bitcast.199), kind=kOutput, calls=%fused_computation.3 | convolution fusion | flops 343406592 | bytes 13377536 | tf_op jit(solution)/shard_map/qgc,kgc->gqk/dot_general | solution.py:102
  59.3 2.8 %multiply_reduce_fusion = (f32[256,8]{0,1:T(8,128)S(1)}, bf16[8,64,256]{2,1,0:T(8,128)(2,1)S(1)}) fusion(bf16[256,8,64]{0,2,1:T(8,128)(2,1)S(1)} %bitcast.212, bf16[1280,8,64]{0,2,1:T(8,128)(2,1)S(1)} %bitcast.209, f32[8,256]{1,0:T(8,128)S(1)} %get-tuple-element.34, f32[256,1280]{1,0:T(8,128)S(1)} %copy-done, f32[8,256,1280]{2,1,0:T(8,128)S(1)} %get-tuple-element.35), kind=kOutput, calls=%fused_computation.80 | convolution fusion | flops 346683392 | bytes 13647872 | tf_op jit(solution)/shard_map/gqk,kgc->qgc/dot_general | solution.py:108
  62.1 3.9 %multiply_convert_fusion = bf16[8,256,1280]{2,1,0:T(8,128)(2,1)S(1)} fusion(bf16[256,8,64]{0,2,1:T(8,128)(2,1)S(1)} %bitcast.213, bf16[1280,8,64]{0,2,1:T(8,128)(2,1)S(1)} %bitcast.210, f32[8,256]{1,0:T(8,128)S(1)} %bitcast.216, f32[8,256]{1,0:T(8,128)S(1)} %get-tuple-element.34, f32[256,1280]{1,0:T(8,128)S(1)} %copy-done, ...), kind=kOutput, calls=%fused_computation | convolution fusion | flops 353894400 | bytes 18628608 | tf_op jit(solution)/shard_map/qgc,kgc->gqk/dot_general | solution.py:112
  71.3 3.6 %collective-permute-start.4 = (bf16[2,2,2,2,40,2,512]{6,4,5,0,1,2,3:T(8,128)(2,1)S(1)}, bf16[2,2,2,2,40,2,512]{6,4,5,0,1,2,3:T(8,128)(2,1)S(1)}, u32[]{:S(2)}, u32[]{:S(2)}) collective-permute-start(bf16[2,2,2,2,40,2,512]{6,4,5,0,1,2,3:T(8,128)(2,1)S(1)} %fusion.32), channel_id=1, source_target_pairs={{0,4},{4,0},{8,12},{12,8},{16,20},{20,16},{24,28},{28,24},{1,5},{5... | collective-permute-start | bytes 3932168 | tf_op jit(solution)/shard_map/ppermute | solution.py:29
  74.9 2.3 %fusion.96 = (bf16[8,64,1280]{2,1,0:T(8,128)(2,1)S(1)}, f32[8,64,1280]{2,1,0:T(8,128)S(1)}) fusion(bf16[256,8,64]{0,2,1:T(8,128)(2,1)S(1)} %bitcast.214, f32[8,256]{1,0:T(8,128)S(1)} %get-tuple-element.34, f32[256,1280]{1,0:T(8,128)S(1)} %copy-done, f32[8,256,1280]{2,1,0:T(8,128)S(1)} %get-tuple-element.35), kind=kOutput, calls=%fused_computation.175 | convolution fusion | flops 346685440 | bytes 15998976 | tf_op jit(solution)/shard_map/gqk,qgc->gck/dot_general | solution.py:122
  85.5 9.7 %collective-permute-done.5 = bf16[2,2,2,40,2,512]{5,3,4,0,1,2:T(8,128)(2,1)S(1)} collective-permute-done((bf16[2,2,2,40,2,512]{5,3,4,0,1,2:T(8,128)(2,1)S(1)}, bf16[2,2,2,40,2,512]{5,3,4,0,1,2:T(8,128)(2,1)S(1)}, u32[]{:S(2)}, u32[]{:S(2)}) %collective-permute-start.5) | collective-permute-done | bytes 655392 | tf_op jit(solution)/shard_map/ppermute | solution.py:29
  95.4 2.7 %collective-permute-start.6 = (bf16[2,2,40,2,512]{4,2,3,0,1:T(8,128)(2,1)S(1)}, bf16[2,2,40,2,512]{4,2,3,0,1:T(8,128)(2,1)S(1)}, u32[]{:S(2)}, u32[]{:S(2)}) collective-permute-start(bf16[2,2,40,2,512]{4,2,3,0,1:T(8,128)(2,1)S(1)} %fusion.59), channel_id=1, source_target_pairs={{0,2},{1,3},{2,0},{3,1},{4,6},{5,7},{6,4},{7,5},{8,10},{9,11},{10,... | collective-permute-start | bytes 983048 | tf_op jit(solution)/shard_map/ppermute | solution.py:29
  99.9 12.7 %collective-permute-done.6 = bf16[2,2,40,2,512]{4,2,3,0,1:T(8,128)(2,1)S(1)} collective-permute-done((bf16[2,2,40,2,512]{4,2,3,0,1:T(8,128)(2,1)S(1)}, bf16[2,2,40,2,512]{4,2,3,0,1:T(8,128)(2,1)S(1)}, u32[]{:S(2)}, u32[]{:S(2)}) %collective-permute-start.6) | collective-permute-done | bytes 327712 | tf_op jit(solution)/shard_map/ppermute | solution.py:29
  112.8 2.3 %collective-permute-start.7 = (bf16[2,40,2,256]{3,1,2,0:T(8,128)(2,1)S(1)}, bf16[2,40,2,256]{3,1,2,0:T(8,128)(2,1)S(1)}, u32[]{:S(2)}, u32[]{:S(2)}) collective-permute-start(bf16[2,40,2,256]{3,1,2,0:T(8,128)(2,1)S(1)} %fusion.76), channel_id=1, source_target_pairs={{0,16},{4,20},{8,24},{12,28},{16,0},{20,4},{24,8},{28,12},{1,17},{... | collective-permute-start | bytes 245768 | tf_op jit(solution)/shard_map/ppermute | solution.py:29
  117.7 4.0 %collective-permute-done.8 = bf16[40,2,256]{2,0,1:T(8,128)(2,1)S(1)} collective-permute-done((bf16[40,2,256]{2,0,1:T(8,128)(2,1)S(1)}, bf16[40,2,256]{2,0,1:T(8,128)(2,1)S(1)}, u32[]{:S(2)}, u32[]{:S(2)}) %collective-permute-start.8) | collective-permute-done | bytes 40992 | tf_op jit(solution)/shard_map/ppermute | solution.py:29
  125.3 2.6 %collective-permute-done.15 = bf16[2,2,2,2,32,2,512]{6,4,5,3,2,1,0:T(8,128)(2,1)S(1)} collective-permute-done((bf16[2,2,2,2,32,2,512]{6,4,5,3,2,1,0:T(8,128)(2,1)S(1)}, bf16[2,2,2,2,32,2,512]{6,4,5,3,2,1,0:T(8,128)(2,1)S(1)}, u32[]{:S(2)}, u32[]{:S(2)}) %collective-permute-start.15) | collective-permute-done | bytes 1048608 | tf_op jit(solution)/shard_map/ppermute | solution.py:29
  133.0 4.4 %collective-permute-done.16 = bf16[2,2,2,32,2,256]{5,3,4,2,1,0:T(8,128)(2,1)S(1)} collective-permute-done((bf16[2,2,2,32,2,256]{5,3,4,2,1,0:T(8,128)(2,1)S(1)}, bf16[2,2,2,32,2,256]{5,3,4,2,1,0:T(8,128)(2,1)S(1)}, u32[]{:S(2)}, u32[]{:S(2)}) %collective-permute-start.16) | collective-permute-done | bytes 262176 | tf_op jit(solution)/shard_map/ppermute | solution.py:29
  137.6 3.9 %collective-permute-done.18 = bf16[2,2,2,32,2,256]{5,3,4,2,1,0:T(8,128)(2,1)S(1)} collective-permute-done((bf16[2,2,2,32,2,256]{5,3,4,2,1,0:T(8,128)(2,1)S(1)}, bf16[2,2,2,32,2,256]{5,3,4,2,1,0:T(8,128)(2,1)S(1)}, u32[]{:S(2)}, u32[]{:S(2)}) %collective-permute-start.18) | collective-permute-done | bytes 262176 | tf_op jit(solution)/shard_map/ppermute | solution.py:29
  143.5 3.1 %collective-permute-done.19 = bf16[2,2,32,2,256]{4,2,3,1,0:T(8,128)(2,1)S(1)} collective-permute-done((bf16[2,2,32,2,256]{4,2,3,1,0:T(8,128)(2,1)S(1)}, bf16[2,2,32,2,256]{4,2,3,1,0:T(8,128)(2,1)S(1)}, u32[]{:S(2)}, u32[]{:S(2)}) %collective-permute-start.19) | collective-permute-done | bytes 131104 | tf_op jit(solution)/shard_map/ppermute | solution.py:29
  147.8 4.6 %collective-permute-done.20 = bf16[2,32,2,512]{3,1,2,0:T(8,128)(2,1)S(1)} collective-permute-done((bf16[2,32,2,512]{3,1,2,0:T(8,128)(2,1)S(1)}, bf16[2,32,2,512]{3,1,2,0:T(8,128)(2,1)S(1)}, u32[]{:S(2)}, u32[]{:S(2)}) %collective-permute-start.20) | collective-permute-done | bytes 131104 | tf_op jit(solution)/shard_map/ppermute | solution.py:29
  152.5 2.4 %collective-permute-start.21 = (bf16[32,2,512]{2,0,1:T(8,128)(2,1)S(1)}, bf16[32,2,512]{2,0,1:T(8,128)(2,1)S(1)}, u32[]{:S(2)}, u32[]{:S(2)}) collective-permute-start(bf16[32,2,512]{2,0,1:T(8,128)(2,1)S(1)} %fusion.78), channel_id=1, source_target_pairs={{0,2},{1,3},{2,0},{3,1},{4,6},{5,7},{6,4},{7,5},{8,10},{9,11},{10,... | collective-permute-start | bytes 196616 | tf_op jit(solution)/shard_map/ppermute | solution.py:29
  155.0 2.8 %collective-permute-done.21 = bf16[32,2,512]{2,0,1:T(8,128)(2,1)S(1)} collective-permute-done((bf16[32,2,512]{2,0,1:T(8,128)(2,1)S(1)}, bf16[32,2,512]{2,0,1:T(8,128)(2,1)S(1)}, u32[]{:S(2)}, u32[]{:S(2)}) %collective-permute-start.21) | collective-permute-done | bytes 65568 | tf_op jit(solution)/shard_map/ppermute | solution.py:29
  (123 shorter events, 48.1 us)
Async XLA Ops:
  1.9 18.9 %copy-start.7 = (s32[1,256]{1,0:T(1,128)S(1)}, s32[1,256]{1,0:T(1,128)}, u32[]{:S(2)}) copy-start(s32[1,256]{1,0:T(1,128)} %param.9) | copy-start | bytes 3076
  1.9 20.1 %copy-start.5 = (bf16[1,256,1024]{2,1,0:T(8,128)(2,1)S(1)}, bf16[1,256,1024]{2,1,0:T(8,128)(2,1)}, u32[]{:S(2)}) copy-start(bf16[1,256,1024]{2,1,0:T(8,128)(2,1)} %param.8) | copy-start | bytes 1572868
  6.7 40.0 %collective-permute-start = (bf16[2,256,512]{2,1,0:T(8,128)(2,1)}, bf16[2,256,512]{2,1,0:T(8,128)(2,1)}, u32[]{:S(2)}, u32[]{:S(2)}) collective-permute-start(bf16[2,256,512]{2,1,0:T(8,128)(2,1)} %slice.128), channel_id=1, source_target_pairs={{0,16},{4,20},{8,24},{12,28},{1,17},{5,21},{9,25},{13,29},{2,18},{... | collective-permute-start | bytes 1572872 | tf_op jit(solution)/shard_map/ppermute | solution.py:16
  12.4 35.4 %collective-permute-start.1 = (bf16[2,256,512]{2,1,0:T(8,128)(2,1)}, bf16[2,256,512]{2,1,0:T(8,128)(2,1)}, u32[]{:S(2)}, u32[]{:S(2)}) collective-permute-start(bf16[2,256,512]{2,1,0:T(8,128)(2,1)} %slice.128), channel_id=1, source_target_pairs={{0,12},{4,16},{8,20},{12,24},{16,28},{1,13},{5,17},{9,21},{13,25},... | collective-permute-start | bytes 1572872 | tf_op jit(solution)/shard_map/ppermute | solution.py:16
  15.7 33.1 %collective-permute-start.2 = (bf16[2,256,512]{2,1,0:T(8,128)(2,1)}, bf16[2,256,512]{2,1,0:T(8,128)(2,1)}, u32[]{:S(2)}, u32[]{:S(2)}) collective-permute-start(bf16[2,256,512]{2,1,0:T(8,128)(2,1)} %slice.128), channel_id=1, source_target_pairs={{0,8},{4,12},{8,16},{12,20},{16,24},{20,28},{1,9},{5,13},{9,17},{1... | collective-permute-start | bytes 1572872 | tf_op jit(solution)/shard_map/ppermute | solution.py:16
  18.6 31.3 %collective-permute-start.3 = (bf16[2,256,512]{2,1,0:T(8,128)(2,1)}, bf16[2,256,512]{2,1,0:T(8,128)(2,1)}, u32[]{:S(2)}, u32[]{:S(2)}) collective-permute-start(bf16[2,256,512]{2,1,0:T(8,128)(2,1)} %slice.128), channel_id=1, source_target_pairs={{0,4},{4,8},{8,12},{12,16},{16,20},{20,24},{24,28},{1,5},{5,9},{9,... | collective-permute-start | bytes 1572872 | tf_op jit(solution)/shard_map/ppermute | solution.py:16
  71.3 6.2 %collective-permute-start.4 = (bf16[2,2,2,2,40,2,512]{6,4,5,0,1,2,3:T(8,128)(2,1)S(1)}, bf16[2,2,2,2,40,2,512]{6,4,5,0,1,2,3:T(8,128)(2,1)S(1)}, u32[]{:S(2)}, u32[]{:S(2)}) collective-permute-start(bf16[2,2,2,2,40,2,512]{6,4,5,0,1,2,3:T(8,128)(2,1)S(1)} %fusion.32), channel_id=1, source_target_pairs={{0,4},{4,0},{8,12},{12,8},{16,20},{20,16},{24,28},{28,24},{1,5},{5... | collective-permute-start | bytes 3932168 | tf_op jit(solution)/shard_map/ppermute | solution.py:29
  78.1 17.1 %collective-permute-start.5 = (bf16[2,2,2,40,2,512]{5,3,4,0,1,2:T(8,128)(2,1)S(1)}, bf16[2,2,2,40,2,512]{5,3,4,0,1,2:T(8,128)(2,1)S(1)}, u32[]{:S(2)}, u32[]{:S(2)}) collective-permute-start(bf16[2,2,2,40,2,512]{5,3,4,0,1,2:T(8,128)(2,1)S(1)} %fusion.53), channel_id=1, source_target_pairs={{0,1},{1,0},{2,3},{3,2},{4,5},{5,4},{6,7},{7,6},{8,9},{9,8},{10,11... | collective-permute-start | bytes 1966088 | tf_op jit(solution)/shard_map/ppermute | solution.py:29
  79.8 18.3 %collective-permute-start.12 = (bf16[2,8,64,256]{3,2,1,0:T(8,128)(2,1)S(1)}, bf16[2,8,64,256]{3,2,1,0:T(8,128)(2,1)S(1)}, u32[]{:S(2)}, u32[]{:S(2)}) collective-permute-start(bf16[2,8,64,256]{3,2,1,0:T(8,128)(2,1)S(1)} %pad_maximum_fusion.4), channel_id=1, source_target_pairs={{16,0},{20,4},{24,8},{28,12},{17,1},{21,5},{25,9},{29,13},{18,2},{... | collective-permute-start | bytes 1572872 | tf_op jit(solution)/shard_map/ppermute | solution.py:16
  81.2 16.9 %collective-permute-start.11 = (bf16[2,8,64,256]{3,2,1,0:T(8,128)(2,1)S(1)}, bf16[2,8,64,256]{3,2,1,0:T(8,128)(2,1)S(1)}, u32[]{:S(2)}, u32[]{:S(2)}) collective-permute-start(bf16[2,8,64,256]{3,2,1,0:T(8,128)(2,1)S(1)} %pad_maximum_fusion.3), channel_id=1, source_target_pairs={{12,0},{16,4},{20,8},{24,12},{28,16},{13,1},{17,5},{21,9},{25,13},... | collective-permute-start | bytes 1572872 | tf_op jit(solution)/shard_map/ppermute | solution.py:16
  82.5 16.8 %collective-permute-start.10 = (bf16[2,8,64,256]{3,2,1,0:T(8,128)(2,1)S(1)}, bf16[2,8,64,256]{3,2,1,0:T(8,128)(2,1)S(1)}, u32[]{:S(2)}, u32[]{:S(2)}) collective-permute-start(bf16[2,8,64,256]{3,2,1,0:T(8,128)(2,1)S(1)} %pad_maximum_fusion.2), channel_id=1, source_target_pairs={{8,0},{12,4},{16,8},{20,12},{24,16},{28,20},{9,1},{13,5},{17,9},{2... | collective-permute-start | bytes 1572872 | tf_op jit(solution)/shard_map/ppermute | solution.py:16
  83.9 15.4 %collective-permute-start.9 = (bf16[2,8,64,256]{3,2,1,0:T(8,128)(2,1)S(1)}, bf16[2,8,64,256]{3,2,1,0:T(8,128)(2,1)S(1)}, u32[]{:S(2)}, u32[]{:S(2)}) collective-permute-start(bf16[2,8,64,256]{3,2,1,0:T(8,128)(2,1)S(1)} %pad_maximum_fusion.1), channel_id=1, source_target_pairs={{4,0},{8,4},{12,8},{16,12},{20,16},{24,20},{28,24},{5,1},{9,5},{13... | collective-permute-start | bytes 1572872 | tf_op jit(solution)/shard_map/ppermute | solution.py:16
  95.4 17.2 %collective-permute-start.6 = (bf16[2,2,40,2,512]{4,2,3,0,1:T(8,128)(2,1)S(1)}, bf16[2,2,40,2,512]{4,2,3,0,1:T(8,128)(2,1)S(1)}, u32[]{:S(2)}, u32[]{:S(2)}) collective-permute-start(bf16[2,2,40,2,512]{4,2,3,0,1:T(8,128)(2,1)S(1)} %fusion.59), channel_id=1, source_target_pairs={{0,2},{1,3},{2,0},{3,1},{4,6},{5,7},{6,4},{7,5},{8,10},{9,11},{10,... | collective-permute-start | bytes 983048 | tf_op jit(solution)/shard_map/ppermute | solution.py:29
  112.8 4.7 %collective-permute-start.7 = (bf16[2,40,2,256]{3,1,2,0:T(8,128)(2,1)S(1)}, bf16[2,40,2,256]{3,1,2,0:T(8,128)(2,1)S(1)}, u32[]{:S(2)}, u32[]{:S(2)}) collective-permute-start(bf16[2,40,2,256]{3,1,2,0:T(8,128)(2,1)S(1)} %fusion.76), channel_id=1, source_target_pairs={{0,16},{4,20},{8,24},{12,28},{16,0},{20,4},{24,8},{28,12},{1,17},{... | collective-permute-start | bytes 245768 | tf_op jit(solution)/shard_map/ppermute | solution.py:29
  117.6 4.1 %collective-permute-start.8 = (bf16[40,2,256]{2,0,1:T(8,128)(2,1)S(1)}, bf16[40,2,256]{2,0,1:T(8,128)(2,1)S(1)}, u32[]{:S(2)}, u32[]{:S(2)}) collective-permute-start(bf16[40,2,256]{2,0,1:T(8,128)(2,1)S(1)} %fusion.79), channel_id=1, source_target_pairs={{0,8},{4,12},{8,0},{12,4},{16,24},{20,28},{24,16},{28,20},{1,9},{5... | collective-permute-start | bytes 122888 | tf_op jit(solution)/shard_map/ppermute | solution.py:29
  125.2 2.7 %collective-permute-start.15 = (bf16[2,2,2,2,32,2,512]{6,4,5,3,2,1,0:T(8,128)(2,1)S(1)}, bf16[2,2,2,2,32,2,512]{6,4,5,3,2,1,0:T(8,128)(2,1)S(1)}, u32[]{:S(2)}, u32[]{:S(2)}) collective-permute-start(bf16[2,2,2,2,32,2,512]{6,4,5,3,2,1,0:T(8,128)(2,1)S(1)} %fusion.48), channel_id=1, source_target_pairs={{0,4},{4,0},{8,12},{12,8},{16,20},{20,16},{24,28},{28,24},{1,5},{5... | collective-permute-start | bytes 3145736 | tf_op jit(solution)/shard_map/ppermute | solution.py:29
  128.7 8.7 %collective-permute-start.16 = (bf16[2,2,2,32,2,256]{5,3,4,2,1,0:T(8,128)(2,1)S(1)}, bf16[2,2,2,32,2,256]{5,3,4,2,1,0:T(8,128)(2,1)S(1)}, u32[]{:S(2)}, u32[]{:S(2)}) collective-permute-start(bf16[2,2,2,32,2,256]{5,3,4,2,1,0:T(8,128)(2,1)S(1)} %fusion.60), channel_id=1, source_target_pairs={{0,16},{4,20},{8,24},{12,28},{16,0},{20,4},{24,8},{28,12},{1,17},{... | collective-permute-start | bytes 786440 | tf_op jit(solution)/shard_map/ppermute | solution.py:29
  130.8 16.9 %collective-permute-start.13 = (bf16[2,40,2,256]{3,1,2,0:T(8,128)(2,1)S(1)}, bf16[2,40,2,256]{3,1,2,0:T(8,128)(2,1)S(1)}, u32[]{:S(2)}, u32[]{:S(2)}) collective-permute-start(bf16[2,40,2,256]{3,1,2,0:T(8,128)(2,1)S(1)} %fusion.77), channel_id=1, source_target_pairs={{0,8},{4,12},{8,0},{12,4},{16,24},{20,28},{24,16},{28,20},{1,9},{5... | collective-permute-start | bytes 245768 | tf_op jit(solution)/shard_map/ppermute | solution.py:29
  130.9 10.6 %collective-permute-start.18 = (bf16[2,2,2,32,2,256]{5,3,4,2,1,0:T(8,128)(2,1)S(1)}, bf16[2,2,2,32,2,256]{5,3,4,2,1,0:T(8,128)(2,1)S(1)}, u32[]{:S(2)}, u32[]{:S(2)}) collective-permute-start(bf16[2,2,2,32,2,256]{5,3,4,2,1,0:T(8,128)(2,1)S(1)} %fusion.61), channel_id=1, source_target_pairs={{0,8},{4,12},{8,0},{12,4},{16,24},{20,28},{24,16},{28,20},{1,9},{5... | collective-permute-start | bytes 786440 | tf_op jit(solution)/shard_map/ppermute | solution.py:29
  137.5 6.0 %collective-permute-start.17 = (bf16[2,2,32,2,256]{4,2,3,1,0:T(8,128)(2,1)S(1)}, bf16[2,2,32,2,256]{4,2,3,1,0:T(8,128)(2,1)S(1)}, u32[]{:S(2)}, u32[]{:S(2)}) collective-permute-start(bf16[2,2,32,2,256]{4,2,3,1,0:T(8,128)(2,1)S(1)} %fusion.73), channel_id=1, source_target_pairs={{0,8},{4,12},{8,0},{12,4},{16,24},{20,28},{24,16},{28,20},{1,9},{5... | collective-permute-start | bytes 393224 | tf_op jit(solution)/shard_map/ppermute | solution.py:29
  141.6 5.0 %collective-permute-start.19 = (bf16[2,2,32,2,256]{4,2,3,1,0:T(8,128)(2,1)S(1)}, bf16[2,2,32,2,256]{4,2,3,1,0:T(8,128)(2,1)S(1)}, u32[]{:S(2)}, u32[]{:S(2)}) collective-permute-start(bf16[2,2,32,2,256]{4,2,3,1,0:T(8,128)(2,1)S(1)} %fusion.74), channel_id=1, source_target_pairs={{0,16},{4,20},{8,24},{12,28},{16,0},{20,4},{24,8},{28,12},{1,17},{... | collective-permute-start | bytes 393224 | tf_op jit(solution)/shard_map/ppermute | solution.py:29
  146.7 5.7 %collective-permute-start.20 = (bf16[2,32,2,512]{3,1,2,0:T(8,128)(2,1)S(1)}, bf16[2,32,2,512]{3,1,2,0:T(8,128)(2,1)S(1)}, u32[]{:S(2)}, u32[]{:S(2)}) collective-permute-start(bf16[2,32,2,512]{3,1,2,0:T(8,128)(2,1)S(1)} %fusion.75), channel_id=1, source_target_pairs={{0,1},{1,0},{2,3},{3,2},{4,5},{5,4},{6,7},{7,6},{8,9},{9,8},{10,11... | collective-permute-start | bytes 393224 | tf_op jit(solution)/shard_map/ppermute | solution.py:29
  147.8 7.1 %collective-permute-start.14 = (bf16[40,2,256]{2,0,1:T(8,128)(2,1)S(1)}, bf16[40,2,256]{2,0,1:T(8,128)(2,1)S(1)}, u32[]{:S(2)}, u32[]{:S(2)}) collective-permute-start(bf16[40,2,256]{2,0,1:T(8,128)(2,1)S(1)} %fusion.80), channel_id=1, source_target_pairs={{0,16},{4,20},{8,24},{12,28},{16,0},{20,4},{24,8},{28,12},{1,17},{... | collective-permute-start | bytes 122888 | tf_op jit(solution)/shard_map/ppermute | solution.py:29
  152.5 5.2 %collective-permute-start.21 = (bf16[32,2,512]{2,0,1:T(8,128)(2,1)S(1)}, bf16[32,2,512]{2,0,1:T(8,128)(2,1)S(1)}, u32[]{:S(2)}, u32[]{:S(2)}) collective-permute-start(bf16[32,2,512]{2,0,1:T(8,128)(2,1)S(1)} %fusion.78), channel_id=1, source_target_pairs={{0,2},{1,3},{2,0},{3,1},{4,6},{5,7},{6,4},{7,5},{8,10},{9,11},{10,... | collective-permute-start | bytes 196616 | tf_op jit(solution)/shard_map/ppermute | solution.py:29
  (8 other events, 38.4 us)

commit v15 on v14

--- a/solution.py
+++ b/solution.py
@@ -196,7 +196,7 @@
             early_terms, local_count, ("tm", "night"), "tm", jnp.bfloat16, tail_first=True
         )
     owned = jnp.stack([grad_key[..., span * rows :], grad_value[..., span * rows :]])
-    for offset in range(1, span + 1):
+    for offset in range(span, 0, -1):
         lower = (span - offset) * rows
         piece = jnp.stack(
             [grad_key[..., lower : lower + rows], grad_value[..., lower : lower + rows]]

time: 159 us -> 171 us (1.075)
  starting transfers between devices: 37.5 us -> 57.3 us
  waiting for transfers between devices: 64.9 us -> 56.8 us
    ppermute x14, starting transfers between devices: 18.1 us -> 37.9 us  [halve(): lax.ppermute(send.astype(send_type), axis, pairs).astype(keep.dtype)]
    ppermute x14, waiting for transfers between devices: 50.4 us -> 34 us  [halve(): lax.ppermute(send.astype(send_type), axis, pairs).astype(keep.dtype)]
    ppermute x8, waiting for transfers between devices: 14.6 us -> 22.7 us  [shifted(): return lax.ppermute(value, axis, pairs)]
  transfers between devices with their start and end apart: 22 -> 22, of which waited for: 14 -> 14; matrix products, arithmetic and copies ran while one was open for 13% -> 12% of each run, Pallas kernels for 0% -> 0%
where the time goes in v15:
time: 171 us; the launch traced here: 170 us
  starting transfers between devices  57.3 us (34%)
  waiting for transfers between devices  56.8 us (33%)
  matrix products  27.9 us (16%)
  local copies, waits for them, and re-layouts  15.9 us (9%)
  other arithmetic  9.67 us (6%)
  between operations  2.69 us (2%)
    ppermute x14, starting transfers between devices, halve(): lax.ppermute(send.astype(send_type), axis, pairs).astype(keep.dtype)  37.9 us
    ppermute x14, waiting for transfers between devices, halve(): lax.ppermute(send.astype(send_type), axis, pairs).astype(keep.dtype)  34 us
    ppermute x8, waiting for transfers between devices, shifted(): return lax.ppermute(value, axis, pairs)  22.7 us
    ppermute x8, starting transfers between devices, shifted(): return lax.ppermute(value, axis, pairs)  19.4 us
    unnamed x24, local copies, waits for them, and re-layouts  7.03 us
    dot_general x1, matrix products, shards(): jnp.einsum('rd,dwh->wrh', grad_out, weights, preferred_element_type=jnp.f...  4.81 us
    dot_general x1, matrix products, shards(): jnp.einsum('rd,dwh->wrh', normed, weights, preferred_element_type=jnp.flo...  3.98 us
    dot_general x1, matrix products, band_block(): jnp.einsum('qgc,kgc->gqk', grad_attn, values_blk, preferred_element_type=...  3.92 us
  transfers between devices with their start and end apart: 22, of which 14 were waited for; matrix products, arithmetic and copies ran while one was open for 12% of the time, Pallas kernels for 0%

profile of v15, /device:TPU:0, one launch (start us, length us, event | category | flops | bytes accessed | tf_op | source)
XLA Modules:
  0.0 170.2 jit_solution(291338459149784919)
XLA Ops:
  1.9 4.0 %fusion.21 = bf16[4,256,512]{2,1,0:T(8,128)(2,1)S(1)} fusion(bf16[1024,4,512]{2,1,0:T(4,128)(2,1)} %param.7, bf16[1,256,1024]{2,1,0:T(8,128)(2,1)} %param.6, f32[256]{0:T(256)S(1)} %add_rsqrt_fusion), kind=kOutput, calls=%fused_computation.24 | convolution fusion | flops 1075052544 | bytes 5768192 | tf_op jit(solution)/shard_map/rd,dwh->wrh/dot_general | solution.py:142
  6.7 5.7 %collective-permute-start = (bf16[2,256,512]{2,1,0:T(8,128)(2,1)}, bf16[2,256,512]{2,1,0:T(8,128)(2,1)}, u32[]{:S(2)}, u32[]{:S(2)}) collective-permute-start(bf16[2,256,512]{2,1,0:T(8,128)(2,1)} %slice.128), channel_id=1, source_target_pairs={{0,16},{4,20},{8,24},{12,28},{1,17},{5,21},{9,25},{13,29},{2,18},{... | collective-permute-start | bytes 1572872 | tf_op jit(solution)/shard_map/ppermute | solution.py:16
  12.4 3.3 %collective-permute-start.1 = (bf16[2,256,512]{2,1,0:T(8,128)(2,1)}, bf16[2,256,512]{2,1,0:T(8,128)(2,1)}, u32[]{:S(2)}, u32[]{:S(2)}) collective-permute-start(bf16[2,256,512]{2,1,0:T(8,128)(2,1)} %slice.128), channel_id=1, source_target_pairs={{0,12},{4,16},{8,20},{12,24},{16,28},{1,13},{5,17},{9,21},{13,25},... | collective-permute-start | bytes 1572872 | tf_op jit(solution)/shard_map/ppermute | solution.py:16
  15.7 2.9 %collective-permute-start.2 = (bf16[2,256,512]{2,1,0:T(8,128)(2,1)}, bf16[2,256,512]{2,1,0:T(8,128)(2,1)}, u32[]{:S(2)}, u32[]{:S(2)}) collective-permute-start(bf16[2,256,512]{2,1,0:T(8,128)(2,1)} %slice.128), channel_id=1, source_target_pairs={{0,8},{4,12},{8,16},{12,20},{16,24},{20,28},{1,9},{5,13},{9,17},{1... | collective-permute-start | bytes 1572872 | tf_op jit(solution)/shard_map/ppermute | solution.py:16
  21.9 4.8 %fusion.18 = bf16[4,256,512]{2,1,0:T(8,128)(2,1)} fusion(bf16[1024,4,512]{2,1,0:T(4,128)(2,1)} %param.7, bf16[1,256,1024]{2,1,0:T(8,128)(2,1)S(1)} %copy-done.5, pred[256]{0:T(512)(128)(4,1)S(1)} %compare_reduce_fusion), kind=kOutput, calls=%fused_computation.23 | convolution fusion | flops 1074528256 | bytes 5767424 | tf_op jit(solution)/shard_map/rd,dwh->wrh/dot_general | solution.py:153
  33.3 13.4 %collective-permute-done = bf16[2,256,512]{2,1,0:T(8,128)(2,1)} collective-permute-done((bf16[2,256,512]{2,1,0:T(8,128)(2,1)}, bf16[2,256,512]{2,1,0:T(8,128)(2,1)}, u32[]{:S(2)}, u32[]{:S(2)}) %collective-permute-start) | collective-permute-done | bytes 524320 | tf_op jit(solution)/shard_map/ppermute | solution.py:16
  55.3 3.9 %fusion.1 = (f32[8,256]{1,0:T(8,128)S(1)}, f32[8,256,1280]{2,1,0:T(8,128)S(1)}) fusion(f32[256,1280]{1,0:T(8,128)} %fusion.37, bf16[256,8,64]{0,2,1:T(8,128)(2,1)S(1)} %bitcast.202, bf16[1280,8,64]{0,2,1:T(8,128)(2,1)S(1)} %bitcast.199), kind=kOutput, calls=%fused_computation.3 | convolution fusion | flops 343406592 | bytes 13377536 | tf_op jit(solution)/shard_map/qgc,kgc->gqk/dot_general | solution.py:102
  59.3 2.8 %multiply_reduce_fusion = (f32[256,8]{0,1:T(8,128)S(1)}, bf16[8,64,256]{2,1,0:T(8,128)(2,1)S(1)}) fusion(bf16[256,8,64]{0,2,1:T(8,128)(2,1)S(1)} %bitcast.212, bf16[1280,8,64]{0,2,1:T(8,128)(2,1)S(1)} %bitcast.209, f32[8,256]{1,0:T(8,128)S(1)} %get-tuple-element.34, f32[256,1280]{1,0:T(8,128)S(1)} %copy-done, f32[8,256,1280]{2,1,0:T(8,128)S(1)} %get-tuple-element.35), kind=kOutput, calls=%fused_computation.80 | convolution fusion | flops 346683392 | bytes 13647872 | tf_op jit(solution)/shard_map/gqk,kgc->qgc/dot_general | solution.py:108
  62.1 3.9 %multiply_convert_fusion = bf16[8,256,1280]{2,1,0:T(8,128)(2,1)S(1)} fusion(bf16[256,8,64]{0,2,1:T(8,128)(2,1)S(1)} %bitcast.213, bf16[1280,8,64]{0,2,1:T(8,128)(2,1)S(1)} %bitcast.210, f32[8,256]{1,0:T(8,128)S(1)} %bitcast.216, f32[8,256]{1,0:T(8,128)S(1)} %get-tuple-element.34, f32[256,1280]{1,0:T(8,128)S(1)} %copy-done, ...), kind=kOutput, calls=%fused_computation | convolution fusion | flops 353894400 | bytes 18628608 | tf_op jit(solution)/shard_map/qgc,kgc->gqk/dot_general | solution.py:112
  71.3 3.6 %collective-permute-start.4 = (bf16[2,2,2,2,40,2,512]{6,4,5,0,1,2,3:T(8,128)(2,1)S(1)}, bf16[2,2,2,2,40,2,512]{6,4,5,0,1,2,3:T(8,128)(2,1)S(1)}, u32[]{:S(2)}, u32[]{:S(2)}) collective-permute-start(bf16[2,2,2,2,40,2,512]{6,4,5,0,1,2,3:T(8,128)(2,1)S(1)} %fusion.32), channel_id=1, source_target_pairs={{0,4},{4,0},{8,12},{12,8},{16,20},{20,16},{24,28},{28,24},{1,5},{5... | collective-permute-start | bytes 3932168 | tf_op jit(solution)/shard_map/ppermute | solution.py:29
  74.9 2.3 %fusion.96 = (bf16[8,64,1280]{2,1,0:T(8,128)(2,1)S(1)}, f32[8,64,1280]{2,1,0:T(8,128)S(1)}) fusion(bf16[256,8,64]{0,2,1:T(8,128)(2,1)S(1)} %bitcast.214, f32[8,256]{1,0:T(8,128)S(1)} %get-tuple-element.34, f32[256,1280]{1,0:T(8,128)S(1)} %copy-done, f32[8,256,1280]{2,1,0:T(8,128)S(1)} %get-tuple-element.35), kind=kOutput, calls=%fused_computation.175 | convolution fusion | flops 346685440 | bytes 15998976 | tf_op jit(solution)/shard_map/gqk,qgc->gck/dot_general | solution.py:122
  85.5 9.7 %collective-permute-done.5 = bf16[2,2,2,40,2,512]{5,3,4,0,1,2:T(8,128)(2,1)S(1)} collective-permute-done((bf16[2,2,2,40,2,512]{5,3,4,0,1,2:T(8,128)(2,1)S(1)}, bf16[2,2,2,40,2,512]{5,3,4,0,1,2:T(8,128)(2,1)S(1)}, u32[]{:S(2)}, u32[]{:S(2)}) %collective-permute-start.5) | collective-permute-done | bytes 655392 | tf_op jit(solution)/shard_map/ppermute | solution.py:29
  95.4 2.7 %collective-permute-start.6 = (bf16[2,2,40,2,512]{4,2,3,0,1:T(8,128)(2,1)S(1)}, bf16[2,2,40,2,512]{4,2,3,0,1:T(8,128)(2,1)S(1)}, u32[]{:S(2)}, u32[]{:S(2)}) collective-permute-start(bf16[2,2,40,2,512]{4,2,3,0,1:T(8,128)(2,1)S(1)} %fusion.59), channel_id=1, source_target_pairs={{0,2},{1,3},{2,0},{3,1},{4,6},{5,7},{6,4},{7,5},{8,10},{9,11},{10,... | collective-permute-start | bytes 983048 | tf_op jit(solution)/shard_map/ppermute | solution.py:29
  98.1 7.4 %collective-permute-done.11 = bf16[2,8,64,256]{3,2,1,0:T(8,128)(2,1)S(1)} collective-permute-done((bf16[2,8,64,256]{3,2,1,0:T(8,128)(2,1)S(1)}, bf16[2,8,64,256]{3,2,1,0:T(8,128)(2,1)S(1)}, u32[]{:S(2)}, u32[]{:S(2)}) %collective-permute-start.11) | collective-permute-done | bytes 524320 | tf_op jit(solution)/shard_map/ppermute | solution.py:16
  108.0 4.6 %collective-permute-done.6 = bf16[2,2,40,2,512]{4,2,3,0,1:T(8,128)(2,1)S(1)} collective-permute-done((bf16[2,2,40,2,512]{4,2,3,0,1:T(8,128)(2,1)S(1)}, bf16[2,2,40,2,512]{4,2,3,0,1:T(8,128)(2,1)S(1)}, u32[]{:S(2)}, u32[]{:S(2)}) %collective-permute-start.6) | collective-permute-done | bytes 327712 | tf_op jit(solution)/shard_map/ppermute | solution.py:29
  112.8 2.3 %collective-permute-start.7 = (bf16[2,40,2,256]{3,1,2,0:T(8,128)(2,1)S(1)}, bf16[2,40,2,256]{3,1,2,0:T(8,128)(2,1)S(1)}, u32[]{:S(2)}, u32[]{:S(2)}) collective-permute-start(bf16[2,40,2,256]{3,1,2,0:T(8,128)(2,1)S(1)} %fusion.76), channel_id=1, source_target_pairs={{0,16},{4,20},{8,24},{12,28},{16,0},{20,4},{24,8},{28,12},{1,17},{... | collective-permute-start | bytes 245768 | tf_op jit(solution)/shard_map/ppermute | solution.py:29
  117.6 15.5 %collective-permute-start.8 = (bf16[40,2,256]{2,0,1:T(8,128)(2,1)S(1)}, bf16[40,2,256]{2,0,1:T(8,128)(2,1)S(1)}, u32[]{:S(2)}, u32[]{:S(2)}) collective-permute-start(bf16[40,2,256]{2,0,1:T(8,128)(2,1)S(1)} %fusion.79), channel_id=1, source_target_pairs={{0,8},{4,12},{8,0},{12,4},{16,24},{20,28},{24,16},{28,20},{1,9},{5... | collective-permute-start | bytes 122888 | tf_op jit(solution)/shard_map/ppermute | solution.py:29
  138.7 2.6 %collective-permute-done.15 = bf16[2,2,2,2,32,2,512]{6,4,5,3,2,1,0:T(8,128)(2,1)S(1)} collective-permute-done((bf16[2,2,2,2,32,2,512]{6,4,5,3,2,1,0:T(8,128)(2,1)S(1)}, bf16[2,2,2,2,32,2,512]{6,4,5,3,2,1,0:T(8,128)(2,1)S(1)}, u32[]{:S(2)}, u32[]{:S(2)}) %collective-permute-start.15) | collective-permute-done | bytes 1048608 | tf_op jit(solution)/shard_map/ppermute | solution.py:29
  144.4 6.1 %collective-permute-done.16 = bf16[2,2,2,32,2,256]{5,3,4,2,1,0:T(8,128)(2,1)S(1)} collective-permute-done((bf16[2,2,2,32,2,256]{5,3,4,2,1,0:T(8,128)(2,1)S(1)}, bf16[2,2,2,32,2,256]{5,3,4,2,1,0:T(8,128)(2,1)S(1)}, u32[]{:S(2)}, u32[]{:S(2)}) %collective-permute-start.16) | collective-permute-done | bytes 262176 | tf_op jit(solution)/shard_map/ppermute | solution.py:29
  152.8 2.5 %collective-permute-start.19 = (bf16[2,2,32,2,256]{4,2,3,1,0:T(8,128)(2,1)S(1)}, bf16[2,2,32,2,256]{4,2,3,1,0:T(8,128)(2,1)S(1)}, u32[]{:S(2)}, u32[]{:S(2)}) collective-permute-start(bf16[2,2,32,2,256]{4,2,3,1,0:T(8,128)(2,1)S(1)} %fusion.74), channel_id=1, source_target_pairs={{0,16},{4,20},{8,24},{12,28},{16,0},{20,4},{24,8},{28,12},{1,17},{... | collective-permute-start | bytes 393224 | tf_op jit(solution)/shard_map/ppermute | solution.py:29
  155.7 2.6 %collective-permute-done.19 = bf16[2,2,32,2,256]{4,2,3,1,0:T(8,128)(2,1)S(1)} collective-permute-done((bf16[2,2,32,2,256]{4,2,3,1,0:T(8,128)(2,1)S(1)}, bf16[2,2,32,2,256]{4,2,3,1,0:T(8,128)(2,1)S(1)}, u32[]{:S(2)}, u32[]{:S(2)}) %collective-permute-start.19) | collective-permute-done | bytes 131104 | tf_op jit(solution)/shard_map/ppermute | solution.py:29
  161.0 2.4 %collective-permute-done.20 = bf16[2,32,2,512]{3,1,2,0:T(8,128)(2,1)S(1)} collective-permute-done((bf16[2,32,2,512]{3,1,2,0:T(8,128)(2,1)S(1)}, bf16[2,32,2,512]{3,1,2,0:T(8,128)(2,1)S(1)}, u32[]{:S(2)}, u32[]{:S(2)}) %collective-permute-start.20) | collective-permute-done | bytes 131104 | tf_op jit(solution)/shard_map/ppermute | solution.py:29
  163.5 2.7 %collective-permute-start.21 = (bf16[32,2,512]{2,0,1:T(8,128)(2,1)S(1)}, bf16[32,2,512]{2,0,1:T(8,128)(2,1)S(1)}, u32[]{:S(2)}, u32[]{:S(2)}) collective-permute-start(bf16[32,2,512]{2,0,1:T(8,128)(2,1)S(1)} %fusion.78), channel_id=1, source_target_pairs={{0,2},{1,3},{2,0},{3,1},{4,6},{5,7},{6,4},{7,5},{8,10},{9,11},{10,... | collective-permute-start | bytes 196616 | tf_op jit(solution)/shard_map/ppermute | solution.py:29
  166.2 3.1 %collective-permute-done.21 = bf16[32,2,512]{2,0,1:T(8,128)(2,1)S(1)} collective-permute-done((bf16[32,2,512]{2,0,1:T(8,128)(2,1)S(1)}, bf16[32,2,512]{2,0,1:T(8,128)(2,1)S(1)}, u32[]{:S(2)}, u32[]{:S(2)}) %collective-permute-start.21) | collective-permute-done | bytes 65568 | tf_op jit(solution)/shard_map/ppermute | solution.py:29
  (123 shorter events, 52.8 us)
Async XLA Ops:
  1.9 18.9 %copy-start.7 = (s32[1,256]{1,0:T(1,128)S(1)}, s32[1,256]{1,0:T(1,128)}, u32[]{:S(2)}) copy-start(s32[1,256]{1,0:T(1,128)} %param.9) | copy-start | bytes 3076
  1.9 20.1 %copy-start.5 = (bf16[1,256,1024]{2,1,0:T(8,128)(2,1)S(1)}, bf16[1,256,1024]{2,1,0:T(8,128)(2,1)}, u32[]{:S(2)}) copy-start(bf16[1,256,1024]{2,1,0:T(8,128)(2,1)} %param.8) | copy-start | bytes 1572868
  6.7 40.0 %collective-permute-start = (bf16[2,256,512]{2,1,0:T(8,128)(2,1)}, bf16[2,256,512]{2,1,0:T(8,128)(2,1)}, u32[]{:S(2)}, u32[]{:S(2)}) collective-permute-start(bf16[2,256,512]{2,1,0:T(8,128)(2,1)} %slice.128), channel_id=1, source_target_pairs={{0,16},{4,20},{8,24},{12,28},{1,17},{5,21},{9,25},{13,29},{2,18},{... | collective-permute-start | bytes 1572872 | tf_op jit(solution)/shard_map/ppermute | solution.py:16
  12.4 35.4 %collective-permute-start.1 = (bf16[2,256,512]{2,1,0:T(8,128)(2,1)}, bf16[2,256,512]{2,1,0:T(8,128)(2,1)}, u32[]{:S(2)}, u32[]{:S(2)}) collective-permute-start(bf16[2,256,512]{2,1,0:T(8,128)(2,1)} %slice.128), channel_id=1, source_target_pairs={{0,12},{4,16},{8,20},{12,24},{16,28},{1,13},{5,17},{9,21},{13,25},... | collective-permute-start | bytes 1572872 | tf_op jit(solution)/shard_map/ppermute | solution.py:16
  15.7 33.1 %collective-permute-start.2 = (bf16[2,256,512]{2,1,0:T(8,128)(2,1)}, bf16[2,256,512]{2,1,0:T(8,128)(2,1)}, u32[]{:S(2)}, u32[]{:S(2)}) collective-permute-start(bf16[2,256,512]{2,1,0:T(8,128)(2,1)} %slice.128), channel_id=1, source_target_pairs={{0,8},{4,12},{8,16},{12,20},{16,24},{20,28},{1,9},{5,13},{9,17},{1... | collective-permute-start | bytes 1572872 | tf_op jit(solution)/shard_map/ppermute | solution.py:16
  18.6 31.3 %collective-permute-start.3 = (bf16[2,256,512]{2,1,0:T(8,128)(2,1)}, bf16[2,256,512]{2,1,0:T(8,128)(2,1)}, u32[]{:S(2)}, u32[]{:S(2)}) collective-permute-start(bf16[2,256,512]{2,1,0:T(8,128)(2,1)} %slice.128), channel_id=1, source_target_pairs={{0,4},{4,8},{8,12},{12,16},{16,20},{20,24},{24,28},{1,5},{5,9},{9,... | collective-permute-start | bytes 1572872 | tf_op jit(solution)/shard_map/ppermute | solution.py:16
  71.3 6.2 %collective-permute-start.4 = (bf16[2,2,2,2,40,2,512]{6,4,5,0,1,2,3:T(8,128)(2,1)S(1)}, bf16[2,2,2,2,40,2,512]{6,4,5,0,1,2,3:T(8,128)(2,1)S(1)}, u32[]{:S(2)}, u32[]{:S(2)}) collective-permute-start(bf16[2,2,2,2,40,2,512]{6,4,5,0,1,2,3:T(8,128)(2,1)S(1)} %fusion.32), channel_id=1, source_target_pairs={{0,4},{4,0},{8,12},{12,8},{16,20},{20,16},{24,28},{28,24},{1,5},{5... | collective-permute-start | bytes 3932168 | tf_op jit(solution)/shard_map/ppermute | solution.py:29
  78.1 17.1 %collective-permute-start.5 = (bf16[2,2,2,40,2,512]{5,3,4,0,1,2:T(8,128)(2,1)S(1)}, bf16[2,2,2,40,2,512]{5,3,4,0,1,2:T(8,128)(2,1)S(1)}, u32[]{:S(2)}, u32[]{:S(2)}) collective-permute-start(bf16[2,2,2,40,2,512]{5,3,4,0,1,2:T(8,128)(2,1)S(1)} %fusion.53), channel_id=1, source_target_pairs={{0,1},{1,0},{2,3},{3,2},{4,5},{5,4},{6,7},{7,6},{8,9},{9,8},{10,11... | collective-permute-start | bytes 1966088 | tf_op jit(solution)/shard_map/ppermute | solution.py:29
  79.8 18.3 %collective-permute-start.12 = (bf16[2,8,64,256]{3,2,1,0:T(8,128)(2,1)S(1)}, bf16[2,8,64,256]{3,2,1,0:T(8,128)(2,1)S(1)}, u32[]{:S(2)}, u32[]{:S(2)}) collective-permute-start(bf16[2,8,64,256]{3,2,1,0:T(8,128)(2,1)S(1)} %pad_maximum_fusion.4), channel_id=1, source_target_pairs={{4,0},{8,4},{12,8},{16,12},{20,16},{24,20},{28,24},{5,1},{9,5},{13... | collective-permute-start | bytes 1572872 | tf_op jit(solution)/shard_map/ppermute | solution.py:16
  81.2 24.4 %collective-permute-start.11 = (bf16[2,8,64,256]{3,2,1,0:T(8,128)(2,1)S(1)}, bf16[2,8,64,256]{3,2,1,0:T(8,128)(2,1)S(1)}, u32[]{:S(2)}, u32[]{:S(2)}) collective-permute-start(bf16[2,8,64,256]{3,2,1,0:T(8,128)(2,1)S(1)} %pad_maximum_fusion.3), channel_id=1, source_target_pairs={{8,0},{12,4},{16,8},{20,12},{24,16},{28,20},{9,1},{13,5},{17,9},{2... | collective-permute-start | bytes 1572872 | tf_op jit(solution)/shard_map/ppermute | solution.py:16
  82.5 24.9 %collective-permute-start.10 = (bf16[2,8,64,256]{3,2,1,0:T(8,128)(2,1)S(1)}, bf16[2,8,64,256]{3,2,1,0:T(8,128)(2,1)S(1)}, u32[]{:S(2)}, u32[]{:S(2)}) collective-permute-start(bf16[2,8,64,256]{3,2,1,0:T(8,128)(2,1)S(1)} %pad_maximum_fusion.2), channel_id=1, source_target_pairs={{12,0},{16,4},{20,8},{24,12},{28,16},{13,1},{17,5},{21,9},{25,13},... | collective-permute-start | bytes 1572872 | tf_op jit(solution)/shard_map/ppermute | solution.py:16
  83.9 23.5 %collective-permute-start.9 = (bf16[2,8,64,256]{3,2,1,0:T(8,128)(2,1)S(1)}, bf16[2,8,64,256]{3,2,1,0:T(8,128)(2,1)S(1)}, u32[]{:S(2)}, u32[]{:S(2)}) collective-permute-start(bf16[2,8,64,256]{3,2,1,0:T(8,128)(2,1)S(1)} %pad_maximum_fusion.1), channel_id=1, source_target_pairs={{16,0},{20,4},{24,8},{28,12},{17,1},{21,5},{25,9},{29,13},{18,2},{... | collective-permute-start | bytes 1572872 | tf_op jit(solution)/shard_map/ppermute | solution.py:16
  95.4 17.2 %collective-permute-start.6 = (bf16[2,2,40,2,512]{4,2,3,0,1:T(8,128)(2,1)S(1)}, bf16[2,2,40,2,512]{4,2,3,0,1:T(8,128)(2,1)S(1)}, u32[]{:S(2)}, u32[]{:S(2)}) collective-permute-start(bf16[2,2,40,2,512]{4,2,3,0,1:T(8,128)(2,1)S(1)} %fusion.59), channel_id=1, source_target_pairs={{0,2},{1,3},{2,0},{3,1},{4,6},{5,7},{6,4},{7,5},{8,10},{9,11},{10,... | collective-permute-start | bytes 983048 | tf_op jit(solution)/shard_map/ppermute | solution.py:29
  112.8 4.7 %collective-permute-start.7 = (bf16[2,40,2,256]{3,1,2,0:T(8,128)(2,1)S(1)}, bf16[2,40,2,256]{3,1,2,0:T(8,128)(2,1)S(1)}, u32[]{:S(2)}, u32[]{:S(2)}) collective-permute-start(bf16[2,40,2,256]{3,1,2,0:T(8,128)(2,1)S(1)} %fusion.76), channel_id=1, source_target_pairs={{0,16},{4,20},{8,24},{12,28},{16,0},{20,4},{24,8},{28,12},{1,17},{... | collective-permute-start | bytes 245768 | tf_op jit(solution)/shard_map/ppermute | solution.py:29
  117.6 17.5 %collective-permute-start.8 = (bf16[40,2,256]{2,0,1:T(8,128)(2,1)S(1)}, bf16[40,2,256]{2,0,1:T(8,128)(2,1)S(1)}, u32[]{:S(2)}, u32[]{:S(2)}) collective-permute-start(bf16[40,2,256]{2,0,1:T(8,128)(2,1)S(1)} %fusion.79), channel_id=1, source_target_pairs={{0,8},{4,12},{8,0},{12,4},{16,24},{20,28},{24,16},{28,20},{1,9},{5... | collective-permute-start | bytes 122888 | tf_op jit(solution)/shard_map/ppermute | solution.py:29
  138.6 2.7 %collective-permute-start.15 = (bf16[2,2,2,2,32,2,512]{6,4,5,3,2,1,0:T(8,128)(2,1)S(1)}, bf16[2,2,2,2,32,2,512]{6,4,5,3,2,1,0:T(8,128)(2,1)S(1)}, u32[]{:S(2)}, u32[]{:S(2)}) collective-permute-start(bf16[2,2,2,2,32,2,512]{6,4,5,3,2,1,0:T(8,128)(2,1)S(1)} %fusion.48), channel_id=1, source_target_pairs={{0,4},{4,0},{8,12},{12,8},{16,20},{20,16},{24,28},{28,24},{1,5},{5... | collective-permute-start | bytes 3145736 | tf_op jit(solution)/shard_map/ppermute | solution.py:29
  142.1 8.4 %collective-permute-start.16 = (bf16[2,2,2,32,2,256]{5,3,4,2,1,0:T(8,128)(2,1)S(1)}, bf16[2,2,2,32,2,256]{5,3,4,2,1,0:T(8,128)(2,1)S(1)}, u32[]{:S(2)}, u32[]{:S(2)}) collective-permute-start(bf16[2,2,2,32,2,256]{5,3,4,2,1,0:T(8,128)(2,1)S(1)} %fusion.60), channel_id=1, source_target_pairs={{0,16},{4,20},{8,24},{12,28},{16,0},{20,4},{24,8},{28,12},{1,17},{... | collective-permute-start | bytes 786440 | tf_op jit(solution)/shard_map/ppermute | solution.py:29
  142.2 16.7 %collective-permute-start.13 = (bf16[2,40,2,256]{3,1,2,0:T(8,128)(2,1)S(1)}, bf16[2,40,2,256]{3,1,2,0:T(8,128)(2,1)S(1)}, u32[]{:S(2)}, u32[]{:S(2)}) collective-permute-start(bf16[2,40,2,256]{3,1,2,0:T(8,128)(2,1)S(1)} %fusion.77), channel_id=1, source_target_pairs={{0,8},{4,12},{8,0},{12,4},{16,24},{20,28},{24,16},{28,20},{1,9},{5... | collective-permute-start | bytes 245768 | tf_op jit(solution)/shard_map/ppermute | solution.py:29
  144.3 8.4 %collective-permute-start.18 = (bf16[2,2,2,32,2,256]{5,3,4,2,1,0:T(8,128)(2,1)S(1)}, bf16[2,2,2,32,2,256]{5,3,4,2,1,0:T(8,128)(2,1)S(1)}, u32[]{:S(2)}, u32[]{:S(2)}) collective-permute-start(bf16[2,2,2,32,2,256]{5,3,4,2,1,0:T(8,128)(2,1)S(1)} %fusion.61), channel_id=1, source_target_pairs={{0,8},{4,12},{8,0},{12,4},{16,24},{20,28},{24,16},{28,20},{1,9},{5... | collective-permute-start | bytes 786440 | tf_op jit(solution)/shard_map/ppermute | solution.py:29
  150.6 5.1 %collective-permute-start.17 = (bf16[2,2,32,2,256]{4,2,3,1,0:T(8,128)(2,1)S(1)}, bf16[2,2,32,2,256]{4,2,3,1,0:T(8,128)(2,1)S(1)}, u32[]{:S(2)}, u32[]{:S(2)}) collective-permute-start(bf16[2,2,32,2,256]{4,2,3,1,0:T(8,128)(2,1)S(1)} %fusion.73), channel_id=1, source_target_pairs={{0,8},{4,12},{8,0},{12,4},{16,24},{20,28},{24,16},{28,20},{1,9},{5... | collective-permute-start | bytes 393224 | tf_op jit(solution)/shard_map/ppermute | solution.py:29
  152.8 5.5 %collective-permute-start.19 = (bf16[2,2,32,2,256]{4,2,3,1,0:T(8,128)(2,1)S(1)}, bf16[2,2,32,2,256]{4,2,3,1,0:T(8,128)(2,1)S(1)}, u32[]{:S(2)}, u32[]{:S(2)}) collective-permute-start(bf16[2,2,32,2,256]{4,2,3,1,0:T(8,128)(2,1)S(1)} %fusion.74), channel_id=1, source_target_pairs={{0,16},{4,20},{8,24},{12,28},{16,0},{20,4},{24,8},{28,12},{1,17},{... | collective-permute-start | bytes 393224 | tf_op jit(solution)/shard_map/ppermute | solution.py:29
  158.4 5.0 %collective-permute-start.20 = (bf16[2,32,2,512]{3,1,2,0:T(8,128)(2,1)S(1)}, bf16[2,32,2,512]{3,1,2,0:T(8,128)(2,1)S(1)}, u32[]{:S(2)}, u32[]{:S(2)}) collective-permute-start(bf16[2,32,2,512]{3,1,2,0:T(8,128)(2,1)S(1)} %fusion.75), channel_id=1, source_target_pairs={{0,1},{1,0},{2,3},{3,2},{4,5},{5,4},{6,7},{7,6},{8,9},{9,8},{10,11... | collective-permute-start | bytes 393224 | tf_op jit(solution)/shard_map/ppermute | solution.py:29
  159.0 7.2 %collective-permute-start.14 = (bf16[40,2,256]{2,0,1:T(8,128)(2,1)S(1)}, bf16[40,2,256]{2,0,1:T(8,128)(2,1)S(1)}, u32[]{:S(2)}, u32[]{:S(2)}) collective-permute-start(bf16[40,2,256]{2,0,1:T(8,128)(2,1)S(1)} %fusion.80), channel_id=1, source_target_pairs={{0,16},{4,20},{8,24},{12,28},{16,0},{20,4},{24,8},{28,12},{1,17},{... | collective-permute-start | bytes 122888 | tf_op jit(solution)/shard_map/ppermute | solution.py:29
  163.5 5.8 %collective-permute-start.21 = (bf16[32,2,512]{2,0,1:T(8,128)(2,1)S(1)}, bf16[32,2,512]{2,0,1:T(8,128)(2,1)S(1)}, u32[]{:S(2)}, u32[]{:S(2)}) collective-permute-start(bf16[32,2,512]{2,0,1:T(8,128)(2,1)S(1)} %fusion.78), channel_id=1, source_target_pairs={{0,2},{1,3},{2,0},{3,1},{4,6},{5,7},{6,4},{7,5},{8,10},{9,11},{10,... | collective-permute-start | bytes 196616 | tf_op jit(solution)/shard_map/ppermute | solution.py:29
  (8 other events, 30.2 us)

commit v16 on v14

--- a/solution.py
+++ b/solution.py
@@ -144,7 +144,8 @@
     ).astype(jnp.bfloat16)
     queries = projected[0]
     key_vals = projected[1:3]
-    earlier = [shifted(key_vals, "tm", offset) for offset in range(span, 0, -1)]
+    arrived = {offset: shifted(key_vals, "tm", offset) for offset in range(1, span + 1)}
+    earlier = [arrived[offset] for offset in range(span, 0, -1)]
     extended = jnp.concatenate(earlier + [key_vals], axis=1)
     local_count = jnp.sum(loss_mask.astype(jnp.int32))
     tokens_all = rows * lax.axis_size("tm") * lax.axis_size("night")

time: 159 us -> 159 us (level)
  no operation moved by 1% of the time
where the time goes in v16:
time: 159 us
  waiting for transfers between devices  64.9 us (41%)
  starting transfers between devices  37.5 us (24%)
  matrix products  27.9 us (18%)
  local copies, waits for them, and re-layouts  15.9 us (10%)
  other arithmetic  9.67 us (6%)
  between operations  2.72 us (2%)
    ppermute x14, waiting for transfers between devices, halve(): lax.ppermute(send.astype(send_type), axis, pairs).astype(keep.dtype)  50.4 us
    ppermute x8, starting transfers between devices, shifted(): return lax.ppermute(value, axis, pairs)  19.4 us
    ppermute x14, starting transfers between devices, halve(): lax.ppermute(send.astype(send_type), axis, pairs).astype(keep.dtype)  18.1 us
    ppermute x8, waiting for transfers between devices, shifted(): return lax.ppermute(value, axis, pairs)  14.6 us
    unnamed x24, local copies, waits for them, and re-layouts  7.03 us
    dot_general x1, matrix products, shards(): jnp.einsum('rd,dwh->wrh', grad_out, weights, preferred_element_type=jnp.f...  4.81 us
    dot_general x1, matrix products, shards(): jnp.einsum('rd,dwh->wrh', normed, weights, preferred_element_type=jnp.flo...  3.98 us
    dot_general x1, matrix products, band_block(): jnp.einsum('qgc,kgc->gqk', grad_attn, values_blk, preferred_element_type=...  3.92 us
  transfers between devices with their start and end apart: 22, of which 14 were waited for; matrix products, arithmetic and copies ran while one was open for 13% of the time, Pallas kernels for 0%

profile of v16, /device:TPU:0, one launch (start us, length us, event | category | flops | bytes accessed | tf_op | source)
XLA Modules:
  0.0 158.7 jit_solution(17596671509240231237)
XLA Ops:
  1.9 4.0 %fusion.21 = bf16[4,256,512]{2,1,0:T(8,128)(2,1)S(1)} fusion(bf16[1024,4,512]{2,1,0:T(4,128)(2,1)} %param.7, bf16[1,256,1024]{2,1,0:T(8,128)(2,1)} %param.6, f32[256]{0:T(256)S(1)} %add_rsqrt_fusion), kind=kOutput, calls=%fused_computation.24 | convolution fusion | flops 1075052544 | bytes 5768192 | tf_op jit(solution)/shard_map/rd,dwh->wrh/dot_general | solution.py:142
  6.7 5.7 %collective-permute-start = (bf16[2,256,512]{2,1,0:T(8,128)(2,1)}, bf16[2,256,512]{2,1,0:T(8,128)(2,1)}, u32[]{:S(2)}, u32[]{:S(2)}) collective-permute-start(bf16[2,256,512]{2,1,0:T(8,128)(2,1)} %slice.128), channel_id=1, source_target_pairs={{0,16},{4,20},{8,24},{12,28},{1,17},{5,21},{9,25},{13,29},{2,18},{... | collective-permute-start | bytes 1572872 | tf_op jit(solution)/shard_map/ppermute | solution.py:16
  12.4 3.3 %collective-permute-start.1 = (bf16[2,256,512]{2,1,0:T(8,128)(2,1)}, bf16[2,256,512]{2,1,0:T(8,128)(2,1)}, u32[]{:S(2)}, u32[]{:S(2)}) collective-permute-start(bf16[2,256,512]{2,1,0:T(8,128)(2,1)} %slice.128), channel_id=1, source_target_pairs={{0,12},{4,16},{8,20},{12,24},{16,28},{1,13},{5,17},{9,21},{13,25},... | collective-permute-start | bytes 1572872 | tf_op jit(solution)/shard_map/ppermute | solution.py:16
  15.7 2.9 %collective-permute-start.2 = (bf16[2,256,512]{2,1,0:T(8,128)(2,1)}, bf16[2,256,512]{2,1,0:T(8,128)(2,1)}, u32[]{:S(2)}, u32[]{:S(2)}) collective-permute-start(bf16[2,256,512]{2,1,0:T(8,128)(2,1)} %slice.128), channel_id=1, source_target_pairs={{0,8},{4,12},{8,16},{12,20},{16,24},{20,28},{1,9},{5,13},{9,17},{1... | collective-permute-start | bytes 1572872 | tf_op jit(solution)/shard_map/ppermute | solution.py:16
  18.6 2.1 %collective-permute-start.3 = (bf16[2,256,512]{2,1,0:T(8,128)(2,1)}, bf16[2,256,512]{2,1,0:T(8,128)(2,1)}, u32[]{:S(2)}, u32[]{:S(2)}) collective-permute-start(bf16[2,256,512]{2,1,0:T(8,128)(2,1)} %slice.128), channel_id=1, source_target_pairs={{0,4},{4,8},{8,12},{12,16},{16,20},{20,24},{24,28},{1,5},{5,9},{9,... | collective-permute-start | bytes 1572872 | tf_op jit(solution)/shard_map/ppermute | solution.py:16
  21.9 4.8 %fusion.18 = bf16[4,256,512]{2,1,0:T(8,128)(2,1)} fusion(bf16[1024,4,512]{2,1,0:T(4,128)(2,1)} %param.7, bf16[1,256,1024]{2,1,0:T(8,128)(2,1)S(1)} %copy-done.5, pred[256]{0:T(512)(128)(4,1)S(1)} %compare_reduce_fusion), kind=kOutput, calls=%fused_computation.23 | convolution fusion | flops 1074528256 | bytes 5767424 | tf_op jit(solution)/shard_map/rd,dwh->wrh/dot_general | solution.py:154
  33.3 13.4 %collective-permute-done = bf16[2,256,512]{2,1,0:T(8,128)(2,1)} collective-permute-done((bf16[2,256,512]{2,1,0:T(8,128)(2,1)}, bf16[2,256,512]{2,1,0:T(8,128)(2,1)}, u32[]{:S(2)}, u32[]{:S(2)}) %collective-permute-start) | collective-permute-done | bytes 524320 | tf_op jit(solution)/shard_map/ppermute | solution.py:16
  55.3 3.9 %fusion.1 = (f32[8,256]{1,0:T(8,128)S(1)}, f32[8,256,1280]{2,1,0:T(8,128)S(1)}) fusion(f32[256,1280]{1,0:T(8,128)} %fusion.37, bf16[256,8,64]{0,2,1:T(8,128)(2,1)S(1)} %bitcast.202, bf16[1280,8,64]{0,2,1:T(8,128)(2,1)S(1)} %bitcast.199), kind=kOutput, calls=%fused_computation.3 | convolution fusion | flops 343406592 | bytes 13377536 | tf_op jit(solution)/shard_map/qgc,kgc->gqk/dot_general | solution.py:102
  59.3 2.8 %multiply_reduce_fusion = (f32[256,8]{0,1:T(8,128)S(1)}, bf16[8,64,256]{2,1,0:T(8,128)(2,1)S(1)}) fusion(bf16[256,8,64]{0,2,1:T(8,128)(2,1)S(1)} %bitcast.212, bf16[1280,8,64]{0,2,1:T(8,128)(2,1)S(1)} %bitcast.209, f32[8,256]{1,0:T(8,128)S(1)} %get-tuple-element.34, f32[256,1280]{1,0:T(8,128)S(1)} %copy-done, f32[8,256,1280]{2,1,0:T(8,128)S(1)} %get-tuple-element.35), kind=kOutput, calls=%fused_computation.80 | convolution fusion | flops 346683392 | bytes 13647872 | tf_op jit(solution)/shard_map/gqk,kgc->qgc/dot_general | solution.py:108
  62.1 3.9 %multiply_convert_fusion = bf16[8,256,1280]{2,1,0:T(8,128)(2,1)S(1)} fusion(bf16[256,8,64]{0,2,1:T(8,128)(2,1)S(1)} %bitcast.213, bf16[1280,8,64]{0,2,1:T(8,128)(2,1)S(1)} %bitcast.210, f32[8,256]{1,0:T(8,128)S(1)} %bitcast.216, f32[8,256]{1,0:T(8,128)S(1)} %get-tuple-element.34, f32[256,1280]{1,0:T(8,128)S(1)} %copy-done, ...), kind=kOutput, calls=%fused_computation | convolution fusion | flops 353894400 | bytes 18628608 | tf_op jit(solution)/shard_map/qgc,kgc->gqk/dot_general | solution.py:112
  71.3 3.6 %collective-permute-start.4 = (bf16[2,2,2,2,40,2,512]{6,4,5,0,1,2,3:T(8,128)(2,1)S(1)}, bf16[2,2,2,2,40,2,512]{6,4,5,0,1,2,3:T(8,128)(2,1)S(1)}, u32[]{:S(2)}, u32[]{:S(2)}) collective-permute-start(bf16[2,2,2,2,40,2,512]{6,4,5,0,1,2,3:T(8,128)(2,1)S(1)} %fusion.32), channel_id=1, source_target_pairs={{0,4},{4,0},{8,12},{12,8},{16,20},{20,16},{24,28},{28,24},{1,5},{5... | collective-permute-start | bytes 3932168 | tf_op jit(solution)/shard_map/ppermute | solution.py:29
  74.9 2.3 %fusion.96 = (bf16[8,64,1280]{2,1,0:T(8,128)(2,1)S(1)}, f32[8,64,1280]{2,1,0:T(8,128)S(1)}) fusion(bf16[256,8,64]{0,2,1:T(8,128)(2,1)S(1)} %bitcast.214, f32[8,256]{1,0:T(8,128)S(1)} %get-tuple-element.34, f32[256,1280]{1,0:T(8,128)S(1)} %copy-done, f32[8,256,1280]{2,1,0:T(8,128)S(1)} %get-tuple-element.35), kind=kOutput, calls=%fused_computation.175 | convolution fusion | flops 346685440 | bytes 15998976 | tf_op jit(solution)/shard_map/gqk,qgc->gck/dot_general | solution.py:122
  85.5 9.7 %collective-permute-done.5 = bf16[2,2,2,40,2,512]{5,3,4,0,1,2:T(8,128)(2,1)S(1)} collective-permute-done((bf16[2,2,2,40,2,512]{5,3,4,0,1,2:T(8,128)(2,1)S(1)}, bf16[2,2,2,40,2,512]{5,3,4,0,1,2:T(8,128)(2,1)S(1)}, u32[]{:S(2)}, u32[]{:S(2)}) %collective-permute-start.5) | collective-permute-done | bytes 655392 | tf_op jit(solution)/shard_map/ppermute | solution.py:29
  95.4 2.7 %collective-permute-start.6 = (bf16[2,2,40,2,512]{4,2,3,0,1:T(8,128)(2,1)S(1)}, bf16[2,2,40,2,512]{4,2,3,0,1:T(8,128)(2,1)S(1)}, u32[]{:S(2)}, u32[]{:S(2)}) collective-permute-start(bf16[2,2,40,2,512]{4,2,3,0,1:T(8,128)(2,1)S(1)} %fusion.59), channel_id=1, source_target_pairs={{0,2},{1,3},{2,0},{3,1},{4,6},{5,7},{6,4},{7,5},{8,10},{9,11},{10,... | collective-permute-start | bytes 983048 | tf_op jit(solution)/shard_map/ppermute | solution.py:29
  99.9 12.7 %collective-permute-done.6 = bf16[2,2,40,2,512]{4,2,3,0,1:T(8,128)(2,1)S(1)} collective-permute-done((bf16[2,2,40,2,512]{4,2,3,0,1:T(8,128)(2,1)S(1)}, bf16[2,2,40,2,512]{4,2,3,0,1:T(8,128)(2,1)S(1)}, u32[]{:S(2)}, u32[]{:S(2)}) %collective-permute-start.6) | collective-permute-done | bytes 327712 | tf_op jit(solution)/shard_map/ppermute | solution.py:29
  112.8 2.3 %collective-permute-start.7 = (bf16[2,40,2,256]{3,1,2,0:T(8,128)(2,1)S(1)}, bf16[2,40,2,256]{3,1,2,0:T(8,128)(2,1)S(1)}, u32[]{:S(2)}, u32[]{:S(2)}) collective-permute-start(bf16[2,40,2,256]{3,1,2,0:T(8,128)(2,1)S(1)} %fusion.76), channel_id=1, source_target_pairs={{0,16},{4,20},{8,24},{12,28},{16,0},{20,4},{24,8},{28,12},{1,17},{... | collective-permute-start | bytes 245768 | tf_op jit(solution)/shard_map/ppermute | solution.py:29
  117.7 4.0 %collective-permute-done.8 = bf16[40,2,256]{2,0,1:T(8,128)(2,1)S(1)} collective-permute-done((bf16[40,2,256]{2,0,1:T(8,128)(2,1)S(1)}, bf16[40,2,256]{2,0,1:T(8,128)(2,1)S(1)}, u32[]{:S(2)}, u32[]{:S(2)}) %collective-permute-start.8) | collective-permute-done | bytes 40992 | tf_op jit(solution)/shard_map/ppermute | solution.py:29
  125.3 2.6 %collective-permute-done.15 = bf16[2,2,2,2,32,2,512]{6,4,5,3,2,1,0:T(8,128)(2,1)S(1)} collective-permute-done((bf16[2,2,2,2,32,2,512]{6,4,5,3,2,1,0:T(8,128)(2,1)S(1)}, bf16[2,2,2,2,32,2,512]{6,4,5,3,2,1,0:T(8,128)(2,1)S(1)}, u32[]{:S(2)}, u32[]{:S(2)}) %collective-permute-start.15) | collective-permute-done | bytes 1048608 | tf_op jit(solution)/shard_map/ppermute | solution.py:29
  133.0 4.4 %collective-permute-done.16 = bf16[2,2,2,32,2,256]{5,3,4,2,1,0:T(8,128)(2,1)S(1)} collective-permute-done((bf16[2,2,2,32,2,256]{5,3,4,2,1,0:T(8,128)(2,1)S(1)}, bf16[2,2,2,32,2,256]{5,3,4,2,1,0:T(8,128)(2,1)S(1)}, u32[]{:S(2)}, u32[]{:S(2)}) %collective-permute-start.16) | collective-permute-done | bytes 262176 | tf_op jit(solution)/shard_map/ppermute | solution.py:29
  137.6 3.9 %collective-permute-done.18 = bf16[2,2,2,32,2,256]{5,3,4,2,1,0:T(8,128)(2,1)S(1)} collective-permute-done((bf16[2,2,2,32,2,256]{5,3,4,2,1,0:T(8,128)(2,1)S(1)}, bf16[2,2,2,32,2,256]{5,3,4,2,1,0:T(8,128)(2,1)S(1)}, u32[]{:S(2)}, u32[]{:S(2)}) %collective-permute-start.18) | collective-permute-done | bytes 262176 | tf_op jit(solution)/shard_map/ppermute | solution.py:29
  143.5 3.1 %collective-permute-done.19 = bf16[2,2,32,2,256]{4,2,3,1,0:T(8,128)(2,1)S(1)} collective-permute-done((bf16[2,2,32,2,256]{4,2,3,1,0:T(8,128)(2,1)S(1)}, bf16[2,2,32,2,256]{4,2,3,1,0:T(8,128)(2,1)S(1)}, u32[]{:S(2)}, u32[]{:S(2)}) %collective-permute-start.19) | collective-permute-done | bytes 131104 | tf_op jit(solution)/shard_map/ppermute | solution.py:29
  147.8 4.6 %collective-permute-done.20 = bf16[2,32,2,512]{3,1,2,0:T(8,128)(2,1)S(1)} collective-permute-done((bf16[2,32,2,512]{3,1,2,0:T(8,128)(2,1)S(1)}, bf16[2,32,2,512]{3,1,2,0:T(8,128)(2,1)S(1)}, u32[]{:S(2)}, u32[]{:S(2)}) %collective-permute-start.20) | collective-permute-done | bytes 131104 | tf_op jit(solution)/shard_map/ppermute | solution.py:29
  152.5 2.4 %collective-permute-start.21 = (bf16[32,2,512]{2,0,1:T(8,128)(2,1)S(1)}, bf16[32,2,512]{2,0,1:T(8,128)(2,1)S(1)}, u32[]{:S(2)}, u32[]{:S(2)}) collective-permute-start(bf16[32,2,512]{2,0,1:T(8,128)(2,1)S(1)} %fusion.78), channel_id=1, source_target_pairs={{0,2},{1,3},{2,0},{3,1},{4,6},{5,7},{6,4},{7,5},{8,10},{9,11},{10,... | collective-permute-start | bytes 196616 | tf_op jit(solution)/shard_map/ppermute | solution.py:29
  155.0 2.8 %collective-permute-done.21 = bf16[32,2,512]{2,0,1:T(8,128)(2,1)S(1)} collective-permute-done((bf16[32,2,512]{2,0,1:T(8,128)(2,1)S(1)}, bf16[32,2,512]{2,0,1:T(8,128)(2,1)S(1)}, u32[]{:S(2)}, u32[]{:S(2)}) %collective-permute-start.21) | collective-permute-done | bytes 65568 | tf_op jit(solution)/shard_map/ppermute | solution.py:29
  (123 shorter events, 48.1 us)
Async XLA Ops:
  1.9 18.9 %copy-start.7 = (s32[1,256]{1,0:T(1,128)S(1)}, s32[1,256]{1,0:T(1,128)}, u32[]{:S(2)}) copy-start(s32[1,256]{1,0:T(1,128)} %param.9) | copy-start | bytes 3076
  1.9 20.1 %copy-start.5 = (bf16[1,256,1024]{2,1,0:T(8,128)(2,1)S(1)}, bf16[1,256,1024]{2,1,0:T(8,128)(2,1)}, u32[]{:S(2)}) copy-start(bf16[1,256,1024]{2,1,0:T(8,128)(2,1)} %param.8) | copy-start | bytes 1572868
  6.7 40.0 %collective-permute-start = (bf16[2,256,512]{2,1,0:T(8,128)(2,1)}, bf16[2,256,512]{2,1,0:T(8,128)(2,1)}, u32[]{:S(2)}, u32[]{:S(2)}) collective-permute-start(bf16[2,256,512]{2,1,0:T(8,128)(2,1)} %slice.128), channel_id=1, source_target_pairs={{0,16},{4,20},{8,24},{12,28},{1,17},{5,21},{9,25},{13,29},{2,18},{... | collective-permute-start | bytes 1572872 | tf_op jit(solution)/shard_map/ppermute | solution.py:16
  12.4 35.4 %collective-permute-start.1 = (bf16[2,256,512]{2,1,0:T(8,128)(2,1)}, bf16[2,256,512]{2,1,0:T(8,128)(2,1)}, u32[]{:S(2)}, u32[]{:S(2)}) collective-permute-start(bf16[2,256,512]{2,1,0:T(8,128)(2,1)} %slice.128), channel_id=1, source_target_pairs={{0,12},{4,16},{8,20},{12,24},{16,28},{1,13},{5,17},{9,21},{13,25},... | collective-permute-start | bytes 1572872 | tf_op jit(solution)/shard_map/ppermute | solution.py:16
  15.7 33.1 %collective-permute-start.2 = (bf16[2,256,512]{2,1,0:T(8,128)(2,1)}, bf16[2,256,512]{2,1,0:T(8,128)(2,1)}, u32[]{:S(2)}, u32[]{:S(2)}) collective-permute-start(bf16[2,256,512]{2,1,0:T(8,128)(2,1)} %slice.128), channel_id=1, source_target_pairs={{0,8},{4,12},{8,16},{12,20},{16,24},{20,28},{1,9},{5,13},{9,17},{1... | collective-permute-start | bytes 1572872 | tf_op jit(solution)/shard_map/ppermute | solution.py:16
  18.6 31.3 %collective-permute-start.3 = (bf16[2,256,512]{2,1,0:T(8,128)(2,1)}, bf16[2,256,512]{2,1,0:T(8,128)(2,1)}, u32[]{:S(2)}, u32[]{:S(2)}) collective-permute-start(bf16[2,256,512]{2,1,0:T(8,128)(2,1)} %slice.128), channel_id=1, source_target_pairs={{0,4},{4,8},{8,12},{12,16},{16,20},{20,24},{24,28},{1,5},{5,9},{9,... | collective-permute-start | bytes 1572872 | tf_op jit(solution)/shard_map/ppermute | solution.py:16
  71.3 6.2 %collective-permute-start.4 = (bf16[2,2,2,2,40,2,512]{6,4,5,0,1,2,3:T(8,128)(2,1)S(1)}, bf16[2,2,2,2,40,2,512]{6,4,5,0,1,2,3:T(8,128)(2,1)S(1)}, u32[]{:S(2)}, u32[]{:S(2)}) collective-permute-start(bf16[2,2,2,2,40,2,512]{6,4,5,0,1,2,3:T(8,128)(2,1)S(1)} %fusion.32), channel_id=1, source_target_pairs={{0,4},{4,0},{8,12},{12,8},{16,20},{20,16},{24,28},{28,24},{1,5},{5... | collective-permute-start | bytes 3932168 | tf_op jit(solution)/shard_map/ppermute | solution.py:29
  78.1 17.1 %collective-permute-start.5 = (bf16[2,2,2,40,2,512]{5,3,4,0,1,2:T(8,128)(2,1)S(1)}, bf16[2,2,2,40,2,512]{5,3,4,0,1,2:T(8,128)(2,1)S(1)}, u32[]{:S(2)}, u32[]{:S(2)}) collective-permute-start(bf16[2,2,2,40,2,512]{5,3,4,0,1,2:T(8,128)(2,1)S(1)} %fusion.53), channel_id=1, source_target_pairs={{0,1},{1,0},{2,3},{3,2},{4,5},{5,4},{6,7},{7,6},{8,9},{9,8},{10,11... | collective-permute-start | bytes 1966088 | tf_op jit(solution)/shard_map/ppermute | solution.py:29
  79.8 18.3 %collective-permute-start.12 = (bf16[2,8,64,256]{3,2,1,0:T(8,128)(2,1)S(1)}, bf16[2,8,64,256]{3,2,1,0:T(8,128)(2,1)S(1)}, u32[]{:S(2)}, u32[]{:S(2)}) collective-permute-start(bf16[2,8,64,256]{3,2,1,0:T(8,128)(2,1)S(1)} %pad_maximum_fusion.4), channel_id=1, source_target_pairs={{16,0},{20,4},{24,8},{28,12},{17,1},{21,5},{25,9},{29,13},{18,2},{... | collective-permute-start | bytes 1572872 | tf_op jit(solution)/shard_map/ppermute | solution.py:16
  81.2 16.9 %collective-permute-start.11 = (bf16[2,8,64,256]{3,2,1,0:T(8,128)(2,1)S(1)}, bf16[2,8,64,256]{3,2,1,0:T(8,128)(2,1)S(1)}, u32[]{:S(2)}, u32[]{:S(2)}) collective-permute-start(bf16[2,8,64,256]{3,2,1,0:T(8,128)(2,1)S(1)} %pad_maximum_fusion.3), channel_id=1, source_target_pairs={{12,0},{16,4},{20,8},{24,12},{28,16},{13,1},{17,5},{21,9},{25,13},... | collective-permute-start | bytes 1572872 | tf_op jit(solution)/shard_map/ppermute | solution.py:16
  82.5 16.8 %collective-permute-start.10 = (bf16[2,8,64,256]{3,2,1,0:T(8,128)(2,1)S(1)}, bf16[2,8,64,256]{3,2,1,0:T(8,128)(2,1)S(1)}, u32[]{:S(2)}, u32[]{:S(2)}) collective-permute-start(bf16[2,8,64,256]{3,2,1,0:T(8,128)(2,1)S(1)} %pad_maximum_fusion.2), channel_id=1, source_target_pairs={{8,0},{12,4},{16,8},{20,12},{24,16},{28,20},{9,1},{13,5},{17,9},{2... | collective-permute-start | bytes 1572872 | tf_op jit(solution)/shard_map/ppermute | solution.py:16
  83.9 15.4 %collective-permute-start.9 = (bf16[2,8,64,256]{3,2,1,0:T(8,128)(2,1)S(1)}, bf16[2,8,64,256]{3,2,1,0:T(8,128)(2,1)S(1)}, u32[]{:S(2)}, u32[]{:S(2)}) collective-permute-start(bf16[2,8,64,256]{3,2,1,0:T(8,128)(2,1)S(1)} %pad_maximum_fusion.1), channel_id=1, source_target_pairs={{4,0},{8,4},{12,8},{16,12},{20,16},{24,20},{28,24},{5,1},{9,5},{13... | collective-permute-start | bytes 1572872 | tf_op jit(solution)/shard_map/ppermute | solution.py:16
  95.4 17.2 %collective-permute-start.6 = (bf16[2,2,40,2,512]{4,2,3,0,1:T(8,128)(2,1)S(1)}, bf16[2,2,40,2,512]{4,2,3,0,1:T(8,128)(2,1)S(1)}, u32[]{:S(2)}, u32[]{:S(2)}) collective-permute-start(bf16[2,2,40,2,512]{4,2,3,0,1:T(8,128)(2,1)S(1)} %fusion.59), channel_id=1, source_target_pairs={{0,2},{1,3},{2,0},{3,1},{4,6},{5,7},{6,4},{7,5},{8,10},{9,11},{10,... | collective-permute-start | bytes 983048 | tf_op jit(solution)/shard_map/ppermute | solution.py:29
  112.8 4.7 %collective-permute-start.7 = (bf16[2,40,2,256]{3,1,2,0:T(8,128)(2,1)S(1)}, bf16[2,40,2,256]{3,1,2,0:T(8,128)(2,1)S(1)}, u32[]{:S(2)}, u32[]{:S(2)}) collective-permute-start(bf16[2,40,2,256]{3,1,2,0:T(8,128)(2,1)S(1)} %fusion.76), channel_id=1, source_target_pairs={{0,16},{4,20},{8,24},{12,28},{16,0},{20,4},{24,8},{28,12},{1,17},{... | collective-permute-start | bytes 245768 | tf_op jit(solution)/shard_map/ppermute | solution.py:29
  117.6 4.1 %collective-permute-start.8 = (bf16[40,2,256]{2,0,1:T(8,128)(2,1)S(1)}, bf16[40,2,256]{2,0,1:T(8,128)(2,1)S(1)}, u32[]{:S(2)}, u32[]{:S(2)}) collective-permute-start(bf16[40,2,256]{2,0,1:T(8,128)(2,1)S(1)} %fusion.79), channel_id=1, source_target_pairs={{0,8},{4,12},{8,0},{12,4},{16,24},{20,28},{24,16},{28,20},{1,9},{5... | collective-permute-start | bytes 122888 | tf_op jit(solution)/shard_map/ppermute | solution.py:29
  125.2 2.7 %collective-permute-start.15 = (bf16[2,2,2,2,32,2,512]{6,4,5,3,2,1,0:T(8,128)(2,1)S(1)}, bf16[2,2,2,2,32,2,512]{6,4,5,3,2,1,0:T(8,128)(2,1)S(1)}, u32[]{:S(2)}, u32[]{:S(2)}) collective-permute-start(bf16[2,2,2,2,32,2,512]{6,4,5,3,2,1,0:T(8,128)(2,1)S(1)} %fusion.48), channel_id=1, source_target_pairs={{0,4},{4,0},{8,12},{12,8},{16,20},{20,16},{24,28},{28,24},{1,5},{5... | collective-permute-start | bytes 3145736 | tf_op jit(solution)/shard_map/ppermute | solution.py:29
  128.7 8.7 %collective-permute-start.16 = (bf16[2,2,2,32,2,256]{5,3,4,2,1,0:T(8,128)(2,1)S(1)}, bf16[2,2,2,32,2,256]{5,3,4,2,1,0:T(8,128)(2,1)S(1)}, u32[]{:S(2)}, u32[]{:S(2)}) collective-permute-start(bf16[2,2,2,32,2,256]{5,3,4,2,1,0:T(8,128)(2,1)S(1)} %fusion.60), channel_id=1, source_target_pairs={{0,16},{4,20},{8,24},{12,28},{16,0},{20,4},{24,8},{28,12},{1,17},{... | collective-permute-start | bytes 786440 | tf_op jit(solution)/shard_map/ppermute | solution.py:29
  130.8 16.9 %collective-permute-start.13 = (bf16[2,40,2,256]{3,1,2,0:T(8,128)(2,1)S(1)}, bf16[2,40,2,256]{3,1,2,0:T(8,128)(2,1)S(1)}, u32[]{:S(2)}, u32[]{:S(2)}) collective-permute-start(bf16[2,40,2,256]{3,1,2,0:T(8,128)(2,1)S(1)} %fusion.77), channel_id=1, source_target_pairs={{0,8},{4,12},{8,0},{12,4},{16,24},{20,28},{24,16},{28,20},{1,9},{5... | collective-permute-start | bytes 245768 | tf_op jit(solution)/shard_map/ppermute | solution.py:29
  130.9 10.6 %collective-permute-start.18 = (bf16[2,2,2,32,2,256]{5,3,4,2,1,0:T(8,128)(2,1)S(1)}, bf16[2,2,2,32,2,256]{5,3,4,2,1,0:T(8,128)(2,1)S(1)}, u32[]{:S(2)}, u32[]{:S(2)}) collective-permute-start(bf16[2,2,2,32,2,256]{5,3,4,2,1,0:T(8,128)(2,1)S(1)} %fusion.61), channel_id=1, source_target_pairs={{0,8},{4,12},{8,0},{12,4},{16,24},{20,28},{24,16},{28,20},{1,9},{5... | collective-permute-start | bytes 786440 | tf_op jit(solution)/shard_map/ppermute | solution.py:29
  137.5 6.0 %collective-permute-start.17 = (bf16[2,2,32,2,256]{4,2,3,1,0:T(8,128)(2,1)S(1)}, bf16[2,2,32,2,256]{4,2,3,1,0:T(8,128)(2,1)S(1)}, u32[]{:S(2)}, u32[]{:S(2)}) collective-permute-start(bf16[2,2,32,2,256]{4,2,3,1,0:T(8,128)(2,1)S(1)} %fusion.73), channel_id=1, source_target_pairs={{0,8},{4,12},{8,0},{12,4},{16,24},{20,28},{24,16},{28,20},{1,9},{5... | collective-permute-start | bytes 393224 | tf_op jit(solution)/shard_map/ppermute | solution.py:29
  141.6 5.0 %collective-permute-start.19 = (bf16[2,2,32,2,256]{4,2,3,1,0:T(8,128)(2,1)S(1)}, bf16[2,2,32,2,256]{4,2,3,1,0:T(8,128)(2,1)S(1)}, u32[]{:S(2)}, u32[]{:S(2)}) collective-permute-start(bf16[2,2,32,2,256]{4,2,3,1,0:T(8,128)(2,1)S(1)} %fusion.74), channel_id=1, source_target_pairs={{0,16},{4,20},{8,24},{12,28},{16,0},{20,4},{24,8},{28,12},{1,17},{... | collective-permute-start | bytes 393224 | tf_op jit(solution)/shard_map/ppermute | solution.py:29
  146.7 5.7 %collective-permute-start.20 = (bf16[2,32,2,512]{3,1,2,0:T(8,128)(2,1)S(1)}, bf16[2,32,2,512]{3,1,2,0:T(8,128)(2,1)S(1)}, u32[]{:S(2)}, u32[]{:S(2)}) collective-permute-start(bf16[2,32,2,512]{3,1,2,0:T(8,128)(2,1)S(1)} %fusion.75), channel_id=1, source_target_pairs={{0,1},{1,0},{2,3},{3,2},{4,5},{5,4},{6,7},{7,6},{8,9},{9,8},{10,11... | collective-permute-start | bytes 393224 | tf_op jit(solution)/shard_map/ppermute | solution.py:29
  147.8 7.1 %collective-permute-start.14 = (bf16[40,2,256]{2,0,1:T(8,128)(2,1)S(1)}, bf16[40,2,256]{2,0,1:T(8,128)(2,1)S(1)}, u32[]{:S(2)}, u32[]{:S(2)}) collective-permute-start(bf16[40,2,256]{2,0,1:T(8,128)(2,1)S(1)} %fusion.80), channel_id=1, source_target_pairs={{0,16},{4,20},{8,24},{12,28},{16,0},{20,4},{24,8},{28,12},{1,17},{... | collective-permute-start | bytes 122888 | tf_op jit(solution)/shard_map/ppermute | solution.py:29
  152.5 5.2 %collective-permute-start.21 = (bf16[32,2,512]{2,0,1:T(8,128)(2,1)S(1)}, bf16[32,2,512]{2,0,1:T(8,128)(2,1)S(1)}, u32[]{:S(2)}, u32[]{:S(2)}) collective-permute-start(bf16[32,2,512]{2,0,1:T(8,128)(2,1)S(1)} %fusion.78), channel_id=1, source_target_pairs={{0,2},{1,3},{2,0},{3,1},{4,6},{5,7},{6,4},{7,5},{8,10},{9,11},{10,... | collective-permute-start | bytes 196616 | tf_op jit(solution)/shard_map/ppermute | solution.py:29
  (8 other events, 38.4 us)

commit v17 on v16

--- a/solution.py
+++ b/solution.py
@@ -36,7 +36,7 @@
     return value + lax.ppermute(value, axis, pairs), anchor
 
 
-def scatter_rows(value, tally, axes, first_axis, wire_type, tail_first=False):
+def scatter_rows(value, tally, axes, first_axis, wire_type, tail_first=False, balance=True):
     sizes = [lax.axis_size(axis) for axis in axes]
     rows = value.shape[0]
     groups = math.prod(sizes)
@@ -78,7 +78,7 @@
     tail = [s for s in stages if s[0] != first[0]][::-1]
     if tail_first:
         value, names, tally = run_tail(value, names, tally)
-    if len(middle) > 1 and rest[-1] % 2 == 0:
+    if balance and len(middle) > 1 and rest[-1] % 2 == 0:
         cut = rest[-1] // 2
         left, right = value[..., :cut], value[..., cut:]
         left_names, right_names = list(names), list(names)
@@ -214,7 +214,9 @@
     key_value_part = jnp.einsum(
         "rd,wgcr->dwgc", normed, grad_proj[1:3], preferred_element_type=jnp.float32
     ).reshape(width, 2, inner)
-    late, _ = scatter_rows(key_value_part, None, ("tm", "night"), "tm", jnp.bfloat16)
+    late, _ = scatter_rows(
+        key_value_part, None, ("tm", "night"), "tm", jnp.bfloat16, balance=False
+    )
     summed = jnp.concatenate([early[:, :1], late, early[:, 1:]], axis=1)
     total_count = count.astype(jnp.float32)
     loss_scale = jnp.float32(tokens_all) / total_count

time: 159 us -> 165 us (1.038)
  waiting for transfers between devices: 64.9 us -> 69.5 us
    ppermute x14 -> x12, waiting for transfers between devices: 50.4 us -> 55 us  [halve(): lax.ppermute(send.astype(send_type), axis, pairs).astype(keep.dtype)]
    ppermute x14 -> x12, starting transfers between devices: 18.1 us -> 19 us  [halve(): lax.ppermute(send.astype(send_type), axis, pairs).astype(keep.dtype)]
  transfers between devices with their start and end apart: 22 -> 20, of which waited for: 14 -> 13; matrix products, arithmetic and copies ran while one was open for 13% -> 13% of each run, Pallas kernels for 0% -> 0%
where the time goes in v17:
time: 165 us; the launch traced here: 164 us
  waiting for transfers between devices  69.5 us (42%)
  starting transfers between devices  38.4 us (23%)
  matrix products  27.9 us (17%)
  local copies, waits for them, and re-layouts  15.7 us (10%)
  other arithmetic  9.67 us (6%)
  between operations  2.67 us (2%)
    ppermute x12, waiting for transfers between devices, halve(): lax.ppermute(send.astype(send_type), axis, pairs).astype(keep.dtype)  55 us
    ppermute x8, starting transfers between devices, shifted(): return lax.ppermute(value, axis, pairs)  19.4 us
    ppermute x12, starting transfers between devices, halve(): lax.ppermute(send.astype(send_type), axis, pairs).astype(keep.dtype)  19 us
    ppermute x8, waiting for transfers between devices, shifted(): return lax.ppermute(value, axis, pairs)  14.6 us
    unnamed x24, local copies, waits for them, and re-layouts  7.03 us
    dot_general x1, matrix products, shards(): jnp.einsum('rd,dwh->wrh', grad_out, weights, preferred_element_type=jnp.f...  4.79 us
    dot_general x1, matrix products, shards(): jnp.einsum('rd,dwh->wrh', normed, weights, preferred_element_type=jnp.flo...  3.98 us
    dot_general x1, matrix products, band_block(): jnp.einsum('qgc,kgc->gqk', grad_attn, values_blk, preferred_element_type=...  3.92 us
  transfers between devices with their start and end apart: 20, of which 13 were waited for; matrix products, arithmetic and copies ran while one was open for 13% of the time, Pallas kernels for 0%

profile of v17, /device:TPU:0, one launch (start us, length us, event | category | flops | bytes accessed | tf_op | source)
XLA Modules:
  0.0 163.9 jit_solution(8316352494137139207)
XLA Ops:
  1.9 4.0 %fusion.21 = bf16[4,256,512]{2,1,0:T(8,128)(2,1)S(1)} fusion(bf16[1024,4,512]{2,1,0:T(4,128)(2,1)} %param.7, bf16[1,256,1024]{2,1,0:T(8,128)(2,1)} %param.6, f32[256]{0:T(256)S(1)} %add_rsqrt_fusion), kind=kOutput, calls=%fused_computation.24 | convolution fusion | flops 1075052544 | bytes 5768192 | tf_op jit(solution)/shard_map/rd,dwh->wrh/dot_general | solution.py:142
  6.7 5.7 %collective-permute-start = (bf16[2,256,512]{2,1,0:T(8,128)(2,1)}, bf16[2,256,512]{2,1,0:T(8,128)(2,1)}, u32[]{:S(2)}, u32[]{:S(2)}) collective-permute-start(bf16[2,256,512]{2,1,0:T(8,128)(2,1)} %slice.120), channel_id=1, source_target_pairs={{0,16},{4,20},{8,24},{12,28},{1,17},{5,21},{9,25},{13,29},{2,18},{... | collective-permute-start | bytes 1572872 | tf_op jit(solution)/shard_map/ppermute | solution.py:16
  12.4 3.3 %collective-permute-start.1 = (bf16[2,256,512]{2,1,0:T(8,128)(2,1)}, bf16[2,256,512]{2,1,0:T(8,128)(2,1)}, u32[]{:S(2)}, u32[]{:S(2)}) collective-permute-start(bf16[2,256,512]{2,1,0:T(8,128)(2,1)} %slice.120), channel_id=1, source_target_pairs={{0,12},{4,16},{8,20},{12,24},{16,28},{1,13},{5,17},{9,21},{13,25},... | collective-permute-start | bytes 1572872 | tf_op jit(solution)/shard_map/ppermute | solution.py:16
  15.7 2.9 %collective-permute-start.2 = (bf16[2,256,512]{2,1,0:T(8,128)(2,1)}, bf16[2,256,512]{2,1,0:T(8,128)(2,1)}, u32[]{:S(2)}, u32[]{:S(2)}) collective-permute-start(bf16[2,256,512]{2,1,0:T(8,128)(2,1)} %slice.120), channel_id=1, source_target_pairs={{0,8},{4,12},{8,16},{12,20},{16,24},{20,28},{1,9},{5,13},{9,17},{1... | collective-permute-start | bytes 1572872 | tf_op jit(solution)/shard_map/ppermute | solution.py:16
  18.6 2.1 %collective-permute-start.3 = (bf16[2,256,512]{2,1,0:T(8,128)(2,1)}, bf16[2,256,512]{2,1,0:T(8,128)(2,1)}, u32[]{:S(2)}, u32[]{:S(2)}) collective-permute-start(bf16[2,256,512]{2,1,0:T(8,128)(2,1)} %slice.120), channel_id=1, source_target_pairs={{0,4},{4,8},{8,12},{12,16},{16,20},{20,24},{24,28},{1,5},{5,9},{9,... | collective-permute-start | bytes 1572872 | tf_op jit(solution)/shard_map/ppermute | solution.py:16
  22.0 4.8 %fusion.18 = bf16[4,256,512]{2,1,0:T(8,128)(2,1)} fusion(bf16[1024,4,512]{2,1,0:T(4,128)(2,1)} %param.7, bf16[1,256,1024]{2,1,0:T(8,128)(2,1)S(1)} %copy-done.5, pred[256]{0:T(512)(128)(4,1)S(1)} %compare_reduce_fusion), kind=kOutput, calls=%fused_computation.23 | convolution fusion | flops 1074528256 | bytes 5767424 | tf_op jit(solution)/shard_map/rd,dwh->wrh/dot_general | solution.py:154
  33.3 13.4 %collective-permute-done = bf16[2,256,512]{2,1,0:T(8,128)(2,1)} collective-permute-done((bf16[2,256,512]{2,1,0:T(8,128)(2,1)}, bf16[2,256,512]{2,1,0:T(8,128)(2,1)}, u32[]{:S(2)}, u32[]{:S(2)}) %collective-permute-start) | collective-permute-done | bytes 524320 | tf_op jit(solution)/shard_map/ppermute | solution.py:16
  55.3 3.9 %fusion.1 = (f32[8,256]{1,0:T(8,128)S(1)}, f32[8,256,1280]{2,1,0:T(8,128)S(1)}) fusion(f32[256,1280]{1,0:T(8,128)} %fusion.37, bf16[256,8,64]{0,2,1:T(8,128)(2,1)S(1)} %bitcast.192, bf16[1280,8,64]{0,2,1:T(8,128)(2,1)S(1)} %bitcast.189), kind=kOutput, calls=%fused_computation.3 | convolution fusion | flops 343406592 | bytes 13377536 | tf_op jit(solution)/shard_map/qgc,kgc->gqk/dot_general | solution.py:102
  59.3 2.8 %multiply_reduce_fusion = (f32[256,8]{0,1:T(8,128)S(1)}, bf16[8,64,256]{2,1,0:T(8,128)(2,1)S(1)}) fusion(bf16[256,8,64]{0,2,1:T(8,128)(2,1)S(1)} %bitcast.202, bf16[1280,8,64]{0,2,1:T(8,128)(2,1)S(1)} %bitcast.199, f32[8,256]{1,0:T(8,128)S(1)} %get-tuple-element.32, f32[256,1280]{1,0:T(8,128)S(1)} %copy-done, f32[8,256,1280]{2,1,0:T(8,128)S(1)} %get-tuple-element.33), kind=kOutput, calls=%fused_computation.77 | convolution fusion | flops 346683392 | bytes 13647872 | tf_op jit(solution)/shard_map/gqk,kgc->qgc/dot_general | solution.py:108
  62.1 3.9 %multiply_convert_fusion = bf16[8,256,1280]{2,1,0:T(8,128)(2,1)S(1)} fusion(bf16[256,8,64]{0,2,1:T(8,128)(2,1)S(1)} %bitcast.203, bf16[1280,8,64]{0,2,1:T(8,128)(2,1)S(1)} %bitcast.200, f32[8,256]{1,0:T(8,128)S(1)} %bitcast.206, f32[8,256]{1,0:T(8,128)S(1)} %get-tuple-element.32, f32[256,1280]{1,0:T(8,128)S(1)} %copy-done, ...), kind=kOutput, calls=%fused_computation | convolution fusion | flops 353894400 | bytes 18628608 | tf_op jit(solution)/shard_map/qgc,kgc->gqk/dot_general | solution.py:112
  71.3 3.6 %collective-permute-start.4 = (bf16[2,2,2,2,40,2,512]{6,4,5,0,1,2,3:T(8,128)(2,1)S(1)}, bf16[2,2,2,2,40,2,512]{6,4,5,0,1,2,3:T(8,128)(2,1)S(1)}, u32[]{:S(2)}, u32[]{:S(2)}) collective-permute-start(bf16[2,2,2,2,40,2,512]{6,4,5,0,1,2,3:T(8,128)(2,1)S(1)} %fusion.32), channel_id=1, source_target_pairs={{0,4},{4,0},{8,12},{12,8},{16,20},{20,16},{24,28},{28,24},{1,5},{5... | collective-permute-start | bytes 3932168 | tf_op jit(solution)/shard_map/ppermute | solution.py:29
  74.9 2.3 %fusion.88 = (bf16[8,64,1280]{2,1,0:T(8,128)(2,1)S(1)}, f32[8,64,1280]{2,1,0:T(8,128)S(1)}) fusion(bf16[256,8,64]{0,2,1:T(8,128)(2,1)S(1)} %bitcast.204, f32[8,256]{1,0:T(8,128)S(1)} %get-tuple-element.32, f32[256,1280]{1,0:T(8,128)S(1)} %copy-done, f32[8,256,1280]{2,1,0:T(8,128)S(1)} %get-tuple-element.33), kind=kOutput, calls=%fused_computation.161 | convolution fusion | flops 346685440 | bytes 15998976 | tf_op jit(solution)/shard_map/gqk,qgc->gck/dot_general | solution.py:122
  85.5 9.7 %collective-permute-done.5 = bf16[2,2,2,40,2,512]{5,3,4,0,1,2:T(8,128)(2,1)S(1)} collective-permute-done((bf16[2,2,2,40,2,512]{5,3,4,0,1,2:T(8,128)(2,1)S(1)}, bf16[2,2,2,40,2,512]{5,3,4,0,1,2:T(8,128)(2,1)S(1)}, u32[]{:S(2)}, u32[]{:S(2)}) %collective-permute-start.5) | collective-permute-done | bytes 655392 | tf_op jit(solution)/shard_map/ppermute | solution.py:29
  95.4 2.7 %collective-permute-start.6 = (bf16[2,2,40,2,512]{4,2,3,0,1:T(8,128)(2,1)S(1)}, bf16[2,2,40,2,512]{4,2,3,0,1:T(8,128)(2,1)S(1)}, u32[]{:S(2)}, u32[]{:S(2)}) collective-permute-start(bf16[2,2,40,2,512]{4,2,3,0,1:T(8,128)(2,1)S(1)} %fusion.60), channel_id=1, source_target_pairs={{0,2},{1,3},{2,0},{3,1},{4,6},{5,7},{6,4},{7,5},{8,10},{9,11},{10,... | collective-permute-start | bytes 983048 | tf_op jit(solution)/shard_map/ppermute | solution.py:29
  99.9 12.7 %collective-permute-done.6 = bf16[2,2,40,2,512]{4,2,3,0,1:T(8,128)(2,1)S(1)} collective-permute-done((bf16[2,2,40,2,512]{4,2,3,0,1:T(8,128)(2,1)S(1)}, bf16[2,2,40,2,512]{4,2,3,0,1:T(8,128)(2,1)S(1)}, u32[]{:S(2)}, u32[]{:S(2)}) %collective-permute-start.6) | collective-permute-done | bytes 327712 | tf_op jit(solution)/shard_map/ppermute | solution.py:29
  112.8 2.3 %collective-permute-start.7 = (bf16[2,40,2,256]{3,1,2,0:T(8,128)(2,1)S(1)}, bf16[2,40,2,256]{3,1,2,0:T(8,128)(2,1)S(1)}, u32[]{:S(2)}, u32[]{:S(2)}) collective-permute-start(bf16[2,40,2,256]{3,1,2,0:T(8,128)(2,1)S(1)} %fusion.69), channel_id=1, source_target_pairs={{0,16},{4,20},{8,24},{12,28},{16,0},{20,4},{24,8},{28,12},{1,17},{... | collective-permute-start | bytes 245768 | tf_op jit(solution)/shard_map/ppermute | solution.py:29
  117.7 4.0 %collective-permute-done.8 = bf16[40,2,256]{2,0,1:T(8,128)(2,1)S(1)} collective-permute-done((bf16[40,2,256]{2,0,1:T(8,128)(2,1)S(1)}, bf16[40,2,256]{2,0,1:T(8,128)(2,1)S(1)}, u32[]{:S(2)}, u32[]{:S(2)}) %collective-permute-start.8) | collective-permute-done | bytes 40992 | tf_op jit(solution)/shard_map/ppermute | solution.py:29
  125.3 2.6 %collective-permute-done.15 = bf16[2,2,2,2,32,2,512]{6,4,5,3,2,1,0:T(8,128)(2,1)S(1)} collective-permute-done((bf16[2,2,2,2,32,2,512]{6,4,5,3,2,1,0:T(8,128)(2,1)S(1)}, bf16[2,2,2,2,32,2,512]{6,4,5,3,2,1,0:T(8,128)(2,1)S(1)}, u32[]{:S(2)}, u32[]{:S(2)}) %collective-permute-start.15) | collective-permute-done | bytes 1048608 | tf_op jit(solution)/shard_map/ppermute | solution.py:29
  128.5 2.1 %collective-permute-start.16 = (bf16[2,2,2,32,2,512]{5,3,4,2,1,0:T(8,128)(2,1)S(1)}, bf16[2,2,2,32,2,512]{5,3,4,2,1,0:T(8,128)(2,1)S(1)}, u32[]{:S(2)}, u32[]{:S(2)}) collective-permute-start(bf16[2,2,2,32,2,512]{5,3,4,2,1,0:T(8,128)(2,1)S(1)} %fusion.54), channel_id=1, source_target_pairs={{0,16},{4,20},{8,24},{12,28},{16,0},{20,4},{24,8},{28,12},{1,17},{... | collective-permute-start | bytes 1572872 | tf_op jit(solution)/shard_map/ppermute | solution.py:29
  130.6 12.2 %collective-permute-done.16 = bf16[2,2,2,32,2,512]{5,3,4,2,1,0:T(8,128)(2,1)S(1)} collective-permute-done((bf16[2,2,2,32,2,512]{5,3,4,2,1,0:T(8,128)(2,1)S(1)}, bf16[2,2,2,32,2,512]{5,3,4,2,1,0:T(8,128)(2,1)S(1)}, u32[]{:S(2)}, u32[]{:S(2)}) %collective-permute-start.16) | collective-permute-done | bytes 524320 | tf_op jit(solution)/shard_map/ppermute | solution.py:29
  145.2 6.6 %collective-permute-done.17 = bf16[2,2,32,2,512]{4,2,3,1,0:T(8,128)(2,1)S(1)} collective-permute-done((bf16[2,2,32,2,512]{4,2,3,1,0:T(8,128)(2,1)S(1)}, bf16[2,2,32,2,512]{4,2,3,1,0:T(8,128)(2,1)S(1)}, u32[]{:S(2)}, u32[]{:S(2)}) %collective-permute-start.17) | collective-permute-done | bytes 262176 | tf_op jit(solution)/shard_map/ppermute | solution.py:29
  154.2 2.7 %collective-permute-done.18 = bf16[2,32,2,512]{3,1,2,0:T(8,128)(2,1)S(1)} collective-permute-done((bf16[2,32,2,512]{3,1,2,0:T(8,128)(2,1)S(1)}, bf16[2,32,2,512]{3,1,2,0:T(8,128)(2,1)S(1)}, u32[]{:S(2)}, u32[]{:S(2)}) %collective-permute-start.18) | collective-permute-done | bytes 131104 | tf_op jit(solution)/shard_map/ppermute | solution.py:29
  157.0 2.4 %collective-permute-start.19 = (bf16[32,2,512]{2,0,1:T(8,128)(2,1)S(1)}, bf16[32,2,512]{2,0,1:T(8,128)(2,1)S(1)}, u32[]{:S(2)}, u32[]{:S(2)}) collective-permute-start(bf16[32,2,512]{2,0,1:T(8,128)(2,1)S(1)} %fusion.71), channel_id=1, source_target_pairs={{0,2},{1,3},{2,0},{3,1},{4,6},{5,7},{6,4},{7,5},{8,10},{9,11},{10,... | collective-permute-start | bytes 196616 | tf_op jit(solution)/shard_map/ppermute | solution.py:29
  159.5 3.4 %collective-permute-done.19 = bf16[32,2,512]{2,0,1:T(8,128)(2,1)S(1)} collective-permute-done((bf16[32,2,512]{2,0,1:T(8,128)(2,1)S(1)}, bf16[32,2,512]{2,0,1:T(8,128)(2,1)S(1)}, u32[]{:S(2)}, u32[]{:S(2)}) %collective-permute-start.19) | collective-permute-done | bytes 65568 | tf_op jit(solution)/shard_map/ppermute | solution.py:29
  (114 shorter events, 45.0 us)
Async XLA Ops:
  1.9 18.9 %copy-start.7 = (s32[1,256]{1,0:T(1,128)S(1)}, s32[1,256]{1,0:T(1,128)}, u32[]{:S(2)}) copy-start(s32[1,256]{1,0:T(1,128)} %param.9) | copy-start | bytes 3076
  1.9 20.1 %copy-start.5 = (bf16[1,256,1024]{2,1,0:T(8,128)(2,1)S(1)}, bf16[1,256,1024]{2,1,0:T(8,128)(2,1)}, u32[]{:S(2)}) copy-start(bf16[1,256,1024]{2,1,0:T(8,128)(2,1)} %param.8) | copy-start | bytes 1572868
  6.7 40.0 %collective-permute-start = (bf16[2,256,512]{2,1,0:T(8,128)(2,1)}, bf16[2,256,512]{2,1,0:T(8,128)(2,1)}, u32[]{:S(2)}, u32[]{:S(2)}) collective-permute-start(bf16[2,256,512]{2,1,0:T(8,128)(2,1)} %slice.120), channel_id=1, source_target_pairs={{0,16},{4,20},{8,24},{12,28},{1,17},{5,21},{9,25},{13,29},{2,18},{... | collective-permute-start | bytes 1572872 | tf_op jit(solution)/shard_map/ppermute | solution.py:16
  12.4 35.4 %collective-permute-start.1 = (bf16[2,256,512]{2,1,0:T(8,128)(2,1)}, bf16[2,256,512]{2,1,0:T(8,128)(2,1)}, u32[]{:S(2)}, u32[]{:S(2)}) collective-permute-start(bf16[2,256,512]{2,1,0:T(8,128)(2,1)} %slice.120), channel_id=1, source_target_pairs={{0,12},{4,16},{8,20},{12,24},{16,28},{1,13},{5,17},{9,21},{13,25},... | collective-permute-start | bytes 1572872 | tf_op jit(solution)/shard_map/ppermute | solution.py:16
  15.7 33.1 %collective-permute-start.2 = (bf16[2,256,512]{2,1,0:T(8,128)(2,1)}, bf16[2,256,512]{2,1,0:T(8,128)(2,1)}, u32[]{:S(2)}, u32[]{:S(2)}) collective-permute-start(bf16[2,256,512]{2,1,0:T(8,128)(2,1)} %slice.120), channel_id=1, source_target_pairs={{0,8},{4,12},{8,16},{12,20},{16,24},{20,28},{1,9},{5,13},{9,17},{1... | collective-permute-start | bytes 1572872 | tf_op jit(solution)/shard_map/ppermute | solution.py:16
  18.6 31.3 %collective-permute-start.3 = (bf16[2,256,512]{2,1,0:T(8,128)(2,1)}, bf16[2,256,512]{2,1,0:T(8,128)(2,1)}, u32[]{:S(2)}, u32[]{:S(2)}) collective-permute-start(bf16[2,256,512]{2,1,0:T(8,128)(2,1)} %slice.120), channel_id=1, source_target_pairs={{0,4},{4,8},{8,12},{12,16},{16,20},{20,24},{24,28},{1,5},{5,9},{9,... | collective-permute-start | bytes 1572872 | tf_op jit(solution)/shard_map/ppermute | solution.py:16
  22.0 4.8 %copy-start.1 = (bf16[1,256,1024]{2,1,0:T(8,128)(2,1)S(1)}, bf16[1,256,1024]{2,1,0:T(8,128)(2,1)}, u32[]{:S(2)}) copy-start(bf16[1,256,1024]{2,1,0:T(8,128)(2,1)} %param.6) | copy-start | bytes 1572868
  71.3 6.2 %collective-permute-start.4 = (bf16[2,2,2,2,40,2,512]{6,4,5,0,1,2,3:T(8,128)(2,1)S(1)}, bf16[2,2,2,2,40,2,512]{6,4,5,0,1,2,3:T(8,128)(2,1)S(1)}, u32[]{:S(2)}, u32[]{:S(2)}) collective-permute-start(bf16[2,2,2,2,40,2,512]{6,4,5,0,1,2,3:T(8,128)(2,1)S(1)} %fusion.32), channel_id=1, source_target_pairs={{0,4},{4,0},{8,12},{12,8},{16,20},{20,16},{24,28},{28,24},{1,5},{5... | collective-permute-start | bytes 3932168 | tf_op jit(solution)/shard_map/ppermute | solution.py:29
  78.1 17.1 %collective-permute-start.5 = (bf16[2,2,2,40,2,512]{5,3,4,0,1,2:T(8,128)(2,1)S(1)}, bf16[2,2,2,40,2,512]{5,3,4,0,1,2:T(8,128)(2,1)S(1)}, u32[]{:S(2)}, u32[]{:S(2)}) collective-permute-start(bf16[2,2,2,40,2,512]{5,3,4,0,1,2:T(8,128)(2,1)S(1)} %fusion.53), channel_id=1, source_target_pairs={{0,1},{1,0},{2,3},{3,2},{4,5},{5,4},{6,7},{7,6},{8,9},{9,8},{10,11... | collective-permute-start | bytes 1966088 | tf_op jit(solution)/shard_map/ppermute | solution.py:29
  79.8 18.3 %collective-permute-start.12 = (bf16[2,8,64,256]{3,2,1,0:T(8,128)(2,1)S(1)}, bf16[2,8,64,256]{3,2,1,0:T(8,128)(2,1)S(1)}, u32[]{:S(2)}, u32[]{:S(2)}) collective-permute-start(bf16[2,8,64,256]{3,2,1,0:T(8,128)(2,1)S(1)} %pad_maximum_fusion.4), channel_id=1, source_target_pairs={{16,0},{20,4},{24,8},{28,12},{17,1},{21,5},{25,9},{29,13},{18,2},{... | collective-permute-start | bytes 1572872 | tf_op jit(solution)/shard_map/ppermute | solution.py:16
  81.2 16.9 %collective-permute-start.11 = (bf16[2,8,64,256]{3,2,1,0:T(8,128)(2,1)S(1)}, bf16[2,8,64,256]{3,2,1,0:T(8,128)(2,1)S(1)}, u32[]{:S(2)}, u32[]{:S(2)}) collective-permute-start(bf16[2,8,64,256]{3,2,1,0:T(8,128)(2,1)S(1)} %pad_maximum_fusion.3), channel_id=1, source_target_pairs={{12,0},{16,4},{20,8},{24,12},{28,16},{13,1},{17,5},{21,9},{25,13},... | collective-permute-start | bytes 1572872 | tf_op jit(solution)/shard_map/ppermute | solution.py:16
  82.5 16.8 %collective-permute-start.10 = (bf16[2,8,64,256]{3,2,1,0:T(8,128)(2,1)S(1)}, bf16[2,8,64,256]{3,2,1,0:T(8,128)(2,1)S(1)}, u32[]{:S(2)}, u32[]{:S(2)}) collective-permute-start(bf16[2,8,64,256]{3,2,1,0:T(8,128)(2,1)S(1)} %pad_maximum_fusion.2), channel_id=1, source_target_pairs={{8,0},{12,4},{16,8},{20,12},{24,16},{28,20},{9,1},{13,5},{17,9},{2... | collective-permute-start | bytes 1572872 | tf_op jit(solution)/shard_map/ppermute | solution.py:16
  83.9 15.4 %collective-permute-start.9 = (bf16[2,8,64,256]{3,2,1,0:T(8,128)(2,1)S(1)}, bf16[2,8,64,256]{3,2,1,0:T(8,128)(2,1)S(1)}, u32[]{:S(2)}, u32[]{:S(2)}) collective-permute-start(bf16[2,8,64,256]{3,2,1,0:T(8,128)(2,1)S(1)} %pad_maximum_fusion.1), channel_id=1, source_target_pairs={{4,0},{8,4},{12,8},{16,12},{20,16},{24,20},{28,24},{5,1},{9,5},{13... | collective-permute-start | bytes 1572872 | tf_op jit(solution)/shard_map/ppermute | solution.py:16
  95.4 17.2 %collective-permute-start.6 = (bf16[2,2,40,2,512]{4,2,3,0,1:T(8,128)(2,1)S(1)}, bf16[2,2,40,2,512]{4,2,3,0,1:T(8,128)(2,1)S(1)}, u32[]{:S(2)}, u32[]{:S(2)}) collective-permute-start(bf16[2,2,40,2,512]{4,2,3,0,1:T(8,128)(2,1)S(1)} %fusion.60), channel_id=1, source_target_pairs={{0,2},{1,3},{2,0},{3,1},{4,6},{5,7},{6,4},{7,5},{8,10},{9,11},{10,... | collective-permute-start | bytes 983048 | tf_op jit(solution)/shard_map/ppermute | solution.py:29
  99.7 15.4 %copy-start.8 = (bf16[1024,4,512]{2,1,0:T(4,128)(2,1)S(1)}, bf16[1024,4,512]{2,1,0:T(4,128)(2,1)}, u32[]{:S(2)}) copy-start(bf16[1024,4,512]{2,1,0:T(4,128)(2,1)} %param.7) | copy-start | bytes 12582916
  112.8 4.7 %collective-permute-start.7 = (bf16[2,40,2,256]{3,1,2,0:T(8,128)(2,1)S(1)}, bf16[2,40,2,256]{3,1,2,0:T(8,128)(2,1)S(1)}, u32[]{:S(2)}, u32[]{:S(2)}) collective-permute-start(bf16[2,40,2,256]{3,1,2,0:T(8,128)(2,1)S(1)} %fusion.69), channel_id=1, source_target_pairs={{0,16},{4,20},{8,24},{12,28},{16,0},{20,4},{24,8},{28,12},{1,17},{... | collective-permute-start | bytes 245768 | tf_op jit(solution)/shard_map/ppermute | solution.py:29
  117.6 4.1 %collective-permute-start.8 = (bf16[40,2,256]{2,0,1:T(8,128)(2,1)S(1)}, bf16[40,2,256]{2,0,1:T(8,128)(2,1)S(1)}, u32[]{:S(2)}, u32[]{:S(2)}) collective-permute-start(bf16[40,2,256]{2,0,1:T(8,128)(2,1)S(1)} %fusion.72), channel_id=1, source_target_pairs={{0,8},{4,12},{8,0},{12,4},{16,24},{20,28},{24,16},{28,20},{1,9},{5... | collective-permute-start | bytes 122888 | tf_op jit(solution)/shard_map/ppermute | solution.py:29
  125.2 2.7 %collective-permute-start.15 = (bf16[2,2,2,2,32,2,512]{6,4,5,3,2,1,0:T(8,128)(2,1)S(1)}, bf16[2,2,2,2,32,2,512]{6,4,5,3,2,1,0:T(8,128)(2,1)S(1)}, u32[]{:S(2)}, u32[]{:S(2)}) collective-permute-start(bf16[2,2,2,2,32,2,512]{6,4,5,3,2,1,0:T(8,128)(2,1)S(1)} %fusion.48), channel_id=1, source_target_pairs={{0,4},{4,0},{8,12},{12,8},{16,20},{20,16},{24,28},{28,24},{1,5},{5... | collective-permute-start | bytes 3145736 | tf_op jit(solution)/shard_map/ppermute | solution.py:29
  128.5 14.3 %collective-permute-start.16 = (bf16[2,2,2,32,2,512]{5,3,4,2,1,0:T(8,128)(2,1)S(1)}, bf16[2,2,2,32,2,512]{5,3,4,2,1,0:T(8,128)(2,1)S(1)}, u32[]{:S(2)}, u32[]{:S(2)}) collective-permute-start(bf16[2,2,2,32,2,512]{5,3,4,2,1,0:T(8,128)(2,1)S(1)} %fusion.54), channel_id=1, source_target_pairs={{0,16},{4,20},{8,24},{12,28},{16,0},{20,4},{24,8},{28,12},{1,17},{... | collective-permute-start | bytes 1572872 | tf_op jit(solution)/shard_map/ppermute | solution.py:29
  143.0 8.8 %collective-permute-start.17 = (bf16[2,2,32,2,512]{4,2,3,1,0:T(8,128)(2,1)S(1)}, bf16[2,2,32,2,512]{4,2,3,1,0:T(8,128)(2,1)S(1)}, u32[]{:S(2)}, u32[]{:S(2)}) collective-permute-start(bf16[2,2,32,2,512]{4,2,3,1,0:T(8,128)(2,1)S(1)} %fusion.61), channel_id=1, source_target_pairs={{0,8},{4,12},{8,0},{12,4},{16,24},{20,28},{24,16},{28,20},{1,9},{5... | collective-permute-start | bytes 786440 | tf_op jit(solution)/shard_map/ppermute | solution.py:29
  143.1 9.6 %collective-permute-start.13 = (bf16[2,40,2,256]{3,1,2,0:T(8,128)(2,1)S(1)}, bf16[2,40,2,256]{3,1,2,0:T(8,128)(2,1)S(1)}, u32[]{:S(2)}, u32[]{:S(2)}) collective-permute-start(bf16[2,40,2,256]{3,1,2,0:T(8,128)(2,1)S(1)} %fusion.70), channel_id=1, source_target_pairs={{0,8},{4,12},{8,0},{12,4},{16,24},{20,28},{24,16},{28,20},{1,9},{5... | collective-permute-start | bytes 245768 | tf_op jit(solution)/shard_map/ppermute | solution.py:29
  151.9 5.0 %collective-permute-start.18 = (bf16[2,32,2,512]{3,1,2,0:T(8,128)(2,1)S(1)}, bf16[2,32,2,512]{3,1,2,0:T(8,128)(2,1)S(1)}, u32[]{:S(2)}, u32[]{:S(2)}) collective-permute-start(bf16[2,32,2,512]{3,1,2,0:T(8,128)(2,1)S(1)} %fusion.68), channel_id=1, source_target_pairs={{0,1},{1,0},{2,3},{3,2},{4,5},{5,4},{6,7},{7,6},{8,9},{9,8},{10,11... | collective-permute-start | bytes 393224 | tf_op jit(solution)/shard_map/ppermute | solution.py:29
  152.7 6.7 %collective-permute-start.14 = (bf16[40,2,256]{2,0,1:T(8,128)(2,1)S(1)}, bf16[40,2,256]{2,0,1:T(8,128)(2,1)S(1)}, u32[]{:S(2)}, u32[]{:S(2)}) collective-permute-start(bf16[40,2,256]{2,0,1:T(8,128)(2,1)S(1)} %fusion.73), channel_id=1, source_target_pairs={{0,16},{4,20},{8,24},{12,28},{16,0},{20,4},{24,8},{28,12},{1,17},{... | collective-permute-start | bytes 122888 | tf_op jit(solution)/shard_map/ppermute | solution.py:29
  157.0 5.9 %collective-permute-start.19 = (bf16[32,2,512]{2,0,1:T(8,128)(2,1)S(1)}, bf16[32,2,512]{2,0,1:T(8,128)(2,1)S(1)}, u32[]{:S(2)}, u32[]{:S(2)}) collective-permute-start(bf16[32,2,512]{2,0,1:T(8,128)(2,1)S(1)} %fusion.71), channel_id=1, source_target_pairs={{0,2},{1,3},{2,0},{3,1},{4,6},{5,7},{6,4},{7,5},{8,10},{9,11},{10,... | collective-permute-start | bytes 196616 | tf_op jit(solution)/shard_map/ppermute | solution.py:29
  (6 other events, 18.1 us)

commit v18 on v17

--- a/solution.py
+++ b/solution.py
@@ -187,7 +187,7 @@
             axis=1,
         ).reshape((-1,) + early_terms.shape[1:])
         early, _ = scatter_rows(
-            payload, None, ("tm", "night"), "tm", jnp.bfloat16, tail_first=True
+            payload, None, ("tm", "night"), "tm", jnp.bfloat16, tail_first=True, balance=False
         )
         digit_sums = early[block_rows_out, 0, :bits].astype(jnp.int32)
         count = jnp.sum(digit_sums * (2 ** jnp.arange(bits, dtype=jnp.int32)))
@@ -214,9 +214,7 @@
     key_value_part = jnp.einsum(
         "rd,wgcr->dwgc", normed, grad_proj[1:3], preferred_element_type=jnp.float32
     ).reshape(width, 2, inner)
-    late, _ = scatter_rows(
-        key_value_part, None, ("tm", "night"), "tm", jnp.bfloat16, balance=False
-    )
+    late, _ = scatter_rows(key_value_part, None, ("tm", "night"), "tm", jnp.bfloat16)
     summed = jnp.concatenate([early[:, :1], late, early[:, 1:]], axis=1)
     total_count = count.astype(jnp.float32)
     loss_scale = jnp.float32(tokens_all) / total_count

time: 165 us -> 159 us (0.964)
  waiting for transfers between devices: 69.5 us -> 62.8 us
    ppermute x12, waiting for transfers between devices: 55 us -> 48.2 us  [halve(): lax.ppermute(send.astype(send_type), axis, pairs).astype(keep.dtype)]
  transfers between devices with their start and end apart: 20 -> 20, of which waited for: 13 -> 14; matrix products, arithmetic and copies ran while one was open for 13% -> 14% of each run, Pallas kernels for 0% -> 0%
where the time goes in v18:
time: 159 us; the launch traced here: 158 us
  waiting for transfers between devices  62.8 us (39%)
  starting transfers between devices  36.9 us (23%)
  matrix products  28.8 us (18%)
  local copies, waits for them, and re-layouts  15.9 us (10%)
  other arithmetic  10.9 us (7%)
  between operations  2.68 us (2%)
    ppermute x12, waiting for transfers between devices, halve(): lax.ppermute(send.astype(send_type), axis, pairs).astype(keep.dtype)  48.2 us
    ppermute x8, starting transfers between devices, shifted(): return lax.ppermute(value, axis, pairs)  19.4 us
    ppermute x12, starting transfers between devices, halve(): lax.ppermute(send.astype(send_type), axis, pairs).astype(keep.dtype)  17.5 us
    ppermute x8, waiting for transfers between devices, shifted(): return lax.ppermute(value, axis, pairs)  14.6 us
    unnamed x24, local copies, waits for them, and re-layouts  7.02 us
    dot_general x1, matrix products, shards(): jnp.einsum('rd,dwh->wrh', grad_out, weights, preferred_element_type=jnp.f...  4.81 us
    dot_general x1, matrix products, shards(): jnp.einsum('rd,dwh->wrh', normed, weights, preferred_element_type=jnp.flo...  3.98 us
    dot_general x1, matrix products, band_block(): jnp.einsum('qgc,kgc->gqk', grad_attn, values_blk, preferred_element_type=...  3.92 us
  transfers between devices with their start and end apart: 20, of which 14 were waited for; matrix products, arithmetic and copies ran while one was open for 14% of the time, Pallas kernels for 0%

profile of v18, /device:TPU:0, one launch (start us, length us, event | category | flops | bytes accessed | tf_op | source)
XLA Modules:
  0.0 157.9 jit_solution(9009348782536162095)
XLA Ops:
  1.9 4.0 %fusion.21 = bf16[4,256,512]{2,1,0:T(8,128)(2,1)S(1)} fusion(bf16[1024,4,512]{2,1,0:T(4,128)(2,1)} %param.7, bf16[1,256,1024]{2,1,0:T(8,128)(2,1)} %param.6, f32[256]{0:T(256)S(1)} %add_rsqrt_fusion), kind=kOutput, calls=%fused_computation.24 | convolution fusion | flops 1075052544 | bytes 5768192 | tf_op jit(solution)/shard_map/rd,dwh->wrh/dot_general | solution.py:142
  6.7 5.7 %collective-permute-start = (bf16[2,256,512]{2,1,0:T(8,128)(2,1)}, bf16[2,256,512]{2,1,0:T(8,128)(2,1)}, u32[]{:S(2)}, u32[]{:S(2)}) collective-permute-start(bf16[2,256,512]{2,1,0:T(8,128)(2,1)} %slice.120), channel_id=1, source_target_pairs={{0,16},{4,20},{8,24},{12,28},{1,17},{5,21},{9,25},{13,29},{2,18},{... | collective-permute-start | bytes 1572872 | tf_op jit(solution)/shard_map/ppermute | solution.py:16
  12.4 3.4 %collective-permute-start.1 = (bf16[2,256,512]{2,1,0:T(8,128)(2,1)}, bf16[2,256,512]{2,1,0:T(8,128)(2,1)}, u32[]{:S(2)}, u32[]{:S(2)}) collective-permute-start(bf16[2,256,512]{2,1,0:T(8,128)(2,1)} %slice.120), channel_id=1, source_target_pairs={{0,12},{4,16},{8,20},{12,24},{16,28},{1,13},{5,17},{9,21},{13,25},... | collective-permute-start | bytes 1572872 | tf_op jit(solution)/shard_map/ppermute | solution.py:16
  15.7 2.9 %collective-permute-start.2 = (bf16[2,256,512]{2,1,0:T(8,128)(2,1)}, bf16[2,256,512]{2,1,0:T(8,128)(2,1)}, u32[]{:S(2)}, u32[]{:S(2)}) collective-permute-start(bf16[2,256,512]{2,1,0:T(8,128)(2,1)} %slice.120), channel_id=1, source_target_pairs={{0,8},{4,12},{8,16},{12,20},{16,24},{20,28},{1,9},{5,13},{9,17},{1... | collective-permute-start | bytes 1572872 | tf_op jit(solution)/shard_map/ppermute | solution.py:16
  22.0 4.8 %fusion.18 = bf16[4,256,512]{2,1,0:T(8,128)(2,1)} fusion(bf16[1024,4,512]{2,1,0:T(4,128)(2,1)} %param.7, bf16[1,256,1024]{2,1,0:T(8,128)(2,1)S(1)} %copy-done.5, pred[256]{0:T(512)(128)(4,1)S(1)} %compare_reduce_fusion), kind=kOutput, calls=%fused_computation.23 | convolution fusion | flops 1074528256 | bytes 5767424 | tf_op jit(solution)/shard_map/rd,dwh->wrh/dot_general | solution.py:154
  33.3 13.4 %collective-permute-done = bf16[2,256,512]{2,1,0:T(8,128)(2,1)} collective-permute-done((bf16[2,256,512]{2,1,0:T(8,128)(2,1)}, bf16[2,256,512]{2,1,0:T(8,128)(2,1)}, u32[]{:S(2)}, u32[]{:S(2)}) %collective-permute-start) | collective-permute-done | bytes 524320 | tf_op jit(solution)/shard_map/ppermute | solution.py:16
  55.3 3.9 %fusion.1 = (f32[8,256]{1,0:T(8,128)S(1)}, f32[8,256,1280]{2,1,0:T(8,128)S(1)}) fusion(f32[256,1280]{1,0:T(8,128)} %fusion.37, bf16[256,8,64]{0,2,1:T(8,128)(2,1)S(1)} %bitcast.194, bf16[1280,8,64]{0,2,1:T(8,128)(2,1)S(1)} %bitcast.191), kind=kOutput, calls=%fused_computation.3 | convolution fusion | flops 343406592 | bytes 13377536 | tf_op jit(solution)/shard_map/qgc,kgc->gqk/dot_general | solution.py:102
  59.3 2.8 %multiply_reduce_fusion = (f32[256,8]{0,1:T(8,128)S(1)}, bf16[8,64,256]{2,1,0:T(8,128)(2,1)S(1)}) fusion(bf16[256,8,64]{0,2,1:T(8,128)(2,1)S(1)} %bitcast.204, bf16[1280,8,64]{0,2,1:T(8,128)(2,1)S(1)} %bitcast.201, f32[8,256]{1,0:T(8,128)S(1)} %get-tuple-element.34, f32[256,1280]{1,0:T(8,128)S(1)} %copy-done, f32[8,256,1280]{2,1,0:T(8,128)S(1)} %get-tuple-element.35), kind=kOutput, calls=%fused_computation.80 | convolution fusion | flops 346683392 | bytes 13647872 | tf_op jit(solution)/shard_map/gqk,kgc->qgc/dot_general | solution.py:108
  62.1 3.9 %multiply_convert_fusion = bf16[8,256,1280]{2,1,0:T(8,128)(2,1)S(1)} fusion(bf16[256,8,64]{0,2,1:T(8,128)(2,1)S(1)} %bitcast.205, bf16[1280,8,64]{0,2,1:T(8,128)(2,1)S(1)} %bitcast.202, f32[8,256]{1,0:T(8,128)S(1)} %bitcast.208, f32[8,256]{1,0:T(8,128)S(1)} %get-tuple-element.34, f32[256,1280]{1,0:T(8,128)S(1)} %copy-done, ...), kind=kOutput, calls=%fused_computation | convolution fusion | flops 353894400 | bytes 18628608 | tf_op jit(solution)/shard_map/qgc,kgc->gqk/dot_general | solution.py:112
  71.3 3.6 %collective-permute-start.4 = (bf16[2,2,2,2,40,2,512]{6,4,5,1,0,2,3:T(8,128)(2,1)S(1)}, bf16[2,2,2,2,40,2,512]{6,4,5,1,0,2,3:T(8,128)(2,1)S(1)}, u32[]{:S(2)}, u32[]{:S(2)}) collective-permute-start(bf16[2,2,2,2,40,2,512]{6,4,5,1,0,2,3:T(8,128)(2,1)S(1)} %fusion.32), channel_id=1, source_target_pairs={{0,4},{4,0},{8,12},{12,8},{16,20},{20,16},{24,28},{28,24},{1,5},{5... | collective-permute-start | bytes 3932168 | tf_op jit(solution)/shard_map/ppermute | solution.py:29
  74.9 2.3 %fusion.91 = (bf16[8,64,1280]{2,1,0:T(8,128)(2,1)S(1)}, f32[8,64,1280]{2,1,0:T(8,128)S(1)}) fusion(bf16[256,8,64]{0,2,1:T(8,128)(2,1)S(1)} %bitcast.206, f32[8,256]{1,0:T(8,128)S(1)} %get-tuple-element.34, f32[256,1280]{1,0:T(8,128)S(1)} %copy-done, f32[8,256,1280]{2,1,0:T(8,128)S(1)} %get-tuple-element.35), kind=kOutput, calls=%fused_computation.163 | convolution fusion | flops 346685440 | bytes 15998976 | tf_op jit(solution)/shard_map/gqk,qgc->gck/dot_general | solution.py:122
  85.5 9.7 %collective-permute-done.5 = bf16[2,2,2,40,2,512]{5,3,4,1,0,2:T(8,128)(2,1)S(1)} collective-permute-done((bf16[2,2,2,40,2,512]{5,3,4,1,0,2:T(8,128)(2,1)S(1)}, bf16[2,2,2,40,2,512]{5,3,4,1,0,2:T(8,128)(2,1)S(1)}, u32[]{:S(2)}, u32[]{:S(2)}) %collective-permute-start.5) | collective-permute-done | bytes 655392 | tf_op jit(solution)/shard_map/ppermute | solution.py:29
  95.4 2.7 %collective-permute-start.6 = (bf16[2,2,40,2,512]{4,2,3,1,0:T(8,128)(2,1)S(1)}, bf16[2,2,40,2,512]{4,2,3,1,0:T(8,128)(2,1)S(1)}, u32[]{:S(2)}, u32[]{:S(2)}) collective-permute-start(bf16[2,2,40,2,512]{4,2,3,1,0:T(8,128)(2,1)S(1)} %fusion.59), channel_id=1, source_target_pairs={{0,2},{1,3},{2,0},{3,1},{4,6},{5,7},{6,4},{7,5},{8,10},{9,11},{10,... | collective-permute-start | bytes 983048 | tf_op jit(solution)/shard_map/ppermute | solution.py:29
  99.9 12.7 %collective-permute-done.6 = bf16[2,2,40,2,512]{4,2,3,1,0:T(8,128)(2,1)S(1)} collective-permute-done((bf16[2,2,40,2,512]{4,2,3,1,0:T(8,128)(2,1)S(1)}, bf16[2,2,40,2,512]{4,2,3,1,0:T(8,128)(2,1)S(1)}, u32[]{:S(2)}, u32[]{:S(2)}) %collective-permute-start.6) | collective-permute-done | bytes 327712 | tf_op jit(solution)/shard_map/ppermute | solution.py:29
  112.7 2.3 %collective-permute-start.7 = (bf16[2,40,2,512]{3,1,2,0:T(8,128)(2,1)S(1)}, bf16[2,40,2,512]{3,1,2,0:T(8,128)(2,1)S(1)}, u32[]{:S(2)}, u32[]{:S(2)}) collective-permute-start(bf16[2,40,2,512]{3,1,2,0:T(8,128)(2,1)S(1)} %fusion.70), channel_id=1, source_target_pairs={{0,16},{4,20},{8,24},{12,28},{16,0},{20,4},{24,8},{28,12},{1,17},{... | collective-permute-start | bytes 491528 | tf_op jit(solution)/shard_map/ppermute | solution.py:29
  115.1 2.7 %fusion.41 = (f32[256]{0:T(256)S(1)}, f32[256,1024]{1,0:T(8,128)}) fusion(bf16[1,256,1024]{2,1,0:T(8,128)(2,1)S(1)} %copy-done.1, f32[256]{0:T(256)S(1)} %add_rsqrt_fusion, bf16[4,256,512]{1,2,0:T(8,128)(2,1)S(1)} %bitcast.203, bf16[1024,4,512]{2,1,0:T(4,128)(2,1)S(1)} %copy-done.8), kind=kOutput, calls=%fused_computation.44 | convolution fusion | flops 1074790144 | bytes 6817792 | tf_op jit(solution)/shard_map/wrh,dwh->rd/dot_general | solution.py:209
  118.5 4.4 %collective-permute-done.8 = bf16[40,2,512]{2,0,1:T(8,128)(2,1)S(1)} collective-permute-done((bf16[40,2,512]{2,0,1:T(8,128)(2,1)S(1)}, bf16[40,2,512]{2,0,1:T(8,128)(2,1)S(1)}, u32[]{:S(2)}, u32[]{:S(2)}) %collective-permute-start.8) | collective-permute-done | bytes 81952 | tf_op jit(solution)/shard_map/ppermute | solution.py:29
  124.3 2.3 %fusion.68 = (bf16[1024,256]{0,1:T(8,128)(2,1)S(1)}, bf16[1,256,1024]{2,1,0:T(8,128)(2,1)}) fusion(f32[256]{0:T(256)S(1)} %add_rsqrt_fusion, bf16[1,256,1024]{2,1,0:T(8,128)(2,1)S(1)} %copy-done.1, f32[256,1024]{1,0:T(8,128)} %get-tuple-element.43, f32[256]{0:T(256)S(1)} %broadcast_multiply_fusion, f32[]{:T(128)S(6)} %div.75), kind=kLoop, calls=%fused_computation.107 | loop fusion | flops 2097152 | bytes 2623492 | tf_op jit(solution)/shard_map/rd,wgcr->dwgc/dot_general | solution.py:214
  127.8 2.6 %collective-permute-done.13 = bf16[2,2,2,2,32,2,512]{6,4,5,3,2,1,0:T(8,128)(2,1)S(1)} collective-permute-done((bf16[2,2,2,2,32,2,512]{6,4,5,3,2,1,0:T(8,128)(2,1)S(1)}, bf16[2,2,2,2,32,2,512]{6,4,5,3,2,1,0:T(8,128)(2,1)S(1)}, u32[]{:S(2)}, u32[]{:S(2)}) %collective-permute-start.13) | collective-permute-done | bytes 1048608 | tf_op jit(solution)/shard_map/ppermute | solution.py:29
  133.4 6.5 %collective-permute-done.14 = bf16[2,2,2,32,2,256]{5,3,4,2,1,0:T(8,128)(2,1)S(1)} collective-permute-done((bf16[2,2,2,32,2,256]{5,3,4,2,1,0:T(8,128)(2,1)S(1)}, bf16[2,2,2,32,2,256]{5,3,4,2,1,0:T(8,128)(2,1)S(1)}, u32[]{:S(2)}, u32[]{:S(2)}) %collective-permute-start.14) | collective-permute-done | bytes 262176 | tf_op jit(solution)/shard_map/ppermute | solution.py:29
  142.0 3.1 %collective-permute-done.15 = bf16[2,2,32,2,256]{4,2,3,1,0:T(8,128)(2,1)S(1)} collective-permute-done((bf16[2,2,32,2,256]{4,2,3,1,0:T(8,128)(2,1)S(1)}, bf16[2,2,32,2,256]{4,2,3,1,0:T(8,128)(2,1)S(1)}, u32[]{:S(2)}, u32[]{:S(2)}) %collective-permute-start.15) | collective-permute-done | bytes 131104 | tf_op jit(solution)/shard_map/ppermute | solution.py:29
  148.2 3.5 %collective-permute-done.18 = bf16[2,32,2,512]{3,1,2,0:T(8,128)(2,1)S(1)} collective-permute-done((bf16[2,32,2,512]{3,1,2,0:T(8,128)(2,1)S(1)}, bf16[2,32,2,512]{3,1,2,0:T(8,128)(2,1)S(1)}, u32[]{:S(2)}, u32[]{:S(2)}) %collective-permute-start.18) | collective-permute-done | bytes 131104 | tf_op jit(solution)/shard_map/ppermute | solution.py:29
  151.8 2.9 %collective-permute-start.19 = (bf16[32,2,512]{2,0,1:T(8,128)(2,1)S(1)}, bf16[32,2,512]{2,0,1:T(8,128)(2,1)S(1)}, u32[]{:S(2)}, u32[]{:S(2)}) collective-permute-start(bf16[32,2,512]{2,0,1:T(8,128)(2,1)S(1)} %fusion.75), channel_id=1, source_target_pairs={{0,2},{1,3},{2,0},{3,1},{4,6},{5,7},{6,4},{7,5},{8,10},{9,11},{10,... | collective-permute-start | bytes 196616 | tf_op jit(solution)/shard_map/ppermute | solution.py:29
  154.7 2.3 %collective-permute-done.19 = bf16[32,2,512]{2,0,1:T(8,128)(2,1)S(1)} collective-permute-done((bf16[32,2,512]{2,0,1:T(8,128)(2,1)S(1)}, bf16[32,2,512]{2,0,1:T(8,128)(2,1)S(1)}, u32[]{:S(2)}, u32[]{:S(2)}) %collective-permute-start.19) | collective-permute-done | bytes 65568 | tf_op jit(solution)/shard_map/ppermute | solution.py:29
  (115 shorter events, 47.0 us)
Async XLA Ops:
  1.9 18.9 %copy-start.7 = (s32[1,256]{1,0:T(1,128)S(1)}, s32[1,256]{1,0:T(1,128)}, u32[]{:S(2)}) copy-start(s32[1,256]{1,0:T(1,128)} %param.9) | copy-start | bytes 3076
  1.9 20.1 %copy-start.5 = (bf16[1,256,1024]{2,1,0:T(8,128)(2,1)S(1)}, bf16[1,256,1024]{2,1,0:T(8,128)(2,1)}, u32[]{:S(2)}) copy-start(bf16[1,256,1024]{2,1,0:T(8,128)(2,1)} %param.8) | copy-start | bytes 1572868
  6.7 40.0 %collective-permute-start = (bf16[2,256,512]{2,1,0:T(8,128)(2,1)}, bf16[2,256,512]{2,1,0:T(8,128)(2,1)}, u32[]{:S(2)}, u32[]{:S(2)}) collective-permute-start(bf16[2,256,512]{2,1,0:T(8,128)(2,1)} %slice.120), channel_id=1, source_target_pairs={{0,16},{4,20},{8,24},{12,28},{1,17},{5,21},{9,25},{13,29},{2,18},{... | collective-permute-start | bytes 1572872 | tf_op jit(solution)/shard_map/ppermute | solution.py:16
  12.4 35.4 %collective-permute-start.1 = (bf16[2,256,512]{2,1,0:T(8,128)(2,1)}, bf16[2,256,512]{2,1,0:T(8,128)(2,1)}, u32[]{:S(2)}, u32[]{:S(2)}) collective-permute-start(bf16[2,256,512]{2,1,0:T(8,128)(2,1)} %slice.120), channel_id=1, source_target_pairs={{0,12},{4,16},{8,20},{12,24},{16,28},{1,13},{5,17},{9,21},{13,25},... | collective-permute-start | bytes 1572872 | tf_op jit(solution)/shard_map/ppermute | solution.py:16
  15.7 33.1 %collective-permute-start.2 = (bf16[2,256,512]{2,1,0:T(8,128)(2,1)}, bf16[2,256,512]{2,1,0:T(8,128)(2,1)}, u32[]{:S(2)}, u32[]{:S(2)}) collective-permute-start(bf16[2,256,512]{2,1,0:T(8,128)(2,1)} %slice.120), channel_id=1, source_target_pairs={{0,8},{4,12},{8,16},{12,20},{16,24},{20,28},{1,9},{5,13},{9,17},{1... | collective-permute-start | bytes 1572872 | tf_op jit(solution)/shard_map/ppermute | solution.py:16
  18.7 31.3 %collective-permute-start.3 = (bf16[2,256,512]{2,1,0:T(8,128)(2,1)}, bf16[2,256,512]{2,1,0:T(8,128)(2,1)}, u32[]{:S(2)}, u32[]{:S(2)}) collective-permute-start(bf16[2,256,512]{2,1,0:T(8,128)(2,1)} %slice.120), channel_id=1, source_target_pairs={{0,4},{4,8},{8,12},{12,16},{16,20},{20,24},{24,28},{1,5},{5,9},{9,... | collective-permute-start | bytes 1572872 | tf_op jit(solution)/shard_map/ppermute | solution.py:16
  22.0 4.8 %copy-start.1 = (bf16[1,256,1024]{2,1,0:T(8,128)(2,1)S(1)}, bf16[1,256,1024]{2,1,0:T(8,128)(2,1)}, u32[]{:S(2)}) copy-start(bf16[1,256,1024]{2,1,0:T(8,128)(2,1)} %param.6) | copy-start | bytes 1572868
  71.3 6.2 %collective-permute-start.4 = (bf16[2,2,2,2,40,2,512]{6,4,5,1,0,2,3:T(8,128)(2,1)S(1)}, bf16[2,2,2,2,40,2,512]{6,4,5,1,0,2,3:T(8,128)(2,1)S(1)}, u32[]{:S(2)}, u32[]{:S(2)}) collective-permute-start(bf16[2,2,2,2,40,2,512]{6,4,5,1,0,2,3:T(8,128)(2,1)S(1)} %fusion.32), channel_id=1, source_target_pairs={{0,4},{4,0},{8,12},{12,8},{16,20},{20,16},{24,28},{28,24},{1,5},{5... | collective-permute-start | bytes 3932168 | tf_op jit(solution)/shard_map/ppermute | solution.py:29
  78.1 17.1 %collective-permute-start.5 = (bf16[2,2,2,40,2,512]{5,3,4,1,0,2:T(8,128)(2,1)S(1)}, bf16[2,2,2,40,2,512]{5,3,4,1,0,2:T(8,128)(2,1)S(1)}, u32[]{:S(2)}, u32[]{:S(2)}) collective-permute-start(bf16[2,2,2,40,2,512]{5,3,4,1,0,2:T(8,128)(2,1)S(1)} %fusion.53), channel_id=1, source_target_pairs={{0,1},{1,0},{2,3},{3,2},{4,5},{5,4},{6,7},{7,6},{8,9},{9,8},{10,11... | collective-permute-start | bytes 1966088 | tf_op jit(solution)/shard_map/ppermute | solution.py:29
  79.8 18.3 %collective-permute-start.12 = (bf16[2,8,64,256]{3,2,1,0:T(8,128)(2,1)S(1)}, bf16[2,8,64,256]{3,2,1,0:T(8,128)(2,1)S(1)}, u32[]{:S(2)}, u32[]{:S(2)}) collective-permute-start(bf16[2,8,64,256]{3,2,1,0:T(8,128)(2,1)S(1)} %pad_maximum_fusion.4), channel_id=1, source_target_pairs={{16,0},{20,4},{24,8},{28,12},{17,1},{21,5},{25,9},{29,13},{18,2},{... | collective-permute-start | bytes 1572872 | tf_op jit(solution)/shard_map/ppermute | solution.py:16
  81.1 16.9 %collective-permute-start.11 = (bf16[2,8,64,256]{3,2,1,0:T(8,128)(2,1)S(1)}, bf16[2,8,64,256]{3,2,1,0:T(8,128)(2,1)S(1)}, u32[]{:S(2)}, u32[]{:S(2)}) collective-permute-start(bf16[2,8,64,256]{3,2,1,0:T(8,128)(2,1)S(1)} %pad_maximum_fusion.3), channel_id=1, source_target_pairs={{12,0},{16,4},{20,8},{24,12},{28,16},{13,1},{17,5},{21,9},{25,13},... | collective-permute-start | bytes 1572872 | tf_op jit(solution)/shard_map/ppermute | solution.py:16
  82.5 16.8 %collective-permute-start.10 = (bf16[2,8,64,256]{3,2,1,0:T(8,128)(2,1)S(1)}, bf16[2,8,64,256]{3,2,1,0:T(8,128)(2,1)S(1)}, u32[]{:S(2)}, u32[]{:S(2)}) collective-permute-start(bf16[2,8,64,256]{3,2,1,0:T(8,128)(2,1)S(1)} %pad_maximum_fusion.2), channel_id=1, source_target_pairs={{8,0},{12,4},{16,8},{20,12},{24,16},{28,20},{9,1},{13,5},{17,9},{2... | collective-permute-start | bytes 1572872 | tf_op jit(solution)/shard_map/ppermute | solution.py:16
  83.9 15.4 %collective-permute-start.9 = (bf16[2,8,64,256]{3,2,1,0:T(8,128)(2,1)S(1)}, bf16[2,8,64,256]{3,2,1,0:T(8,128)(2,1)S(1)}, u32[]{:S(2)}, u32[]{:S(2)}) collective-permute-start(bf16[2,8,64,256]{3,2,1,0:T(8,128)(2,1)S(1)} %pad_maximum_fusion.1), channel_id=1, source_target_pairs={{4,0},{8,4},{12,8},{16,12},{20,16},{24,20},{28,24},{5,1},{9,5},{13... | collective-permute-start | bytes 1572872 | tf_op jit(solution)/shard_map/ppermute | solution.py:16
  95.4 17.2 %collective-permute-start.6 = (bf16[2,2,40,2,512]{4,2,3,1,0:T(8,128)(2,1)S(1)}, bf16[2,2,40,2,512]{4,2,3,1,0:T(8,128)(2,1)S(1)}, u32[]{:S(2)}, u32[]{:S(2)}) collective-permute-start(bf16[2,2,40,2,512]{4,2,3,1,0:T(8,128)(2,1)S(1)} %fusion.59), channel_id=1, source_target_pairs={{0,2},{1,3},{2,0},{3,1},{4,6},{5,7},{6,4},{7,5},{8,10},{9,11},{10,... | collective-permute-start | bytes 983048 | tf_op jit(solution)/shard_map/ppermute | solution.py:29
  99.3 15.8 %copy-start.8 = (bf16[1024,4,512]{2,1,0:T(4,128)(2,1)S(1)}, bf16[1024,4,512]{2,1,0:T(4,128)(2,1)}, u32[]{:S(2)}) copy-start(bf16[1024,4,512]{2,1,0:T(4,128)(2,1)} %param.7) | copy-start | bytes 12582916
  112.7 5.6 %collective-permute-start.7 = (bf16[2,40,2,512]{3,1,2,0:T(8,128)(2,1)S(1)}, bf16[2,40,2,512]{3,1,2,0:T(8,128)(2,1)S(1)}, u32[]{:S(2)}, u32[]{:S(2)}) collective-permute-start(bf16[2,40,2,512]{3,1,2,0:T(8,128)(2,1)S(1)} %fusion.70), channel_id=1, source_target_pairs={{0,16},{4,20},{8,24},{12,28},{16,0},{20,4},{24,8},{28,12},{1,17},{... | collective-permute-start | bytes 491528 | tf_op jit(solution)/shard_map/ppermute | solution.py:29
  118.4 4.5 %collective-permute-start.8 = (bf16[40,2,512]{2,0,1:T(8,128)(2,1)S(1)}, bf16[40,2,512]{2,0,1:T(8,128)(2,1)S(1)}, u32[]{:S(2)}, u32[]{:S(2)}) collective-permute-start(bf16[40,2,512]{2,0,1:T(8,128)(2,1)S(1)} %fusion.74), channel_id=1, source_target_pairs={{0,8},{4,12},{8,0},{12,4},{16,24},{20,28},{24,16},{28,20},{1,9},{5... | collective-permute-start | bytes 245768 | tf_op jit(solution)/shard_map/ppermute | solution.py:29
  127.7 2.7 %collective-permute-start.13 = (bf16[2,2,2,2,32,2,512]{6,4,5,3,2,1,0:T(8,128)(2,1)S(1)}, bf16[2,2,2,2,32,2,512]{6,4,5,3,2,1,0:T(8,128)(2,1)S(1)}, u32[]{:S(2)}, u32[]{:S(2)}) collective-permute-start(bf16[2,2,2,2,32,2,512]{6,4,5,3,2,1,0:T(8,128)(2,1)S(1)} %fusion.48), channel_id=1, source_target_pairs={{0,4},{4,0},{8,12},{12,8},{16,20},{20,16},{24,28},{28,24},{1,5},{5... | collective-permute-start | bytes 3145736 | tf_op jit(solution)/shard_map/ppermute | solution.py:29
  131.2 8.7 %collective-permute-start.14 = (bf16[2,2,2,32,2,256]{5,3,4,2,1,0:T(8,128)(2,1)S(1)}, bf16[2,2,2,32,2,256]{5,3,4,2,1,0:T(8,128)(2,1)S(1)}, u32[]{:S(2)}, u32[]{:S(2)}) collective-permute-start(bf16[2,2,2,32,2,256]{5,3,4,2,1,0:T(8,128)(2,1)S(1)} %fusion.60), channel_id=1, source_target_pairs={{0,16},{4,20},{8,24},{12,28},{16,0},{20,4},{24,8},{28,12},{1,17},{... | collective-permute-start | bytes 786440 | tf_op jit(solution)/shard_map/ppermute | solution.py:29
  133.3 8.1 %collective-permute-start.16 = (bf16[2,2,2,32,2,256]{5,3,4,2,1,0:T(8,128)(2,1)S(1)}, bf16[2,2,2,32,2,256]{5,3,4,2,1,0:T(8,128)(2,1)S(1)}, u32[]{:S(2)}, u32[]{:S(2)}) collective-permute-start(bf16[2,2,2,32,2,256]{5,3,4,2,1,0:T(8,128)(2,1)S(1)} %fusion.61), channel_id=1, source_target_pairs={{0,8},{4,12},{8,0},{12,4},{16,24},{20,28},{24,16},{28,20},{1,9},{5... | collective-permute-start | bytes 786440 | tf_op jit(solution)/shard_map/ppermute | solution.py:29
  140.0 5.1 %collective-permute-start.15 = (bf16[2,2,32,2,256]{4,2,3,1,0:T(8,128)(2,1)S(1)}, bf16[2,2,32,2,256]{4,2,3,1,0:T(8,128)(2,1)S(1)}, u32[]{:S(2)}, u32[]{:S(2)}) collective-permute-start(bf16[2,2,32,2,256]{4,2,3,1,0:T(8,128)(2,1)S(1)} %fusion.71), channel_id=1, source_target_pairs={{0,8},{4,12},{8,0},{12,4},{16,24},{20,28},{24,16},{28,20},{1,9},{5... | collective-permute-start | bytes 393224 | tf_op jit(solution)/shard_map/ppermute | solution.py:29
  141.6 5.0 %collective-permute-start.17 = (bf16[2,2,32,2,256]{4,2,3,1,0:T(8,128)(2,1)S(1)}, bf16[2,2,32,2,256]{4,2,3,1,0:T(8,128)(2,1)S(1)}, u32[]{:S(2)}, u32[]{:S(2)}) collective-permute-start(bf16[2,2,32,2,256]{4,2,3,1,0:T(8,128)(2,1)S(1)} %fusion.72), channel_id=1, source_target_pairs={{0,16},{4,20},{8,24},{12,28},{16,0},{20,4},{24,8},{28,12},{1,17},{... | collective-permute-start | bytes 393224 | tf_op jit(solution)/shard_map/ppermute | solution.py:29
  146.7 5.0 %collective-permute-start.18 = (bf16[2,32,2,512]{3,1,2,0:T(8,128)(2,1)S(1)}, bf16[2,32,2,512]{3,1,2,0:T(8,128)(2,1)S(1)}, u32[]{:S(2)}, u32[]{:S(2)}) collective-permute-start(bf16[2,32,2,512]{3,1,2,0:T(8,128)(2,1)S(1)} %fusion.73), channel_id=1, source_target_pairs={{0,1},{1,0},{2,3},{3,2},{4,5},{5,4},{6,7},{7,6},{8,9},{9,8},{10,11... | collective-permute-start | bytes 393224 | tf_op jit(solution)/shard_map/ppermute | solution.py:29
  151.8 5.2 %collective-permute-start.19 = (bf16[32,2,512]{2,0,1:T(8,128)(2,1)S(1)}, bf16[32,2,512]{2,0,1:T(8,128)(2,1)S(1)}, u32[]{:S(2)}, u32[]{:S(2)}) collective-permute-start(bf16[32,2,512]{2,0,1:T(8,128)(2,1)S(1)} %fusion.75), channel_id=1, source_target_pairs={{0,2},{1,3},{2,0},{3,1},{4,6},{5,7},{6,4},{7,5},{8,10},{9,11},{10,... | collective-permute-start | bytes 196616 | tf_op jit(solution)/shard_map/ppermute | solution.py:29
  (6 other events, 18.2 us)

commit v19 on v18

--- a/solution.py
+++ b/solution.py
@@ -139,9 +139,16 @@
     inv_rms = lax.rsqrt(jnp.mean(local_in * local_in, axis=-1) + 1e-06)
     normed_full = local_in * inv_rms[:, None]
     normed = normed_full.astype(jnp.bfloat16)
-    projected = jnp.einsum(
-        "rd,dwh->wrh", normed, weights, preferred_element_type=jnp.float32
+    local_cot = cotangent[0]
+    grad_out = jnp.where(loss_mask[0][:, None] > 0, local_cot, jnp.zeros_like(local_cot))
+    both = jnp.einsum(
+        "rd,dwh->wrh",
+        jnp.concatenate([normed, grad_out], axis=0),
+        weights,
+        preferred_element_type=jnp.float32,
     ).astype(jnp.bfloat16)
+    projected = both[:, :rows]
+    grad_attn = both[3, rows:]
     queries = projected[0]
     key_vals = projected[1:3]
     arrived = {offset: shifted(key_vals, "tm", offset) for offset in range(1, span + 1)}
@@ -149,11 +156,6 @@
     extended = jnp.concatenate(earlier + [key_vals], axis=1)
     local_count = jnp.sum(loss_mask.astype(jnp.int32))
     tokens_all = rows * lax.axis_size("tm") * lax.axis_size("night")
-    local_cot = cotangent[0]
-    grad_out = jnp.where(loss_mask[0][:, None] > 0, local_cot, jnp.zeros_like(local_cot))
-    grad_attn = jnp.einsum(
-        "rd,dwh->wrh", grad_out, weights, preferred_element_type=jnp.float32
-    )[3].astype(jnp.bfloat16)
     base = lax.axis_index("tm") * rows
     query_idx = jnp.arange(block_rows, dtype=jnp.int32)[:, None]
     key_idx = jnp.arange(key_len, dtype=jnp.int32)[None, :]

time: 159 us -> 160 us (level)
  starting transfers between devices: 36.9 us -> 45.9 us
  matrix products: 28.8 us -> 22.5 us
  local copies, waits for them, and re-layouts: 15.9 us -> 10.4 us
  waiting for transfers between devices: 62.8 us -> 66 us
    ppermute x8, waiting for transfers between devices: 14.6 us -> 32.5 us  [shifted(): return lax.ppermute(value, axis, pairs)]
    ppermute x12, waiting for transfers between devices: 48.2 us -> 33.5 us  [halve(): lax.ppermute(send.astype(send_type), axis, pairs).astype(keep.dtype)]
    ppermute x12, starting transfers between devices: 17.5 us -> 26.3 us  [halve(): lax.ppermute(send.astype(send_type), axis, pairs).astype(keep.dtype)]
    dot_general x2 -> x1, matrix products: 8.78 us -> 4.85 us  [shards(): jnp.einsum('rd,dwh->wrh', jnp.concatenate([normed, grad_out], axis=0), we...]
    slice x2 -> x1, local copies, waits for them, and re-layouts: 2.66 us -> 0.17 us  [shards(): extended[1].reshape(key_len, HEADS, HSIZE)]
    slice x4 -> x0, local copies, waits for them, and re-layouts: 2.44 us -> none  [the longest x1 1.6 us: shards(): extended[0].reshape(key_len, HEADS, HSIZE)]
    dot_general x1, other arithmetic: 2.33 us -> 0.15 us  [shards(): jnp.einsum('rd,wgcr->dwgc', normed, grad_proj[1:3], preferred_element_typ...]
    unnamed x24 -> x18, local copies, waits for them, and re-layouts: 7.02 us -> 5.42 us
  transfers between devices with their start and end apart: 20 -> 20, of which waited for: 14 -> 10; matrix products, arithmetic and copies ran while one was open for 14% -> 9% of each run, Pallas kernels for 0% -> 0%
where the time goes in v19:
time: 160 us; the launch traced here: 159 us
  waiting for transfers between devices  66 us (41%)
  starting transfers between devices  45.9 us (29%)
  matrix products  22.5 us (14%)
  other arithmetic  11.7 us (7%)
  local copies, waits for them, and re-layouts  10.4 us (6%)
  between operations  2.71 us (2%)
    ppermute x12, waiting for transfers between devices, halve(): lax.ppermute(send.astype(send_type), axis, pairs).astype(keep.dtype)  33.5 us
    ppermute x8, waiting for transfers between devices, shifted(): return lax.ppermute(value, axis, pairs)  32.5 us
    ppermute x12, starting transfers between devices, halve(): lax.ppermute(send.astype(send_type), axis, pairs).astype(keep.dtype)  26.3 us
    ppermute x8, starting transfers between devices, shifted(): return lax.ppermute(value, axis, pairs)  19.6 us
    unnamed x18, local copies, waits for them, and re-layouts  5.42 us
    dot_general x1, matrix products, shards(): jnp.einsum('rd,dwh->wrh', jnp.concatenate([normed, grad_out], axis=0), we...  4.85 us
    dot_general x1, matrix products, band_block(): jnp.einsum('qgc,kgc->gqk', grad_attn, values_blk, preferred_element_type=...  3.92 us
  transfers between devices with their start and end apart: 20, of which 10 were waited for; matrix products, arithmetic and copies ran while one was open for 9% of the time, Pallas kernels for 0%

profile of v19, /device:TPU:0, one launch (start us, length us, event | category | flops | bytes accessed | tf_op | source)
XLA Modules:
  0.0 159.2 jit_solution(14757035681426344377)
XLA Ops:
  4.9 4.8 %convert_bitcast_fusion = bf16[4,512,512]{1,2,0:T(8,128)(2,1)S(1)} fusion(bf16[1024,4,512]{2,1,0:T(4,128)(2,1)} %param.7, bf16[256,1024]{1,0:T(8,128)(2,1)S(1)} %bitcast_select_fusion, bf16[256,1024]{1,0:T(8,128)(2,1)S(1)} %fusion.19), kind=kOutput, calls=%fused_computation.17 | convolution fusion | flops 2150629376 | bytes 7340032 | tf_op jit(solution)/shard_map/rd,dwh->wrh/dot_general | solution.py:144
  10.7 5.7 %collective-permute-start = (bf16[2,256,512]{1,2,0:T(8,128)(2,1)}, bf16[2,256,512]{1,2,0:T(8,128)(2,1)}, u32[]{:S(2)}, u32[]{:S(2)}) collective-permute-start(bf16[2,256,512]{1,2,0:T(8,128)(2,1)} %slice.122), channel_id=1, source_target_pairs={{0,16},{4,20},{8,24},{12,28},{1,17},{5,21},{9,25},{13,29},{2,18},{... | collective-permute-start | bytes 1572872 | tf_op jit(solution)/shard_map/ppermute | solution.py:16
  16.4 3.3 %collective-permute-start.1 = (bf16[2,256,512]{1,2,0:T(8,128)(2,1)}, bf16[2,256,512]{1,2,0:T(8,128)(2,1)}, u32[]{:S(2)}, u32[]{:S(2)}) collective-permute-start(bf16[2,256,512]{1,2,0:T(8,128)(2,1)} %slice.122), channel_id=1, source_target_pairs={{0,12},{4,16},{8,20},{12,24},{16,28},{1,13},{5,17},{9,21},{13,25},... | collective-permute-start | bytes 1572872 | tf_op jit(solution)/shard_map/ppermute | solution.py:16
  19.7 2.9 %collective-permute-start.2 = (bf16[2,256,512]{1,2,0:T(8,128)(2,1)}, bf16[2,256,512]{1,2,0:T(8,128)(2,1)}, u32[]{:S(2)}, u32[]{:S(2)}) collective-permute-start(bf16[2,256,512]{1,2,0:T(8,128)(2,1)} %slice.122), channel_id=1, source_target_pairs={{0,8},{4,12},{8,16},{12,20},{16,24},{20,28},{1,9},{5,13},{9,17},{1... | collective-permute-start | bytes 1572872 | tf_op jit(solution)/shard_map/ppermute | solution.py:16
  22.7 2.1 %collective-permute-start.3 = (bf16[2,256,512]{1,2,0:T(8,128)(2,1)}, bf16[2,256,512]{1,2,0:T(8,128)(2,1)}, u32[]{:S(2)}, u32[]{:S(2)}) collective-permute-start(bf16[2,256,512]{1,2,0:T(8,128)(2,1)} %slice.122), channel_id=1, source_target_pairs={{0,4},{4,8},{8,12},{12,16},{16,20},{20,24},{24,28},{1,5},{5,9},{9,... | collective-permute-start | bytes 1572872 | tf_op jit(solution)/shard_map/ppermute | solution.py:16
  30.1 20.6 %collective-permute-done = bf16[2,256,512]{1,2,0:T(8,128)(2,1)} collective-permute-done((bf16[2,256,512]{1,2,0:T(8,128)(2,1)}, bf16[2,256,512]{1,2,0:T(8,128)(2,1)}, u32[]{:S(2)}, u32[]{:S(2)}) %collective-permute-start) | collective-permute-done | bytes 524320 | tf_op jit(solution)/shard_map/ppermute | solution.py:16
  56.3 2.4 %fusion.1 = (f32[8,256]{1,0:T(8,128)S(1)}, f32[8,256,1280]{2,1,0:T(8,128)S(1)}) fusion(f32[256,1280]{1,0:T(8,128)S(1)} %fusion.25, bf16[256,8,64]{0,2,1:T(8,128)(2,1)S(1)} %bitcast.183, bf16[1280,8,64]{0,2,1:T(8,128)(2,1)S(1)} %bitcast.180), kind=kOutput, calls=%fused_computation.3 | convolution fusion | flops 343406592 | bytes 13377536 | tf_op jit(solution)/shard_map/qgc,kgc->gqk/dot_general | solution.py:102
  58.7 2.3 %fusion.76 = (bf16[8,64,1280]{2,1,0:T(8,128)(2,1)S(1)}, f32[8,64,1280]{2,1,0:T(8,128)S(1)}) fusion(bf16[256,8,64]{0,2,1:T(8,128)(2,1)S(1)} %bitcast.193, f32[8,256]{1,0:T(8,128)S(1)} %get-tuple-element.34, f32[256,1280]{1,0:T(8,128)S(1)} %fusion.25, f32[8,256,1280]{2,1,0:T(8,128)S(1)} %get-tuple-element.35), kind=kOutput, calls=%fused_computation.157 | convolution fusion | flops 346685440 | bytes 15998976 | tf_op jit(solution)/shard_map/gqk,qgc->gck/dot_general | solution.py:122
  61.1 2.8 %multiply_reduce_fusion = (f32[256,8]{0,1:T(8,128)S(1)}, bf16[8,64,256]{2,1,0:T(8,128)(2,1)S(1)}) fusion(bf16[256,8,64]{0,2,1:T(8,128)(2,1)S(1)} %bitcast.194, bf16[1280,8,64]{0,2,1:T(8,128)(2,1)S(1)} %bitcast.190, f32[8,256]{1,0:T(8,128)S(1)} %get-tuple-element.34, f32[256,1280]{1,0:T(8,128)S(1)} %fusion.25, f32[8,256,1280]{2,1,0:T(8,128)S(1)} %get-tuple-element.35), kind=kOutput, calls=%fused_computation.76 | convolution fusion | flops 346683392 | bytes 13647872 | tf_op jit(solution)/shard_map/gqk,kgc->qgc/dot_general | solution.py:108
  63.8 3.9 %multiply_convert_fusion = bf16[8,256,1280]{2,1,0:T(8,128)(2,1)S(1)} fusion(bf16[256,8,64]{0,2,1:T(8,128)(2,1)S(1)} %bitcast.195, bf16[1280,8,64]{0,2,1:T(8,128)(2,1)S(1)} %bitcast.191, f32[8,256]{1,0:T(8,128)S(1)} %bitcast.197, f32[8,256]{1,0:T(8,128)S(1)} %get-tuple-element.34, f32[256,1280]{1,0:T(8,128)S(1)} %fusion.25, ...), kind=kOutput, calls=%fused_computation | convolution fusion | flops 353894400 | bytes 18628608 | tf_op jit(solution)/shard_map/qgc,kgc->gqk/dot_general | solution.py:112
  68.8 1.7 %convolution_convert_fusion = bf16[8,64,256]{2,1,0:T(8,128)(2,1)S(1)} fusion(bf16[1280,8,64]{0,2,1:T(8,128)(2,1)S(1)} %bitcast.181, bf16[8,256,1280]{2,1,0:T(8,128)(2,1)S(1)} %multiply_convert_fusion), kind=kOutput, calls=%fused_computation.38 | convolution fusion | flops 335675392 | bytes 6815744 | tf_op jit(solution)/shard_map/gqk,kgc->gcq/dot_general | solution.py:118
  78.5 11.7 %collective-permute-done.12 = bf16[2,8,64,256]{3,2,1,0:T(8,128)(2,1)S(1)} collective-permute-done((bf16[2,8,64,256]{3,2,1,0:T(8,128)(2,1)S(1)}, bf16[2,8,64,256]{3,2,1,0:T(8,128)(2,1)S(1)}, u32[]{:S(2)}, u32[]{:S(2)}) %collective-permute-start.12) | collective-permute-done | bytes 524320 | tf_op jit(solution)/shard_map/ppermute | solution.py:16
  91.8 9.1 %collective-permute-start.13 = (bf16[2,2,2,2,32,2,512]{6,4,5,3,2,1,0:T(8,128)(2,1)S(1)}, bf16[2,2,2,2,32,2,512]{6,4,5,3,2,1,0:T(8,128)(2,1)S(1)}, u32[]{:S(2)}, u32[]{:S(2)}) collective-permute-start(bf16[2,2,2,2,32,2,512]{6,4,5,3,2,1,0:T(8,128)(2,1)S(1)} %fusion.36), channel_id=1, source_target_pairs={{0,4},{4,0},{8,12},{12,8},{16,20},{20,16},{24,28},{28,24},{1,5},{5... | collective-permute-start | bytes 3145736 | tf_op jit(solution)/shard_map/ppermute | solution.py:29
  101.3 1.8 %fusion.29 = (f32[256]{0:T(256)S(1)}, f32[256,1024]{1,0:T(8,128)S(1)}) fusion(bf16[1,256,1024]{2,1,0:T(8,128)(2,1)S(1)} %copy-done, f32[256]{0:T(256)S(1)} %add_rsqrt_fusion, bf16[4,256,512]{1,2,0:T(8,128)(2,1)S(1)} %bitcast.192, bf16[1024,4,512]{2,1,0:T(4,128)(2,1)S(1)} %copy-done.5), kind=kOutput, calls=%fused_computation.39 | convolution fusion | flops 1074790144 | bytes 6817792 | tf_op jit(solution)/shard_map/wrh,dwh->rd/dot_general | solution.py:211
  103.7 6.0 %collective-permute-start.14 = (bf16[2,2,2,32,2,256]{5,3,4,2,1,0:T(8,128)(2,1)S(1)}, bf16[2,2,2,32,2,256]{5,3,4,2,1,0:T(8,128)(2,1)S(1)}, u32[]{:S(2)}, u32[]{:S(2)}) collective-permute-start(bf16[2,2,2,32,2,256]{5,3,4,2,1,0:T(8,128)(2,1)S(1)} %fusion.47), channel_id=1, source_target_pairs={{0,16},{4,20},{8,24},{12,28},{16,0},{20,4},{24,8},{28,12},{1,17},{... | collective-permute-start | bytes 786440 | tf_op jit(solution)/shard_map/ppermute | solution.py:29
  110.2 1.6 %collective-permute-start.5 = (bf16[2,2,2,40,2,512]{5,3,4,1,0,2:T(8,128)(2,1)S(1)}, bf16[2,2,2,40,2,512]{5,3,4,1,0,2:T(8,128)(2,1)S(1)}, u32[]{:S(2)}, u32[]{:S(2)}) collective-permute-start(bf16[2,2,2,40,2,512]{5,3,4,1,0,2:T(8,128)(2,1)S(1)} %fusion.43), channel_id=1, source_target_pairs={{0,1},{1,0},{2,3},{3,2},{4,5},{5,4},{6,7},{7,6},{8,9},{9,8},{10,11... | collective-permute-start | bytes 1966088 | tf_op jit(solution)/shard_map/ppermute | solution.py:29
  113.3 2.6 %collective-permute-done.14 = bf16[2,2,2,32,2,256]{5,3,4,2,1,0:T(8,128)(2,1)S(1)} collective-permute-done((bf16[2,2,2,32,2,256]{5,3,4,2,1,0:T(8,128)(2,1)S(1)}, bf16[2,2,2,32,2,256]{5,3,4,2,1,0:T(8,128)(2,1)S(1)}, u32[]{:S(2)}, u32[]{:S(2)}) %collective-permute-start.14) | collective-permute-done | bytes 262176 | tf_op jit(solution)/shard_map/ppermute | solution.py:29
  116.0 2.3 %collective-permute-start.15 = (bf16[2,2,32,2,256]{4,2,3,1,0:T(8,128)(2,1)S(1)}, bf16[2,2,32,2,256]{4,2,3,1,0:T(8,128)(2,1)S(1)}, u32[]{:S(2)}, u32[]{:S(2)}) collective-permute-start(bf16[2,2,32,2,256]{4,2,3,1,0:T(8,128)(2,1)S(1)} %fusion.55), channel_id=1, source_target_pairs={{0,8},{4,12},{8,0},{12,4},{16,24},{20,28},{24,16},{28,20},{1,9},{5... | collective-permute-start | bytes 393224 | tf_op jit(solution)/shard_map/ppermute | solution.py:29
  118.3 2.7 %collective-permute-done.16 = bf16[2,2,2,32,2,256]{5,3,4,2,1,0:T(8,128)(2,1)S(1)} collective-permute-done((bf16[2,2,2,32,2,256]{5,3,4,2,1,0:T(8,128)(2,1)S(1)}, bf16[2,2,2,32,2,256]{5,3,4,2,1,0:T(8,128)(2,1)S(1)}, u32[]{:S(2)}, u32[]{:S(2)}) %collective-permute-start.16) | collective-permute-done | bytes 262176 | tf_op jit(solution)/shard_map/ppermute | solution.py:29
  121.8 5.8 %collective-permute-done.5 = bf16[2,2,2,40,2,512]{5,3,4,1,0,2:T(8,128)(2,1)S(1)} collective-permute-done((bf16[2,2,2,40,2,512]{5,3,4,1,0,2:T(8,128)(2,1)S(1)}, bf16[2,2,2,40,2,512]{5,3,4,1,0,2:T(8,128)(2,1)S(1)}, u32[]{:S(2)}, u32[]{:S(2)}) %collective-permute-start.5) | collective-permute-done | bytes 655392 | tf_op jit(solution)/shard_map/ppermute | solution.py:29
  127.8 2.7 %collective-permute-start.6 = (bf16[2,2,40,2,512]{4,2,3,1,0:T(8,128)(2,1)S(1)}, bf16[2,2,40,2,512]{4,2,3,1,0:T(8,128)(2,1)S(1)}, u32[]{:S(2)}, u32[]{:S(2)}) collective-permute-start(bf16[2,2,40,2,512]{4,2,3,1,0:T(8,128)(2,1)S(1)} %fusion.46), channel_id=1, source_target_pairs={{0,2},{1,3},{2,0},{3,1},{4,6},{5,7},{6,4},{7,5},{8,10},{9,11},{10,... | collective-permute-start | bytes 983048 | tf_op jit(solution)/shard_map/ppermute | solution.py:29
  132.2 13.3 %collective-permute-done.6 = bf16[2,2,40,2,512]{4,2,3,1,0:T(8,128)(2,1)S(1)} collective-permute-done((bf16[2,2,40,2,512]{4,2,3,1,0:T(8,128)(2,1)S(1)}, bf16[2,2,40,2,512]{4,2,3,1,0:T(8,128)(2,1)S(1)}, u32[]{:S(2)}, u32[]{:S(2)}) %collective-permute-start.6) | collective-permute-done | bytes 327712 | tf_op jit(solution)/shard_map/ppermute | solution.py:29
  146.5 4.7 %collective-permute-done.7 = bf16[2,40,2,512]{3,1,2,0:T(8,128)(2,1)S(1)} collective-permute-done((bf16[2,40,2,512]{3,1,2,0:T(8,128)(2,1)S(1)}, bf16[2,40,2,512]{3,1,2,0:T(8,128)(2,1)S(1)}, u32[]{:S(2)}, u32[]{:S(2)}) %collective-permute-start.7) | collective-permute-done | bytes 163872 | tf_op jit(solution)/shard_map/ppermute | solution.py:29
  152.7 3.1 %collective-permute-done.8 = bf16[40,2,512]{2,0,1:T(8,128)(2,1)S(1)} collective-permute-done((bf16[40,2,512]{2,0,1:T(8,128)(2,1)S(1)}, bf16[40,2,512]{2,0,1:T(8,128)(2,1)S(1)}, u32[]{:S(2)}, u32[]{:S(2)}) %collective-permute-start.8) | collective-permute-done | bytes 81952 | tf_op jit(solution)/shard_map/ppermute | solution.py:29
  (105 shorter events, 36.5 us)
Async XLA Ops:
  4.9 19.9 %copy-start.1 = (bf16[1,256,1024]{2,1,0:T(8,128)(2,1)S(1)}, bf16[1,256,1024]{2,1,0:T(8,128)(2,1)}, u32[]{:S(2)}) copy-start(bf16[1,256,1024]{2,1,0:T(8,128)(2,1)} %param.8) | copy-start | bytes 1572868
  4.9 20.1 %copy-start = (bf16[1,256,1024]{2,1,0:T(8,128)(2,1)S(1)}, bf16[1,256,1024]{2,1,0:T(8,128)(2,1)}, u32[]{:S(2)}) copy-start(bf16[1,256,1024]{2,1,0:T(8,128)(2,1)} %param.6) | copy-start | bytes 1572868
  9.8 15.0 %copy-start.3 = (bf16[4,512,512]{1,2,0:T(8,128)(2,1)}, bf16[4,512,512]{1,2,0:T(8,128)(2,1)S(1)}, u32[]{:S(2)}) copy-start(bf16[4,512,512]{1,2,0:T(8,128)(2,1)S(1)} %convert_bitcast_fusion) | copy-start | bytes 6291460
  10.7 40.0 %collective-permute-start = (bf16[2,256,512]{1,2,0:T(8,128)(2,1)}, bf16[2,256,512]{1,2,0:T(8,128)(2,1)}, u32[]{:S(2)}, u32[]{:S(2)}) collective-permute-start(bf16[2,256,512]{1,2,0:T(8,128)(2,1)} %slice.122), channel_id=1, source_target_pairs={{0,16},{4,20},{8,24},{12,28},{1,17},{5,21},{9,25},{13,29},{2,18},{... | collective-permute-start | bytes 1572872 | tf_op jit(solution)/shard_map/ppermute | solution.py:16
  16.4 35.4 %collective-permute-start.1 = (bf16[2,256,512]{1,2,0:T(8,128)(2,1)}, bf16[2,256,512]{1,2,0:T(8,128)(2,1)}, u32[]{:S(2)}, u32[]{:S(2)}) collective-permute-start(bf16[2,256,512]{1,2,0:T(8,128)(2,1)} %slice.122), channel_id=1, source_target_pairs={{0,12},{4,16},{8,20},{12,24},{16,28},{1,13},{5,17},{9,21},{13,25},... | collective-permute-start | bytes 1572872 | tf_op jit(solution)/shard_map/ppermute | solution.py:16
  19.7 33.1 %collective-permute-start.2 = (bf16[2,256,512]{1,2,0:T(8,128)(2,1)}, bf16[2,256,512]{1,2,0:T(8,128)(2,1)}, u32[]{:S(2)}, u32[]{:S(2)}) collective-permute-start(bf16[2,256,512]{1,2,0:T(8,128)(2,1)} %slice.122), channel_id=1, source_target_pairs={{0,8},{4,12},{8,16},{12,20},{16,24},{20,28},{1,9},{5,13},{9,17},{1... | collective-permute-start | bytes 1572872 | tf_op jit(solution)/shard_map/ppermute | solution.py:16
  22.7 31.3 %collective-permute-start.3 = (bf16[2,256,512]{1,2,0:T(8,128)(2,1)}, bf16[2,256,512]{1,2,0:T(8,128)(2,1)}, u32[]{:S(2)}, u32[]{:S(2)}) collective-permute-start(bf16[2,256,512]{1,2,0:T(8,128)(2,1)} %slice.122), channel_id=1, source_target_pairs={{0,4},{4,8},{8,12},{12,16},{16,20},{20,24},{24,28},{1,5},{5,9},{9,... | collective-permute-start | bytes 1572872 | tf_op jit(solution)/shard_map/ppermute | solution.py:16
  70.8 19.4 %collective-permute-start.12 = (bf16[2,8,64,256]{3,2,1,0:T(8,128)(2,1)S(1)}, bf16[2,8,64,256]{3,2,1,0:T(8,128)(2,1)S(1)}, u32[]{:S(2)}, u32[]{:S(2)}) collective-permute-start(bf16[2,8,64,256]{3,2,1,0:T(8,128)(2,1)S(1)} %pad_maximum_fusion.4), channel_id=1, source_target_pairs={{16,0},{20,4},{24,8},{28,12},{17,1},{21,5},{25,9},{29,13},{18,2},{... | collective-permute-start | bytes 1572872 | tf_op jit(solution)/shard_map/ppermute | solution.py:16
  72.3 17.9 %collective-permute-start.11 = (bf16[2,8,64,256]{3,2,1,0:T(8,128)(2,1)S(1)}, bf16[2,8,64,256]{3,2,1,0:T(8,128)(2,1)S(1)}, u32[]{:S(2)}, u32[]{:S(2)}) collective-permute-start(bf16[2,8,64,256]{3,2,1,0:T(8,128)(2,1)S(1)} %pad_maximum_fusion.3), channel_id=1, source_target_pairs={{12,0},{16,4},{20,8},{24,12},{28,16},{13,1},{17,5},{21,9},{25,13},... | collective-permute-start | bytes 1572872 | tf_op jit(solution)/shard_map/ppermute | solution.py:16
  73.6 16.8 %collective-permute-start.10 = (bf16[2,8,64,256]{3,2,1,0:T(8,128)(2,1)S(1)}, bf16[2,8,64,256]{3,2,1,0:T(8,128)(2,1)S(1)}, u32[]{:S(2)}, u32[]{:S(2)}) collective-permute-start(bf16[2,8,64,256]{3,2,1,0:T(8,128)(2,1)S(1)} %pad_maximum_fusion.2), channel_id=1, source_target_pairs={{8,0},{12,4},{16,8},{20,12},{24,16},{28,20},{9,1},{13,5},{17,9},{2... | collective-permute-start | bytes 1572872 | tf_op jit(solution)/shard_map/ppermute | solution.py:16
  75.0 15.4 %collective-permute-start.9 = (bf16[2,8,64,256]{3,2,1,0:T(8,128)(2,1)S(1)}, bf16[2,8,64,256]{3,2,1,0:T(8,128)(2,1)S(1)}, u32[]{:S(2)}, u32[]{:S(2)}) collective-permute-start(bf16[2,8,64,256]{3,2,1,0:T(8,128)(2,1)S(1)} %pad_maximum_fusion.1), channel_id=1, source_target_pairs={{4,0},{8,4},{12,8},{16,12},{20,16},{24,20},{28,24},{5,1},{9,5},{13... | collective-permute-start | bytes 1572872 | tf_op jit(solution)/shard_map/ppermute | solution.py:16
  91.7 9.6 %copy-start.5 = (bf16[1024,4,512]{2,1,0:T(4,128)(2,1)S(1)}, bf16[1024,4,512]{2,1,0:T(4,128)(2,1)}, u32[]{:S(2)}) copy-start(bf16[1024,4,512]{2,1,0:T(4,128)(2,1)} %param.7) | copy-start | bytes 12582916
  91.8 11.4 %collective-permute-start.13 = (bf16[2,2,2,2,32,2,512]{6,4,5,3,2,1,0:T(8,128)(2,1)S(1)}, bf16[2,2,2,2,32,2,512]{6,4,5,3,2,1,0:T(8,128)(2,1)S(1)}, u32[]{:S(2)}, u32[]{:S(2)}) collective-permute-start(bf16[2,2,2,2,32,2,512]{6,4,5,3,2,1,0:T(8,128)(2,1)S(1)} %fusion.36), channel_id=1, source_target_pairs={{0,4},{4,0},{8,12},{12,8},{16,20},{20,16},{24,28},{28,24},{1,5},{5... | collective-permute-start | bytes 3145736 | tf_op jit(solution)/shard_map/ppermute | solution.py:29
  101.1 8.6 %collective-permute-start.4 = (bf16[2,2,2,2,40,2,512]{6,4,5,1,0,2,3:T(8,128)(2,1)S(1)}, bf16[2,2,2,2,40,2,512]{6,4,5,1,0,2,3:T(8,128)(2,1)S(1)}, u32[]{:S(2)}, u32[]{:S(2)}) collective-permute-start(bf16[2,2,2,2,40,2,512]{6,4,5,1,0,2,3:T(8,128)(2,1)S(1)} %fusion.20), channel_id=1, source_target_pairs={{0,4},{4,0},{8,12},{12,8},{16,20},{20,16},{24,28},{28,24},{1,5},{5... | collective-permute-start | bytes 3932168 | tf_op jit(solution)/shard_map/ppermute | solution.py:29
  103.7 12.2 %collective-permute-start.14 = (bf16[2,2,2,32,2,256]{5,3,4,2,1,0:T(8,128)(2,1)S(1)}, bf16[2,2,2,32,2,256]{5,3,4,2,1,0:T(8,128)(2,1)S(1)}, u32[]{:S(2)}, u32[]{:S(2)}) collective-permute-start(bf16[2,2,2,32,2,256]{5,3,4,2,1,0:T(8,128)(2,1)S(1)} %fusion.47), channel_id=1, source_target_pairs={{0,16},{4,20},{8,24},{12,28},{16,0},{20,4},{24,8},{28,12},{1,17},{... | collective-permute-start | bytes 786440 | tf_op jit(solution)/shard_map/ppermute | solution.py:29
  110.2 17.3 %collective-permute-start.5 = (bf16[2,2,2,40,2,512]{5,3,4,1,0,2:T(8,128)(2,1)S(1)}, bf16[2,2,2,40,2,512]{5,3,4,1,0,2:T(8,128)(2,1)S(1)}, u32[]{:S(2)}, u32[]{:S(2)}) collective-permute-start(bf16[2,2,2,40,2,512]{5,3,4,1,0,2:T(8,128)(2,1)S(1)} %fusion.43), channel_id=1, source_target_pairs={{0,1},{1,0},{2,3},{3,2},{4,5},{5,4},{6,7},{7,6},{8,9},{9,8},{10,11... | collective-permute-start | bytes 1966088 | tf_op jit(solution)/shard_map/ppermute | solution.py:29
  111.9 9.1 %collective-permute-start.16 = (bf16[2,2,2,32,2,256]{5,3,4,2,1,0:T(8,128)(2,1)S(1)}, bf16[2,2,2,32,2,256]{5,3,4,2,1,0:T(8,128)(2,1)S(1)}, u32[]{:S(2)}, u32[]{:S(2)}) collective-permute-start(bf16[2,2,2,32,2,256]{5,3,4,2,1,0:T(8,128)(2,1)S(1)} %fusion.48), channel_id=1, source_target_pairs={{0,8},{4,12},{8,0},{12,4},{16,24},{20,28},{24,16},{28,20},{1,9},{5... | collective-permute-start | bytes 786440 | tf_op jit(solution)/shard_map/ppermute | solution.py:29
  116.0 14.5 %collective-permute-start.15 = (bf16[2,2,32,2,256]{4,2,3,1,0:T(8,128)(2,1)S(1)}, bf16[2,2,32,2,256]{4,2,3,1,0:T(8,128)(2,1)S(1)}, u32[]{:S(2)}, u32[]{:S(2)}) collective-permute-start(bf16[2,2,32,2,256]{4,2,3,1,0:T(8,128)(2,1)S(1)} %fusion.55), channel_id=1, source_target_pairs={{0,8},{4,12},{8,0},{12,4},{16,24},{20,28},{24,16},{28,20},{1,9},{5... | collective-permute-start | bytes 393224 | tf_op jit(solution)/shard_map/ppermute | solution.py:29
  121.1 9.4 %collective-permute-start.17 = (bf16[2,2,32,2,256]{4,2,3,1,0:T(8,128)(2,1)S(1)}, bf16[2,2,32,2,256]{4,2,3,1,0:T(8,128)(2,1)S(1)}, u32[]{:S(2)}, u32[]{:S(2)}) collective-permute-start(bf16[2,2,32,2,256]{4,2,3,1,0:T(8,128)(2,1)S(1)} %fusion.56), channel_id=1, source_target_pairs={{0,16},{4,20},{8,24},{12,28},{16,0},{20,4},{24,8},{28,12},{1,17},{... | collective-permute-start | bytes 393224 | tf_op jit(solution)/shard_map/ppermute | solution.py:29
  127.8 17.8 %collective-permute-start.6 = (bf16[2,2,40,2,512]{4,2,3,1,0:T(8,128)(2,1)S(1)}, bf16[2,2,40,2,512]{4,2,3,1,0:T(8,128)(2,1)S(1)}, u32[]{:S(2)}, u32[]{:S(2)}) collective-permute-start(bf16[2,2,40,2,512]{4,2,3,1,0:T(8,128)(2,1)S(1)} %fusion.46), channel_id=1, source_target_pairs={{0,2},{1,3},{2,0},{3,1},{4,6},{5,7},{6,4},{7,5},{8,10},{9,11},{10,... | collective-permute-start | bytes 983048 | tf_op jit(solution)/shard_map/ppermute | solution.py:29
  130.6 15.8 %collective-permute-start.18 = (bf16[2,32,2,512]{3,1,2,0:T(8,128)(2,1)S(1)}, bf16[2,32,2,512]{3,1,2,0:T(8,128)(2,1)S(1)}, u32[]{:S(2)}, u32[]{:S(2)}) collective-permute-start(bf16[2,32,2,512]{3,1,2,0:T(8,128)(2,1)S(1)} %fusion.57), channel_id=1, source_target_pairs={{0,1},{1,0},{2,3},{3,2},{4,5},{5,4},{6,7},{7,6},{8,9},{9,8},{10,11... | collective-permute-start | bytes 393224 | tf_op jit(solution)/shard_map/ppermute | solution.py:29
  145.7 5.5 %collective-permute-start.7 = (bf16[2,40,2,512]{3,1,2,0:T(8,128)(2,1)S(1)}, bf16[2,40,2,512]{3,1,2,0:T(8,128)(2,1)S(1)}, u32[]{:S(2)}, u32[]{:S(2)}) collective-permute-start(bf16[2,40,2,512]{3,1,2,0:T(8,128)(2,1)S(1)} %fusion.54), channel_id=1, source_target_pairs={{0,16},{4,20},{8,24},{12,28},{16,0},{20,4},{24,8},{28,12},{1,17},{... | collective-permute-start | bytes 491528 | tf_op jit(solution)/shard_map/ppermute | solution.py:29
  146.4 6.3 %collective-permute-start.19 = (bf16[32,2,512]{2,0,1:T(8,128)(2,1)S(1)}, bf16[32,2,512]{2,0,1:T(8,128)(2,1)S(1)}, u32[]{:S(2)}, u32[]{:S(2)}) collective-permute-start(bf16[32,2,512]{2,0,1:T(8,128)(2,1)S(1)} %fusion.59), channel_id=1, source_target_pairs={{0,2},{1,3},{2,0},{3,1},{4,6},{5,7},{6,4},{7,5},{8,10},{9,11},{10,... | collective-permute-start | bytes 196616 | tf_op jit(solution)/shard_map/ppermute | solution.py:29
  151.3 4.5 %collective-permute-start.8 = (bf16[40,2,512]{2,0,1:T(8,128)(2,1)S(1)}, bf16[40,2,512]{2,0,1:T(8,128)(2,1)S(1)}, u32[]{:S(2)}, u32[]{:S(2)}) collective-permute-start(bf16[40,2,512]{2,0,1:T(8,128)(2,1)S(1)} %fusion.58), channel_id=1, source_target_pairs={{0,8},{4,12},{8,0},{12,4},{16,24},{20,28},{24,16},{28,20},{1,9},{5... | collective-permute-start | bytes 245768 | tf_op jit(solution)/shard_map/ppermute | solution.py:29
  (2 other events, 7.3 us)

commit v20 on v18

--- a/solution.py
+++ b/solution.py
@@ -214,7 +214,9 @@
     key_value_part = jnp.einsum(
         "rd,wgcr->dwgc", normed, grad_proj[1:3], preferred_element_type=jnp.float32
     ).reshape(width, 2, inner)
-    late, _ = scatter_rows(key_value_part, None, ("tm", "night"), "tm", jnp.bfloat16)
+    late, _ = scatter_rows(
+        key_value_part, None, ("tm", "night"), "tm", jnp.bfloat16, tail_first=True
+    )
     summed = jnp.concatenate([early[:, :1], late, early[:, 1:]], axis=1)
     total_count = count.astype(jnp.float32)
     loss_scale = jnp.float32(tokens_all) / total_count

time: 159 us -> 172 us (1.082)
  waiting for transfers between devices: 62.8 us -> 74.6 us
  starting transfers between devices: 36.9 us -> 39 us
    ppermute x12, waiting for transfers between devices: 48.2 us -> 60 us  [halve(): lax.ppermute(send.astype(send_type), axis, pairs).astype(keep.dtype)]
    ppermute x12, starting transfers between devices: 17.5 us -> 19.6 us  [halve(): lax.ppermute(send.astype(send_type), axis, pairs).astype(keep.dtype)]
  transfers between devices with their start and end apart: 20 -> 20, of which waited for: 14 -> 13; matrix products, arithmetic and copies ran while one was open for 14% -> 13% of each run, Pallas kernels for 0% -> 0%
where the time goes in v20:
time: 172 us
  waiting for transfers between devices  74.6 us (43%)
  starting transfers between devices  39 us (23%)
  matrix products  28.8 us (17%)
  local copies, waits for them, and re-layouts  15.7 us (9%)
  other arithmetic  10.9 us (6%)
  between operations  2.68 us (2%)
    ppermute x12, waiting for transfers between devices, halve(): lax.ppermute(send.astype(send_type), axis, pairs).astype(keep.dtype)  60 us
    ppermute x12, starting transfers between devices, halve(): lax.ppermute(send.astype(send_type), axis, pairs).astype(keep.dtype)  19.6 us
    ppermute x8, starting transfers between devices, shifted(): return lax.ppermute(value, axis, pairs)  19.4 us
    ppermute x8, waiting for transfers between devices, shifted(): return lax.ppermute(value, axis, pairs)  14.5 us
    unnamed x24, local copies, waits for them, and re-layouts  7.03 us
    dot_general x1, matrix products, shards(): jnp.einsum('rd,dwh->wrh', grad_out, weights, preferred_element_type=jnp.f...  4.81 us
    dot_general x1, matrix products, shards(): jnp.einsum('rd,dwh->wrh', normed, weights, preferred_element_type=jnp.flo...  3.98 us
    dot_general x1, matrix products, band_block(): jnp.einsum('qgc,kgc->gqk', grad_attn, values_blk, preferred_element_type=...  3.92 us
  transfers between devices with their start and end apart: 20, of which 13 were waited for; matrix products, arithmetic and copies ran while one was open for 13% of the time, Pallas kernels for 0%

profile of v20, /device:TPU:0, one launch (start us, length us, event | category | flops | bytes accessed | tf_op | source)
XLA Modules:
  0.0 171.7 jit_solution(1433854926130442171)
XLA Ops:
  1.9 4.0 %fusion.21 = bf16[4,256,512]{2,1,0:T(8,128)(2,1)S(1)} fusion(bf16[1024,4,512]{2,1,0:T(4,128)(2,1)} %param.7, bf16[1,256,1024]{2,1,0:T(8,128)(2,1)} %param.6, f32[256]{0:T(256)S(1)} %add_rsqrt_fusion), kind=kOutput, calls=%fused_computation.24 | convolution fusion | flops 1075052544 | bytes 5768192 | tf_op jit(solution)/shard_map/rd,dwh->wrh/dot_general | solution.py:142
  6.7 5.7 %collective-permute-start = (bf16[2,256,512]{2,1,0:T(8,128)(2,1)}, bf16[2,256,512]{2,1,0:T(8,128)(2,1)}, u32[]{:S(2)}, u32[]{:S(2)}) collective-permute-start(bf16[2,256,512]{2,1,0:T(8,128)(2,1)} %slice.120), channel_id=1, source_target_pairs={{0,16},{4,20},{8,24},{12,28},{1,17},{5,21},{9,25},{13,29},{2,18},{... | collective-permute-start | bytes 1572872 | tf_op jit(solution)/shard_map/ppermute | solution.py:16
  12.4 3.4 %collective-permute-start.1 = (bf16[2,256,512]{2,1,0:T(8,128)(2,1)}, bf16[2,256,512]{2,1,0:T(8,128)(2,1)}, u32[]{:S(2)}, u32[]{:S(2)}) collective-permute-start(bf16[2,256,512]{2,1,0:T(8,128)(2,1)} %slice.120), channel_id=1, source_target_pairs={{0,12},{4,16},{8,20},{12,24},{16,28},{1,13},{5,17},{9,21},{13,25},... | collective-permute-start | bytes 1572872 | tf_op jit(solution)/shard_map/ppermute | solution.py:16
  15.7 2.9 %collective-permute-start.2 = (bf16[2,256,512]{2,1,0:T(8,128)(2,1)}, bf16[2,256,512]{2,1,0:T(8,128)(2,1)}, u32[]{:S(2)}, u32[]{:S(2)}) collective-permute-start(bf16[2,256,512]{2,1,0:T(8,128)(2,1)} %slice.120), channel_id=1, source_target_pairs={{0,8},{4,12},{8,16},{12,20},{16,24},{20,28},{1,9},{5,13},{9,17},{1... | collective-permute-start | bytes 1572872 | tf_op jit(solution)/shard_map/ppermute | solution.py:16
  18.7 2.1 %collective-permute-start.3 = (bf16[2,256,512]{2,1,0:T(8,128)(2,1)}, bf16[2,256,512]{2,1,0:T(8,128)(2,1)}, u32[]{:S(2)}, u32[]{:S(2)}) collective-permute-start(bf16[2,256,512]{2,1,0:T(8,128)(2,1)} %slice.120), channel_id=1, source_target_pairs={{0,4},{4,8},{8,12},{12,16},{16,20},{20,24},{24,28},{1,5},{5,9},{9,... | collective-permute-start | bytes 1572872 | tf_op jit(solution)/shard_map/ppermute | solution.py:16
  22.0 4.8 %fusion.18 = bf16[4,256,512]{2,1,0:T(8,128)(2,1)} fusion(bf16[1024,4,512]{2,1,0:T(4,128)(2,1)} %param.7, bf16[1,256,1024]{2,1,0:T(8,128)(2,1)S(1)} %copy-done.5, pred[256]{0:T(512)(128)(4,1)S(1)} %compare_reduce_fusion), kind=kOutput, calls=%fused_computation.23 | convolution fusion | flops 1074528256 | bytes 5767424 | tf_op jit(solution)/shard_map/rd,dwh->wrh/dot_general | solution.py:154
  33.3 13.4 %collective-permute-done = bf16[2,256,512]{2,1,0:T(8,128)(2,1)} collective-permute-done((bf16[2,256,512]{2,1,0:T(8,128)(2,1)}, bf16[2,256,512]{2,1,0:T(8,128)(2,1)}, u32[]{:S(2)}, u32[]{:S(2)}) %collective-permute-start) | collective-permute-done | bytes 524320 | tf_op jit(solution)/shard_map/ppermute | solution.py:16
  55.3 3.9 %fusion.1 = (f32[8,256]{1,0:T(8,128)S(1)}, f32[8,256,1280]{2,1,0:T(8,128)S(1)}) fusion(f32[256,1280]{1,0:T(8,128)} %fusion.37, bf16[256,8,64]{0,2,1:T(8,128)(2,1)S(1)} %bitcast.192, bf16[1280,8,64]{0,2,1:T(8,128)(2,1)S(1)} %bitcast.189), kind=kOutput, calls=%fused_computation.3 | convolution fusion | flops 343406592 | bytes 13377536 | tf_op jit(solution)/shard_map/qgc,kgc->gqk/dot_general | solution.py:102
  59.3 2.8 %multiply_reduce_fusion = (f32[256,8]{0,1:T(8,128)S(1)}, bf16[8,64,256]{2,1,0:T(8,128)(2,1)S(1)}) fusion(bf16[256,8,64]{0,2,1:T(8,128)(2,1)S(1)} %bitcast.202, bf16[1280,8,64]{0,2,1:T(8,128)(2,1)S(1)} %bitcast.199, f32[8,256]{1,0:T(8,128)S(1)} %get-tuple-element.34, f32[256,1280]{1,0:T(8,128)S(1)} %copy-done, f32[8,256,1280]{2,1,0:T(8,128)S(1)} %get-tuple-element.35), kind=kOutput, calls=%fused_computation.77 | convolution fusion | flops 346683392 | bytes 13647872 | tf_op jit(solution)/shard_map/gqk,kgc->qgc/dot_general | solution.py:108
  62.1 3.9 %multiply_convert_fusion = bf16[8,256,1280]{2,1,0:T(8,128)(2,1)S(1)} fusion(bf16[256,8,64]{0,2,1:T(8,128)(2,1)S(1)} %bitcast.203, bf16[1280,8,64]{0,2,1:T(8,128)(2,1)S(1)} %bitcast.200, f32[8,256]{1,0:T(8,128)S(1)} %bitcast.206, f32[8,256]{1,0:T(8,128)S(1)} %get-tuple-element.34, f32[256,1280]{1,0:T(8,128)S(1)} %copy-done, ...), kind=kOutput, calls=%fused_computation | convolution fusion | flops 353894400 | bytes 18628608 | tf_op jit(solution)/shard_map/qgc,kgc->gqk/dot_general | solution.py:112
  71.3 3.6 %collective-permute-start.4 = (bf16[2,2,2,2,40,2,512]{6,4,5,1,0,2,3:T(8,128)(2,1)S(1)}, bf16[2,2,2,2,40,2,512]{6,4,5,1,0,2,3:T(8,128)(2,1)S(1)}, u32[]{:S(2)}, u32[]{:S(2)}) collective-permute-start(bf16[2,2,2,2,40,2,512]{6,4,5,1,0,2,3:T(8,128)(2,1)S(1)} %fusion.32), channel_id=1, source_target_pairs={{0,4},{4,0},{8,12},{12,8},{16,20},{20,16},{24,28},{28,24},{1,5},{5... | collective-permute-start | bytes 3932168 | tf_op jit(solution)/shard_map/ppermute | solution.py:29
  74.9 2.3 %fusion.86 = (bf16[8,64,1280]{2,1,0:T(8,128)(2,1)S(1)}, f32[8,64,1280]{2,1,0:T(8,128)S(1)}) fusion(bf16[256,8,64]{0,2,1:T(8,128)(2,1)S(1)} %bitcast.204, f32[8,256]{1,0:T(8,128)S(1)} %get-tuple-element.34, f32[256,1280]{1,0:T(8,128)S(1)} %copy-done, f32[8,256,1280]{2,1,0:T(8,128)S(1)} %get-tuple-element.35), kind=kOutput, calls=%fused_computation.156 | convolution fusion | flops 346685440 | bytes 15998976 | tf_op jit(solution)/shard_map/gqk,qgc->gck/dot_general | solution.py:122
  85.5 9.7 %collective-permute-done.5 = bf16[2,2,2,40,2,512]{5,3,4,1,0,2:T(8,128)(2,1)S(1)} collective-permute-done((bf16[2,2,2,40,2,512]{5,3,4,1,0,2:T(8,128)(2,1)S(1)}, bf16[2,2,2,40,2,512]{5,3,4,1,0,2:T(8,128)(2,1)S(1)}, u32[]{:S(2)}, u32[]{:S(2)}) %collective-permute-start.5) | collective-permute-done | bytes 655392 | tf_op jit(solution)/shard_map/ppermute | solution.py:29
  95.4 2.7 %collective-permute-start.6 = (bf16[2,2,40,2,512]{4,2,3,1,0:T(8,128)(2,1)S(1)}, bf16[2,2,40,2,512]{4,2,3,1,0:T(8,128)(2,1)S(1)}, u32[]{:S(2)}, u32[]{:S(2)}) collective-permute-start(bf16[2,2,40,2,512]{4,2,3,1,0:T(8,128)(2,1)S(1)} %fusion.60), channel_id=1, source_target_pairs={{0,2},{1,3},{2,0},{3,1},{4,6},{5,7},{6,4},{7,5},{8,10},{9,11},{10,... | collective-permute-start | bytes 983048 | tf_op jit(solution)/shard_map/ppermute | solution.py:29
  99.9 12.7 %collective-permute-done.6 = bf16[2,2,40,2,512]{4,2,3,1,0:T(8,128)(2,1)S(1)} collective-permute-done((bf16[2,2,40,2,512]{4,2,3,1,0:T(8,128)(2,1)S(1)}, bf16[2,2,40,2,512]{4,2,3,1,0:T(8,128)(2,1)S(1)}, u32[]{:S(2)}, u32[]{:S(2)}) %collective-permute-start.6) | collective-permute-done | bytes 327712 | tf_op jit(solution)/shard_map/ppermute | solution.py:29
  112.7 2.3 %collective-permute-start.7 = (bf16[2,40,2,512]{3,1,2,0:T(8,128)(2,1)S(1)}, bf16[2,40,2,512]{3,1,2,0:T(8,128)(2,1)S(1)}, u32[]{:S(2)}, u32[]{:S(2)}) collective-permute-start(bf16[2,40,2,512]{3,1,2,0:T(8,128)(2,1)S(1)} %fusion.65), channel_id=1, source_target_pairs={{0,16},{4,20},{8,24},{12,28},{16,0},{20,4},{24,8},{28,12},{1,17},{... | collective-permute-start | bytes 491528 | tf_op jit(solution)/shard_map/ppermute | solution.py:29
  115.1 2.7 %fusion.41 = (f32[256]{0:T(256)S(1)}, f32[256,1024]{1,0:T(8,128)}) fusion(bf16[1,256,1024]{2,1,0:T(8,128)(2,1)S(1)} %copy-done.1, f32[256]{0:T(256)S(1)} %add_rsqrt_fusion, bf16[4,256,512]{1,2,0:T(8,128)(2,1)S(1)} %bitcast.201, bf16[1024,4,512]{2,1,0:T(4,128)(2,1)S(1)} %copy-done.8), kind=kOutput, calls=%fused_computation.44 | convolution fusion | flops 1074790144 | bytes 6817792 | tf_op jit(solution)/shard_map/wrh,dwh->rd/dot_general | solution.py:209
  118.5 4.4 %collective-permute-done.8 = bf16[40,2,512]{2,0,1:T(8,128)(2,1)S(1)} collective-permute-done((bf16[40,2,512]{2,0,1:T(8,128)(2,1)S(1)}, bf16[40,2,512]{2,0,1:T(8,128)(2,1)S(1)}, u32[]{:S(2)}, u32[]{:S(2)}) %collective-permute-start.8) | collective-permute-done | bytes 81952 | tf_op jit(solution)/shard_map/ppermute | solution.py:29
  124.3 2.3 %fusion.63 = (bf16[1024,256]{0,1:T(8,128)(2,1)S(1)}, bf16[1,256,1024]{2,1,0:T(8,128)(2,1)}) fusion(f32[256]{0:T(256)S(1)} %add_rsqrt_fusion, bf16[1,256,1024]{2,1,0:T(8,128)(2,1)S(1)} %copy-done.1, f32[256,1024]{1,0:T(8,128)} %get-tuple-element.43, f32[256]{0:T(256)S(1)} %broadcast_multiply_fusion, f32[]{:T(128)S(6)} %div.75), kind=kLoop, calls=%fused_computation.94 | loop fusion | flops 2097152 | bytes 2623492 | tf_op jit(solution)/shard_map/rd,wgcr->dwgc/dot_general | solution.py:214
  127.8 2.6 %collective-permute-done.13 = bf16[2,2,2,2,32,2,512]{6,4,5,3,2,1,0:T(8,128)(2,1)S(1)} collective-permute-done((bf16[2,2,2,2,32,2,512]{6,4,5,3,2,1,0:T(8,128)(2,1)S(1)}, bf16[2,2,2,2,32,2,512]{6,4,5,3,2,1,0:T(8,128)(2,1)S(1)}, u32[]{:S(2)}, u32[]{:S(2)}) %collective-permute-start.13) | collective-permute-done | bytes 1048608 | tf_op jit(solution)/shard_map/ppermute | solution.py:29
  132.8 12.2 %collective-permute-done.14 = bf16[2,2,2,32,2,512]{5,3,4,2,1,0:T(8,128)(2,1)S(1)} collective-permute-done((bf16[2,2,2,32,2,512]{5,3,4,2,1,0:T(8,128)(2,1)S(1)}, bf16[2,2,2,32,2,512]{5,3,4,2,1,0:T(8,128)(2,1)S(1)}, u32[]{:S(2)}, u32[]{:S(2)}) %collective-permute-start.14) | collective-permute-done | bytes 524320 | tf_op jit(solution)/shard_map/ppermute | solution.py:29
  145.3 3.4 %collective-permute-start.15 = (bf16[2,2,32,2,512]{4,2,3,1,0:T(8,128)(2,1)S(1)}, bf16[2,2,32,2,512]{4,2,3,1,0:T(8,128)(2,1)S(1)}, u32[]{:S(2)}, u32[]{:S(2)}) collective-permute-start(bf16[2,2,32,2,512]{4,2,3,1,0:T(8,128)(2,1)S(1)} %fusion.61), channel_id=1, source_target_pairs={{0,2},{1,3},{2,0},{3,1},{4,6},{5,7},{6,4},{7,5},{8,10},{9,11},{10,... | collective-permute-start | bytes 786440 | tf_op jit(solution)/shard_map/ppermute | solution.py:29
  148.8 11.6 %collective-permute-done.15 = bf16[2,2,32,2,512]{4,2,3,1,0:T(8,128)(2,1)S(1)} collective-permute-done((bf16[2,2,32,2,512]{4,2,3,1,0:T(8,128)(2,1)S(1)}, bf16[2,2,32,2,512]{4,2,3,1,0:T(8,128)(2,1)S(1)}, u32[]{:S(2)}, u32[]{:S(2)}) %collective-permute-start.15) | collective-permute-done | bytes 262176 | tf_op jit(solution)/shard_map/ppermute | solution.py:29
  162.5 2.4 %collective-permute-done.18 = bf16[2,32,2,256]{3,1,2,0:T(8,128)(2,1)S(1)} collective-permute-done((bf16[2,32,2,256]{3,1,2,0:T(8,128)(2,1)S(1)}, bf16[2,32,2,256]{3,1,2,0:T(8,128)(2,1)S(1)}, u32[]{:S(2)}, u32[]{:S(2)}) %collective-permute-start.18) | collective-permute-done | bytes 65568 | tf_op jit(solution)/shard_map/ppermute | solution.py:29
  (115 shorter events, 47.2 us)
Async XLA Ops:
  1.9 18.9 %copy-start.7 = (s32[1,256]{1,0:T(1,128)S(1)}, s32[1,256]{1,0:T(1,128)}, u32[]{:S(2)}) copy-start(s32[1,256]{1,0:T(1,128)} %param.9) | copy-start | bytes 3076
  1.9 20.1 %copy-start.5 = (bf16[1,256,1024]{2,1,0:T(8,128)(2,1)S(1)}, bf16[1,256,1024]{2,1,0:T(8,128)(2,1)}, u32[]{:S(2)}) copy-start(bf16[1,256,1024]{2,1,0:T(8,128)(2,1)} %param.8) | copy-start | bytes 1572868
  6.7 40.0 %collective-permute-start = (bf16[2,256,512]{2,1,0:T(8,128)(2,1)}, bf16[2,256,512]{2,1,0:T(8,128)(2,1)}, u32[]{:S(2)}, u32[]{:S(2)}) collective-permute-start(bf16[2,256,512]{2,1,0:T(8,128)(2,1)} %slice.120), channel_id=1, source_target_pairs={{0,16},{4,20},{8,24},{12,28},{1,17},{5,21},{9,25},{13,29},{2,18},{... | collective-permute-start | bytes 1572872 | tf_op jit(solution)/shard_map/ppermute | solution.py:16
  12.4 35.4 %collective-permute-start.1 = (bf16[2,256,512]{2,1,0:T(8,128)(2,1)}, bf16[2,256,512]{2,1,0:T(8,128)(2,1)}, u32[]{:S(2)}, u32[]{:S(2)}) collective-permute-start(bf16[2,256,512]{2,1,0:T(8,128)(2,1)} %slice.120), channel_id=1, source_target_pairs={{0,12},{4,16},{8,20},{12,24},{16,28},{1,13},{5,17},{9,21},{13,25},... | collective-permute-start | bytes 1572872 | tf_op jit(solution)/shard_map/ppermute | solution.py:16
  15.7 33.1 %collective-permute-start.2 = (bf16[2,256,512]{2,1,0:T(8,128)(2,1)}, bf16[2,256,512]{2,1,0:T(8,128)(2,1)}, u32[]{:S(2)}, u32[]{:S(2)}) collective-permute-start(bf16[2,256,512]{2,1,0:T(8,128)(2,1)} %slice.120), channel_id=1, source_target_pairs={{0,8},{4,12},{8,16},{12,20},{16,24},{20,28},{1,9},{5,13},{9,17},{1... | collective-permute-start | bytes 1572872 | tf_op jit(solution)/shard_map/ppermute | solution.py:16
  18.7 31.3 %collective-permute-start.3 = (bf16[2,256,512]{2,1,0:T(8,128)(2,1)}, bf16[2,256,512]{2,1,0:T(8,128)(2,1)}, u32[]{:S(2)}, u32[]{:S(2)}) collective-permute-start(bf16[2,256,512]{2,1,0:T(8,128)(2,1)} %slice.120), channel_id=1, source_target_pairs={{0,4},{4,8},{8,12},{12,16},{16,20},{20,24},{24,28},{1,5},{5,9},{9,... | collective-permute-start | bytes 1572872 | tf_op jit(solution)/shard_map/ppermute | solution.py:16
  22.0 4.8 %copy-start.1 = (bf16[1,256,1024]{2,1,0:T(8,128)(2,1)S(1)}, bf16[1,256,1024]{2,1,0:T(8,128)(2,1)}, u32[]{:S(2)}) copy-start(bf16[1,256,1024]{2,1,0:T(8,128)(2,1)} %param.6) | copy-start | bytes 1572868
  71.3 6.2 %collective-permute-start.4 = (bf16[2,2,2,2,40,2,512]{6,4,5,1,0,2,3:T(8,128)(2,1)S(1)}, bf16[2,2,2,2,40,2,512]{6,4,5,1,0,2,3:T(8,128)(2,1)S(1)}, u32[]{:S(2)}, u32[]{:S(2)}) collective-permute-start(bf16[2,2,2,2,40,2,512]{6,4,5,1,0,2,3:T(8,128)(2,1)S(1)} %fusion.32), channel_id=1, source_target_pairs={{0,4},{4,0},{8,12},{12,8},{16,20},{20,16},{24,28},{28,24},{1,5},{5... | collective-permute-start | bytes 3932168 | tf_op jit(solution)/shard_map/ppermute | solution.py:29
  78.1 17.1 %collective-permute-start.5 = (bf16[2,2,2,40,2,512]{5,3,4,1,0,2:T(8,128)(2,1)S(1)}, bf16[2,2,2,40,2,512]{5,3,4,1,0,2:T(8,128)(2,1)S(1)}, u32[]{:S(2)}, u32[]{:S(2)}) collective-permute-start(bf16[2,2,2,40,2,512]{5,3,4,1,0,2:T(8,128)(2,1)S(1)} %fusion.53), channel_id=1, source_target_pairs={{0,1},{1,0},{2,3},{3,2},{4,5},{5,4},{6,7},{7,6},{8,9},{9,8},{10,11... | collective-permute-start | bytes 1966088 | tf_op jit(solution)/shard_map/ppermute | solution.py:29
  79.8 18.3 %collective-permute-start.12 = (bf16[2,8,64,256]{3,2,1,0:T(8,128)(2,1)S(1)}, bf16[2,8,64,256]{3,2,1,0:T(8,128)(2,1)S(1)}, u32[]{:S(2)}, u32[]{:S(2)}) collective-permute-start(bf16[2,8,64,256]{3,2,1,0:T(8,128)(2,1)S(1)} %pad_maximum_fusion.4), channel_id=1, source_target_pairs={{16,0},{20,4},{24,8},{28,12},{17,1},{21,5},{25,9},{29,13},{18,2},{... | collective-permute-start | bytes 1572872 | tf_op jit(solution)/shard_map/ppermute | solution.py:16
  81.1 16.9 %collective-permute-start.11 = (bf16[2,8,64,256]{3,2,1,0:T(8,128)(2,1)S(1)}, bf16[2,8,64,256]{3,2,1,0:T(8,128)(2,1)S(1)}, u32[]{:S(2)}, u32[]{:S(2)}) collective-permute-start(bf16[2,8,64,256]{3,2,1,0:T(8,128)(2,1)S(1)} %pad_maximum_fusion.3), channel_id=1, source_target_pairs={{12,0},{16,4},{20,8},{24,12},{28,16},{13,1},{17,5},{21,9},{25,13},... | collective-permute-start | bytes 1572872 | tf_op jit(solution)/shard_map/ppermute | solution.py:16
  82.5 16.8 %collective-permute-start.10 = (bf16[2,8,64,256]{3,2,1,0:T(8,128)(2,1)S(1)}, bf16[2,8,64,256]{3,2,1,0:T(8,128)(2,1)S(1)}, u32[]{:S(2)}, u32[]{:S(2)}) collective-permute-start(bf16[2,8,64,256]{3,2,1,0:T(8,128)(2,1)S(1)} %pad_maximum_fusion.2), channel_id=1, source_target_pairs={{8,0},{12,4},{16,8},{20,12},{24,16},{28,20},{9,1},{13,5},{17,9},{2... | collective-permute-start | bytes 1572872 | tf_op jit(solution)/shard_map/ppermute | solution.py:16
  83.9 15.4 %collective-permute-start.9 = (bf16[2,8,64,256]{3,2,1,0:T(8,128)(2,1)S(1)}, bf16[2,8,64,256]{3,2,1,0:T(8,128)(2,1)S(1)}, u32[]{:S(2)}, u32[]{:S(2)}) collective-permute-start(bf16[2,8,64,256]{3,2,1,0:T(8,128)(2,1)S(1)} %pad_maximum_fusion.1), channel_id=1, source_target_pairs={{4,0},{8,4},{12,8},{16,12},{20,16},{24,20},{28,24},{5,1},{9,5},{13... | collective-permute-start | bytes 1572872 | tf_op jit(solution)/shard_map/ppermute | solution.py:16
  95.4 17.2 %collective-permute-start.6 = (bf16[2,2,40,2,512]{4,2,3,1,0:T(8,128)(2,1)S(1)}, bf16[2,2,40,2,512]{4,2,3,1,0:T(8,128)(2,1)S(1)}, u32[]{:S(2)}, u32[]{:S(2)}) collective-permute-start(bf16[2,2,40,2,512]{4,2,3,1,0:T(8,128)(2,1)S(1)} %fusion.60), channel_id=1, source_target_pairs={{0,2},{1,3},{2,0},{3,1},{4,6},{5,7},{6,4},{7,5},{8,10},{9,11},{10,... | collective-permute-start | bytes 983048 | tf_op jit(solution)/shard_map/ppermute | solution.py:29
  99.3 15.8 %copy-start.8 = (bf16[1024,4,512]{2,1,0:T(4,128)(2,1)S(1)}, bf16[1024,4,512]{2,1,0:T(4,128)(2,1)}, u32[]{:S(2)}) copy-start(bf16[1024,4,512]{2,1,0:T(4,128)(2,1)} %param.7) | copy-start | bytes 12582916
  112.7 5.6 %collective-permute-start.7 = (bf16[2,40,2,512]{3,1,2,0:T(8,128)(2,1)S(1)}, bf16[2,40,2,512]{3,1,2,0:T(8,128)(2,1)S(1)}, u32[]{:S(2)}, u32[]{:S(2)}) collective-permute-start(bf16[2,40,2,512]{3,1,2,0:T(8,128)(2,1)S(1)} %fusion.65), channel_id=1, source_target_pairs={{0,16},{4,20},{8,24},{12,28},{16,0},{20,4},{24,8},{28,12},{1,17},{... | collective-permute-start | bytes 491528 | tf_op jit(solution)/shard_map/ppermute | solution.py:29
  118.4 4.5 %collective-permute-start.8 = (bf16[40,2,512]{2,0,1:T(8,128)(2,1)S(1)}, bf16[40,2,512]{2,0,1:T(8,128)(2,1)S(1)}, u32[]{:S(2)}, u32[]{:S(2)}) collective-permute-start(bf16[40,2,512]{2,0,1:T(8,128)(2,1)S(1)} %fusion.66), channel_id=1, source_target_pairs={{0,8},{4,12},{8,0},{12,4},{16,24},{20,28},{24,16},{28,20},{1,9},{5... | collective-permute-start | bytes 245768 | tf_op jit(solution)/shard_map/ppermute | solution.py:29
  127.7 2.7 %collective-permute-start.13 = (bf16[2,2,2,2,32,2,512]{6,4,5,3,2,1,0:T(8,128)(2,1)S(1)}, bf16[2,2,2,2,32,2,512]{6,4,5,3,2,1,0:T(8,128)(2,1)S(1)}, u32[]{:S(2)}, u32[]{:S(2)}) collective-permute-start(bf16[2,2,2,2,32,2,512]{6,4,5,3,2,1,0:T(8,128)(2,1)S(1)} %fusion.48), channel_id=1, source_target_pairs={{0,4},{4,0},{8,12},{12,8},{16,20},{20,16},{24,28},{28,24},{1,5},{5... | collective-permute-start | bytes 3145736 | tf_op jit(solution)/shard_map/ppermute | solution.py:29
  131.0 14.0 %collective-permute-start.14 = (bf16[2,2,2,32,2,512]{5,3,4,2,1,0:T(8,128)(2,1)S(1)}, bf16[2,2,2,32,2,512]{5,3,4,2,1,0:T(8,128)(2,1)S(1)}, u32[]{:S(2)}, u32[]{:S(2)}) collective-permute-start(bf16[2,2,2,32,2,512]{5,3,4,2,1,0:T(8,128)(2,1)S(1)} %fusion.54), channel_id=1, source_target_pairs={{0,1},{1,0},{2,3},{3,2},{4,5},{5,4},{6,7},{7,6},{8,9},{9,8},{10,11... | collective-permute-start | bytes 1572872 | tf_op jit(solution)/shard_map/ppermute | solution.py:29
  145.3 15.2 %collective-permute-start.15 = (bf16[2,2,32,2,512]{4,2,3,1,0:T(8,128)(2,1)S(1)}, bf16[2,2,32,2,512]{4,2,3,1,0:T(8,128)(2,1)S(1)}, u32[]{:S(2)}, u32[]{:S(2)}) collective-permute-start(bf16[2,2,32,2,512]{4,2,3,1,0:T(8,128)(2,1)S(1)} %fusion.61), channel_id=1, source_target_pairs={{0,2},{1,3},{2,0},{3,1},{4,6},{5,7},{6,4},{7,5},{8,10},{9,11},{10,... | collective-permute-start | bytes 786440 | tf_op jit(solution)/shard_map/ppermute | solution.py:29
  160.6 4.3 %collective-permute-start.18 = (bf16[2,32,2,256]{3,1,2,0:T(8,128)(2,1)S(1)}, bf16[2,32,2,256]{3,1,2,0:T(8,128)(2,1)S(1)}, u32[]{:S(2)}, u32[]{:S(2)}) collective-permute-start(bf16[2,32,2,256]{3,1,2,0:T(8,128)(2,1)S(1)} %fusion.68), channel_id=1, source_target_pairs={{0,8},{4,12},{8,0},{12,4},{16,24},{20,28},{24,16},{28,20},{1,9},{5... | collective-permute-start | bytes 196616 | tf_op jit(solution)/shard_map/ppermute | solution.py:29
  160.7 6.1 %collective-permute-start.16 = (bf16[2,32,2,256]{3,1,2,0:T(8,128)(2,1)S(1)}, bf16[2,32,2,256]{3,1,2,0:T(8,128)(2,1)S(1)}, u32[]{:S(2)}, u32[]{:S(2)}) collective-permute-start(bf16[2,32,2,256]{3,1,2,0:T(8,128)(2,1)S(1)} %fusion.67), channel_id=1, source_target_pairs={{0,16},{4,20},{8,24},{12,28},{16,0},{20,4},{24,8},{28,12},{1,17},{... | collective-permute-start | bytes 196616 | tf_op jit(solution)/shard_map/ppermute | solution.py:29
  165.0 4.0 %collective-permute-start.19 = (bf16[32,2,256]{2,0,1:T(8,128)(2,1)S(1)}, bf16[32,2,256]{2,0,1:T(8,128)(2,1)S(1)}, u32[]{:S(2)}, u32[]{:S(2)}) collective-permute-start(bf16[32,2,256]{2,0,1:T(8,128)(2,1)S(1)} %fusion.70), channel_id=1, source_target_pairs={{0,16},{4,20},{8,24},{12,28},{16,0},{20,4},{24,8},{28,12},{1,17},{... | collective-permute-start | bytes 98312 | tf_op jit(solution)/shard_map/ppermute | solution.py:29
  166.8 4.0 %collective-permute-start.17 = (bf16[32,2,256]{2,0,1:T(8,128)(2,1)S(1)}, bf16[32,2,256]{2,0,1:T(8,128)(2,1)S(1)}, u32[]{:S(2)}, u32[]{:S(2)}) collective-permute-start(bf16[32,2,256]{2,0,1:T(8,128)(2,1)S(1)} %fusion.69), channel_id=1, source_target_pairs={{0,8},{4,12},{8,0},{12,4},{16,24},{20,28},{24,16},{28,20},{1,9},{5... | collective-permute-start | bytes 98312 | tf_op jit(solution)/shard_map/ppermute | solution.py:29
  (6 other events, 18.2 us)

commit v21 on v18

--- a/solution.py
+++ b/solution.py
@@ -210,7 +210,7 @@
         "wrh,dwh->rd", grad_rows, weights, preferred_element_type=jnp.float32
     )
     along = jnp.sum(grad_normed * normed_full, axis=-1) / width
-    unscaled_input = inv_rms[:, None] * (grad_normed - normed_full * along[:, None])
+    centred_grad = grad_normed - normed_full * along[:, None]
     key_value_part = jnp.einsum(
         "rd,wgcr->dwgc", normed, grad_proj[1:3], preferred_element_type=jnp.float32
     ).reshape(width, 2, inner)
@@ -218,7 +218,7 @@
     summed = jnp.concatenate([early[:, :1], late, early[:, 1:]], axis=1)
     total_count = count.astype(jnp.float32)
     loss_scale = jnp.float32(tokens_all) / total_count
-    grad_input = (loss_scale * unscaled_input).astype(jnp.bfloat16)
+    grad_input = (loss_scale * inv_rms[:, None] * centred_grad).astype(jnp.bfloat16)
     grad_weights = summed * (jnp.sqrt(jnp.float32(tokens_all)) / total_count)
     return (grad_input[None], grad_weights)
 

time: 159 us -> 159 us (level)
  no operation moved by 1% of the time
where the time goes in v21:
time: 159 us; the launch traced here: 158 us
  waiting for transfers between devices  62.8 us (39%)
  starting transfers between devices  36.9 us (23%)
  matrix products  28.8 us (18%)
  local copies, waits for them, and re-layouts  15.9 us (10%)
  other arithmetic  10.9 us (7%)
  between operations  2.68 us (2%)
    ppermute x12, waiting for transfers between devices, halve(): lax.ppermute(send.astype(send_type), axis, pairs).astype(keep.dtype)  48.2 us
    ppermute x8, starting transfers between devices, shifted(): return lax.ppermute(value, axis, pairs)  19.4 us
    ppermute x12, starting transfers between devices, halve(): lax.ppermute(send.astype(send_type), axis, pairs).astype(keep.dtype)  17.5 us
    ppermute x8, waiting for transfers between devices, shifted(): return lax.ppermute(value, axis, pairs)  14.6 us
    unnamed x24, local copies, waits for them, and re-layouts  7.02 us
    dot_general x1, matrix products, shards(): jnp.einsum('rd,dwh->wrh', grad_out, weights, preferred_element_type=jnp.f...  4.81 us
    dot_general x1, matrix products, shards(): jnp.einsum('rd,dwh->wrh', normed, weights, preferred_element_type=jnp.flo...  3.98 us
    dot_general x1, matrix products, band_block(): jnp.einsum('qgc,kgc->gqk', queries, keys_blk, preferred_element_type=jnp....  3.91 us
  transfers between devices with their start and end apart: 20, of which 14 were waited for; matrix products, arithmetic and copies ran while one was open for 14% of the time, Pallas kernels for 0%

profile of v21, /device:TPU:0, one launch (start us, length us, event | category | flops | bytes accessed | tf_op | source)
XLA Modules:
  0.0 157.9 jit_solution(6877205827482537522)
XLA Ops:
  1.9 4.0 %fusion.21 = bf16[4,256,512]{2,1,0:T(8,128)(2,1)S(1)} fusion(bf16[1024,4,512]{2,1,0:T(4,128)(2,1)} %param.7, bf16[1,256,1024]{2,1,0:T(8,128)(2,1)} %param.6, f32[256]{0:T(256)S(1)} %add_rsqrt_fusion), kind=kOutput, calls=%fused_computation.24 | convolution fusion | flops 1075052544 | bytes 5768192 | tf_op jit(solution)/shard_map/rd,dwh->wrh/dot_general | solution.py:142
  6.7 5.7 %collective-permute-start = (bf16[2,256,512]{2,1,0:T(8,128)(2,1)}, bf16[2,256,512]{2,1,0:T(8,128)(2,1)}, u32[]{:S(2)}, u32[]{:S(2)}) collective-permute-start(bf16[2,256,512]{2,1,0:T(8,128)(2,1)} %slice.120), channel_id=1, source_target_pairs={{0,16},{4,20},{8,24},{12,28},{1,17},{5,21},{9,25},{13,29},{2,18},{... | collective-permute-start | bytes 1572872 | tf_op jit(solution)/shard_map/ppermute | solution.py:16
  12.4 3.4 %collective-permute-start.1 = (bf16[2,256,512]{2,1,0:T(8,128)(2,1)}, bf16[2,256,512]{2,1,0:T(8,128)(2,1)}, u32[]{:S(2)}, u32[]{:S(2)}) collective-permute-start(bf16[2,256,512]{2,1,0:T(8,128)(2,1)} %slice.120), channel_id=1, source_target_pairs={{0,12},{4,16},{8,20},{12,24},{16,28},{1,13},{5,17},{9,21},{13,25},... | collective-permute-start | bytes 1572872 | tf_op jit(solution)/shard_map/ppermute | solution.py:16
  15.7 2.9 %collective-permute-start.2 = (bf16[2,256,512]{2,1,0:T(8,128)(2,1)}, bf16[2,256,512]{2,1,0:T(8,128)(2,1)}, u32[]{:S(2)}, u32[]{:S(2)}) collective-permute-start(bf16[2,256,512]{2,1,0:T(8,128)(2,1)} %slice.120), channel_id=1, source_target_pairs={{0,8},{4,12},{8,16},{12,20},{16,24},{20,28},{1,9},{5,13},{9,17},{1... | collective-permute-start | bytes 1572872 | tf_op jit(solution)/shard_map/ppermute | solution.py:16
  22.0 4.8 %fusion.18 = bf16[4,256,512]{2,1,0:T(8,128)(2,1)} fusion(bf16[1024,4,512]{2,1,0:T(4,128)(2,1)} %param.7, bf16[1,256,1024]{2,1,0:T(8,128)(2,1)S(1)} %copy-done.5, pred[256]{0:T(512)(128)(4,1)S(1)} %compare_reduce_fusion), kind=kOutput, calls=%fused_computation.23 | convolution fusion | flops 1074528256 | bytes 5767424 | tf_op jit(solution)/shard_map/rd,dwh->wrh/dot_general | solution.py:154
  33.3 13.4 %collective-permute-done = bf16[2,256,512]{2,1,0:T(8,128)(2,1)} collective-permute-done((bf16[2,256,512]{2,1,0:T(8,128)(2,1)}, bf16[2,256,512]{2,1,0:T(8,128)(2,1)}, u32[]{:S(2)}, u32[]{:S(2)}) %collective-permute-start) | collective-permute-done | bytes 524320 | tf_op jit(solution)/shard_map/ppermute | solution.py:16
  55.3 3.9 %fusion.1 = (f32[8,256]{1,0:T(8,128)S(1)}, f32[8,256,1280]{2,1,0:T(8,128)S(1)}) fusion(f32[256,1280]{1,0:T(8,128)} %fusion.37, bf16[256,8,64]{0,2,1:T(8,128)(2,1)S(1)} %bitcast.192, bf16[1280,8,64]{0,2,1:T(8,128)(2,1)S(1)} %bitcast.189), kind=kOutput, calls=%fused_computation.3 | convolution fusion | flops 343406592 | bytes 13377536 | tf_op jit(solution)/shard_map/qgc,kgc->gqk/dot_general | solution.py:102
  59.3 2.8 %multiply_reduce_fusion = (f32[256,8]{0,1:T(8,128)S(1)}, bf16[8,64,256]{2,1,0:T(8,128)(2,1)S(1)}) fusion(bf16[256,8,64]{0,2,1:T(8,128)(2,1)S(1)} %bitcast.202, bf16[1280,8,64]{0,2,1:T(8,128)(2,1)S(1)} %bitcast.199, f32[8,256]{1,0:T(8,128)S(1)} %get-tuple-element.34, f32[256,1280]{1,0:T(8,128)S(1)} %copy-done, f32[8,256,1280]{2,1,0:T(8,128)S(1)} %get-tuple-element.35), kind=kOutput, calls=%fused_computation.79 | convolution fusion | flops 346683392 | bytes 13647872 | tf_op jit(solution)/shard_map/gqk,kgc->qgc/dot_general | solution.py:108
  62.1 3.9 %multiply_convert_fusion = bf16[8,256,1280]{2,1,0:T(8,128)(2,1)S(1)} fusion(bf16[256,8,64]{0,2,1:T(8,128)(2,1)S(1)} %bitcast.203, bf16[1280,8,64]{0,2,1:T(8,128)(2,1)S(1)} %bitcast.200, f32[8,256]{1,0:T(8,128)S(1)} %bitcast.206, f32[8,256]{1,0:T(8,128)S(1)} %get-tuple-element.34, f32[256,1280]{1,0:T(8,128)S(1)} %copy-done, ...), kind=kOutput, calls=%fused_computation | convolution fusion | flops 353894400 | bytes 18628608 | tf_op jit(solution)/shard_map/qgc,kgc->gqk/dot_general | solution.py:112
  71.3 3.6 %collective-permute-start.4 = (bf16[2,2,2,2,40,2,512]{6,4,5,1,0,2,3:T(8,128)(2,1)S(1)}, bf16[2,2,2,2,40,2,512]{6,4,5,1,0,2,3:T(8,128)(2,1)S(1)}, u32[]{:S(2)}, u32[]{:S(2)}) collective-permute-start(bf16[2,2,2,2,40,2,512]{6,4,5,1,0,2,3:T(8,128)(2,1)S(1)} %fusion.32), channel_id=1, source_target_pairs={{0,4},{4,0},{8,12},{12,8},{16,20},{20,16},{24,28},{28,24},{1,5},{5... | collective-permute-start | bytes 3932168 | tf_op jit(solution)/shard_map/ppermute | solution.py:29
  74.8 2.3 %fusion.90 = (bf16[8,64,1280]{2,1,0:T(8,128)(2,1)S(1)}, f32[8,64,1280]{2,1,0:T(8,128)S(1)}) fusion(bf16[256,8,64]{0,2,1:T(8,128)(2,1)S(1)} %bitcast.204, f32[8,256]{1,0:T(8,128)S(1)} %get-tuple-element.34, f32[256,1280]{1,0:T(8,128)S(1)} %copy-done, f32[8,256,1280]{2,1,0:T(8,128)S(1)} %get-tuple-element.35), kind=kOutput, calls=%fused_computation.163 | convolution fusion | flops 346685440 | bytes 15998976 | tf_op jit(solution)/shard_map/gqk,qgc->gck/dot_general | solution.py:122
  85.5 9.7 %collective-permute-done.5 = bf16[2,2,2,40,2,512]{5,3,4,1,0,2:T(8,128)(2,1)S(1)} collective-permute-done((bf16[2,2,2,40,2,512]{5,3,4,1,0,2:T(8,128)(2,1)S(1)}, bf16[2,2,2,40,2,512]{5,3,4,1,0,2:T(8,128)(2,1)S(1)}, u32[]{:S(2)}, u32[]{:S(2)}) %collective-permute-start.5) | collective-permute-done | bytes 655392 | tf_op jit(solution)/shard_map/ppermute | solution.py:29
  95.4 2.7 %collective-permute-start.6 = (bf16[2,2,40,2,512]{4,2,3,1,0:T(8,128)(2,1)S(1)}, bf16[2,2,40,2,512]{4,2,3,1,0:T(8,128)(2,1)S(1)}, u32[]{:S(2)}, u32[]{:S(2)}) collective-permute-start(bf16[2,2,40,2,512]{4,2,3,1,0:T(8,128)(2,1)S(1)} %fusion.58), channel_id=1, source_target_pairs={{0,2},{1,3},{2,0},{3,1},{4,6},{5,7},{6,4},{7,5},{8,10},{9,11},{10,... | collective-permute-start | bytes 983048 | tf_op jit(solution)/shard_map/ppermute | solution.py:29
  99.8 12.7 %collective-permute-done.6 = bf16[2,2,40,2,512]{4,2,3,1,0:T(8,128)(2,1)S(1)} collective-permute-done((bf16[2,2,40,2,512]{4,2,3,1,0:T(8,128)(2,1)S(1)}, bf16[2,2,40,2,512]{4,2,3,1,0:T(8,128)(2,1)S(1)}, u32[]{:S(2)}, u32[]{:S(2)}) %collective-permute-start.6) | collective-permute-done | bytes 327712 | tf_op jit(solution)/shard_map/ppermute | solution.py:29
  112.7 2.3 %collective-permute-start.7 = (bf16[2,40,2,512]{3,1,2,0:T(8,128)(2,1)S(1)}, bf16[2,40,2,512]{3,1,2,0:T(8,128)(2,1)S(1)}, u32[]{:S(2)}, u32[]{:S(2)}) collective-permute-start(bf16[2,40,2,512]{3,1,2,0:T(8,128)(2,1)S(1)} %fusion.69), channel_id=1, source_target_pairs={{0,16},{4,20},{8,24},{12,28},{16,0},{20,4},{24,8},{28,12},{1,17},{... | collective-permute-start | bytes 491528 | tf_op jit(solution)/shard_map/ppermute | solution.py:29
  115.0 2.7 %fusion.41 = (f32[256]{0:T(256)S(1)}, f32[256,1024]{1,0:T(8,128)}) fusion(bf16[1,256,1024]{2,1,0:T(8,128)(2,1)S(1)} %copy-done.1, f32[256]{0:T(256)S(1)} %add_rsqrt_fusion, bf16[4,256,512]{1,2,0:T(8,128)(2,1)S(1)} %bitcast.201, bf16[1024,4,512]{2,1,0:T(4,128)(2,1)S(1)} %copy-done.8), kind=kOutput, calls=%fused_computation.44 | convolution fusion | flops 1074790144 | bytes 6817792 | tf_op jit(solution)/shard_map/wrh,dwh->rd/dot_general | solution.py:209
  118.5 4.4 %collective-permute-done.8 = bf16[40,2,512]{2,0,1:T(8,128)(2,1)S(1)} collective-permute-done((bf16[40,2,512]{2,0,1:T(8,128)(2,1)S(1)}, bf16[40,2,512]{2,0,1:T(8,128)(2,1)S(1)}, u32[]{:S(2)}, u32[]{:S(2)}) %collective-permute-start.8) | collective-permute-done | bytes 81952 | tf_op jit(solution)/shard_map/ppermute | solution.py:29
  124.3 2.3 %fusion.67 = (bf16[1024,256]{0,1:T(8,128)(2,1)S(1)}, bf16[1,256,1024]{2,1,0:T(8,128)(2,1)}) fusion(f32[256]{0:T(256)S(1)} %add_rsqrt_fusion, bf16[1,256,1024]{2,1,0:T(8,128)(2,1)S(1)} %copy-done.1, f32[256,1024]{1,0:T(8,128)} %get-tuple-element.43, f32[256]{0:T(256)S(1)} %broadcast_multiply_fusion.1, f32[256]{0:T(256)S(1)} %broadcast_multiply_fusion), kind=kLoop, calls=%fused_computation.106 | loop fusion | flops 1835008 | bytes 2624512 | tf_op jit(solution)/shard_map/rd,wgcr->dwgc/dot_general | solution.py:214
  127.8 2.6 %collective-permute-done.13 = bf16[2,2,2,2,32,2,512]{6,4,5,3,2,1,0:T(8,128)(2,1)S(1)} collective-permute-done((bf16[2,2,2,2,32,2,512]{6,4,5,3,2,1,0:T(8,128)(2,1)S(1)}, bf16[2,2,2,2,32,2,512]{6,4,5,3,2,1,0:T(8,128)(2,1)S(1)}, u32[]{:S(2)}, u32[]{:S(2)}) %collective-permute-start.13) | collective-permute-done | bytes 1048608 | tf_op jit(solution)/shard_map/ppermute | solution.py:29
  133.4 6.5 %collective-permute-done.14 = bf16[2,2,2,32,2,256]{5,3,4,2,1,0:T(8,128)(2,1)S(1)} collective-permute-done((bf16[2,2,2,32,2,256]{5,3,4,2,1,0:T(8,128)(2,1)S(1)}, bf16[2,2,2,32,2,256]{5,3,4,2,1,0:T(8,128)(2,1)S(1)}, u32[]{:S(2)}, u32[]{:S(2)}) %collective-permute-start.14) | collective-permute-done | bytes 262176 | tf_op jit(solution)/shard_map/ppermute | solution.py:29
  142.0 3.1 %collective-permute-done.15 = bf16[2,2,32,2,256]{4,2,3,1,0:T(8,128)(2,1)S(1)} collective-permute-done((bf16[2,2,32,2,256]{4,2,3,1,0:T(8,128)(2,1)S(1)}, bf16[2,2,32,2,256]{4,2,3,1,0:T(8,128)(2,1)S(1)}, u32[]{:S(2)}, u32[]{:S(2)}) %collective-permute-start.15) | collective-permute-done | bytes 131104 | tf_op jit(solution)/shard_map/ppermute | solution.py:29
  148.2 3.5 %collective-permute-done.18 = bf16[2,32,2,512]{3,1,2,0:T(8,128)(2,1)S(1)} collective-permute-done((bf16[2,32,2,512]{3,1,2,0:T(8,128)(2,1)S(1)}, bf16[2,32,2,512]{3,1,2,0:T(8,128)(2,1)S(1)}, u32[]{:S(2)}, u32[]{:S(2)}) %collective-permute-start.18) | collective-permute-done | bytes 131104 | tf_op jit(solution)/shard_map/ppermute | solution.py:29
  151.8 2.9 %collective-permute-start.19 = (bf16[32,2,512]{2,0,1:T(8,128)(2,1)S(1)}, bf16[32,2,512]{2,0,1:T(8,128)(2,1)S(1)}, u32[]{:S(2)}, u32[]{:S(2)}) collective-permute-start(bf16[32,2,512]{2,0,1:T(8,128)(2,1)S(1)} %fusion.74), channel_id=1, source_target_pairs={{0,2},{1,3},{2,0},{3,1},{4,6},{5,7},{6,4},{7,5},{8,10},{9,11},{10,... | collective-permute-start | bytes 196616 | tf_op jit(solution)/shard_map/ppermute | solution.py:29
  154.7 2.3 %collective-permute-done.19 = bf16[32,2,512]{2,0,1:T(8,128)(2,1)S(1)} collective-permute-done((bf16[32,2,512]{2,0,1:T(8,128)(2,1)S(1)}, bf16[32,2,512]{2,0,1:T(8,128)(2,1)S(1)}, u32[]{:S(2)}, u32[]{:S(2)}) %collective-permute-start.19) | collective-permute-done | bytes 65568 | tf_op jit(solution)/shard_map/ppermute | solution.py:29
  (116 shorter events, 47.0 us)
Async XLA Ops:
  1.9 18.9 %copy-start.7 = (s32[1,256]{1,0:T(1,128)S(1)}, s32[1,256]{1,0:T(1,128)}, u32[]{:S(2)}) copy-start(s32[1,256]{1,0:T(1,128)} %param.9) | copy-start | bytes 3076
  1.9 20.1 %copy-start.5 = (bf16[1,256,1024]{2,1,0:T(8,128)(2,1)S(1)}, bf16[1,256,1024]{2,1,0:T(8,128)(2,1)}, u32[]{:S(2)}) copy-start(bf16[1,256,1024]{2,1,0:T(8,128)(2,1)} %param.8) | copy-start | bytes 1572868
  6.7 40.0 %collective-permute-start = (bf16[2,256,512]{2,1,0:T(8,128)(2,1)}, bf16[2,256,512]{2,1,0:T(8,128)(2,1)}, u32[]{:S(2)}, u32[]{:S(2)}) collective-permute-start(bf16[2,256,512]{2,1,0:T(8,128)(2,1)} %slice.120), channel_id=1, source_target_pairs={{0,16},{4,20},{8,24},{12,28},{1,17},{5,21},{9,25},{13,29},{2,18},{... | collective-permute-start | bytes 1572872 | tf_op jit(solution)/shard_map/ppermute | solution.py:16
  12.4 35.4 %collective-permute-start.1 = (bf16[2,256,512]{2,1,0:T(8,128)(2,1)}, bf16[2,256,512]{2,1,0:T(8,128)(2,1)}, u32[]{:S(2)}, u32[]{:S(2)}) collective-permute-start(bf16[2,256,512]{2,1,0:T(8,128)(2,1)} %slice.120), channel_id=1, source_target_pairs={{0,12},{4,16},{8,20},{12,24},{16,28},{1,13},{5,17},{9,21},{13,25},... | collective-permute-start | bytes 1572872 | tf_op jit(solution)/shard_map/ppermute | solution.py:16
  15.7 33.1 %collective-permute-start.2 = (bf16[2,256,512]{2,1,0:T(8,128)(2,1)}, bf16[2,256,512]{2,1,0:T(8,128)(2,1)}, u32[]{:S(2)}, u32[]{:S(2)}) collective-permute-start(bf16[2,256,512]{2,1,0:T(8,128)(2,1)} %slice.120), channel_id=1, source_target_pairs={{0,8},{4,12},{8,16},{12,20},{16,24},{20,28},{1,9},{5,13},{9,17},{1... | collective-permute-start | bytes 1572872 | tf_op jit(solution)/shard_map/ppermute | solution.py:16
  18.7 31.3 %collective-permute-start.3 = (bf16[2,256,512]{2,1,0:T(8,128)(2,1)}, bf16[2,256,512]{2,1,0:T(8,128)(2,1)}, u32[]{:S(2)}, u32[]{:S(2)}) collective-permute-start(bf16[2,256,512]{2,1,0:T(8,128)(2,1)} %slice.120), channel_id=1, source_target_pairs={{0,4},{4,8},{8,12},{12,16},{16,20},{20,24},{24,28},{1,5},{5,9},{9,... | collective-permute-start | bytes 1572872 | tf_op jit(solution)/shard_map/ppermute | solution.py:16
  22.0 4.8 %copy-start.1 = (bf16[1,256,1024]{2,1,0:T(8,128)(2,1)S(1)}, bf16[1,256,1024]{2,1,0:T(8,128)(2,1)}, u32[]{:S(2)}) copy-start(bf16[1,256,1024]{2,1,0:T(8,128)(2,1)} %param.6) | copy-start | bytes 1572868
  71.3 6.2 %collective-permute-start.4 = (bf16[2,2,2,2,40,2,512]{6,4,5,1,0,2,3:T(8,128)(2,1)S(1)}, bf16[2,2,2,2,40,2,512]{6,4,5,1,0,2,3:T(8,128)(2,1)S(1)}, u32[]{:S(2)}, u32[]{:S(2)}) collective-permute-start(bf16[2,2,2,2,40,2,512]{6,4,5,1,0,2,3:T(8,128)(2,1)S(1)} %fusion.32), channel_id=1, source_target_pairs={{0,4},{4,0},{8,12},{12,8},{16,20},{20,16},{24,28},{28,24},{1,5},{5... | collective-permute-start | bytes 3932168 | tf_op jit(solution)/shard_map/ppermute | solution.py:29
  78.0 17.1 %collective-permute-start.5 = (bf16[2,2,2,40,2,512]{5,3,4,1,0,2:T(8,128)(2,1)S(1)}, bf16[2,2,2,40,2,512]{5,3,4,1,0,2:T(8,128)(2,1)S(1)}, u32[]{:S(2)}, u32[]{:S(2)}) collective-permute-start(bf16[2,2,2,40,2,512]{5,3,4,1,0,2:T(8,128)(2,1)S(1)} %fusion.52), channel_id=1, source_target_pairs={{0,1},{1,0},{2,3},{3,2},{4,5},{5,4},{6,7},{7,6},{8,9},{9,8},{10,11... | collective-permute-start | bytes 1966088 | tf_op jit(solution)/shard_map/ppermute | solution.py:29
  79.8 18.3 %collective-permute-start.12 = (bf16[2,8,64,256]{3,2,1,0:T(8,128)(2,1)S(1)}, bf16[2,8,64,256]{3,2,1,0:T(8,128)(2,1)S(1)}, u32[]{:S(2)}, u32[]{:S(2)}) collective-permute-start(bf16[2,8,64,256]{3,2,1,0:T(8,128)(2,1)S(1)} %pad_maximum_fusion.4), channel_id=1, source_target_pairs={{16,0},{20,4},{24,8},{28,12},{17,1},{21,5},{25,9},{29,13},{18,2},{... | collective-permute-start | bytes 1572872 | tf_op jit(solution)/shard_map/ppermute | solution.py:16
  81.1 16.9 %collective-permute-start.11 = (bf16[2,8,64,256]{3,2,1,0:T(8,128)(2,1)S(1)}, bf16[2,8,64,256]{3,2,1,0:T(8,128)(2,1)S(1)}, u32[]{:S(2)}, u32[]{:S(2)}) collective-permute-start(bf16[2,8,64,256]{3,2,1,0:T(8,128)(2,1)S(1)} %pad_maximum_fusion.3), channel_id=1, source_target_pairs={{12,0},{16,4},{20,8},{24,12},{28,16},{13,1},{17,5},{21,9},{25,13},... | collective-permute-start | bytes 1572872 | tf_op jit(solution)/shard_map/ppermute | solution.py:16
  82.5 16.8 %collective-permute-start.10 = (bf16[2,8,64,256]{3,2,1,0:T(8,128)(2,1)S(1)}, bf16[2,8,64,256]{3,2,1,0:T(8,128)(2,1)S(1)}, u32[]{:S(2)}, u32[]{:S(2)}) collective-permute-start(bf16[2,8,64,256]{3,2,1,0:T(8,128)(2,1)S(1)} %pad_maximum_fusion.2), channel_id=1, source_target_pairs={{8,0},{12,4},{16,8},{20,12},{24,16},{28,20},{9,1},{13,5},{17,9},{2... | collective-permute-start | bytes 1572872 | tf_op jit(solution)/shard_map/ppermute | solution.py:16
  83.8 15.4 %collective-permute-start.9 = (bf16[2,8,64,256]{3,2,1,0:T(8,128)(2,1)S(1)}, bf16[2,8,64,256]{3,2,1,0:T(8,128)(2,1)S(1)}, u32[]{:S(2)}, u32[]{:S(2)}) collective-permute-start(bf16[2,8,64,256]{3,2,1,0:T(8,128)(2,1)S(1)} %pad_maximum_fusion.1), channel_id=1, source_target_pairs={{4,0},{8,4},{12,8},{16,12},{20,16},{24,20},{28,24},{5,1},{9,5},{13... | collective-permute-start | bytes 1572872 | tf_op jit(solution)/shard_map/ppermute | solution.py:16
  95.4 17.2 %collective-permute-start.6 = (bf16[2,2,40,2,512]{4,2,3,1,0:T(8,128)(2,1)S(1)}, bf16[2,2,40,2,512]{4,2,3,1,0:T(8,128)(2,1)S(1)}, u32[]{:S(2)}, u32[]{:S(2)}) collective-permute-start(bf16[2,2,40,2,512]{4,2,3,1,0:T(8,128)(2,1)S(1)} %fusion.58), channel_id=1, source_target_pairs={{0,2},{1,3},{2,0},{3,1},{4,6},{5,7},{6,4},{7,5},{8,10},{9,11},{10,... | collective-permute-start | bytes 983048 | tf_op jit(solution)/shard_map/ppermute | solution.py:29
  99.2 15.8 %copy-start.8 = (bf16[1024,4,512]{2,1,0:T(4,128)(2,1)S(1)}, bf16[1024,4,512]{2,1,0:T(4,128)(2,1)}, u32[]{:S(2)}) copy-start(bf16[1024,4,512]{2,1,0:T(4,128)(2,1)} %param.7) | copy-start | bytes 12582916
  112.7 5.6 %collective-permute-start.7 = (bf16[2,40,2,512]{3,1,2,0:T(8,128)(2,1)S(1)}, bf16[2,40,2,512]{3,1,2,0:T(8,128)(2,1)S(1)}, u32[]{:S(2)}, u32[]{:S(2)}) collective-permute-start(bf16[2,40,2,512]{3,1,2,0:T(8,128)(2,1)S(1)} %fusion.69), channel_id=1, source_target_pairs={{0,16},{4,20},{8,24},{12,28},{16,0},{20,4},{24,8},{28,12},{1,17},{... | collective-permute-start | bytes 491528 | tf_op jit(solution)/shard_map/ppermute | solution.py:29
  118.4 4.5 %collective-permute-start.8 = (bf16[40,2,512]{2,0,1:T(8,128)(2,1)S(1)}, bf16[40,2,512]{2,0,1:T(8,128)(2,1)S(1)}, u32[]{:S(2)}, u32[]{:S(2)}) collective-permute-start(bf16[40,2,512]{2,0,1:T(8,128)(2,1)S(1)} %fusion.73), channel_id=1, source_target_pairs={{0,8},{4,12},{8,0},{12,4},{16,24},{20,28},{24,16},{28,20},{1,9},{5... | collective-permute-start | bytes 245768 | tf_op jit(solution)/shard_map/ppermute | solution.py:29
  127.7 2.7 %collective-permute-start.13 = (bf16[2,2,2,2,32,2,512]{6,4,5,3,2,1,0:T(8,128)(2,1)S(1)}, bf16[2,2,2,2,32,2,512]{6,4,5,3,2,1,0:T(8,128)(2,1)S(1)}, u32[]{:S(2)}, u32[]{:S(2)}) collective-permute-start(bf16[2,2,2,2,32,2,512]{6,4,5,3,2,1,0:T(8,128)(2,1)S(1)} %fusion.47), channel_id=1, source_target_pairs={{0,4},{4,0},{8,12},{12,8},{16,20},{20,16},{24,28},{28,24},{1,5},{5... | collective-permute-start | bytes 3145736 | tf_op jit(solution)/shard_map/ppermute | solution.py:29
  131.2 8.7 %collective-permute-start.14 = (bf16[2,2,2,32,2,256]{5,3,4,2,1,0:T(8,128)(2,1)S(1)}, bf16[2,2,2,32,2,256]{5,3,4,2,1,0:T(8,128)(2,1)S(1)}, u32[]{:S(2)}, u32[]{:S(2)}) collective-permute-start(bf16[2,2,2,32,2,256]{5,3,4,2,1,0:T(8,128)(2,1)S(1)} %fusion.59), channel_id=1, source_target_pairs={{0,16},{4,20},{8,24},{12,28},{16,0},{20,4},{24,8},{28,12},{1,17},{... | collective-permute-start | bytes 786440 | tf_op jit(solution)/shard_map/ppermute | solution.py:29
  133.3 8.1 %collective-permute-start.16 = (bf16[2,2,2,32,2,256]{5,3,4,2,1,0:T(8,128)(2,1)S(1)}, bf16[2,2,2,32,2,256]{5,3,4,2,1,0:T(8,128)(2,1)S(1)}, u32[]{:S(2)}, u32[]{:S(2)}) collective-permute-start(bf16[2,2,2,32,2,256]{5,3,4,2,1,0:T(8,128)(2,1)S(1)} %fusion.60), channel_id=1, source_target_pairs={{0,8},{4,12},{8,0},{12,4},{16,24},{20,28},{24,16},{28,20},{1,9},{5... | collective-permute-start | bytes 786440 | tf_op jit(solution)/shard_map/ppermute | solution.py:29
  140.0 5.1 %collective-permute-start.15 = (bf16[2,2,32,2,256]{4,2,3,1,0:T(8,128)(2,1)S(1)}, bf16[2,2,32,2,256]{4,2,3,1,0:T(8,128)(2,1)S(1)}, u32[]{:S(2)}, u32[]{:S(2)}) collective-permute-start(bf16[2,2,32,2,256]{4,2,3,1,0:T(8,128)(2,1)S(1)} %fusion.70), channel_id=1, source_target_pairs={{0,8},{4,12},{8,0},{12,4},{16,24},{20,28},{24,16},{28,20},{1,9},{5... | collective-permute-start | bytes 393224 | tf_op jit(solution)/shard_map/ppermute | solution.py:29
  141.6 5.0 %collective-permute-start.17 = (bf16[2,2,32,2,256]{4,2,3,1,0:T(8,128)(2,1)S(1)}, bf16[2,2,32,2,256]{4,2,3,1,0:T(8,128)(2,1)S(1)}, u32[]{:S(2)}, u32[]{:S(2)}) collective-permute-start(bf16[2,2,32,2,256]{4,2,3,1,0:T(8,128)(2,1)S(1)} %fusion.71), channel_id=1, source_target_pairs={{0,16},{4,20},{8,24},{12,28},{16,0},{20,4},{24,8},{28,12},{1,17},{... | collective-permute-start | bytes 393224 | tf_op jit(solution)/shard_map/ppermute | solution.py:29
  146.7 5.0 %collective-permute-start.18 = (bf16[2,32,2,512]{3,1,2,0:T(8,128)(2,1)S(1)}, bf16[2,32,2,512]{3,1,2,0:T(8,128)(2,1)S(1)}, u32[]{:S(2)}, u32[]{:S(2)}) collective-permute-start(bf16[2,32,2,512]{3,1,2,0:T(8,128)(2,1)S(1)} %fusion.72), channel_id=1, source_target_pairs={{0,1},{1,0},{2,3},{3,2},{4,5},{5,4},{6,7},{7,6},{8,9},{9,8},{10,11... | collective-permute-start | bytes 393224 | tf_op jit(solution)/shard_map/ppermute | solution.py:29
  151.8 5.2 %collective-permute-start.19 = (bf16[32,2,512]{2,0,1:T(8,128)(2,1)S(1)}, bf16[32,2,512]{2,0,1:T(8,128)(2,1)S(1)}, u32[]{:S(2)}, u32[]{:S(2)}) collective-permute-start(bf16[32,2,512]{2,0,1:T(8,128)(2,1)S(1)} %fusion.74), channel_id=1, source_target_pairs={{0,2},{1,3},{2,0},{3,1},{4,6},{5,7},{6,4},{7,5},{8,10},{9,11},{10,... | collective-permute-start | bytes 196616 | tf_op jit(solution)/shard_map/ppermute | solution.py:29
  (6 other events, 18.2 us)

commit v22 on v21

--- a/solution.py
+++ b/solution.py
@@ -102,7 +102,7 @@
         jnp.einsum("qgc,kgc->gqk", queries, keys_blk, preferred_element_type=jnp.float32)
         * inv_scale
     )
-    exp_terms = jnp.exp(scores) * valid[None]
+    exp_terms = jnp.where(valid[None], jnp.exp(scores), 0.0)
     probs = exp_terms / jnp.sum(exp_terms, axis=-1, keepdims=True)
     probs_low = probs.astype(jnp.bfloat16)
     attended = jnp.einsum(
@@ -159,7 +159,7 @@
     key_idx = jnp.arange(key_len, dtype=jnp.int32)[None, :]
     offsets = query_idx - key_idx + span * rows
     band = (offsets >= 0) & (offsets < WIN)
-    valid = (band & (key_idx >= span * rows - base)).astype(jnp.float32)
+    valid = band & (key_idx >= span * rows - base)
     attended, grad_query, grad_key, grad_value = band_block(
         queries.reshape(rows, HEADS, HSIZE),
         extended[0].reshape(key_len, HEADS, HSIZE),

time: 159 us -> 160 us (level)
  matrix products: 28.8 us -> 30.9 us
    unnamed x24 -> x26, local copies, waits for them, and re-layouts: 7.02 us -> 7.03 us
  transfers between devices with their start and end apart: 20 -> 20, of which waited for: 14 -> 13; matrix products, arithmetic and copies ran while one was open for 14% -> 14% of each run, Pallas kernels for 0% -> 0%
where the time goes in v22:
time: 160 us; the launch traced here: 159 us
  waiting for transfers between devices  62.3 us (39%)
  starting transfers between devices  38 us (24%)
  matrix products  30.9 us (19%)
  local copies, waits for them, and re-layouts  14.6 us (9%)
  other arithmetic  10.7 us (7%)
  between operations  2.7 us (2%)
    ppermute x12, waiting for transfers between devices, halve(): lax.ppermute(send.astype(send_type), axis, pairs).astype(keep.dtype)  47.1 us
    ppermute x8, starting transfers between devices, shifted(): return lax.ppermute(value, axis, pairs)  19.5 us
    ppermute x12, starting transfers between devices, halve(): lax.ppermute(send.astype(send_type), axis, pairs).astype(keep.dtype)  18.6 us
    ppermute x8, waiting for transfers between devices, shifted(): return lax.ppermute(value, axis, pairs)  15.2 us
    unnamed x26, local copies, waits for them, and re-layouts  7.03 us
    dot_general x1, matrix products, band_block(): jnp.einsum('qgc,kgc->gqk', grad_attn, values_blk, preferred_element_type=...  4.84 us
    dot_general x1, matrix products, shards(): jnp.einsum('rd,dwh->wrh', grad_out, weights, preferred_element_type=jnp.f...  4.83 us
    dot_general x1, matrix products, band_block(): jnp.einsum('qgc,kgc->gqk', queries, keys_blk, preferred_element_type=jnp....  4.09 us
  transfers between devices with their start and end apart: 20, of which 13 were waited for; matrix products, arithmetic and copies ran while one was open for 14% of the time, Pallas kernels for 0%

profile of v22, /device:TPU:0, one launch (start us, length us, event | category | flops | bytes accessed | tf_op | source)
XLA Modules:
  0.0 159.3 jit_solution(13769431116073623298)
XLA Ops:
  1.9 4.0 %fusion.21 = bf16[4,256,512]{2,1,0:T(8,128)(2,1)S(1)} fusion(bf16[1024,4,512]{2,1,0:T(4,128)(2,1)} %param.7, bf16[1,256,1024]{2,1,0:T(8,128)(2,1)} %param.6, f32[256]{0:T(256)S(1)} %add_rsqrt_fusion), kind=kOutput, calls=%fused_computation.24 | convolution fusion | flops 1075052544 | bytes 5768192 | tf_op jit(solution)/shard_map/rd,dwh->wrh/dot_general | solution.py:142
  6.7 5.7 %collective-permute-start = (bf16[2,256,512]{2,1,0:T(8,128)(2,1)}, bf16[2,256,512]{2,1,0:T(8,128)(2,1)}, u32[]{:S(2)}, u32[]{:S(2)}) collective-permute-start(bf16[2,256,512]{2,1,0:T(8,128)(2,1)} %slice.120), channel_id=1, source_target_pairs={{0,16},{4,20},{8,24},{12,28},{1,17},{5,21},{9,25},{13,29},{2,18},{... | collective-permute-start | bytes 1572872 | tf_op jit(solution)/shard_map/ppermute | solution.py:16
  12.4 3.4 %collective-permute-start.1 = (bf16[2,256,512]{2,1,0:T(8,128)(2,1)}, bf16[2,256,512]{2,1,0:T(8,128)(2,1)}, u32[]{:S(2)}, u32[]{:S(2)}) collective-permute-start(bf16[2,256,512]{2,1,0:T(8,128)(2,1)} %slice.120), channel_id=1, source_target_pairs={{0,12},{4,16},{8,20},{12,24},{16,28},{1,13},{5,17},{9,21},{13,25},... | collective-permute-start | bytes 1572872 | tf_op jit(solution)/shard_map/ppermute | solution.py:16
  15.7 2.9 %collective-permute-start.2 = (bf16[2,256,512]{2,1,0:T(8,128)(2,1)}, bf16[2,256,512]{2,1,0:T(8,128)(2,1)}, u32[]{:S(2)}, u32[]{:S(2)}) collective-permute-start(bf16[2,256,512]{2,1,0:T(8,128)(2,1)} %slice.120), channel_id=1, source_target_pairs={{0,8},{4,12},{8,16},{12,20},{16,24},{20,28},{1,9},{5,13},{9,17},{1... | collective-permute-start | bytes 1572872 | tf_op jit(solution)/shard_map/ppermute | solution.py:16
  21.6 4.8 %fusion.18 = bf16[4,256,512]{2,1,0:T(8,128)(2,1)} fusion(bf16[1024,4,512]{2,1,0:T(4,128)(2,1)} %param.7, bf16[1,256,1024]{2,1,0:T(8,128)(2,1)S(1)} %copy-done.5, pred[256]{0:T(512)(128)(4,1)S(1)} %compare_reduce_fusion), kind=kOutput, calls=%fused_computation.23 | convolution fusion | flops 1074528256 | bytes 5767424 | tf_op jit(solution)/shard_map/rd,dwh->wrh/dot_general | solution.py:154
  33.0 13.6 %collective-permute-done = bf16[2,256,512]{2,1,0:T(8,128)(2,1)} collective-permute-done((bf16[2,256,512]{2,1,0:T(8,128)(2,1)}, bf16[2,256,512]{2,1,0:T(8,128)(2,1)}, u32[]{:S(2)}, u32[]{:S(2)}) %collective-permute-start) | collective-permute-done | bytes 524320 | tf_op jit(solution)/shard_map/ppermute | solution.py:16
  54.1 4.1 %fusion.1 = (f32[8,256]{1,0:T(8,128)S(1)}, f32[8,256,1280]{2,1,0:T(8,128)S(1)}) fusion(pred[256,1280]{1,0:T(8,128)(4,1)} %fusion.36, bf16[256,8,64]{0,2,1:T(8,128)(2,1)S(1)} %bitcast.197, bf16[1280,8,64]{0,2,1:T(8,128)(2,1)S(1)} %bitcast.189), kind=kOutput, calls=%fused_computation.3 | convolution fusion | flops 343406592 | bytes 12394496 | tf_op jit(solution)/shard_map/qgc,kgc->gqk/dot_general | solution.py:102
  58.3 3.1 %multiply_reduce_fusion = (f32[256,8]{0,1:T(8,128)S(1)}, bf16[8,64,256]{2,1,0:T(8,128)(2,1)S(1)}) fusion(bf16[256,8,64]{0,2,1:T(8,128)(2,1)S(1)} %bitcast.202, bf16[1280,8,64]{0,2,1:T(8,128)(2,1)S(1)} %bitcast.199, f32[8,256]{1,0:T(8,128)S(1)} %get-tuple-element.34, f32[8,256,1280]{2,1,0:T(8,128)S(1)} %get-tuple-element.35, pred[256,1280]{1,0:T(8,128)(4,1)S(1)} %copy-done.6), kind=kOutput, calls=%fused_computation.78 | convolution fusion | flops 346683392 | bytes 12664832 | tf_op jit(solution)/shard_map/gqk,kgc->qgc/dot_general | solution.py:108
  61.4 4.8 %multiply_convert_fusion = bf16[8,256,1280]{2,1,0:T(8,128)(2,1)S(1)} fusion(bf16[256,8,64]{0,2,1:T(8,128)(2,1)S(1)} %bitcast.203, bf16[1280,8,64]{0,2,1:T(8,128)(2,1)S(1)} %bitcast.200, f32[8,256]{1,0:T(8,128)S(1)} %bitcast.206, f32[8,256]{1,0:T(8,128)S(1)} %get-tuple-element.34, f32[8,256,1280]{2,1,0:T(8,128)S(1)} %get-tuple-element.35, ...), kind=kOutput, calls=%fused_computation | convolution fusion | flops 353894400 | bytes 17645568 | tf_op jit(solution)/shard_map/qgc,kgc->gqk/dot_general | solution.py:112
  71.7 3.6 %collective-permute-start.4 = (bf16[2,2,2,2,40,2,512]{6,4,5,1,0,2,3:T(8,128)(2,1)S(1)}, bf16[2,2,2,2,40,2,512]{6,4,5,1,0,2,3:T(8,128)(2,1)S(1)}, u32[]{:S(2)}, u32[]{:S(2)}) collective-permute-start(bf16[2,2,2,2,40,2,512]{6,4,5,1,0,2,3:T(8,128)(2,1)S(1)} %fusion.32), channel_id=1, source_target_pairs={{0,4},{4,0},{8,12},{12,8},{16,20},{20,16},{24,28},{28,24},{1,5},{5... | collective-permute-start | bytes 3932168 | tf_op jit(solution)/shard_map/ppermute | solution.py:29
  75.2 2.9 %fusion.89 = (bf16[8,64,1280]{2,1,0:T(8,128)(2,1)S(1)}, f32[8,64,1280]{2,1,0:T(8,128)S(1)}) fusion(bf16[256,8,64]{0,2,1:T(8,128)(2,1)S(1)} %bitcast.204, f32[8,256]{1,0:T(8,128)S(1)} %get-tuple-element.34, f32[8,256,1280]{2,1,0:T(8,128)S(1)} %get-tuple-element.35, pred[256,1280]{1,0:T(8,128)(4,1)S(1)} %copy-done.6), kind=kOutput, calls=%fused_computation.162 | convolution fusion | flops 346685440 | bytes 15015936 | tf_op jit(solution)/shard_map/gqk,qgc->gck/dot_general | solution.py:122
  86.4 9.3 %collective-permute-done.5 = bf16[2,2,2,40,2,512]{5,3,4,1,0,2:T(8,128)(2,1)S(1)} collective-permute-done((bf16[2,2,2,40,2,512]{5,3,4,1,0,2:T(8,128)(2,1)S(1)}, bf16[2,2,2,40,2,512]{5,3,4,1,0,2:T(8,128)(2,1)S(1)}, u32[]{:S(2)}, u32[]{:S(2)}) %collective-permute-start.5) | collective-permute-done | bytes 655392 | tf_op jit(solution)/shard_map/ppermute | solution.py:29
  96.0 2.7 %collective-permute-start.6 = (bf16[2,2,40,2,512]{4,2,3,1,0:T(8,128)(2,1)S(1)}, bf16[2,2,40,2,512]{4,2,3,1,0:T(8,128)(2,1)S(1)}, u32[]{:S(2)}, u32[]{:S(2)}) collective-permute-start(bf16[2,2,40,2,512]{4,2,3,1,0:T(8,128)(2,1)S(1)} %fusion.57), channel_id=1, source_target_pairs={{0,2},{1,3},{2,0},{3,1},{4,6},{5,7},{6,4},{7,5},{8,10},{9,11},{10,... | collective-permute-start | bytes 983048 | tf_op jit(solution)/shard_map/ppermute | solution.py:29
  100.8 12.0 %collective-permute-done.6 = bf16[2,2,40,2,512]{4,2,3,1,0:T(8,128)(2,1)S(1)} collective-permute-done((bf16[2,2,40,2,512]{4,2,3,1,0:T(8,128)(2,1)S(1)}, bf16[2,2,40,2,512]{4,2,3,1,0:T(8,128)(2,1)S(1)}, u32[]{:S(2)}, u32[]{:S(2)}) %collective-permute-start.6) | collective-permute-done | bytes 327712 | tf_op jit(solution)/shard_map/ppermute | solution.py:29
  112.9 3.5 %collective-permute-start.7 = (bf16[2,40,2,512]{3,1,2,0:T(8,128)(2,1)S(1)}, bf16[2,40,2,512]{3,1,2,0:T(8,128)(2,1)S(1)}, u32[]{:S(2)}, u32[]{:S(2)}) collective-permute-start(bf16[2,40,2,512]{3,1,2,0:T(8,128)(2,1)S(1)} %fusion.68), channel_id=1, source_target_pairs={{0,16},{4,20},{8,24},{12,28},{16,0},{20,4},{24,8},{28,12},{1,17},{... | collective-permute-start | bytes 491528 | tf_op jit(solution)/shard_map/ppermute | solution.py:29
  116.4 2.7 %fusion.40 = (f32[256]{0:T(256)S(1)}, f32[256,1024]{1,0:T(8,128)}) fusion(bf16[1,256,1024]{2,1,0:T(8,128)(2,1)S(1)} %copy-done.1, f32[256]{0:T(256)S(1)} %add_rsqrt_fusion, bf16[4,256,512]{1,2,0:T(8,128)(2,1)S(1)} %bitcast.201, bf16[1024,4,512]{2,1,0:T(4,128)(2,1)S(1)} %copy-done.9), kind=kOutput, calls=%fused_computation.43 | convolution fusion | flops 1074790144 | bytes 6817792 | tf_op jit(solution)/shard_map/wrh,dwh->rd/dot_general | solution.py:209
  119.9 4.4 %collective-permute-done.8 = bf16[40,2,512]{2,0,1:T(8,128)(2,1)S(1)} collective-permute-done((bf16[40,2,512]{2,0,1:T(8,128)(2,1)S(1)}, bf16[40,2,512]{2,0,1:T(8,128)(2,1)S(1)}, u32[]{:S(2)}, u32[]{:S(2)}) %collective-permute-start.8) | collective-permute-done | bytes 81952 | tf_op jit(solution)/shard_map/ppermute | solution.py:29
  125.6 2.3 %fusion.66 = (bf16[1024,256]{0,1:T(8,128)(2,1)S(1)}, bf16[1,256,1024]{2,1,0:T(8,128)(2,1)}) fusion(f32[256]{0:T(256)S(1)} %add_rsqrt_fusion, bf16[1,256,1024]{2,1,0:T(8,128)(2,1)S(1)} %copy-done.1, f32[256,1024]{1,0:T(8,128)} %get-tuple-element.43, f32[256]{0:T(256)S(1)} %broadcast_multiply_fusion.1, f32[256]{0:T(256)S(1)} %broadcast_multiply_fusion), kind=kLoop, calls=%fused_computation.105 | loop fusion | flops 1835008 | bytes 2624512 | tf_op jit(solution)/shard_map/rd,wgcr->dwgc/dot_general | solution.py:214
  129.2 2.6 %collective-permute-done.13 = bf16[2,2,2,2,32,2,512]{6,4,5,3,2,1,0:T(8,128)(2,1)S(1)} collective-permute-done((bf16[2,2,2,2,32,2,512]{6,4,5,3,2,1,0:T(8,128)(2,1)S(1)}, bf16[2,2,2,2,32,2,512]{6,4,5,3,2,1,0:T(8,128)(2,1)S(1)}, u32[]{:S(2)}, u32[]{:S(2)}) %collective-permute-start.13) | collective-permute-done | bytes 1048608 | tf_op jit(solution)/shard_map/ppermute | solution.py:29
  134.7 6.5 %collective-permute-done.14 = bf16[2,2,2,32,2,256]{5,3,4,2,1,0:T(8,128)(2,1)S(1)} collective-permute-done((bf16[2,2,2,32,2,256]{5,3,4,2,1,0:T(8,128)(2,1)S(1)}, bf16[2,2,2,32,2,256]{5,3,4,2,1,0:T(8,128)(2,1)S(1)}, u32[]{:S(2)}, u32[]{:S(2)}) %collective-permute-start.14) | collective-permute-done | bytes 262176 | tf_op jit(solution)/shard_map/ppermute | solution.py:29
  143.4 3.0 %collective-permute-done.15 = bf16[2,2,32,2,256]{4,2,3,1,0:T(8,128)(2,1)S(1)} collective-permute-done((bf16[2,2,32,2,256]{4,2,3,1,0:T(8,128)(2,1)S(1)}, bf16[2,2,32,2,256]{4,2,3,1,0:T(8,128)(2,1)S(1)}, u32[]{:S(2)}, u32[]{:S(2)}) %collective-permute-start.15) | collective-permute-done | bytes 131104 | tf_op jit(solution)/shard_map/ppermute | solution.py:29
  149.6 3.5 %collective-permute-done.18 = bf16[2,32,2,512]{3,1,2,0:T(8,128)(2,1)S(1)} collective-permute-done((bf16[2,32,2,512]{3,1,2,0:T(8,128)(2,1)S(1)}, bf16[2,32,2,512]{3,1,2,0:T(8,128)(2,1)S(1)}, u32[]{:S(2)}, u32[]{:S(2)}) %collective-permute-start.18) | collective-permute-done | bytes 131104 | tf_op jit(solution)/shard_map/ppermute | solution.py:29
  153.1 2.9 %collective-permute-start.19 = (bf16[32,2,512]{2,0,1:T(8,128)(2,1)S(1)}, bf16[32,2,512]{2,0,1:T(8,128)(2,1)S(1)}, u32[]{:S(2)}, u32[]{:S(2)}) collective-permute-start(bf16[32,2,512]{2,0,1:T(8,128)(2,1)S(1)} %fusion.73), channel_id=1, source_target_pairs={{0,2},{1,3},{2,0},{3,1},{4,6},{5,7},{6,4},{7,5},{8,10},{9,11},{10,... | collective-permute-start | bytes 196616 | tf_op jit(solution)/shard_map/ppermute | solution.py:29
  156.1 2.3 %collective-permute-done.19 = bf16[32,2,512]{2,0,1:T(8,128)(2,1)S(1)} collective-permute-done((bf16[32,2,512]{2,0,1:T(8,128)(2,1)S(1)}, bf16[32,2,512]{2,0,1:T(8,128)(2,1)S(1)}, u32[]{:S(2)}, u32[]{:S(2)}) %collective-permute-start.19) | collective-permute-done | bytes 65568 | tf_op jit(solution)/shard_map/ppermute | solution.py:29
  (118 shorter events, 45.9 us)
Async XLA Ops:
  1.9 18.9 %copy-start.8 = (s32[1,256]{1,0:T(1,128)S(1)}, s32[1,256]{1,0:T(1,128)}, u32[]{:S(2)}) copy-start(s32[1,256]{1,0:T(1,128)} %param.9) | copy-start | bytes 3076
  1.9 19.8 %copy-start.5 = (bf16[1,256,1024]{2,1,0:T(8,128)(2,1)S(1)}, bf16[1,256,1024]{2,1,0:T(8,128)(2,1)}, u32[]{:S(2)}) copy-start(bf16[1,256,1024]{2,1,0:T(8,128)(2,1)} %param.8) | copy-start | bytes 1572868
  6.7 40.0 %collective-permute-start = (bf16[2,256,512]{2,1,0:T(8,128)(2,1)}, bf16[2,256,512]{2,1,0:T(8,128)(2,1)}, u32[]{:S(2)}, u32[]{:S(2)}) collective-permute-start(bf16[2,256,512]{2,1,0:T(8,128)(2,1)} %slice.120), channel_id=1, source_target_pairs={{0,16},{4,20},{8,24},{12,28},{1,17},{5,21},{9,25},{13,29},{2,18},{... | collective-permute-start | bytes 1572872 | tf_op jit(solution)/shard_map/ppermute | solution.py:16
  12.4 35.4 %collective-permute-start.1 = (bf16[2,256,512]{2,1,0:T(8,128)(2,1)}, bf16[2,256,512]{2,1,0:T(8,128)(2,1)}, u32[]{:S(2)}, u32[]{:S(2)}) collective-permute-start(bf16[2,256,512]{2,1,0:T(8,128)(2,1)} %slice.120), channel_id=1, source_target_pairs={{0,12},{4,16},{8,20},{12,24},{16,28},{1,13},{5,17},{9,21},{13,25},... | collective-permute-start | bytes 1572872 | tf_op jit(solution)/shard_map/ppermute | solution.py:16
  15.7 33.1 %collective-permute-start.2 = (bf16[2,256,512]{2,1,0:T(8,128)(2,1)}, bf16[2,256,512]{2,1,0:T(8,128)(2,1)}, u32[]{:S(2)}, u32[]{:S(2)}) collective-permute-start(bf16[2,256,512]{2,1,0:T(8,128)(2,1)} %slice.120), channel_id=1, source_target_pairs={{0,8},{4,12},{8,16},{12,20},{16,24},{20,28},{1,9},{5,13},{9,17},{1... | collective-permute-start | bytes 1572872 | tf_op jit(solution)/shard_map/ppermute | solution.py:16
  18.7 31.3 %collective-permute-start.3 = (bf16[2,256,512]{2,1,0:T(8,128)(2,1)}, bf16[2,256,512]{2,1,0:T(8,128)(2,1)}, u32[]{:S(2)}, u32[]{:S(2)}) collective-permute-start(bf16[2,256,512]{2,1,0:T(8,128)(2,1)} %slice.120), channel_id=1, source_target_pairs={{0,4},{4,8},{8,12},{12,16},{16,20},{20,24},{24,28},{1,5},{5,9},{9,... | collective-permute-start | bytes 1572872 | tf_op jit(solution)/shard_map/ppermute | solution.py:16
  21.6 4.8 %copy-start.1 = (bf16[1,256,1024]{2,1,0:T(8,128)(2,1)S(1)}, bf16[1,256,1024]{2,1,0:T(8,128)(2,1)}, u32[]{:S(2)}) copy-start(bf16[1,256,1024]{2,1,0:T(8,128)(2,1)} %param.6) | copy-start | bytes 1572868
  71.7 6.8 %collective-permute-start.4 = (bf16[2,2,2,2,40,2,512]{6,4,5,1,0,2,3:T(8,128)(2,1)S(1)}, bf16[2,2,2,2,40,2,512]{6,4,5,1,0,2,3:T(8,128)(2,1)S(1)}, u32[]{:S(2)}, u32[]{:S(2)}) collective-permute-start(bf16[2,2,2,2,40,2,512]{6,4,5,1,0,2,3:T(8,128)(2,1)S(1)} %fusion.32), channel_id=1, source_target_pairs={{0,4},{4,0},{8,12},{12,8},{16,20},{20,16},{24,28},{28,24},{1,5},{5... | collective-permute-start | bytes 3932168 | tf_op jit(solution)/shard_map/ppermute | solution.py:29
  79.0 16.7 %collective-permute-start.5 = (bf16[2,2,2,40,2,512]{5,3,4,1,0,2:T(8,128)(2,1)S(1)}, bf16[2,2,2,40,2,512]{5,3,4,1,0,2:T(8,128)(2,1)S(1)}, u32[]{:S(2)}, u32[]{:S(2)}) collective-permute-start(bf16[2,2,2,40,2,512]{5,3,4,1,0,2:T(8,128)(2,1)S(1)} %fusion.51), channel_id=1, source_target_pairs={{0,1},{1,0},{2,3},{3,2},{4,5},{5,4},{6,7},{7,6},{8,9},{9,8},{10,11... | collective-permute-start | bytes 1966088 | tf_op jit(solution)/shard_map/ppermute | solution.py:29
  80.7 17.9 %collective-permute-start.12 = (bf16[2,8,64,256]{3,2,1,0:T(8,128)(2,1)S(1)}, bf16[2,8,64,256]{3,2,1,0:T(8,128)(2,1)S(1)}, u32[]{:S(2)}, u32[]{:S(2)}) collective-permute-start(bf16[2,8,64,256]{3,2,1,0:T(8,128)(2,1)S(1)} %pad_maximum_fusion.4), channel_id=1, source_target_pairs={{16,0},{20,4},{24,8},{28,12},{17,1},{21,5},{25,9},{29,13},{18,2},{... | collective-permute-start | bytes 1572872 | tf_op jit(solution)/shard_map/ppermute | solution.py:16
  82.1 16.6 %collective-permute-start.11 = (bf16[2,8,64,256]{3,2,1,0:T(8,128)(2,1)S(1)}, bf16[2,8,64,256]{3,2,1,0:T(8,128)(2,1)S(1)}, u32[]{:S(2)}, u32[]{:S(2)}) collective-permute-start(bf16[2,8,64,256]{3,2,1,0:T(8,128)(2,1)S(1)} %pad_maximum_fusion.3), channel_id=1, source_target_pairs={{12,0},{16,4},{20,8},{24,12},{28,16},{13,1},{17,5},{21,9},{25,13},... | collective-permute-start | bytes 1572872 | tf_op jit(solution)/shard_map/ppermute | solution.py:16
  83.4 16.8 %collective-permute-start.10 = (bf16[2,8,64,256]{3,2,1,0:T(8,128)(2,1)S(1)}, bf16[2,8,64,256]{3,2,1,0:T(8,128)(2,1)S(1)}, u32[]{:S(2)}, u32[]{:S(2)}) collective-permute-start(bf16[2,8,64,256]{3,2,1,0:T(8,128)(2,1)S(1)} %pad_maximum_fusion.2), channel_id=1, source_target_pairs={{8,0},{12,4},{16,8},{20,12},{24,16},{28,20},{9,1},{13,5},{17,9},{2... | collective-permute-start | bytes 1572872 | tf_op jit(solution)/shard_map/ppermute | solution.py:16
  84.8 15.4 %collective-permute-start.9 = (bf16[2,8,64,256]{3,2,1,0:T(8,128)(2,1)S(1)}, bf16[2,8,64,256]{3,2,1,0:T(8,128)(2,1)S(1)}, u32[]{:S(2)}, u32[]{:S(2)}) collective-permute-start(bf16[2,8,64,256]{3,2,1,0:T(8,128)(2,1)S(1)} %pad_maximum_fusion.1), channel_id=1, source_target_pairs={{4,0},{8,4},{12,8},{16,12},{20,16},{24,20},{28,24},{5,1},{9,5},{13... | collective-permute-start | bytes 1572872 | tf_op jit(solution)/shard_map/ppermute | solution.py:16
  96.0 16.8 %collective-permute-start.6 = (bf16[2,2,40,2,512]{4,2,3,1,0:T(8,128)(2,1)S(1)}, bf16[2,2,40,2,512]{4,2,3,1,0:T(8,128)(2,1)S(1)}, u32[]{:S(2)}, u32[]{:S(2)}) collective-permute-start(bf16[2,2,40,2,512]{4,2,3,1,0:T(8,128)(2,1)S(1)} %fusion.57), channel_id=1, source_target_pairs={{0,2},{1,3},{2,0},{3,1},{4,6},{5,7},{6,4},{7,5},{8,10},{9,11},{10,... | collective-permute-start | bytes 983048 | tf_op jit(solution)/shard_map/ppermute | solution.py:29
  100.2 16.2 %copy-start.9 = (bf16[1024,4,512]{2,1,0:T(4,128)(2,1)S(1)}, bf16[1024,4,512]{2,1,0:T(4,128)(2,1)}, u32[]{:S(2)}) copy-start(bf16[1024,4,512]{2,1,0:T(4,128)(2,1)} %param.7) | copy-start | bytes 12582916
  112.9 6.8 %collective-permute-start.7 = (bf16[2,40,2,512]{3,1,2,0:T(8,128)(2,1)S(1)}, bf16[2,40,2,512]{3,1,2,0:T(8,128)(2,1)S(1)}, u32[]{:S(2)}, u32[]{:S(2)}) collective-permute-start(bf16[2,40,2,512]{3,1,2,0:T(8,128)(2,1)S(1)} %fusion.68), channel_id=1, source_target_pairs={{0,16},{4,20},{8,24},{12,28},{16,0},{20,4},{24,8},{28,12},{1,17},{... | collective-permute-start | bytes 491528 | tf_op jit(solution)/shard_map/ppermute | solution.py:29
  119.8 4.5 %collective-permute-start.8 = (bf16[40,2,512]{2,0,1:T(8,128)(2,1)S(1)}, bf16[40,2,512]{2,0,1:T(8,128)(2,1)S(1)}, u32[]{:S(2)}, u32[]{:S(2)}) collective-permute-start(bf16[40,2,512]{2,0,1:T(8,128)(2,1)S(1)} %fusion.72), channel_id=1, source_target_pairs={{0,8},{4,12},{8,0},{12,4},{16,24},{20,28},{24,16},{28,20},{1,9},{5... | collective-permute-start | bytes 245768 | tf_op jit(solution)/shard_map/ppermute | solution.py:29
  129.1 2.7 %collective-permute-start.13 = (bf16[2,2,2,2,32,2,512]{6,4,5,3,2,1,0:T(8,128)(2,1)S(1)}, bf16[2,2,2,2,32,2,512]{6,4,5,3,2,1,0:T(8,128)(2,1)S(1)}, u32[]{:S(2)}, u32[]{:S(2)}) collective-permute-start(bf16[2,2,2,2,32,2,512]{6,4,5,3,2,1,0:T(8,128)(2,1)S(1)} %fusion.46), channel_id=1, source_target_pairs={{0,4},{4,0},{8,12},{12,8},{16,20},{20,16},{24,28},{28,24},{1,5},{5... | collective-permute-start | bytes 3145736 | tf_op jit(solution)/shard_map/ppermute | solution.py:29
  132.6 8.7 %collective-permute-start.14 = (bf16[2,2,2,32,2,256]{5,3,4,2,1,0:T(8,128)(2,1)S(1)}, bf16[2,2,2,32,2,256]{5,3,4,2,1,0:T(8,128)(2,1)S(1)}, u32[]{:S(2)}, u32[]{:S(2)}) collective-permute-start(bf16[2,2,2,32,2,256]{5,3,4,2,1,0:T(8,128)(2,1)S(1)} %fusion.58), channel_id=1, source_target_pairs={{0,16},{4,20},{8,24},{12,28},{16,0},{20,4},{24,8},{28,12},{1,17},{... | collective-permute-start | bytes 786440 | tf_op jit(solution)/shard_map/ppermute | solution.py:29
  134.7 8.1 %collective-permute-start.16 = (bf16[2,2,2,32,2,256]{5,3,4,2,1,0:T(8,128)(2,1)S(1)}, bf16[2,2,2,32,2,256]{5,3,4,2,1,0:T(8,128)(2,1)S(1)}, u32[]{:S(2)}, u32[]{:S(2)}) collective-permute-start(bf16[2,2,2,32,2,256]{5,3,4,2,1,0:T(8,128)(2,1)S(1)} %fusion.59), channel_id=1, source_target_pairs={{0,8},{4,12},{8,0},{12,4},{16,24},{20,28},{24,16},{28,20},{1,9},{5... | collective-permute-start | bytes 786440 | tf_op jit(solution)/shard_map/ppermute | solution.py:29
  141.4 5.1 %collective-permute-start.15 = (bf16[2,2,32,2,256]{4,2,3,1,0:T(8,128)(2,1)S(1)}, bf16[2,2,32,2,256]{4,2,3,1,0:T(8,128)(2,1)S(1)}, u32[]{:S(2)}, u32[]{:S(2)}) collective-permute-start(bf16[2,2,32,2,256]{4,2,3,1,0:T(8,128)(2,1)S(1)} %fusion.69), channel_id=1, source_target_pairs={{0,8},{4,12},{8,0},{12,4},{16,24},{20,28},{24,16},{28,20},{1,9},{5... | collective-permute-start | bytes 393224 | tf_op jit(solution)/shard_map/ppermute | solution.py:29
  142.9 5.0 %collective-permute-start.17 = (bf16[2,2,32,2,256]{4,2,3,1,0:T(8,128)(2,1)S(1)}, bf16[2,2,32,2,256]{4,2,3,1,0:T(8,128)(2,1)S(1)}, u32[]{:S(2)}, u32[]{:S(2)}) collective-permute-start(bf16[2,2,32,2,256]{4,2,3,1,0:T(8,128)(2,1)S(1)} %fusion.70), channel_id=1, source_target_pairs={{0,16},{4,20},{8,24},{12,28},{16,0},{20,4},{24,8},{28,12},{1,17},{... | collective-permute-start | bytes 393224 | tf_op jit(solution)/shard_map/ppermute | solution.py:29
  148.0 5.0 %collective-permute-start.18 = (bf16[2,32,2,512]{3,1,2,0:T(8,128)(2,1)S(1)}, bf16[2,32,2,512]{3,1,2,0:T(8,128)(2,1)S(1)}, u32[]{:S(2)}, u32[]{:S(2)}) collective-permute-start(bf16[2,32,2,512]{3,1,2,0:T(8,128)(2,1)S(1)} %fusion.71), channel_id=1, source_target_pairs={{0,1},{1,0},{2,3},{3,2},{4,5},{5,4},{6,7},{7,6},{8,9},{9,8},{10,11... | collective-permute-start | bytes 393224 | tf_op jit(solution)/shard_map/ppermute | solution.py:29
  153.1 5.2 %collective-permute-start.19 = (bf16[32,2,512]{2,0,1:T(8,128)(2,1)S(1)}, bf16[32,2,512]{2,0,1:T(8,128)(2,1)S(1)}, u32[]{:S(2)}, u32[]{:S(2)}) collective-permute-start(bf16[32,2,512]{2,0,1:T(8,128)(2,1)S(1)} %fusion.73), channel_id=1, source_target_pairs={{0,2},{1,3},{2,0},{3,1},{4,6},{5,7},{6,4},{7,5},{8,10},{9,11},{10,... | collective-permute-start | bytes 196616 | tf_op jit(solution)/shard_map/ppermute | solution.py:29
  (7 other events, 20.2 us)

commit v23 on v21

--- a/solution.py
+++ b/solution.py
@@ -79,14 +79,15 @@
     if tail_first:
         value, names, tally = run_tail(value, names, tally)
     if balance and len(middle) > 1 and rest[-1] % 2 == 0:
-        cut = rest[-1] // 2
-        left, right = value[..., :cut], value[..., cut:]
+        axis = -2 if len(rest) > 1 and rest[-2] % 2 == 0 else -1
+        cut = rest[axis] // 2
+        left, right = jnp.split(value, [cut], axis=axis)
         left_names, right_names = list(names), list(names)
         for a, b in zip(middle, middle[::-1]):
             left, left_names = step(left, left_names, a, wire_type)
             tally, left = count_along(tally, left, a)
             right, right_names = step(right, right_names, b, wire_type)
-        value = jnp.concatenate([left, right], axis=-1)
+        value = jnp.concatenate([left, right], axis=axis)
         names = left_names
     else:
         for stage in middle:

time: 159 us -> 159 us (level)
  no operation moved by 1% of the time
where the time goes in v23:
time: 159 us; the launch traced here: 158 us
  waiting for transfers between devices  62.8 us (39%)
  starting transfers between devices  36.9 us (23%)
  matrix products  28.8 us (18%)
  local copies, waits for them, and re-layouts  15.8 us (10%)
  other arithmetic  10.9 us (7%)
  between operations  2.68 us (2%)
    ppermute x12, waiting for transfers between devices, halve(): lax.ppermute(send.astype(send_type), axis, pairs).astype(keep.dtype)  48.3 us
    ppermute x8, starting transfers between devices, shifted(): return lax.ppermute(value, axis, pairs)  19.4 us
    ppermute x12, starting transfers between devices, halve(): lax.ppermute(send.astype(send_type), axis, pairs).astype(keep.dtype)  17.5 us
    ppermute x8, waiting for transfers between devices, shifted(): return lax.ppermute(value, axis, pairs)  14.6 us
    unnamed x24, local copies, waits for them, and re-layouts  7.02 us
    dot_general x1, matrix products, shards(): jnp.einsum('rd,dwh->wrh', grad_out, weights, preferred_element_type=jnp.f...  4.81 us
    dot_general x1, matrix products, shards(): jnp.einsum('rd,dwh->wrh', normed, weights, preferred_element_type=jnp.flo...  3.98 us
    dot_general x1, matrix products, band_block(): jnp.einsum('qgc,kgc->gqk', queries, keys_blk, preferred_element_type=jnp....  3.91 us
  transfers between devices with their start and end apart: 20, of which 14 were waited for; matrix products, arithmetic and copies ran while one was open for 14% of the time, Pallas kernels for 0%

profile of v23, /device:TPU:0, one launch (start us, length us, event | category | flops | bytes accessed | tf_op | source)
XLA Modules:
  0.0 157.9 jit_solution(3419765393760295734)
XLA Ops:
  1.9 4.0 %fusion.21 = bf16[4,256,512]{2,1,0:T(8,128)(2,1)S(1)} fusion(bf16[1024,4,512]{2,1,0:T(4,128)(2,1)} %param.7, bf16[1,256,1024]{2,1,0:T(8,128)(2,1)} %param.6, f32[256]{0:T(256)S(1)} %add_rsqrt_fusion), kind=kOutput, calls=%fused_computation.24 | convolution fusion | flops 1075052544 | bytes 5768192 | tf_op jit(solution)/shard_map/rd,dwh->wrh/dot_general | solution.py:143
  6.7 5.7 %collective-permute-start = (bf16[2,256,512]{2,1,0:T(8,128)(2,1)}, bf16[2,256,512]{2,1,0:T(8,128)(2,1)}, u32[]{:S(2)}, u32[]{:S(2)}) collective-permute-start(bf16[2,256,512]{2,1,0:T(8,128)(2,1)} %slice.112), channel_id=1, source_target_pairs={{0,16},{4,20},{8,24},{12,28},{1,17},{5,21},{9,25},{13,29},{2,18},{... | collective-permute-start | bytes 1572872 | tf_op jit(solution)/shard_map/ppermute | solution.py:16
  12.4 3.4 %collective-permute-start.1 = (bf16[2,256,512]{2,1,0:T(8,128)(2,1)}, bf16[2,256,512]{2,1,0:T(8,128)(2,1)}, u32[]{:S(2)}, u32[]{:S(2)}) collective-permute-start(bf16[2,256,512]{2,1,0:T(8,128)(2,1)} %slice.112), channel_id=1, source_target_pairs={{0,12},{4,16},{8,20},{12,24},{16,28},{1,13},{5,17},{9,21},{13,25},... | collective-permute-start | bytes 1572872 | tf_op jit(solution)/shard_map/ppermute | solution.py:16
  15.7 2.9 %collective-permute-start.2 = (bf16[2,256,512]{2,1,0:T(8,128)(2,1)}, bf16[2,256,512]{2,1,0:T(8,128)(2,1)}, u32[]{:S(2)}, u32[]{:S(2)}) collective-permute-start(bf16[2,256,512]{2,1,0:T(8,128)(2,1)} %slice.112), channel_id=1, source_target_pairs={{0,8},{4,12},{8,16},{12,20},{16,24},{20,28},{1,9},{5,13},{9,17},{1... | collective-permute-start | bytes 1572872 | tf_op jit(solution)/shard_map/ppermute | solution.py:16
  22.0 4.8 %fusion.18 = bf16[4,256,512]{2,1,0:T(8,128)(2,1)} fusion(bf16[1024,4,512]{2,1,0:T(4,128)(2,1)} %param.7, bf16[1,256,1024]{2,1,0:T(8,128)(2,1)S(1)} %copy-done.5, pred[256]{0:T(512)(128)(4,1)S(1)} %compare_reduce_fusion), kind=kOutput, calls=%fused_computation.23 | convolution fusion | flops 1074528256 | bytes 5767424 | tf_op jit(solution)/shard_map/rd,dwh->wrh/dot_general | solution.py:155
  33.3 13.4 %collective-permute-done = bf16[2,256,512]{2,1,0:T(8,128)(2,1)} collective-permute-done((bf16[2,256,512]{2,1,0:T(8,128)(2,1)}, bf16[2,256,512]{2,1,0:T(8,128)(2,1)}, u32[]{:S(2)}, u32[]{:S(2)}) %collective-permute-start) | collective-permute-done | bytes 524320 | tf_op jit(solution)/shard_map/ppermute | solution.py:16
  55.3 3.9 %fusion.1 = (f32[8,256]{1,0:T(8,128)S(1)}, f32[8,256,1280]{2,1,0:T(8,128)S(1)}) fusion(f32[256,1280]{1,0:T(8,128)} %fusion.37, bf16[256,8,64]{0,2,1:T(8,128)(2,1)S(1)} %bitcast.199, bf16[1280,8,64]{0,2,1:T(8,128)(2,1)S(1)} %bitcast.196), kind=kOutput, calls=%fused_computation.3 | convolution fusion | flops 343406592 | bytes 13377536 | tf_op jit(solution)/shard_map/qgc,kgc->gqk/dot_general | solution.py:103
  59.3 2.8 %multiply_reduce_fusion = (f32[256,8]{0,1:T(8,128)S(1)}, bf16[8,64,256]{2,1,0:T(8,128)(2,1)S(1)}) fusion(bf16[256,8,64]{0,2,1:T(8,128)(2,1)S(1)} %bitcast.209, bf16[1280,8,64]{0,2,1:T(8,128)(2,1)S(1)} %bitcast.206, f32[8,256]{1,0:T(8,128)S(1)} %get-tuple-element.34, f32[256,1280]{1,0:T(8,128)S(1)} %copy-done, f32[8,256,1280]{2,1,0:T(8,128)S(1)} %get-tuple-element.35), kind=kOutput, calls=%fused_computation.79 | convolution fusion | flops 346683392 | bytes 13647872 | tf_op jit(solution)/shard_map/gqk,kgc->qgc/dot_general | solution.py:109
  62.1 3.9 %multiply_convert_fusion = bf16[8,256,1280]{2,1,0:T(8,128)(2,1)S(1)} fusion(bf16[256,8,64]{0,2,1:T(8,128)(2,1)S(1)} %bitcast.210, bf16[1280,8,64]{0,2,1:T(8,128)(2,1)S(1)} %bitcast.207, f32[8,256]{1,0:T(8,128)S(1)} %bitcast.213, f32[8,256]{1,0:T(8,128)S(1)} %get-tuple-element.34, f32[256,1280]{1,0:T(8,128)S(1)} %copy-done, ...), kind=kOutput, calls=%fused_computation | convolution fusion | flops 353894400 | bytes 18628608 | tf_op jit(solution)/shard_map/qgc,kgc->gqk/dot_general | solution.py:113
  71.3 3.6 %collective-permute-start.4 = (bf16[2,2,2,2,40,2,512]{6,4,5,1,0,2,3:T(8,128)(2,1)S(1)}, bf16[2,2,2,2,40,2,512]{6,4,5,1,0,2,3:T(8,128)(2,1)S(1)}, u32[]{:S(2)}, u32[]{:S(2)}) collective-permute-start(bf16[2,2,2,2,40,2,512]{6,4,5,1,0,2,3:T(8,128)(2,1)S(1)} %fusion.32), channel_id=1, source_target_pairs={{0,4},{4,0},{8,12},{12,8},{16,20},{20,16},{24,28},{28,24},{1,5},{5... | collective-permute-start | bytes 3932168 | tf_op jit(solution)/shard_map/ppermute | solution.py:29
  74.8 2.3 %fusion.90 = (bf16[8,64,1280]{2,1,0:T(8,128)(2,1)S(1)}, f32[8,64,1280]{2,1,0:T(8,128)S(1)}) fusion(bf16[256,8,64]{0,2,1:T(8,128)(2,1)S(1)} %bitcast.211, f32[8,256]{1,0:T(8,128)S(1)} %get-tuple-element.34, f32[256,1280]{1,0:T(8,128)S(1)} %copy-done, f32[8,256,1280]{2,1,0:T(8,128)S(1)} %get-tuple-element.35), kind=kOutput, calls=%fused_computation.163 | convolution fusion | flops 346685440 | bytes 15998976 | tf_op jit(solution)/shard_map/gqk,qgc->gck/dot_general | solution.py:123
  85.5 9.7 %collective-permute-done.5 = bf16[2,2,2,40,2,512]{5,3,4,1,0,2:T(8,128)(2,1)S(1)} collective-permute-done((bf16[2,2,2,40,2,512]{5,3,4,1,0,2:T(8,128)(2,1)S(1)}, bf16[2,2,2,40,2,512]{5,3,4,1,0,2:T(8,128)(2,1)S(1)}, u32[]{:S(2)}, u32[]{:S(2)}) %collective-permute-start.5) | collective-permute-done | bytes 655392 | tf_op jit(solution)/shard_map/ppermute | solution.py:29
  95.4 2.7 %collective-permute-start.6 = (bf16[2,2,40,2,512]{4,2,3,1,0:T(8,128)(2,1)S(1)}, bf16[2,2,40,2,512]{4,2,3,1,0:T(8,128)(2,1)S(1)}, u32[]{:S(2)}, u32[]{:S(2)}) collective-permute-start(bf16[2,2,40,2,512]{4,2,3,1,0:T(8,128)(2,1)S(1)} %fusion.58), channel_id=1, source_target_pairs={{0,2},{1,3},{2,0},{3,1},{4,6},{5,7},{6,4},{7,5},{8,10},{9,11},{10,... | collective-permute-start | bytes 983048 | tf_op jit(solution)/shard_map/ppermute | solution.py:29
  99.8 12.7 %collective-permute-done.6 = bf16[2,2,40,2,512]{4,2,3,1,0:T(8,128)(2,1)S(1)} collective-permute-done((bf16[2,2,40,2,512]{4,2,3,1,0:T(8,128)(2,1)S(1)}, bf16[2,2,40,2,512]{4,2,3,1,0:T(8,128)(2,1)S(1)}, u32[]{:S(2)}, u32[]{:S(2)}) %collective-permute-start.6) | collective-permute-done | bytes 327712 | tf_op jit(solution)/shard_map/ppermute | solution.py:29
  112.7 2.3 %collective-permute-start.7 = (bf16[2,40,2,512]{3,1,2,0:T(8,128)(2,1)S(1)}, bf16[2,40,2,512]{3,1,2,0:T(8,128)(2,1)S(1)}, u32[]{:S(2)}, u32[]{:S(2)}) collective-permute-start(bf16[2,40,2,512]{3,1,2,0:T(8,128)(2,1)S(1)} %fusion.69), channel_id=1, source_target_pairs={{0,16},{4,20},{8,24},{12,28},{16,0},{20,4},{24,8},{28,12},{1,17},{... | collective-permute-start | bytes 491528 | tf_op jit(solution)/shard_map/ppermute | solution.py:29
  115.0 2.7 %fusion.41 = (f32[256]{0:T(256)S(1)}, f32[256,1024]{1,0:T(8,128)}) fusion(bf16[1,256,1024]{2,1,0:T(8,128)(2,1)S(1)} %copy-done.1, f32[256]{0:T(256)S(1)} %add_rsqrt_fusion, bf16[4,256,512]{1,2,0:T(8,128)(2,1)S(1)} %bitcast.208, bf16[1024,4,512]{2,1,0:T(4,128)(2,1)S(1)} %copy-done.8), kind=kOutput, calls=%fused_computation.44 | convolution fusion | flops 1074790144 | bytes 6817792 | tf_op jit(solution)/shard_map/wrh,dwh->rd/dot_general | solution.py:210
  118.5 4.4 %collective-permute-done.8 = bf16[40,2,512]{2,0,1:T(8,128)(2,1)S(1)} collective-permute-done((bf16[40,2,512]{2,0,1:T(8,128)(2,1)S(1)}, bf16[40,2,512]{2,0,1:T(8,128)(2,1)S(1)}, u32[]{:S(2)}, u32[]{:S(2)}) %collective-permute-start.8) | collective-permute-done | bytes 81952 | tf_op jit(solution)/shard_map/ppermute | solution.py:29
  124.3 2.3 %fusion.67 = (bf16[1024,256]{0,1:T(8,128)(2,1)S(1)}, bf16[1,256,1024]{2,1,0:T(8,128)(2,1)}) fusion(f32[256]{0:T(256)S(1)} %add_rsqrt_fusion, bf16[1,256,1024]{2,1,0:T(8,128)(2,1)S(1)} %copy-done.1, f32[256,1024]{1,0:T(8,128)} %get-tuple-element.43, f32[256]{0:T(256)S(1)} %broadcast_multiply_fusion.1, f32[256]{0:T(256)S(1)} %broadcast_multiply_fusion), kind=kLoop, calls=%fused_computation.106 | loop fusion | flops 1835008 | bytes 2624512 | tf_op jit(solution)/shard_map/rd,wgcr->dwgc/dot_general | solution.py:215
  127.8 2.6 %collective-permute-done.13 = bf16[2,2,2,2,32,2,512]{6,4,5,3,2,1,0:T(8,128)(2,1)S(1)} collective-permute-done((bf16[2,2,2,2,32,2,512]{6,4,5,3,2,1,0:T(8,128)(2,1)S(1)}, bf16[2,2,2,2,32,2,512]{6,4,5,3,2,1,0:T(8,128)(2,1)S(1)}, u32[]{:S(2)}, u32[]{:S(2)}) %collective-permute-start.13) | collective-permute-done | bytes 1048608 | tf_op jit(solution)/shard_map/ppermute | solution.py:29
  133.3 6.5 %collective-permute-done.14 = bf16[2,2,2,32,1,512]{5,3,2,1,4,0:T(8,128)(2,1)S(1)} collective-permute-done((bf16[2,2,2,32,1,512]{5,3,2,1,4,0:T(8,128)(2,1)S(1)}, bf16[2,2,2,32,1,512]{5,3,2,1,4,0:T(8,128)(2,1)S(1)}, u32[]{:S(2)}, u32[]{:S(2)}) %collective-permute-start.14) | collective-permute-done | bytes 262176 | tf_op jit(solution)/shard_map/ppermute | solution.py:29
  142.0 3.1 %collective-permute-done.15 = bf16[2,2,32,1,512]{4,2,1,0,3:T(8,128)(2,1)S(1)} collective-permute-done((bf16[2,2,32,1,512]{4,2,1,0,3:T(8,128)(2,1)S(1)}, bf16[2,2,32,1,512]{4,2,1,0,3:T(8,128)(2,1)S(1)}, u32[]{:S(2)}, u32[]{:S(2)}) %collective-permute-start.15) | collective-permute-done | bytes 131104 | tf_op jit(solution)/shard_map/ppermute | solution.py:29
  148.2 3.5 %collective-permute-done.18 = bf16[2,32,2,512]{3,1,0,2:T(8,128)(2,1)S(1)} collective-permute-done((bf16[2,32,2,512]{3,1,0,2:T(8,128)(2,1)S(1)}, bf16[2,32,2,512]{3,1,0,2:T(8,128)(2,1)S(1)}, u32[]{:S(2)}, u32[]{:S(2)}) %collective-permute-start.18) | collective-permute-done | bytes 131104 | tf_op jit(solution)/shard_map/ppermute | solution.py:29
  151.7 2.9 %collective-permute-start.19 = (bf16[32,2,512]{2,0,1:T(8,128)(2,1)S(1)}, bf16[32,2,512]{2,0,1:T(8,128)(2,1)S(1)}, u32[]{:S(2)}, u32[]{:S(2)}) collective-permute-start(bf16[32,2,512]{2,0,1:T(8,128)(2,1)S(1)} %fusion.74), channel_id=1, source_target_pairs={{0,2},{1,3},{2,0},{3,1},{4,6},{5,7},{6,4},{7,5},{8,10},{9,11},{10,... | collective-permute-start | bytes 196616 | tf_op jit(solution)/shard_map/ppermute | solution.py:29
  154.7 2.3 %collective-permute-done.19 = bf16[32,2,512]{2,0,1:T(8,128)(2,1)S(1)} collective-permute-done((bf16[32,2,512]{2,0,1:T(8,128)(2,1)S(1)}, bf16[32,2,512]{2,0,1:T(8,128)(2,1)S(1)}, u32[]{:S(2)}, u32[]{:S(2)}) %collective-permute-start.19) | collective-permute-done | bytes 65568 | tf_op jit(solution)/shard_map/ppermute | solution.py:29
  (116 shorter events, 46.9 us)
Async XLA Ops:
  1.9 18.9 %copy-start.7 = (s32[1,256]{1,0:T(1,128)S(1)}, s32[1,256]{1,0:T(1,128)}, u32[]{:S(2)}) copy-start(s32[1,256]{1,0:T(1,128)} %param.9) | copy-start | bytes 3076
  1.9 20.1 %copy-start.5 = (bf16[1,256,1024]{2,1,0:T(8,128)(2,1)S(1)}, bf16[1,256,1024]{2,1,0:T(8,128)(2,1)}, u32[]{:S(2)}) copy-start(bf16[1,256,1024]{2,1,0:T(8,128)(2,1)} %param.8) | copy-start | bytes 1572868
  6.7 40.0 %collective-permute-start = (bf16[2,256,512]{2,1,0:T(8,128)(2,1)}, bf16[2,256,512]{2,1,0:T(8,128)(2,1)}, u32[]{:S(2)}, u32[]{:S(2)}) collective-permute-start(bf16[2,256,512]{2,1,0:T(8,128)(2,1)} %slice.112), channel_id=1, source_target_pairs={{0,16},{4,20},{8,24},{12,28},{1,17},{5,21},{9,25},{13,29},{2,18},{... | collective-permute-start | bytes 1572872 | tf_op jit(solution)/shard_map/ppermute | solution.py:16
  12.4 35.4 %collective-permute-start.1 = (bf16[2,256,512]{2,1,0:T(8,128)(2,1)}, bf16[2,256,512]{2,1,0:T(8,128)(2,1)}, u32[]{:S(2)}, u32[]{:S(2)}) collective-permute-start(bf16[2,256,512]{2,1,0:T(8,128)(2,1)} %slice.112), channel_id=1, source_target_pairs={{0,12},{4,16},{8,20},{12,24},{16,28},{1,13},{5,17},{9,21},{13,25},... | collective-permute-start | bytes 1572872 | tf_op jit(solution)/shard_map/ppermute | solution.py:16
  15.7 33.1 %collective-permute-start.2 = (bf16[2,256,512]{2,1,0:T(8,128)(2,1)}, bf16[2,256,512]{2,1,0:T(8,128)(2,1)}, u32[]{:S(2)}, u32[]{:S(2)}) collective-permute-start(bf16[2,256,512]{2,1,0:T(8,128)(2,1)} %slice.112), channel_id=1, source_target_pairs={{0,8},{4,12},{8,16},{12,20},{16,24},{20,28},{1,9},{5,13},{9,17},{1... | collective-permute-start | bytes 1572872 | tf_op jit(solution)/shard_map/ppermute | solution.py:16
  18.7 31.3 %collective-permute-start.3 = (bf16[2,256,512]{2,1,0:T(8,128)(2,1)}, bf16[2,256,512]{2,1,0:T(8,128)(2,1)}, u32[]{:S(2)}, u32[]{:S(2)}) collective-permute-start(bf16[2,256,512]{2,1,0:T(8,128)(2,1)} %slice.112), channel_id=1, source_target_pairs={{0,4},{4,8},{8,12},{12,16},{16,20},{20,24},{24,28},{1,5},{5,9},{9,... | collective-permute-start | bytes 1572872 | tf_op jit(solution)/shard_map/ppermute | solution.py:16
  22.0 4.8 %copy-start.1 = (bf16[1,256,1024]{2,1,0:T(8,128)(2,1)S(1)}, bf16[1,256,1024]{2,1,0:T(8,128)(2,1)}, u32[]{:S(2)}) copy-start(bf16[1,256,1024]{2,1,0:T(8,128)(2,1)} %param.6) | copy-start | bytes 1572868
  71.3 6.2 %collective-permute-start.4 = (bf16[2,2,2,2,40,2,512]{6,4,5,1,0,2,3:T(8,128)(2,1)S(1)}, bf16[2,2,2,2,40,2,512]{6,4,5,1,0,2,3:T(8,128)(2,1)S(1)}, u32[]{:S(2)}, u32[]{:S(2)}) collective-permute-start(bf16[2,2,2,2,40,2,512]{6,4,5,1,0,2,3:T(8,128)(2,1)S(1)} %fusion.32), channel_id=1, source_target_pairs={{0,4},{4,0},{8,12},{12,8},{16,20},{20,16},{24,28},{28,24},{1,5},{5... | collective-permute-start | bytes 3932168 | tf_op jit(solution)/shard_map/ppermute | solution.py:29
  78.0 17.1 %collective-permute-start.5 = (bf16[2,2,2,40,2,512]{5,3,4,1,0,2:T(8,128)(2,1)S(1)}, bf16[2,2,2,40,2,512]{5,3,4,1,0,2:T(8,128)(2,1)S(1)}, u32[]{:S(2)}, u32[]{:S(2)}) collective-permute-start(bf16[2,2,2,40,2,512]{5,3,4,1,0,2:T(8,128)(2,1)S(1)} %fusion.52), channel_id=1, source_target_pairs={{0,1},{1,0},{2,3},{3,2},{4,5},{5,4},{6,7},{7,6},{8,9},{9,8},{10,11... | collective-permute-start | bytes 1966088 | tf_op jit(solution)/shard_map/ppermute | solution.py:29
  79.8 18.3 %collective-permute-start.12 = (bf16[2,8,64,256]{3,2,1,0:T(8,128)(2,1)S(1)}, bf16[2,8,64,256]{3,2,1,0:T(8,128)(2,1)S(1)}, u32[]{:S(2)}, u32[]{:S(2)}) collective-permute-start(bf16[2,8,64,256]{3,2,1,0:T(8,128)(2,1)S(1)} %pad_maximum_fusion.4), channel_id=1, source_target_pairs={{16,0},{20,4},{24,8},{28,12},{17,1},{21,5},{25,9},{29,13},{18,2},{... | collective-permute-start | bytes 1572872 | tf_op jit(solution)/shard_map/ppermute | solution.py:16
  81.1 16.9 %collective-permute-start.11 = (bf16[2,8,64,256]{3,2,1,0:T(8,128)(2,1)S(1)}, bf16[2,8,64,256]{3,2,1,0:T(8,128)(2,1)S(1)}, u32[]{:S(2)}, u32[]{:S(2)}) collective-permute-start(bf16[2,8,64,256]{3,2,1,0:T(8,128)(2,1)S(1)} %pad_maximum_fusion.3), channel_id=1, source_target_pairs={{12,0},{16,4},{20,8},{24,12},{28,16},{13,1},{17,5},{21,9},{25,13},... | collective-permute-start | bytes 1572872 | tf_op jit(solution)/shard_map/ppermute | solution.py:16
  82.5 16.8 %collective-permute-start.10 = (bf16[2,8,64,256]{3,2,1,0:T(8,128)(2,1)S(1)}, bf16[2,8,64,256]{3,2,1,0:T(8,128)(2,1)S(1)}, u32[]{:S(2)}, u32[]{:S(2)}) collective-permute-start(bf16[2,8,64,256]{3,2,1,0:T(8,128)(2,1)S(1)} %pad_maximum_fusion.2), channel_id=1, source_target_pairs={{8,0},{12,4},{16,8},{20,12},{24,16},{28,20},{9,1},{13,5},{17,9},{2... | collective-permute-start | bytes 1572872 | tf_op jit(solution)/shard_map/ppermute | solution.py:16
  83.8 15.4 %collective-permute-start.9 = (bf16[2,8,64,256]{3,2,1,0:T(8,128)(2,1)S(1)}, bf16[2,8,64,256]{3,2,1,0:T(8,128)(2,1)S(1)}, u32[]{:S(2)}, u32[]{:S(2)}) collective-permute-start(bf16[2,8,64,256]{3,2,1,0:T(8,128)(2,1)S(1)} %pad_maximum_fusion.1), channel_id=1, source_target_pairs={{4,0},{8,4},{12,8},{16,12},{20,16},{24,20},{28,24},{5,1},{9,5},{13... | collective-permute-start | bytes 1572872 | tf_op jit(solution)/shard_map/ppermute | solution.py:16
  95.4 17.2 %collective-permute-start.6 = (bf16[2,2,40,2,512]{4,2,3,1,0:T(8,128)(2,1)S(1)}, bf16[2,2,40,2,512]{4,2,3,1,0:T(8,128)(2,1)S(1)}, u32[]{:S(2)}, u32[]{:S(2)}) collective-permute-start(bf16[2,2,40,2,512]{4,2,3,1,0:T(8,128)(2,1)S(1)} %fusion.58), channel_id=1, source_target_pairs={{0,2},{1,3},{2,0},{3,1},{4,6},{5,7},{6,4},{7,5},{8,10},{9,11},{10,... | collective-permute-start | bytes 983048 | tf_op jit(solution)/shard_map/ppermute | solution.py:29
  99.2 15.8 %copy-start.8 = (bf16[1024,4,512]{2,1,0:T(4,128)(2,1)S(1)}, bf16[1024,4,512]{2,1,0:T(4,128)(2,1)}, u32[]{:S(2)}) copy-start(bf16[1024,4,512]{2,1,0:T(4,128)(2,1)} %param.7) | copy-start | bytes 12582916
  112.7 5.6 %collective-permute-start.7 = (bf16[2,40,2,512]{3,1,2,0:T(8,128)(2,1)S(1)}, bf16[2,40,2,512]{3,1,2,0:T(8,128)(2,1)S(1)}, u32[]{:S(2)}, u32[]{:S(2)}) collective-permute-start(bf16[2,40,2,512]{3,1,2,0:T(8,128)(2,1)S(1)} %fusion.69), channel_id=1, source_target_pairs={{0,16},{4,20},{8,24},{12,28},{16,0},{20,4},{24,8},{28,12},{1,17},{... | collective-permute-start | bytes 491528 | tf_op jit(solution)/shard_map/ppermute | solution.py:29
  118.4 4.5 %collective-permute-start.8 = (bf16[40,2,512]{2,0,1:T(8,128)(2,1)S(1)}, bf16[40,2,512]{2,0,1:T(8,128)(2,1)S(1)}, u32[]{:S(2)}, u32[]{:S(2)}) collective-permute-start(bf16[40,2,512]{2,0,1:T(8,128)(2,1)S(1)} %fusion.73), channel_id=1, source_target_pairs={{0,8},{4,12},{8,0},{12,4},{16,24},{20,28},{24,16},{28,20},{1,9},{5... | collective-permute-start | bytes 245768 | tf_op jit(solution)/shard_map/ppermute | solution.py:29
  127.7 2.7 %collective-permute-start.13 = (bf16[2,2,2,2,32,2,512]{6,4,5,3,2,1,0:T(8,128)(2,1)S(1)}, bf16[2,2,2,2,32,2,512]{6,4,5,3,2,1,0:T(8,128)(2,1)S(1)}, u32[]{:S(2)}, u32[]{:S(2)}) collective-permute-start(bf16[2,2,2,2,32,2,512]{6,4,5,3,2,1,0:T(8,128)(2,1)S(1)} %fusion.47), channel_id=1, source_target_pairs={{0,4},{4,0},{8,12},{12,8},{16,20},{20,16},{24,28},{28,24},{1,5},{5... | collective-permute-start | bytes 3145736 | tf_op jit(solution)/shard_map/ppermute | solution.py:29
  131.1 8.7 %collective-permute-start.14 = (bf16[2,2,2,32,1,512]{5,3,2,1,4,0:T(8,128)(2,1)S(1)}, bf16[2,2,2,32,1,512]{5,3,2,1,4,0:T(8,128)(2,1)S(1)}, u32[]{:S(2)}, u32[]{:S(2)}) collective-permute-start(bf16[2,2,2,32,1,512]{5,3,2,1,4,0:T(8,128)(2,1)S(1)} %fusion.60), channel_id=1, source_target_pairs={{0,16},{4,20},{8,24},{12,28},{16,0},{20,4},{24,8},{28,12},{1,17},{... | collective-permute-start | bytes 786440 | tf_op jit(solution)/shard_map/ppermute | solution.py:29
  133.3 8.1 %collective-permute-start.16 = (bf16[2,2,2,32,1,512]{5,3,2,1,0,4:T(8,128)(2,1)S(1)}, bf16[2,2,2,32,1,512]{5,3,2,1,0,4:T(8,128)(2,1)S(1)}, u32[]{:S(2)}, u32[]{:S(2)}) collective-permute-start(bf16[2,2,2,32,1,512]{5,3,2,1,0,4:T(8,128)(2,1)S(1)} %fusion.59), channel_id=1, source_target_pairs={{0,8},{4,12},{8,0},{12,4},{16,24},{20,28},{24,16},{28,20},{1,9},{5... | collective-permute-start | bytes 786440 | tf_op jit(solution)/shard_map/ppermute | solution.py:29
  140.0 5.1 %collective-permute-start.15 = (bf16[2,2,32,1,512]{4,2,1,0,3:T(8,128)(2,1)S(1)}, bf16[2,2,32,1,512]{4,2,1,0,3:T(8,128)(2,1)S(1)}, u32[]{:S(2)}, u32[]{:S(2)}) collective-permute-start(bf16[2,2,32,1,512]{4,2,1,0,3:T(8,128)(2,1)S(1)} %fusion.70), channel_id=1, source_target_pairs={{0,8},{4,12},{8,0},{12,4},{16,24},{20,28},{24,16},{28,20},{1,9},{5... | collective-permute-start | bytes 393224 | tf_op jit(solution)/shard_map/ppermute | solution.py:29
  141.5 5.0 %collective-permute-start.17 = (bf16[2,2,32,1,512]{4,2,1,0,3:T(8,128)(2,1)S(1)}, bf16[2,2,32,1,512]{4,2,1,0,3:T(8,128)(2,1)S(1)}, u32[]{:S(2)}, u32[]{:S(2)}) collective-permute-start(bf16[2,2,32,1,512]{4,2,1,0,3:T(8,128)(2,1)S(1)} %fusion.71), channel_id=1, source_target_pairs={{0,16},{4,20},{8,24},{12,28},{16,0},{20,4},{24,8},{28,12},{1,17},{... | collective-permute-start | bytes 393224 | tf_op jit(solution)/shard_map/ppermute | solution.py:29
  146.6 5.0 %collective-permute-start.18 = (bf16[2,32,2,512]{3,1,0,2:T(8,128)(2,1)S(1)}, bf16[2,32,2,512]{3,1,0,2:T(8,128)(2,1)S(1)}, u32[]{:S(2)}, u32[]{:S(2)}) collective-permute-start(bf16[2,32,2,512]{3,1,0,2:T(8,128)(2,1)S(1)} %fusion.72), channel_id=1, source_target_pairs={{0,1},{1,0},{2,3},{3,2},{4,5},{5,4},{6,7},{7,6},{8,9},{9,8},{10,11... | collective-permute-start | bytes 393224 | tf_op jit(solution)/shard_map/ppermute | solution.py:29
  151.7 5.2 %collective-permute-start.19 = (bf16[32,2,512]{2,0,1:T(8,128)(2,1)S(1)}, bf16[32,2,512]{2,0,1:T(8,128)(2,1)S(1)}, u32[]{:S(2)}, u32[]{:S(2)}) collective-permute-start(bf16[32,2,512]{2,0,1:T(8,128)(2,1)S(1)} %fusion.74), channel_id=1, source_target_pairs={{0,2},{1,3},{2,0},{3,1},{4,6},{5,7},{6,4},{7,5},{8,10},{9,11},{10,... | collective-permute-start | bytes 196616 | tf_op jit(solution)/shard_map/ppermute | solution.py:29
  (6 other events, 18.2 us)
